TPU v7x, 256 devices: a whole 4x4x8 slice. The times are simulated.
256 devices in a mesh: row: 4 (over x), col: 16 (over y_lo, z), batch: 4 (over y_hi, core).
Axes of the slice: x: 4, y: 4 (y_hi: 2, y_lo: 2; y = y_hi * 2 + y_lo), z: 8, core: 2. Of those that a mesh axis runs over, the one named last changes fastest.
Arguments:
- grid_feats: bfloat16 [4, 128, 1024, 128], P('batch', 'row', 'col'), may hold values from -6 to 6
- station_values: bfloat16 [4, 40960, 512], P('batch', ('row', 'col')), may hold values from -6 to 6
- station_tile: int32 [4, 40960, 1], P('batch', ('row', 'col')), may hold values from 0 to 63; in each aligned block of 640 rows (0 to 639, 640 to 1279, ..., all dimensions but the last counted through in order) at most 20 rows name the same one
- station_cell: int32 [4, 40960], P('batch', ('row', 'col')), may hold values from 0 to 2047
- w_embed: bfloat16 [512, 128], replicated, may hold values from -0.25 to 0.25
- w_first: bfloat16 [3, 3, 128, 128], replicated, may hold values from -0.1875 to 0.1875
- w_second: bfloat16 [3, 3, 128, 128], replicated, may hold values from -0.1875 to 0.1875
- cotangent: bfloat16 [4, 128, 1024, 128], P('batch', 'row', 'col'), may hold values from -6 to 6
Outputs:
- output: bfloat16 [4, 128, 1024, 128], P('batch', 'row', 'col')
- grad_first: float32 [3, 3, 128, 128], replicated
- grad_second: float32 [3, 3, 128, 128], replicated
Inputs may be any that keep to these rules, and one draw needn't show every extreme that they name: `station_tile`: within the 640 reports of one device (aligned blocks of 640 rows), at most 20 name the same tile, a bound that some block reaches.
All inputs are finite; a program needn't handle non-finite values.
Results may differ from a plain program's by a relative error of at most 0.0054.
Values may be sent and summed in bfloat16 or wider, within the bound.
No kernel may reach another device: no remote copies, remote signals or barrier semaphores. Data moves between devices by JAX's collectives and lax.ppermute only.
A program may use at most 128 MiB of HBM per device.

v0:
```python
import math

import jax
import jax.numpy as jnp
from jax import lax
from jax.sharding import PartitionSpec as P


def with_halo(array, sides, width):
    for axis, dim in sides:
        count, length = (lax.axis_size(axis), array.shape[dim])
        up = [(i, (i + 1) % count) for i in range(count - 1)]
        down = [(j, i) for i, j in up]
        last = lax.slice_in_dim(array, length - width, length, axis=dim)
        leading = lax.slice_in_dim(array, 0, width, axis=dim)
        before = lax.ppermute(last, axis, up)
        after = lax.ppermute(leading, axis, down)
        array = jnp.concatenate([before, array, after], axis=dim)
    return array


def unfold(padded, step, rows, cols):
    windows = [
        padded[step * u : step * u + rows, step * q : step * q + cols, :]
        for u in range(3)
        for q in range(3)
    ]
    return jnp.concatenate(windows, axis=-1).reshape(rows * cols, -1)


def contract_rows(left, right):
    return lax.dot_general(
        left, right, (((0,), (0,)), ((), ())), preferred_element_type=jnp.float32
    )


def on_device(
    grid_feats, station_values, station_tile, station_cell, w_embed, w_first, w_second, cotangent
):
    cells = grid_feats[0]
    rows, cols, chans = cells.shape
    values = station_values[0]
    tiles = station_tile[0, :, 0]
    where = station_cell[0]
    n_tiles = lax.axis_size("row") * lax.axis_size("col")
    count = values.shape[0]
    capacity = max(2, 2 * count // n_tiles)
    slots = n_tiles * capacity
    hits = (tiles[:, None] == jnp.arange(n_tiles, dtype=jnp.int32)[None, :]).astype(jnp.int32)
    ranks = jnp.sum(jnp.cumsum(hits, axis=0) * hits, axis=1) - 1
    target = tiles * capacity + ranks
    cell_ids = jnp.zeros((slots,), jnp.int32).at[target].set(where)
    local_rows = jnp.dot(values, w_embed, preferred_element_type=jnp.float32)
    outgoing = jnp.zeros((slots, chans), jnp.float32).at[target].set(local_rows)
    embedded, arrived_ids = (
        lax.all_to_all(outgoing, ("row", "col"), split_axis=0, concat_axis=0, tiled=True),
        lax.all_to_all(cell_ids, ("row", "col"), split_axis=0, concat_axis=0, tiled=True),
    )
    placed = jax.ops.segment_sum(embedded, arrived_ids, num_segments=rows * cols)
    first_in = (
        (cells.astype(jnp.float32).reshape(rows * cols, chans) + placed)
        .astype(jnp.bfloat16)
        .reshape(rows, cols, chans)
    )
    w_one = w_first.reshape(9 * chans, chans)
    w_two = w_second.reshape(9 * chans, chans)
    deep = with_halo(first_in, (("row", 0), ("col", 1)), 3)
    pre_wide = jnp.dot(
        unfold(deep, 1, rows + 4, cols + 4), w_one, preferred_element_type=jnp.float32
    ).reshape(rows + 4, cols + 4, chans)
    row_ids = lax.axis_index("row") * rows - 2 + jnp.arange(rows + 4, dtype=jnp.int32)
    col_ids = lax.axis_index("col") * cols - 2 + jnp.arange(cols + 4, dtype=jnp.int32)
    inside_rows = (row_ids >= 0) & (row_ids < rows * lax.axis_size("row"))
    inside_cols = (col_ids >= 0) & (col_ids < cols * lax.axis_size("col"))
    inside = inside_rows[:, None] & inside_cols[None, :]
    padded1 = jnp.where(inside[:, :, None], jax.nn.silu(pre_wide), 0.0).astype(jnp.bfloat16)
    pre1 = pre_wide[2:-2, 2:-2].reshape(rows * cols, chans)
    act1 = padded1[2:-2, 2:-2]
    patches0 = unfold(deep[2:-2, 2:-2], 1, rows, cols)
    patches1 = unfold(padded1, 2, rows, cols)
    pre2 = jnp.dot(patches1, w_two, preferred_element_type=jnp.float32)
    output = (
        (act1.astype(jnp.float32).reshape(rows * cols, chans) + pre2)
        .astype(jnp.bfloat16)
        .reshape(1, rows, cols, chans)
    )
    back = cotangent[0]
    padded_back = with_halo(back, (("row", 0), ("col", 1)), 2)
    w_turned = jnp.transpose(w_second[::-1, ::-1], (0, 1, 3, 2)).reshape(9 * chans, chans)
    back_flat = back.reshape(rows * cols, chans)
    grad_act1 = back_flat.astype(jnp.float32) + jnp.dot(
        unfold(padded_back, 2, rows, cols), w_turned, preferred_element_type=jnp.float32
    )
    sigmoid_pre = jax.nn.sigmoid(pre1)
    grad_pre1 = (grad_act1 * sigmoid_pre * (1.0 + pre1 * (1.0 - sigmoid_pre))).astype(jnp.bfloat16)
    first_term = contract_rows(patches0, grad_pre1)
    second_term = contract_rows(patches1, back_flat)
    first_sum, second_sum = lax.psum((first_term, second_term), ("row", "col", "batch"))
    total_cells = (
        rows
        * lax.axis_size("row")
        * cols
        * lax.axis_size("col")
        * lax.axis_size("batch")
        * cells_per_sample_factor(grid_feats)
    )
    scale = 1.0 / math.sqrt(total_cells)
    grad_first = (first_sum * scale).reshape(3, 3, chans, chans)
    grad_second = (second_sum * scale).reshape(3, 3, chans, chans)
    return (output, grad_first, grad_second)


def cells_per_sample_factor(grid_feats):
    return grid_feats.shape[0]


def solution(mesh):
    return jax.shard_map(
        on_device,
        mesh=mesh,
        in_specs=(
            P("batch", "row", "col", None),
            P("batch", ("row", "col"), None),
            P("batch", ("row", "col"), None),
            P("batch", ("row", "col")),
            P(),
            P(),
            P(),
            P("batch", "row", "col", None),
        ),
        out_specs=(P("batch", "row", "col", None), P(), P()),
        check_vma=False,
    )
```

profile of v0, /device:TPU:1, one launch (start us, length us, event | category | flops | bytes accessed | tf_op | source)
XLA Modules:
  0.0 412.0 jit_solution(6331063639558545348)
XLA Ops:
  7.2 0.8 reduce
  8.0 1.5 reduce-window.6
  10.0 0.7 fusion.18
  10.7 0.7 reduce.4
  11.4 4.1 scatter_custom_fusion
  15.5 0.7 all_to_all.14
  16.2 13.5 %all-to-all-start = ((s32[64,20,1]{1,2,0:T(1,128)}), s32[64,20,1]{1,2,0:T(1,128)S(1)}, u32[]{:S(2)}, u32[]{:S(2)}) async-start(s32[64,20,1]{1,2,0:T(1,128)} %bitcast.3), calls=%async_computation | async-start | bytes 65536 | tf_op jit(solution)/shard_map/all_to_all | solution.py:57
  29.7 0.8 slice_bitcast_fusion.1
  30.5 2.9 collective-permute-start.4
  33.4 1.3 collective-permute-start.5
  34.7 1.1 bitcast_convert_fusion
  35.8 1.2 fusion.9
  37.2 4.3 %scatter_custom_fusion.1 = f32[1280,128]{1,0:T(8,128)S(1)} fusion(s32[640]{0:T(1024)S(1)} %fusion.18, f32[640,128]{1,0:T(8,128)S(1)} %fusion.9, f32[]{:T(128)} %constant.47.clone.1), kind=kCustom, calls=%fused_computation.46 | custom fusion | bytes 655364 | tf_op jit(solution)/shard_map/scatter | solution.py:54
  41.5 0.9 all_to_all.16
  42.4 1.2 copy.15
  43.6 0.8 rev.3
  44.4 11.8 %all-to-all-start.1 = ((f32[64,20,128]{2,1,0:T(8,128)}), f32[64,20,128]{2,1,0:T(8,128)S(1)}, u32[]{:S(2)}, u32[]{:S(2)}) async-start(f32[64,20,128]{2,1,0:T(8,128)} %all_to_all.16), calls=%async_computation.1 | async-start | bytes 1572864 | tf_op jit(solution)/shard_map/all_to_all | solution.py:56
  56.2 0.5 broadcast.131
  56.7 0.7 reduce.10
  57.6 2.9 collective-permute-start.6
  60.5 1.3 collective-permute-start.7
  61.9 5.8 %collective-permute-done.6 = bf16[36,2,128]{2,1,0:T(2,128)(2,1)S(1)} collective-permute-done((bf16[36,2,128]{2,1,0:T(2,128)(2,1)S(1)}, bf16[36,2,128]{2,1,0:T(2,128)(2,1)S(1)}, u32[]{:S(2)}, u32[]{:S(2)}) %collective-permute-start.6) | collective-permute-done | bytes 18464 | tf_op jit(solution)/shard_map/ppermute | solution.py:16
  67.7 5.1 %collective-permute-done.7 = bf16[36,2,128]{2,1,0:T(2,128)(2,1)S(1)} collective-permute-done((bf16[36,2,128]{2,1,0:T(2,128)(2,1)S(1)}, bf16[36,2,128]{2,1,0:T(2,128)(2,1)S(1)}, u32[]{:S(2)}, u32[]{:S(2)}) %collective-permute-start.7) | collective-permute-done | bytes 18464 | tf_op jit(solution)/shard_map/ppermute | solution.py:17
  72.8 0.4 pad_maximum_fusion.2
  73.1 0.6 fusion.21
  73.7 0.9 constant_dynamic-update-slice_fusion.18
  74.6 0.9 constant_dynamic-update-slice_fusion.17
  75.4 0.9 constant_dynamic-update-slice_fusion.16
  76.3 0.9 constant_dynamic-update-slice_fusion.15
  77.2 0.8 constant_dynamic-update-slice_fusion.14
  78.0 0.9 constant_dynamic-update-slice_fusion.13
  78.9 0.9 constant_dynamic-update-slice_fusion.12
  79.8 0.9 constant_dynamic-update-slice_fusion.11
  80.7 0.9 reshape.204
  81.6 9.6 %scatter_fusion = f32[2048,128]{1,0:T(8,128)S(1)} fusion(f32[2048,128]{1,0:T(8,128)S(1)} %bitcast_convert_fusion, s32[1280]{0:T(1024)S(1)} %reshape.202, f32[1280,128]{1,0:T(8,128)} %reshape.204), kind=kCustom, calls=%fused_computation.2 | custom fusion | flops 163840 | bytes 1971200 | tf_op jit(solution)/shard_map/scatter-add | solution.py:59
  91.2 3.1 collective-permute-start
  94.3 1.3 collective-permute-start.1
  95.6 0.9 constant_dynamic-update-slice_fusion.10
  96.5 2.6 collective-permute-done.1
  99.2 2.3 collective-permute-start.2
  101.5 1.5 collective-permute-start.3
  103.1 4.1 %collective-permute-done.3 = bf16[38,3,128]{2,1,0:T(4,128)(2,1)S(1)} collective-permute-done((bf16[38,3,128]{2,1,0:T(4,128)(2,1)S(1)}, bf16[38,3,128]{2,1,0:T(4,128)(2,1)S(1)}, u32[]{:S(2)}, u32[]{:S(2)}) %collective-permute-start.3) | collective-permute-done | bytes 29216 | tf_op jit(solution)/shard_map/ppermute | solution.py:17
  107.2 0.4 pad_maximum_fusion.1
  107.6 0.7 fusion.19
  108.3 0.9 constant_dynamic-update-slice_fusion.9
  109.2 0.9 constant_dynamic-update-slice_fusion.8
  110.1 0.9 constant_dynamic-update-slice_fusion.7
  111.0 0.9 constant_dynamic-update-slice_fusion.6
  111.9 0.9 constant_dynamic-update-slice_fusion.5
  112.8 0.3 pad_maximum_fusion
  113.2 0.3 slice_dynamic-update-slice_fusion.7
  115.4 2.2 select_convert_fusion
  117.8 1.3 fusion.6
  119.8 1.1 fusion.23
  121.8 2.3 fusion.25
  124.2 0.9 constant_dynamic-update-slice_fusion.4
  125.1 0.9 constant_dynamic-update-slice_fusion.3
  126.0 0.9 constant_dynamic-update-slice_fusion.2
  126.8 0.9 constant_dynamic-update-slice_fusion.1
  127.7 8.8 %fusion.8 = f32[1152,128]{1,0:T(8,128)} fusion(bf16[2048,1152]{1,0:T(8,128)(2,1)} %constant_dynamic-update-slice_fusion.1, f32[2048,128]{1,0:T(8,128)S(1)} %copy-done.3, f32[2048,128]{1,0:T(8,128)S(1)} %get-tuple-element.5, bf16[2048,1152]{1,0:T(8,128)(2,1)} %constant_dynamic-update-slice_fusion.10, bf16[1152,128]{1,0:T(8,128)(2,1)} %bitcast.118, ...), kind=kOutput, calls=%fused_computation.16 | convolution fusion | flops 1209270272 | bytes 12943360 | tf_op jit(solution)/shard_map/dot_general | solution.py:32
  136.5 4.7 %fusion.3 = bf16[2048,128]{1,0:T(8,128)(2,1)} fusion(bf16[2048,1152]{1,0:T(8,128)(2,1)} %bitcast.101, bf16[1152,128]{1,0:T(8,128)(2,1)} %bitcast.122, bf16[2048,128]{1,0:T(8,128)(2,1)} %bitcast.121), kind=kOutput, calls=%fused_computation.8 | convolution fusion | flops 604766208 | bytes 6062080 | tf_op jit(solution)/shard_map/dot_general | solution.py:81
  141.2 260.0 %all-reduce.3.cloned.1.call-done = (f32[1152,128]{1,0:T(8,128)}, f32[1152,128]{1,0:T(8,128)}) async-done(((f32[1152,128]{1,0:T(8,128)}, f32[1152,128]{1,0:T(8,128)}), (f32[1152,128]{1,0:T(8,128)}, f32[1152,128]{1,0:T(8,128)})) %all-reduce.3.cloned.1.call-update) | async-done | bytes 1179664 | tf_op jit(solution)/shard_map/psum | solution.py:98
  401.3 1.9 broadcast_multiply_fusion.1
  403.2 1.9 broadcast_multiply_fusion
  (50 shorter events, 4.7 us)
Async XLA Ops:
  7.2 28.7 %copy-start = (bf16[1,640,512]{2,1,0:T(8,128)(2,1)S(1)}, bf16[1,640,512]{2,1,0:T(8,128)(2,1)}, u32[]{:S(2)}) copy-start(bf16[1,640,512]{2,1,0:T(8,128)(2,1)} %param.9) | copy-start | bytes 1966084
  7.2 50.4 %copy-start.1 = (bf16[1,32,64,128]{3,2,1,0:T(8,128)(2,1)S(1)}, bf16[1,32,64,128]{3,2,1,0:T(8,128)(2,1)}, u32[]{:S(2)}) copy-start(bf16[1,32,64,128]{3,2,1,0:T(8,128)(2,1)} %param.15) | copy-start | bytes 1572868
  16.2 28.2 %all-to-all-start = ((s32[64,20,1]{1,2,0:T(1,128)}), s32[64,20,1]{1,2,0:T(1,128)S(1)}, u32[]{:S(2)}, u32[]{:S(2)}) async-start(s32[64,20,1]{1,2,0:T(1,128)} %bitcast.3), calls=%async_computation | async-start | bytes 65536 | tf_op jit(solution)/shard_map/all_to_all | solution.py:57
  30.5 27.1 %collective-permute-start.4 = (bf16[2,64,128]{2,1,0:T(8,128)(2,1)S(1)}, bf16[2,64,128]{2,1,0:T(8,128)(2,1)S(1)}, u32[]{:S(2)}, u32[]{:S(2)}) collective-permute-start(bf16[2,64,128]{2,1,0:T(8,128)(2,1)S(1)} %get-tuple-element.31), channel_id=1, source_target_pairs={{0,64},{64,128},{128,192},{1,65},{65,129},{129,193},{2,66},{66,130... | collective-permute-start | bytes 98312 | tf_op jit(solution)/shard_map/ppermute | solution.py:16
  33.4 24.2 %collective-permute-start.5 = (bf16[2,64,128]{2,1,0:T(8,128)(2,1)S(1)}, bf16[2,64,128]{2,1,0:T(8,128)(2,1)S(1)}, u32[]{:S(2)}, u32[]{:S(2)}) collective-permute-start(bf16[2,64,128]{2,1,0:T(8,128)(2,1)S(1)} %get-tuple-element.32), channel_id=1, source_target_pairs={{64,0},{128,64},{192,128},{65,1},{129,65},{193,129},{66,2},{130,66... | collective-permute-start | bytes 98312 | tf_op jit(solution)/shard_map/ppermute | solution.py:17
  44.4 36.3 %all-to-all-start.1 = ((f32[64,20,128]{2,1,0:T(8,128)}), f32[64,20,128]{2,1,0:T(8,128)S(1)}, u32[]{:S(2)}, u32[]{:S(2)}) async-start(f32[64,20,128]{2,1,0:T(8,128)} %all_to_all.16), calls=%async_computation.1 | async-start | bytes 1572864 | tf_op jit(solution)/shard_map/all_to_all | solution.py:56
  56.1 345.1 %all-reduce.3.cloned.1.call-start = ((), (), s32[]{:S(2)}) async-start(), calls=%async_computation.2 | async-start | bytes 2359296 | tf_op jit(solution)/shard_map/psum | solution.py:98
  57.6 10.1 %collective-permute-start.6 = (bf16[36,2,128]{2,1,0:T(2,128)(2,1)S(1)}, bf16[36,2,128]{2,1,0:T(2,128)(2,1)S(1)}, u32[]{:S(2)}, u32[]{:S(2)}) collective-permute-start(bf16[36,2,128]{2,1,0:T(2,128)(2,1)S(1)} %get-tuple-element.28), channel_id=1, source_target_pairs={{0,4},{4,8},{8,12},{12,16},{16,20},{20,24},{24,28},{28,32},{32,36}... | collective-permute-start | bytes 55304 | tf_op jit(solution)/shard_map/ppermute | solution.py:16
  60.5 12.2 %collective-permute-start.7 = (bf16[36,2,128]{2,1,0:T(2,128)(2,1)S(1)}, bf16[36,2,128]{2,1,0:T(2,128)(2,1)S(1)}, u32[]{:S(2)}, u32[]{:S(2)}) collective-permute-start(bf16[36,2,128]{2,1,0:T(2,128)(2,1)S(1)} %get-tuple-element.27), channel_id=1, source_target_pairs={{4,0},{8,4},{12,8},{16,12},{20,16},{24,20},{28,24},{32,28},{36,32}... | collective-permute-start | bytes 55304 | tf_op jit(solution)/shard_map/ppermute | solution.py:17
  91.2 5.3 %collective-permute-start = (bf16[3,64,128]{2,1,0:T(8,128)(2,1)S(1)}, bf16[3,64,128]{2,1,0:T(8,128)(2,1)S(1)}, u32[]{:S(2)}, u32[]{:S(2)}) collective-permute-start(bf16[3,64,128]{2,1,0:T(8,128)(2,1)S(1)} %bitcast.124), channel_id=1, source_target_pairs={{0,64},{64,128},{128,192},{1,65},{65,129},{129,193},{2,66},{66,130... | collective-permute-start | bytes 147464 | tf_op jit(solution)/shard_map/ppermute | solution.py:16
  94.3 4.8 %collective-permute-start.1 = (bf16[3,64,128]{2,1,0:T(8,128)(2,1)S(1)}, bf16[3,64,128]{2,1,0:T(8,128)(2,1)S(1)}, u32[]{:S(2)}, u32[]{:S(2)}) collective-permute-start(bf16[3,64,128]{2,1,0:T(8,128)(2,1)S(1)} %bitcast.123), channel_id=1, source_target_pairs={{64,0},{128,64},{192,128},{65,1},{129,65},{193,129},{66,2},{130,66... | collective-permute-start | bytes 147464 | tf_op jit(solution)/shard_map/ppermute | solution.py:17
  99.2 3.9 collective-permute-start.2
  101.5 5.7 %collective-permute-start.3 = (bf16[38,3,128]{2,1,0:T(4,128)(2,1)S(1)}, bf16[38,3,128]{2,1,0:T(4,128)(2,1)S(1)}, u32[]{:S(2)}, u32[]{:S(2)}) collective-permute-start(bf16[38,3,128]{2,1,0:T(4,128)(2,1)S(1)} %get-tuple-element.24), channel_id=1, source_target_pairs={{4,0},{8,4},{12,8},{16,12},{20,16},{24,20},{28,24},{32,28},{36,32}... | collective-permute-start | bytes 87560 | tf_op jit(solution)/shard_map/ppermute | solution.py:17
  113.5 1.9 copy-start.4
  121.8 5.9 %copy-start.2 = (bf16[32,64,1152]{2,1,0:T(8,128)(2,1)}, bf16[32,64,1152]{2,1,0:T(8,128)(2,1)S(1)}, u32[]{:S(2)}) copy-start(bf16[32,64,1152]{2,1,0:T(8,128)(2,1)S(1)} %slice_dynamic-update-slice_fusion.9) | copy-start | bytes 14155780
  121.8 5.9 %copy-start.3 = (f32[2048,128]{1,0:T(8,128)S(1)}, f32[2048,128]{1,0:T(8,128)}, u32[]{:S(2)}) copy-start(f32[2048,128]{1,0:T(8,128)} %get-tuple-element.6) | copy-start | bytes 3145732
Sparse Core Ops, SparseCore 0:
  136.6 264.5 all-reduce.2
where the time goes:
time: 414 us; the launch traced here: 412 us
  waiting for transfers between devices  278 us (67%)
  starting transfers between devices  41.8 us (10%)
  local copies, waits for them, and re-layouts  35.9 us (9%)
  other arithmetic  22.8 us (6%)
  matrix products  19.3 us (5%)
  between operations  14.5 us (4%)
    psum x1, waiting for transfers between devices, on_device(): lax.psum((first_term, second_term), ('row', 'col', 'batch'))  260 us
    unnamed x41, local copies, waits for them, and re-layouts  17.7 us
    all_to_all x1, starting transfers between devices, on_device(): lax.all_to_all(cell_ids, ('row', 'col'), split_axis=0, concat_axis=0, til...  13.5 us
    ppermute x4, waiting for transfers between devices, with_halo(): after = lax.ppermute(leading, axis, down)  11.8 us
    all_to_all x1, starting transfers between devices, on_device(): lax.all_to_all(outgoing, ('row', 'col'), split_axis=0, concat_axis=0, til...  11.8 us
    ppermute x4, starting transfers between devices, with_halo(): before = lax.ppermute(last, axis, up)  11.2 us
    dot_general x2, matrix products, contract_rows(): lax.dot_general(left, right, (((0,), (0,)), ((), ())), preferred_element_...  11.1 us
    scatter-add x1, other arithmetic, on_device(): jax.ops.segment_sum(embedded, arrived_ids, num_segments=rows * cols)  9.59 us
  transfers between devices with their start and end apart: 11, of which 5 were waited for; matrix products, arithmetic and copies ran while one was open for 6% of the time, Pallas kernels for 0%

commit v1 on v0

--- a/solution.py
+++ b/solution.py
@@ -17,6 +17,38 @@
         after = lax.ppermute(leading, axis, down)
         array = jnp.concatenate([before, array, after], axis=dim)
     return array
+
+
+def halving_steps():
+    steps = [("batch", 1)]
+    for axis in ("row", "col"):
+        d = 1
+        while d < lax.axis_size(axis):
+            steps.append((axis, d))
+            d *= 2
+    d = 2
+    while d < lax.axis_size("batch"):
+        steps.append(("batch", d))
+        d *= 2
+    return steps
+
+
+def tree_sum(x):
+    steps = halving_steps()
+    for axis, d in steps:
+        pairs = [(i, i ^ d) for i in range(lax.axis_size(axis))]
+        upper = (lax.axis_index(axis) // d) % 2 == 1
+        half = x.shape[0] // 2
+        low, high = x[:half], x[half:]
+        kept = jnp.where(upper, high, low)
+        sent = jnp.where(upper, low, high)
+        x = kept + lax.ppermute(sent, axis, pairs)
+    for axis, d in steps[::-1]:
+        pairs = [(i, i ^ d) for i in range(lax.axis_size(axis))]
+        upper = (lax.axis_index(axis) // d) % 2 == 1
+        got = lax.ppermute(x, axis, pairs)
+        x = jnp.where(upper, jnp.concatenate([got, x]), jnp.concatenate([x, got]))
+    return x
 
 
 def unfold(padded, step, rows, cols):
@@ -95,7 +127,7 @@
     grad_pre1 = (grad_act1 * sigmoid_pre * (1.0 + pre1 * (1.0 - sigmoid_pre))).astype(jnp.bfloat16)
     first_term = contract_rows(patches0, grad_pre1)
     second_term = contract_rows(patches1, back_flat)
-    first_sum, second_sum = lax.psum((first_term, second_term), ("row", "col", "batch"))
+    first_sum, second_sum = jnp.split(tree_sum(jnp.concatenate([first_term, second_term])), 2)
     total_cells = (
         rows
         * lax.axis_size("row")

time: 414 us -> 230 us (0.56)
  waiting for transfers between devices: 278 us -> 49.1 us
  starting transfers between devices: 41.8 us -> 102 us
  between operations: 14.5 us -> 1.23 us
    psum x1 -> x0, waiting for transfers between devices: 260 us -> none  [on_device(): lax.psum((first_term, second_term), ('row', 'col', 'batch'))]
    ppermute x0 -> x16, starting transfers between devices: none -> 56.2 us  [the longest x8 28.6 us: tree_sum(): x = kept + lax.ppermute(sent, axis, pairs)]
    ppermute x0 -> x16, waiting for transfers between devices: none -> 38.2 us  [the longest x8 19.2 us: tree_sum(): got = lax.ppermute(x, axis, pairs)]
    ppermute x4, starting transfers between devices: 11.2 us -> 16.2 us  [with_halo(): before = lax.ppermute(last, axis, up)]
    ppermute x4, waiting for transfers between devices: 5.83 us -> 1.07 us  [with_halo(): before = lax.ppermute(last, axis, up)]
    unnamed x41 -> x45, local copies, waits for them, and re-layouts: 17.7 us -> 19.8 us
  transfers between devices with their start and end apart: 11 -> 26, of which waited for: 5 -> 18; matrix products, arithmetic and copies ran while one was open for 6% -> 11% of each run, Pallas kernels for 0% -> 0%
where the time goes in v1:
time: 230 us; the launch traced here: 229 us
  starting transfers between devices  102 us (44%)
  waiting for transfers between devices  49.1 us (21%)
  local copies, waits for them, and re-layouts  38.1 us (17%)
  other arithmetic  20.8 us (9%)
  matrix products  18.5 us (8%)
    ppermute x8, starting transfers between devices, tree_sum(): x = kept + lax.ppermute(sent, axis, pairs)  28.6 us
    ppermute x8, starting transfers between devices, tree_sum(): got = lax.ppermute(x, axis, pairs)  27.6 us
    unnamed x45, local copies, waits for them, and re-layouts  19.8 us
    ppermute x8, waiting for transfers between devices, tree_sum(): got = lax.ppermute(x, axis, pairs)  19.2 us
    ppermute x8, waiting for transfers between devices, tree_sum(): x = kept + lax.ppermute(sent, axis, pairs)  18.9 us
    ppermute x4, starting transfers between devices, with_halo(): before = lax.ppermute(last, axis, up)  16.2 us
    all_to_all x1, starting transfers between devices, on_device(): lax.all_to_all(cell_ids, ('row', 'col'), split_axis=0, concat_axis=0, til...  13.5 us
    all_to_all x1, starting transfers between devices, on_device(): lax.all_to_all(outgoing, ('row', 'col'), split_axis=0, concat_axis=0, til...  10.7 us
  transfers between devices with their start and end apart: 26, of which 18 were waited for; matrix products, arithmetic and copies ran while one was open for 11% of the time, Pallas kernels for 0%

profile of v1, /device:TPU:1, one launch (start us, length us, event | category | flops | bytes accessed | tf_op | source)
XLA Modules:
  0.0 229.4 jit_solution(5560898608820968999)
XLA Ops:
  1.5 1.5 reduce-window.6
  4.8 4.1 %scatter_custom_fusion = s32[1280]{0:T(1024)S(1)} fusion(s32[640]{0:T(1024)S(1)} %fusion.18, s32[640]{0:T(1024)S(1)} %reduce.4, s32[]{:T(128)} %constant.174.clone.1), kind=kCustom, calls=%fused_computation.111 | custom fusion | bytes 5124 | tf_op jit(solution)/shard_map/scatter | solution.py:84
  9.6 13.5 %all-to-all-start = ((s32[64,20,1]{1,2,0:T(1,128)}), s32[64,20,1]{1,2,0:T(1,128)S(1)}, u32[]{:S(2)}, u32[]{:S(2)}) async-start(s32[64,20,1]{1,2,0:T(1,128)} %bitcast.3), calls=%async_computation | async-start | bytes 65536 | tf_op jit(solution)/shard_map/all_to_all | solution.py:89
  23.9 1.3 collective-permute-start.5
  25.2 4.0 %collective-permute-start.4 = (bf16[2,64,128]{2,1,0:T(8,128)(2,1)S(1)}, bf16[2,64,128]{2,1,0:T(8,128)(2,1)S(1)}, u32[]{:S(2)}, u32[]{:S(2)}) collective-permute-start(bf16[2,64,128]{2,1,0:T(8,128)(2,1)S(1)} %get-tuple-element.31), channel_id=1, source_target_pairs={{0,64},{64,128},{128,192},{1,65},{65,129},{129,193},{2,66},{66,130... | collective-permute-start | bytes 98312 | tf_op jit(solution)/shard_map/ppermute | solution.py:16
  29.2 1.1 bitcast_convert_fusion
  30.4 1.2 fusion.9
  31.7 4.3 %scatter_custom_fusion.1 = f32[1280,128]{1,0:T(8,128)S(1)} fusion(s32[640]{0:T(1024)S(1)} %fusion.18, f32[640,128]{1,0:T(8,128)S(1)} %fusion.9, f32[]{:T(128)} %constant.183.clone.1), kind=kCustom, calls=%fused_computation.51 | custom fusion | bytes 655364 | tf_op jit(solution)/shard_map/scatter | solution.py:86
  36.0 0.9 all_to_all.16
  37.0 1.2 copy.15
  38.9 10.7 %all-to-all-start.1 = ((f32[64,20,128]{2,1,0:T(8,128)}), f32[64,20,128]{2,1,0:T(8,128)S(1)}, u32[]{:S(2)}, u32[]{:S(2)}) async-start(f32[64,20,128]{2,1,0:T(8,128)} %all_to_all.16), calls=%async_computation.1 | async-start | bytes 1572864 | tf_op jit(solution)/shard_map/all_to_all | solution.py:88
  51.0 1.3 collective-permute-start.7
  52.3 4.0 %collective-permute-start.6 = (bf16[36,2,128]{2,1,0:T(2,128)(2,1)S(1)}, bf16[36,2,128]{2,1,0:T(2,128)(2,1)S(1)}, u32[]{:S(2)}, u32[]{:S(2)}) collective-permute-start(bf16[36,2,128]{2,1,0:T(2,128)(2,1)S(1)} %get-tuple-element.28), channel_id=1, source_target_pairs={{0,4},{4,8},{8,12},{12,16},{16,20},{20,24},{24,28},{28,32},{32,36}... | collective-permute-start | bytes 55304 | tf_op jit(solution)/shard_map/ppermute | solution.py:16
  56.4 9.9 %collective-permute-done.7 = bf16[36,2,128]{2,1,0:T(2,128)(2,1)S(1)} collective-permute-done((bf16[36,2,128]{2,1,0:T(2,128)(2,1)S(1)}, bf16[36,2,128]{2,1,0:T(2,128)(2,1)S(1)}, u32[]{:S(2)}, u32[]{:S(2)}) %collective-permute-start.7) | collective-permute-done | bytes 18464 | tf_op jit(solution)/shard_map/ppermute | solution.py:17
  70.7 0.9 constant_dynamic-update-slice_fusion.14
  71.5 0.9 constant_dynamic-update-slice_fusion.13
  74.2 0.9 reshape.204
  75.1 9.6 %scatter_fusion = f32[2048,128]{1,0:T(8,128)S(1)} fusion(f32[2048,128]{1,0:T(8,128)S(1)} %bitcast_convert_fusion, s32[1280]{0:T(1024)S(1)} %reshape.202, f32[1280,128]{1,0:T(8,128)} %reshape.204), kind=kCustom, calls=%fused_computation.2 | custom fusion | flops 163840 | bytes 1971200 | tf_op jit(solution)/shard_map/scatter-add | solution.py:91
  84.7 1.3 collective-permute-start.1
  86.0 4.1 %collective-permute-start = (bf16[3,64,128]{2,1,0:T(8,128)(2,1)S(1)}, bf16[3,64,128]{2,1,0:T(8,128)(2,1)S(1)}, u32[]{:S(2)}, u32[]{:S(2)}) collective-permute-start(bf16[3,64,128]{2,1,0:T(8,128)(2,1)S(1)} %bitcast.123), channel_id=1, source_target_pairs={{0,64},{64,128},{128,192},{1,65},{65,129},{129,193},{2,66},{66,130... | collective-permute-start | bytes 147464 | tf_op jit(solution)/shard_map/ppermute | solution.py:16
  91.3 1.3 collective-permute-start.3
  92.6 4.2 %collective-permute-start.2 = (bf16[38,3,128]{2,1,0:T(4,128)(2,1)S(1)}, bf16[38,3,128]{2,1,0:T(4,128)(2,1)S(1)}, u32[]{:S(2)}, u32[]{:S(2)}) collective-permute-start(bf16[38,3,128]{2,1,0:T(4,128)(2,1)S(1)} %get-tuple-element.23), channel_id=1, source_target_pairs={{0,4},{4,8},{8,12},{12,16},{16,20},{20,24},{24,28},{28,32},{32,36}... | collective-permute-start | bytes 87560 | tf_op jit(solution)/shard_map/ppermute | solution.py:16
  100.3 2.2 select_convert_fusion
  103.3 1.1 fusion.23
  105.3 2.1 copy-done.2
  107.4 1.4 fusion.25
  110.1 0.9 constant_dynamic-update-slice_fusion.9
  111.8 0.9 constant_dynamic-update-slice_fusion.7
  113.6 0.9 constant_dynamic-update-slice_fusion.5
  114.6 1.6 fusion.6
  116.2 0.9 constant_dynamic-update-slice_fusion.4
  117.1 0.9 constant_dynamic-update-slice_fusion.3
  119.7 9.1 %broadcast_select_fusion = (f32[1152,128]{1,0:T(8,128)}, f32[1152,128]{1,0:T(8,128)S(1)}) fusion(f32[1152,128]{1,0:T(8,128)S(1)} %fusion.25, pred[]{:T(512)S(6)} %eq.82, bf16[2048,1152]{1,0:T(8,128)(2,1)} %constant_dynamic-update-slice_fusion.1, f32[2048,128]{1,0:T(8,128)} %get-tuple-element.6, f32[2048,128]{1,0:T(8,128)S(1)} %copy-done.3, ...), kind=kOutput, calls=%fused_computation.55 | convolution fusion | flops 1209417728 | bytes 14123009 | tf_op jit(solution)/shard_map/dot_general | solution.py:64
  128.8 5.3 %collective-permute-start.8 = (f32[1152,128]{1,0:T(8,128)}, f32[1152,128]{1,0:T(8,128)S(1)}, u32[]{:S(2)}, u32[]{:S(2)}) collective-permute-start(f32[1152,128]{1,0:T(8,128)} %get-tuple-element.39), channel_id=1, source_target_pairs={{0,1},{1,0},{2,3},{3,2},{4,5},{5,4},{6,7},{7,6},{8,9},{9,8},{10,11... | collective-permute-start | bytes 1769480 | tf_op jit(solution)/shard_map/ppermute | solution.py:45
  134.1 1.8 collective-permute-done.8
  136.0 2.1 collective-permute-start.9
  138.2 7.0 %collective-permute-done.9 = f32[576,128]{1,0:T(8,128)S(1)} collective-permute-done((f32[576,128]{1,0:T(8,128)S(1)}, f32[576,128]{1,0:T(8,128)S(1)}, u32[]{:S(2)}, u32[]{:S(2)}) %collective-permute-start.9) | collective-permute-done | bytes 294944 | tf_op jit(solution)/shard_map/ppermute | solution.py:45
  145.3 3.0 %collective-permute-start.10 = (f32[288,128]{1,0:T(8,128)S(1)}, f32[288,128]{1,0:T(8,128)S(1)}, u32[]{:S(2)}, u32[]{:S(2)}) collective-permute-start(f32[288,128]{1,0:T(8,128)S(1)} %slice_select_fusion.1), channel_id=1, source_target_pairs={{0,128},{64,192},{128,0},{192,64},{1,129},{65,193},{129,1},{193,65... | collective-permute-start | bytes 442376 | tf_op jit(solution)/shard_map/ppermute | solution.py:45
  148.3 3.0 %collective-permute-done.10 = f32[288,128]{1,0:T(8,128)S(1)} collective-permute-done((f32[288,128]{1,0:T(8,128)S(1)}, f32[288,128]{1,0:T(8,128)S(1)}, u32[]{:S(2)}, u32[]{:S(2)}) %collective-permute-start.10) | collective-permute-done | bytes 147488 | tf_op jit(solution)/shard_map/ppermute | solution.py:45
  151.4 2.1 collective-permute-start.11
  153.5 1.7 collective-permute-done.11
  155.3 3.8 %collective-permute-start.12 = (f32[72,128]{1,0:T(8,128)S(1)}, f32[72,128]{1,0:T(8,128)S(1)}, u32[]{:S(2)}, u32[]{:S(2)}) collective-permute-start(f32[72,128]{1,0:T(8,128)S(1)} %slice_select_fusion.3), channel_id=1, source_target_pairs={{0,8},{4,12},{8,0},{12,4},{16,24},{20,28},{24,16},{28,20},{32,40},... | collective-permute-start | bytes 110600 | tf_op jit(solution)/shard_map/ppermute | solution.py:45
  159.1 1.3 collective-permute-done.12
  160.5 6.7 %collective-permute-start.13 = (f32[36,128]{1,0:T(8,128)S(1)}, f32[36,128]{1,0:T(8,128)S(1)}, u32[]{:S(2)}, u32[]{:S(2)}) collective-permute-start(f32[36,128]{1,0:T(8,128)S(1)} %slice_select_fusion.4), channel_id=1, source_target_pairs={{0,16},{4,20},{8,24},{12,28},{16,0},{20,4},{24,8},{28,12},{32,48},... | collective-permute-start | bytes 55304 | tf_op jit(solution)/shard_map/ppermute | solution.py:45
  167.2 1.2 collective-permute-done.13
  168.4 2.8 %collective-permute-start.14 = (f32[18,128]{1,0:T(8,128)S(1)}, f32[18,128]{1,0:T(8,128)S(1)}, u32[]{:S(2)}, u32[]{:S(2)}) collective-permute-start(f32[18,128]{1,0:T(8,128)S(1)} %slice_select_fusion.5), channel_id=1, source_target_pairs={{0,32},{4,36},{8,40},{12,44},{16,48},{20,52},{24,56},{28,60},{32,0... | collective-permute-start | bytes 27656 | tf_op jit(solution)/shard_map/ppermute | solution.py:45
  171.2 1.4 collective-permute-done.14
  172.6 2.7 %collective-permute-start.15 = (f32[9,128]{1,0:T(8,128)S(1)}, f32[9,128]{1,0:T(8,128)S(1)}, u32[]{:S(2)}, u32[]{:S(2)}) collective-permute-start(f32[9,128]{1,0:T(8,128)S(1)} %slice_select_fusion.6), channel_id=1, source_target_pairs={{0,2},{1,3},{2,0},{3,1},{4,6},{5,7},{6,4},{7,5},{8,10},{9,11},{10,... | collective-permute-start | bytes 13832 | tf_op jit(solution)/shard_map/ppermute | solution.py:45
  175.3 1.4 collective-permute-done.15
  176.7 2.6 %collective-permute-start.16 = (f32[9,128]{1,0:T(8,128)S(1)}, f32[9,128]{1,0:T(8,128)S(1)}, u32[]{:S(2)}, u32[]{:S(2)}) collective-permute-start(f32[9,128]{1,0:T(8,128)S(1)} %select_add_fusion.7), channel_id=1, source_target_pairs={{0,2},{1,3},{2,0},{3,1},{4,6},{5,7},{6,4},{7,5},{8,10},{9,11},{10,... | collective-permute-start | bytes 13832 | tf_op jit(solution)/shard_map/ppermute | solution.py:49
  179.3 1.4 collective-permute-done.16
  180.7 1.5 collective-permute-start.17
  182.3 1.1 collective-permute-done.17
  183.3 4.3 %collective-permute-start.18 = (f32[36,128]{1,0:T(8,128)S(1)}, f32[36,128]{1,0:T(8,128)S(1)}, u32[]{:S(2)}, u32[]{:S(2)}) collective-permute-start(f32[36,128]{1,0:T(8,128)S(1)} %maximum_select_fusion.6), channel_id=1, source_target_pairs={{0,16},{4,20},{8,24},{12,28},{16,0},{20,4},{24,8},{28,12},{32,48},... | collective-permute-start | bytes 55304 | tf_op jit(solution)/shard_map/ppermute | solution.py:49
  187.7 2.3 %collective-permute-done.18 = f32[36,128]{1,0:T(8,128)S(1)} collective-permute-done((f32[36,128]{1,0:T(8,128)S(1)}, f32[36,128]{1,0:T(8,128)S(1)}, u32[]{:S(2)}, u32[]{:S(2)}) %collective-permute-start.18) | collective-permute-done | bytes 18464 | tf_op jit(solution)/shard_map/ppermute | solution.py:49
  190.1 3.7 %collective-permute-done.19 = f32[72,128]{1,0:T(8,128)S(1)} collective-permute-done((f32[72,128]{1,0:T(8,128)S(1)}, f32[72,128]{1,0:T(8,128)S(1)}, u32[]{:S(2)}, u32[]{:S(2)}) %collective-permute-start.19) | collective-permute-done | bytes 36896 | tf_op jit(solution)/shard_map/ppermute | solution.py:49
  193.9 3.2 %collective-permute-done.20 = f32[144,128]{1,0:T(8,128)S(1)} collective-permute-done((f32[144,128]{1,0:T(8,128)S(1)}, f32[144,128]{1,0:T(8,128)S(1)}, u32[]{:S(2)}, u32[]{:S(2)}) %collective-permute-start.20) | collective-permute-done | bytes 73760 | tf_op jit(solution)/shard_map/ppermute | solution.py:49
  197.1 2.6 %collective-permute-start.21 = (f32[288,128]{1,0:T(8,128)S(1)}, f32[288,128]{1,0:T(8,128)S(1)}, u32[]{:S(2)}, u32[]{:S(2)}) collective-permute-start(f32[288,128]{1,0:T(8,128)S(1)} %maximum_select_fusion.3), channel_id=1, source_target_pairs={{0,128},{64,192},{128,0},{192,64},{1,129},{65,193},{129,1},{193,65... | collective-permute-start | bytes 442376 | tf_op jit(solution)/shard_map/ppermute | solution.py:49
  199.7 3.0 %collective-permute-done.21 = f32[288,128]{1,0:T(8,128)S(1)} collective-permute-done((f32[288,128]{1,0:T(8,128)S(1)}, f32[288,128]{1,0:T(8,128)S(1)}, u32[]{:S(2)}, u32[]{:S(2)}) %collective-permute-start.21) | collective-permute-done | bytes 147488 | tf_op jit(solution)/shard_map/ppermute | solution.py:49
  202.7 1.1 collective-permute-start.22
  203.8 4.6 %collective-permute-done.22 = f32[576,128]{1,0:T(8,128)S(1)} collective-permute-done((f32[576,128]{1,0:T(8,128)S(1)}, f32[576,128]{1,0:T(8,128)S(1)}, u32[]{:S(2)}, u32[]{:S(2)}) %collective-permute-start.22) | collective-permute-done | bytes 294944 | tf_op jit(solution)/shard_map/ppermute | solution.py:49
  208.4 15.2 %collective-permute-start.23 = (f32[1152,128]{1,0:T(8,128)S(1)}, f32[1152,128]{1,0:T(8,128)S(1)}, u32[]{:S(2)}, u32[]{:S(2)}) collective-permute-start(f32[1152,128]{1,0:T(8,128)S(1)} %maximum_select_fusion.1), channel_id=1, source_target_pairs={{0,1},{1,0},{2,3},{3,2},{4,5},{5,4},{6,7},{7,6},{8,9},{9,8},{10,11... | collective-permute-start | bytes 1769480 | tf_op jit(solution)/shard_map/ppermute | solution.py:49
  223.6 4.5 %fusion.3 = bf16[2048,128]{1,0:T(8,128)(2,1)} fusion(bf16[2048,1152]{1,0:T(8,128)(2,1)} %bitcast.101, bf16[1152,128]{1,0:T(8,128)(2,1)S(1)} %bitcast.122, bf16[2048,128]{1,0:T(8,128)(2,1)S(1)} %bitcast.121), kind=kOutput, calls=%fused_computation.8 | convolution fusion | flops 604766208 | bytes 6062080 | tf_op jit(solution)/shard_map/dot_general | solution.py:113
  228.3 1.1 slice_multiply_fusion
  (105 shorter events, 24.4 us)
Async XLA Ops:
  0.6 29.7 %copy-start = (bf16[1,640,512]{2,1,0:T(8,128)(2,1)S(1)}, bf16[1,640,512]{2,1,0:T(8,128)(2,1)}, u32[]{:S(2)}) copy-start(bf16[1,640,512]{2,1,0:T(8,128)(2,1)} %param.9) | copy-start | bytes 1966084
  0.6 50.3 %copy-start.1 = (bf16[1,32,64,128]{3,2,1,0:T(8,128)(2,1)S(1)}, bf16[1,32,64,128]{3,2,1,0:T(8,128)(2,1)}, u32[]{:S(2)}) copy-start(bf16[1,32,64,128]{3,2,1,0:T(8,128)(2,1)} %param.15) | copy-start | bytes 1572868
  9.6 29.2 %all-to-all-start = ((s32[64,20,1]{1,2,0:T(1,128)}), s32[64,20,1]{1,2,0:T(1,128)S(1)}, u32[]{:S(2)}, u32[]{:S(2)}) async-start(s32[64,20,1]{1,2,0:T(1,128)} %bitcast.3), calls=%async_computation | async-start | bytes 65536 | tf_op jit(solution)/shard_map/all_to_all | solution.py:89
  23.9 27.0 %collective-permute-start.5 = (bf16[2,64,128]{2,1,0:T(8,128)(2,1)S(1)}, bf16[2,64,128]{2,1,0:T(8,128)(2,1)S(1)}, u32[]{:S(2)}, u32[]{:S(2)}) collective-permute-start(bf16[2,64,128]{2,1,0:T(8,128)(2,1)S(1)} %get-tuple-element.32), channel_id=1, source_target_pairs={{64,0},{128,64},{192,128},{65,1},{129,65},{193,129},{66,2},{130,66... | collective-permute-start | bytes 98312 | tf_op jit(solution)/shard_map/ppermute | solution.py:17
  25.2 25.7 %collective-permute-start.4 = (bf16[2,64,128]{2,1,0:T(8,128)(2,1)S(1)}, bf16[2,64,128]{2,1,0:T(8,128)(2,1)S(1)}, u32[]{:S(2)}, u32[]{:S(2)}) collective-permute-start(bf16[2,64,128]{2,1,0:T(8,128)(2,1)S(1)} %get-tuple-element.31), channel_id=1, source_target_pairs={{0,64},{64,128},{128,192},{1,65},{65,129},{129,193},{2,66},{66,130... | collective-permute-start | bytes 98312 | tf_op jit(solution)/shard_map/ppermute | solution.py:16
  38.9 35.3 %all-to-all-start.1 = ((f32[64,20,128]{2,1,0:T(8,128)}), f32[64,20,128]{2,1,0:T(8,128)S(1)}, u32[]{:S(2)}, u32[]{:S(2)}) async-start(f32[64,20,128]{2,1,0:T(8,128)} %all_to_all.16), calls=%async_computation.1 | async-start | bytes 1572864 | tf_op jit(solution)/shard_map/all_to_all | solution.py:88
  51.0 15.2 %collective-permute-start.7 = (bf16[36,2,128]{2,1,0:T(2,128)(2,1)S(1)}, bf16[36,2,128]{2,1,0:T(2,128)(2,1)S(1)}, u32[]{:S(2)}, u32[]{:S(2)}) collective-permute-start(bf16[36,2,128]{2,1,0:T(2,128)(2,1)S(1)} %get-tuple-element.27), channel_id=1, source_target_pairs={{4,0},{8,4},{12,8},{16,12},{20,16},{24,20},{28,24},{32,28},{36,32}... | collective-permute-start | bytes 55304 | tf_op jit(solution)/shard_map/ppermute | solution.py:17
  52.3 13.9 %collective-permute-start.6 = (bf16[36,2,128]{2,1,0:T(2,128)(2,1)S(1)}, bf16[36,2,128]{2,1,0:T(2,128)(2,1)S(1)}, u32[]{:S(2)}, u32[]{:S(2)}) collective-permute-start(bf16[36,2,128]{2,1,0:T(2,128)(2,1)S(1)} %get-tuple-element.28), channel_id=1, source_target_pairs={{0,4},{4,8},{8,12},{12,16},{16,20},{20,24},{24,28},{28,32},{32,36}... | collective-permute-start | bytes 55304 | tf_op jit(solution)/shard_map/ppermute | solution.py:16
  84.7 6.3 %collective-permute-start.1 = (bf16[3,64,128]{2,1,0:T(8,128)(2,1)S(1)}, bf16[3,64,128]{2,1,0:T(8,128)(2,1)S(1)}, u32[]{:S(2)}, u32[]{:S(2)}) collective-permute-start(bf16[3,64,128]{2,1,0:T(8,128)(2,1)S(1)} %bitcast.124), channel_id=1, source_target_pairs={{64,0},{128,64},{192,128},{65,1},{129,65},{193,129},{66,2},{130,66... | collective-permute-start | bytes 147464 | tf_op jit(solution)/shard_map/ppermute | solution.py:17
  86.0 5.2 %collective-permute-start = (bf16[3,64,128]{2,1,0:T(8,128)(2,1)S(1)}, bf16[3,64,128]{2,1,0:T(8,128)(2,1)S(1)}, u32[]{:S(2)}, u32[]{:S(2)}) collective-permute-start(bf16[3,64,128]{2,1,0:T(8,128)(2,1)S(1)} %bitcast.123), channel_id=1, source_target_pairs={{0,64},{64,128},{128,192},{1,65},{65,129},{129,193},{2,66},{66,130... | collective-permute-start | bytes 147464 | tf_op jit(solution)/shard_map/ppermute | solution.py:16
  91.3 5.6 %collective-permute-start.3 = (bf16[38,3,128]{2,1,0:T(4,128)(2,1)S(1)}, bf16[38,3,128]{2,1,0:T(4,128)(2,1)S(1)}, u32[]{:S(2)}, u32[]{:S(2)}) collective-permute-start(bf16[38,3,128]{2,1,0:T(4,128)(2,1)S(1)} %get-tuple-element.24), channel_id=1, source_target_pairs={{4,0},{8,4},{12,8},{16,12},{20,16},{24,20},{28,24},{32,28},{36,32}... | collective-permute-start | bytes 87560 | tf_op jit(solution)/shard_map/ppermute | solution.py:17
  92.6 5.1 %collective-permute-start.2 = (bf16[38,3,128]{2,1,0:T(4,128)(2,1)S(1)}, bf16[38,3,128]{2,1,0:T(4,128)(2,1)S(1)}, u32[]{:S(2)}, u32[]{:S(2)}) collective-permute-start(bf16[38,3,128]{2,1,0:T(4,128)(2,1)S(1)} %get-tuple-element.23), channel_id=1, source_target_pairs={{0,4},{4,8},{8,12},{12,16},{16,20},{20,24},{24,28},{28,32},{32,36}... | collective-permute-start | bytes 87560 | tf_op jit(solution)/shard_map/ppermute | solution.py:16
  98.4 1.9 copy-start.6
  105.3 2.1 copy-start.2
  116.2 3.5 %copy-start.3 = (f32[2048,128]{1,0:T(8,128)S(1)}, f32[2048,128]{1,0:T(8,128)}, u32[]{:S(2)}) copy-start(f32[2048,128]{1,0:T(8,128)} %get-tuple-element.5) | copy-start | bytes 3145732
  128.8 7.1 %collective-permute-start.8 = (f32[1152,128]{1,0:T(8,128)}, f32[1152,128]{1,0:T(8,128)S(1)}, u32[]{:S(2)}, u32[]{:S(2)}) collective-permute-start(f32[1152,128]{1,0:T(8,128)} %get-tuple-element.39), channel_id=1, source_target_pairs={{0,1},{1,0},{2,3},{3,2},{4,5},{5,4},{6,7},{7,6},{8,9},{9,8},{10,11... | collective-permute-start | bytes 1769480 | tf_op jit(solution)/shard_map/ppermute | solution.py:45
  136.0 87.7 %copy-start.4 = (bf16[32,64,128]{2,1,0:T(8,128)(2,1)S(1)}, bf16[32,64,128]{2,1,0:T(8,128)(2,1)}, u32[]{:S(2)}) copy-start(bf16[32,64,128]{2,1,0:T(8,128)(2,1)} %get-tuple-element.19) | copy-start | bytes 1572868
  136.0 87.6 %copy-start.5 = (bf16[3,3,128,128]{3,2,1,0:T(8,128)(2,1)S(1)}, bf16[3,3,128,128]{3,2,1,0:T(8,128)(2,1)}, u32[]{:S(2)}) copy-start(bf16[3,3,128,128]{3,2,1,0:T(8,128)(2,1)} %param.14) | copy-start | bytes 884740
  136.0 9.2 %collective-permute-start.9 = (f32[576,128]{1,0:T(8,128)S(1)}, f32[576,128]{1,0:T(8,128)S(1)}, u32[]{:S(2)}, u32[]{:S(2)}) collective-permute-start(f32[576,128]{1,0:T(8,128)S(1)} %slice_select_fusion), channel_id=1, source_target_pairs={{0,64},{64,0},{128,192},{192,128},{1,65},{65,1},{129,193},{193,129... | collective-permute-start | bytes 884744 | tf_op jit(solution)/shard_map/ppermute | solution.py:45
  145.3 6.0 %collective-permute-start.10 = (f32[288,128]{1,0:T(8,128)S(1)}, f32[288,128]{1,0:T(8,128)S(1)}, u32[]{:S(2)}, u32[]{:S(2)}) collective-permute-start(f32[288,128]{1,0:T(8,128)S(1)} %slice_select_fusion.1), channel_id=1, source_target_pairs={{0,128},{64,192},{128,0},{192,64},{1,129},{65,193},{129,1},{193,65... | collective-permute-start | bytes 442376 | tf_op jit(solution)/shard_map/ppermute | solution.py:45
  151.4 3.9 %collective-permute-start.11 = (f32[144,128]{1,0:T(8,128)S(1)}, f32[144,128]{1,0:T(8,128)S(1)}, u32[]{:S(2)}, u32[]{:S(2)}) collective-permute-start(f32[144,128]{1,0:T(8,128)S(1)} %slice_select_fusion.2), channel_id=1, source_target_pairs={{0,4},{4,0},{8,12},{12,8},{16,20},{20,16},{24,28},{28,24},{32,36},... | collective-permute-start | bytes 221192 | tf_op jit(solution)/shard_map/ppermute | solution.py:45
  155.3 5.2 %collective-permute-start.12 = (f32[72,128]{1,0:T(8,128)S(1)}, f32[72,128]{1,0:T(8,128)S(1)}, u32[]{:S(2)}, u32[]{:S(2)}) collective-permute-start(f32[72,128]{1,0:T(8,128)S(1)} %slice_select_fusion.3), channel_id=1, source_target_pairs={{0,8},{4,12},{8,0},{12,4},{16,24},{20,28},{24,16},{28,20},{32,40},... | collective-permute-start | bytes 110600 | tf_op jit(solution)/shard_map/ppermute | solution.py:45
  160.5 7.9 %collective-permute-start.13 = (f32[36,128]{1,0:T(8,128)S(1)}, f32[36,128]{1,0:T(8,128)S(1)}, u32[]{:S(2)}, u32[]{:S(2)}) collective-permute-start(f32[36,128]{1,0:T(8,128)S(1)} %slice_select_fusion.4), channel_id=1, source_target_pairs={{0,16},{4,20},{8,24},{12,28},{16,0},{20,4},{24,8},{28,12},{32,48},... | collective-permute-start | bytes 55304 | tf_op jit(solution)/shard_map/ppermute | solution.py:45
  168.4 4.2 %collective-permute-start.14 = (f32[18,128]{1,0:T(8,128)S(1)}, f32[18,128]{1,0:T(8,128)S(1)}, u32[]{:S(2)}, u32[]{:S(2)}) collective-permute-start(f32[18,128]{1,0:T(8,128)S(1)} %slice_select_fusion.5), channel_id=1, source_target_pairs={{0,32},{4,36},{8,40},{12,44},{16,48},{20,52},{24,56},{28,60},{32,0... | collective-permute-start | bytes 27656 | tf_op jit(solution)/shard_map/ppermute | solution.py:45
  172.6 4.1 %collective-permute-start.15 = (f32[9,128]{1,0:T(8,128)S(1)}, f32[9,128]{1,0:T(8,128)S(1)}, u32[]{:S(2)}, u32[]{:S(2)}) collective-permute-start(f32[9,128]{1,0:T(8,128)S(1)} %slice_select_fusion.6), channel_id=1, source_target_pairs={{0,2},{1,3},{2,0},{3,1},{4,6},{5,7},{6,4},{7,5},{8,10},{9,11},{10,... | collective-permute-start | bytes 13832 | tf_op jit(solution)/shard_map/ppermute | solution.py:45
  176.7 4.0 %collective-permute-start.16 = (f32[9,128]{1,0:T(8,128)S(1)}, f32[9,128]{1,0:T(8,128)S(1)}, u32[]{:S(2)}, u32[]{:S(2)}) collective-permute-start(f32[9,128]{1,0:T(8,128)S(1)} %select_add_fusion.7), channel_id=1, source_target_pairs={{0,2},{1,3},{2,0},{3,1},{4,6},{5,7},{6,4},{7,5},{8,10},{9,11},{10,... | collective-permute-start | bytes 13832 | tf_op jit(solution)/shard_map/ppermute | solution.py:49
  180.7 2.6 %collective-permute-start.17 = (f32[18,128]{1,0:T(8,128)S(1)}, f32[18,128]{1,0:T(8,128)S(1)}, u32[]{:S(2)}, u32[]{:S(2)}) collective-permute-start(f32[18,128]{1,0:T(8,128)S(1)} %maximum_select_fusion.7), channel_id=1, source_target_pairs={{0,32},{4,36},{8,40},{12,44},{16,48},{20,52},{24,56},{28,60},{32,0... | collective-permute-start | bytes 27656 | tf_op jit(solution)/shard_map/ppermute | solution.py:49
  183.3 6.6 %collective-permute-start.18 = (f32[36,128]{1,0:T(8,128)S(1)}, f32[36,128]{1,0:T(8,128)S(1)}, u32[]{:S(2)}, u32[]{:S(2)}) collective-permute-start(f32[36,128]{1,0:T(8,128)S(1)} %maximum_select_fusion.6), channel_id=1, source_target_pairs={{0,16},{4,20},{8,24},{12,28},{16,0},{20,4},{24,8},{28,12},{32,48},... | collective-permute-start | bytes 55304 | tf_op jit(solution)/shard_map/ppermute | solution.py:49
  190.0 3.8 %collective-permute-start.19 = (f32[72,128]{1,0:T(8,128)S(1)}, f32[72,128]{1,0:T(8,128)S(1)}, u32[]{:S(2)}, u32[]{:S(2)}) collective-permute-start(f32[72,128]{1,0:T(8,128)S(1)} %maximum_select_fusion.5), channel_id=1, source_target_pairs={{0,8},{4,12},{8,0},{12,4},{16,24},{20,28},{24,16},{28,20},{32,40},... | collective-permute-start | bytes 110600 | tf_op jit(solution)/shard_map/ppermute | solution.py:49
  193.8 3.3 %collective-permute-start.20 = (f32[144,128]{1,0:T(8,128)S(1)}, f32[144,128]{1,0:T(8,128)S(1)}, u32[]{:S(2)}, u32[]{:S(2)}) collective-permute-start(f32[144,128]{1,0:T(8,128)S(1)} %maximum_select_fusion.4), channel_id=1, source_target_pairs={{0,4},{4,0},{8,12},{12,8},{16,20},{20,16},{24,28},{28,24},{32,36},... | collective-permute-start | bytes 221192 | tf_op jit(solution)/shard_map/ppermute | solution.py:49
  197.1 5.6 %collective-permute-start.21 = (f32[288,128]{1,0:T(8,128)S(1)}, f32[288,128]{1,0:T(8,128)S(1)}, u32[]{:S(2)}, u32[]{:S(2)}) collective-permute-start(f32[288,128]{1,0:T(8,128)S(1)} %maximum_select_fusion.3), channel_id=1, source_target_pairs={{0,128},{64,192},{128,0},{192,64},{1,129},{65,193},{129,1},{193,65... | collective-permute-start | bytes 442376 | tf_op jit(solution)/shard_map/ppermute | solution.py:49
  202.7 5.7 %collective-permute-start.22 = (f32[576,128]{1,0:T(8,128)S(1)}, f32[576,128]{1,0:T(8,128)S(1)}, u32[]{:S(2)}, u32[]{:S(2)}) collective-permute-start(f32[576,128]{1,0:T(8,128)S(1)} %maximum_select_fusion.2), channel_id=1, source_target_pairs={{0,64},{64,0},{128,192},{192,128},{1,65},{65,1},{129,193},{193,129... | collective-permute-start | bytes 884744 | tf_op jit(solution)/shard_map/ppermute | solution.py:49
  208.4 19.7 %collective-permute-start.23 = (f32[1152,128]{1,0:T(8,128)S(1)}, f32[1152,128]{1,0:T(8,128)S(1)}, u32[]{:S(2)}, u32[]{:S(2)}) collective-permute-start(f32[1152,128]{1,0:T(8,128)S(1)} %maximum_select_fusion.1), channel_id=1, source_target_pairs={{0,1},{1,0},{2,3},{3,2},{4,5},{5,4},{6,7},{7,6},{8,9},{9,8},{10,11... | collective-permute-start | bytes 1769480 | tf_op jit(solution)/shard_map/ppermute | solution.py:49

commit v2 on v1

--- a/solution.py
+++ b/solution.py
@@ -39,15 +39,20 @@
         pairs = [(i, i ^ d) for i in range(lax.axis_size(axis))]
         upper = (lax.axis_index(axis) // d) % 2 == 1
         half = x.shape[0] // 2
-        low, high = x[:half], x[half:]
-        kept = jnp.where(upper, high, low)
-        sent = jnp.where(upper, low, high)
+        side = upper.astype(jnp.int32)
+        kept = lax.dynamic_slice_in_dim(x, side * half, half)
+        sent = lax.dynamic_slice_in_dim(x, (1 - side) * half, half)
         x = kept + lax.ppermute(sent, axis, pairs)
     for axis, d in steps[::-1]:
         pairs = [(i, i ^ d) for i in range(lax.axis_size(axis))]
         upper = (lax.axis_index(axis) // d) % 2 == 1
         got = lax.ppermute(x, axis, pairs)
-        x = jnp.where(upper, jnp.concatenate([got, x]), jnp.concatenate([x, got]))
+        both = jnp.stack([x, got])
+        side = upper.astype(jnp.int32)
+        x = jnp.concatenate(
+            [lax.dynamic_index_in_dim(both, side, keepdims=False),
+             lax.dynamic_index_in_dim(both, 1 - side, keepdims=False)]
+        )
     return x
 
 
@@ -81,14 +86,30 @@
     hits = (tiles[:, None] == jnp.arange(n_tiles, dtype=jnp.int32)[None, :]).astype(jnp.int32)
     ranks = jnp.sum(jnp.cumsum(hits, axis=0) * hits, axis=1) - 1
     target = tiles * capacity + ranks
-    cell_ids = jnp.zeros((slots,), jnp.int32).at[target].set(where)
-    local_rows = jnp.dot(values, w_embed, preferred_element_type=jnp.float32)
-    outgoing = jnp.zeros((slots, chans), jnp.float32).at[target].set(local_rows)
-    embedded, arrived_ids = (
-        lax.all_to_all(outgoing, ("row", "col"), split_axis=0, concat_axis=0, tiled=True),
-        lax.all_to_all(cell_ids, ("row", "col"), split_axis=0, concat_axis=0, tiled=True),
+    chooser = (target[None, :] == jnp.arange(slots, dtype=jnp.int32)[:, None]).astype(jnp.bfloat16)
+    chosen = jnp.dot(chooser, values, preferred_element_type=jnp.float32).astype(jnp.bfloat16)
+    outgoing = jnp.dot(chosen, w_embed, preferred_element_type=jnp.float32)
+    id_parts = jnp.zeros((count, chans), jnp.bfloat16)
+    id_parts = id_parts.at[:, 0].set((where // 64 * 64).astype(jnp.bfloat16))
+    id_parts = id_parts.at[:, 1].set((where % 64).astype(jnp.bfloat16))
+    id_sums = jnp.dot(chooser, id_parts, preferred_element_type=jnp.float32)
+    slot_ids = (id_sums[:, 0] + id_sums[:, 1]).reshape(n_tiles, capacity)
+    id_row = jnp.zeros((n_tiles, 1, chans), jnp.float32).at[:, 0, :capacity].set(slot_ids)
+    payload = jnp.concatenate([outgoing.reshape(n_tiles, capacity, chans), id_row], axis=1)
+    arrived = lax.all_to_all(payload, ("row", "col"), split_axis=0, concat_axis=0, tiled=True)
+    embedded = arrived[:, :capacity, :].reshape(slots, chans)
+    arrived_ids = arrived[:, capacity, :capacity].reshape(slots)
+    spread = (
+        arrived_ids[None, :] == jnp.arange(rows * cols, dtype=jnp.float32)[:, None]
+    ).astype(jnp.bfloat16)
+    top = embedded.astype(jnp.bfloat16)
+    rest = embedded - top.astype(jnp.float32)
+    middle = rest.astype(jnp.bfloat16)
+    bottom = (rest - middle.astype(jnp.float32)).astype(jnp.bfloat16)
+    pieces = jnp.dot(
+        spread, jnp.concatenate([top, middle, bottom], axis=1), preferred_element_type=jnp.float32
     )
-    placed = jax.ops.segment_sum(embedded, arrived_ids, num_segments=rows * cols)
+    placed = pieces[:, :chans] + pieces[:, chans : 2 * chans] + pieces[:, 2 * chans :]
     first_in = (
         (cells.astype(jnp.float32).reshape(rows * cols, chans) + placed)
         .astype(jnp.bfloat16)

time: 230 us -> 201 us (0.87)
  starting transfers between devices: 102 us -> 80.6 us
  local copies, waits for them, and re-layouts: 38.1 us -> 24.1 us
  waiting for transfers between devices: 49.1 us -> 55.5 us
  other arithmetic: 20.8 us -> 14.8 us
  matrix products: 18.5 us -> 23.9 us
    all_to_all x2 -> x1, starting transfers between devices: 24.2 us -> 13.5 us  [on_device(): lax.all_to_all(payload, ('row', 'col'), split_axis=0, concat_axis=0, tile...]
    scatter-add x1 -> x0, other arithmetic: 9.59 us -> none  [on_device(): jax.ops.segment_sum(embedded, arrived_ids, num_segments=rows * cols)]
    scatter x2, local copies, waits for them, and re-layouts: 8.43 us -> 0.06 us  [the longest x1 0.05 us: on_device(): id_parts = id_parts.at[:, 1].set((where % 64).astype(jnp.bfloat16))]
    ppermute x8, starting transfers between devices: 28.6 us -> 21.7 us  [tree_sum(): x = kept + lax.ppermute(sent, axis, pairs)]
    dot_general x1 -> x3, matrix products: 1.23 us -> 7.44 us  [the longest x1 4.05 us: on_device(): jnp.dot(spread, jnp.concatenate([top, middle, bottom], axis=1), preferred...]
    ppermute x4, starting transfers between devices: 16.2 us -> 11.8 us  [with_halo(): before = lax.ppermute(last, axis, up)]
    another operation x2 -> x9, other arithmetic: 1.52 us -> 5.52 us
    ppermute x8, waiting for transfers between devices: 18.9 us -> 22.2 us  [tree_sum(): x = kept + lax.ppermute(sent, axis, pairs)]
  transfers between devices with their start and end apart: 26 -> 25, of which waited for: 18 -> 20; matrix products, arithmetic and copies ran while one was open for 11% -> 7% of each run, Pallas kernels for 0% -> 0%
where the time goes in v2:
time: 201 us; the launch traced here: 200 us
  starting transfers between devices  80.6 us (40%)
  waiting for transfers between devices  55.5 us (28%)
  local copies, waits for them, and re-layouts  24.1 us (12%)
  matrix products  23.9 us (12%)
  other arithmetic  14.8 us (7%)
    ppermute x8, starting transfers between devices, tree_sum(): got = lax.ppermute(x, axis, pairs)  28.3 us
    ppermute x8, waiting for transfers between devices, tree_sum(): x = kept + lax.ppermute(sent, axis, pairs)  22.2 us
    ppermute x8, starting transfers between devices, tree_sum(): x = kept + lax.ppermute(sent, axis, pairs)  21.7 us
    ppermute x8, waiting for transfers between devices, tree_sum(): got = lax.ppermute(x, axis, pairs)  19.3 us
    unnamed x48, local copies, waits for them, and re-layouts  17.6 us
    all_to_all x1, starting transfers between devices, on_device(): lax.all_to_all(payload, ('row', 'col'), split_axis=0, concat_axis=0, tile...  13.5 us
    ppermute x4, waiting for transfers between devices, with_halo(): after = lax.ppermute(leading, axis, down)  12.7 us
    ppermute x4, starting transfers between devices, with_halo(): before = lax.ppermute(last, axis, up)  11.8 us
  transfers between devices with their start and end apart: 25, of which 20 were waited for; matrix products, arithmetic and copies ran while one was open for 7% of the time, Pallas kernels for 0%

profile of v2, /device:TPU:1, one launch (start us, length us, event | category | flops | bytes accessed | tf_op | source)
XLA Modules:
  0.0 200.1 jit_solution(8608707553765081990)
XLA Ops:
  2.6 1.5 reduce-window.6
  4.6 1.3 broadcast_select_fusion
  5.9 1.4 broadcast_select_fusion.1
  8.2 2.7 %fusion.11 = f32[1280,128]{1,0:T(8,128)S(1)} fusion(bf16[512,128]{1,0:T(8,128)(2,1)} %param.18, s32[640]{0:T(1024)S(1)} %add_add_fusion, bf16[1,640,512]{2,1,0:T(8,128)(2,1)S(1)} %copy-done), kind=kOutput, calls=%fused_computation.23 | convolution fusion | flops 1008107520 | bytes 1444352 | tf_op jit(solution)/shard_map/dot_general | solution.py:91
  11.0 1.0 select_maximum_fusion
  12.0 13.5 %all-to-all-start = ((f32[64,21,128]{2,1,0:T(8,128)}), f32[64,21,128]{2,1,0:T(8,128)S(1)}, u32[]{:S(2)}, u32[]{:S(2)}) async-start(f32[64,21,128]{2,1,0:T(8,128)} %select_maximum_fusion), calls=%async_computation | async-start | bytes 1572864 | tf_op jit(solution)/shard_map/all_to_all | solution.py:99
  25.5 2.9 %collective-permute-start.4 = (bf16[2,64,128]{2,1,0:T(8,128)(2,1)S(1)}, bf16[2,64,128]{2,1,0:T(8,128)(2,1)S(1)}, u32[]{:S(2)}, u32[]{:S(2)}) collective-permute-start(bf16[2,64,128]{2,1,0:T(8,128)(2,1)S(1)} %get-tuple-element.76), channel_id=1, source_target_pairs={{0,64},{64,128},{128,192},{1,65},{65,129},{129,193},{2,66},{66,130... | collective-permute-start | bytes 98312 | tf_op jit(solution)/shard_map/ppermute | solution.py:16
  28.4 1.3 collective-permute-start.5
  30.8 3.0 %collective-permute-done.5 = bf16[2,64,128]{2,1,0:T(8,128)(2,1)S(1)} collective-permute-done((bf16[2,64,128]{2,1,0:T(8,128)(2,1)S(1)}, bf16[2,64,128]{2,1,0:T(8,128)(2,1)S(1)}, u32[]{:S(2)}, u32[]{:S(2)}) %collective-permute-start.5) | collective-permute-done | bytes 32800 | tf_op jit(solution)/shard_map/ppermute | solution.py:17
  33.9 2.7 %collective-permute-start.6 = (bf16[36,2,128]{2,1,0:T(2,128)(2,1)S(1)}, bf16[36,2,128]{2,1,0:T(2,128)(2,1)S(1)}, u32[]{:S(2)}, u32[]{:S(2)}) collective-permute-start(bf16[36,2,128]{2,1,0:T(2,128)(2,1)S(1)} %get-tuple-element.73), channel_id=1, source_target_pairs={{0,4},{4,8},{8,12},{12,16},{16,20},{20,24},{24,28},{28,32},{32,36}... | collective-permute-start | bytes 55304 | tf_op jit(solution)/shard_map/ppermute | solution.py:16
  36.5 1.3 collective-permute-start.7
  37.9 1.3 collective-permute-done.6
  39.2 3.9 %collective-permute-done.7 = bf16[36,2,128]{2,1,0:T(2,128)(2,1)S(1)} collective-permute-done((bf16[36,2,128]{2,1,0:T(2,128)(2,1)S(1)}, bf16[36,2,128]{2,1,0:T(2,128)(2,1)S(1)}, u32[]{:S(2)}, u32[]{:S(2)}) %collective-permute-start.7) | collective-permute-done | bytes 18464 | tf_op jit(solution)/shard_map/ppermute | solution.py:17
  45.7 0.9 constant_dynamic-update-slice_fusion.16
  51.1 1.0 fusion.79
  52.2 4.0 %fusion = f32[2048,384]{1,0:T(8,128)S(1)} fusion(f32[1280]{0:T(1024)S(1)} %eq.112, bf16[1280,128]{1,0:T(8,128)(2,1)} %get-tuple-element.60, bf16[1280,128]{1,0:T(8,128)(2,1)} %get-tuple-element.61, bf16[1280,128]{1,0:T(8,128)(2,1)S(1)} %get-tuple-element.59), kind=kOutput, calls=%fused_computation.1 | convolution fusion | flops 2018836480 | bytes 4133888 | tf_op jit(solution)/shard_map/dot_general | solution.py:109
  56.6 3.2 %collective-permute-start = (bf16[3,64,128]{2,1,0:T(8,128)(2,1)S(1)}, bf16[3,64,128]{2,1,0:T(8,128)(2,1)S(1)}, u32[]{:S(2)}, u32[]{:S(2)}) collective-permute-start(bf16[3,64,128]{2,1,0:T(8,128)(2,1)S(1)} %bitcast.194), channel_id=1, source_target_pairs={{0,64},{64,128},{128,192},{1,65},{65,129},{129,193},{2,66},{66,130... | collective-permute-start | bytes 147464 | tf_op jit(solution)/shard_map/ppermute | solution.py:16
  59.8 1.3 collective-permute-start.1
  61.9 2.7 %collective-permute-done.1 = bf16[3,64,128]{2,1,0:T(8,128)(2,1)S(1)} collective-permute-done((bf16[3,64,128]{2,1,0:T(8,128)(2,1)S(1)}, bf16[3,64,128]{2,1,0:T(8,128)(2,1)S(1)}, u32[]{:S(2)}, u32[]{:S(2)}) %collective-permute-start.1) | collective-permute-done | bytes 49184 | tf_op jit(solution)/shard_map/ppermute | solution.py:17
  64.6 3.0 %collective-permute-start.2 = (bf16[38,3,128]{2,1,0:T(4,128)(2,1)S(1)}, bf16[38,3,128]{2,1,0:T(4,128)(2,1)S(1)}, u32[]{:S(2)}, u32[]{:S(2)}) collective-permute-start(bf16[38,3,128]{2,1,0:T(4,128)(2,1)S(1)} %get-tuple-element.64), channel_id=1, source_target_pairs={{0,4},{4,8},{8,12},{12,16},{16,20},{20,24},{24,28},{28,32},{32,36}... | collective-permute-start | bytes 87560 | tf_op jit(solution)/shard_map/ppermute | solution.py:16
  67.7 1.5 collective-permute-start.3
  69.2 3.2 %collective-permute-done.3 = bf16[38,3,128]{2,1,0:T(4,128)(2,1)S(1)} collective-permute-done((bf16[38,3,128]{2,1,0:T(4,128)(2,1)S(1)}, bf16[38,3,128]{2,1,0:T(4,128)(2,1)S(1)}, u32[]{:S(2)}, u32[]{:S(2)}) %collective-permute-start.3) | collective-permute-done | bytes 29216 | tf_op jit(solution)/shard_map/ppermute | solution.py:17
  73.5 0.9 constant_dynamic-update-slice_fusion.9
  75.3 0.9 constant_dynamic-update-slice_fusion.7
  80.6 2.2 %select_convert_fusion = (bf16[36,68,128]{2,1,0:T(8,128)(2,1)S(1)}, f32[36,68,128]{2,1,0:T(8,128)S(1)}) fusion(pred[36,68]{1,0:T(8,128)(4,1)S(1)} %broadcast_and_fusion, bf16[36,68,1152]{2,1,0:T(8,128)(2,1)S(1)} %slice_dynamic-update-slice_fusion, bf16[1152,128,1]{1,0,2:T(8,128)(2,1)S(1)} %bitcast.201), kind=kOutput, calls=%fused_computation.24 | convolution fusion | flops 723824640 | bytes 7817616 | tf_op jit(solution)/shard_map/dot_general | solution.py:121
  82.9 1.3 fusion.16
  85.0 1.1 fusion.78
  87.0 1.4 fusion.81
  89.3 0.9 constant_dynamic-update-slice_fusion.3
  91.9 8.3 %fusion.23 = f32[1152,128]{1,0:T(8,128)S(1)} fusion(bf16[2048,1152]{1,0:T(8,128)(2,1)} %constant_dynamic-update-slice_fusion.1, f32[2048,128]{1,0:T(8,128)} %get-tuple-element.44, f32[2048,128]{1,0:T(8,128)S(1)} %get-tuple-element.43, bf16[2048,1152]{1,0:T(8,128)(2,1)} %constant_dynamic-update-slice_fusion.10, bf16[1152,128]{1,0:T(8,128)(2,1)} %bitcast.182, ...), kind=kOutput, calls=%fused_computation.42 | convolution fusion | flops 1209270272 | bytes 12943360 | tf_op jit(solution)/shard_map/dot_general | solution.py:69
  100.6 5.4 %collective-permute-start.8 = (f32[1152,128]{1,0:T(8,128)S(1)}, f32[1152,128]{1,0:T(8,128)}, u32[]{:S(2)}, u32[]{:S(2)}) collective-permute-start(f32[1152,128]{1,0:T(8,128)S(1)} %fusion.30), channel_id=1, source_target_pairs={{0,1},{1,0},{2,3},{3,2},{4,5},{5,4},{6,7},{7,6},{8,9},{9,8},{10,11... | collective-permute-start | bytes 1769480 | tf_op jit(solution)/shard_map/ppermute | solution.py:45
  106.0 1.8 collective-permute-done.8
  107.7 1.4 fusion.32
  109.2 1.4 collective-permute-start.9
  110.5 6.9 %collective-permute-done.9 = f32[576,128]{1,0:T(8,128)S(1)} collective-permute-done((f32[576,128]{1,0:T(8,128)S(1)}, f32[576,128]{1,0:T(8,128)S(1)}, u32[]{:S(2)}, u32[]{:S(2)}) %collective-permute-start.9) | collective-permute-done | bytes 294944 | tf_op jit(solution)/shard_map/ppermute | solution.py:45
  117.5 1.7 collective-permute-start.10
  119.3 3.9 %collective-permute-done.10 = f32[288,128]{1,0:T(8,128)S(1)} collective-permute-done((f32[288,128]{1,0:T(8,128)S(1)}, f32[288,128]{1,0:T(8,128)S(1)}, u32[]{:S(2)}, u32[]{:S(2)}) %collective-permute-start.10) | collective-permute-done | bytes 147488 | tf_op jit(solution)/shard_map/ppermute | solution.py:45
  123.2 2.9 %collective-permute-start.11 = (f32[144,128]{1,0:T(8,128)S(1)}, f32[144,128]{1,0:T(8,128)S(1)}, u32[]{:S(2)}, u32[]{:S(2)}) collective-permute-start(f32[144,128]{1,0:T(8,128)S(1)} %constant_dynamic-slice_fusion.6), channel_id=1, source_target_pairs={{0,4},{4,0},{8,12},{12,8},{16,20},{20,16},{24,28},{28,24},{32,36},... | collective-permute-start | bytes 221192 | tf_op jit(solution)/shard_map/ppermute | solution.py:45
  126.1 1.7 collective-permute-done.11
  127.8 3.0 %collective-permute-start.12 = (f32[72,128]{1,0:T(8,128)S(1)}, f32[72,128]{1,0:T(8,128)S(1)}, u32[]{:S(2)}, u32[]{:S(2)}) collective-permute-start(f32[72,128]{1,0:T(8,128)S(1)} %constant_dynamic-slice_fusion.5), channel_id=1, source_target_pairs={{0,8},{4,12},{8,0},{12,4},{16,24},{20,28},{24,16},{28,20},{32,40},... | collective-permute-start | bytes 110600 | tf_op jit(solution)/shard_map/ppermute | solution.py:45
  130.9 1.3 collective-permute-done.12
  132.2 2.6 %collective-permute-start.13 = (f32[36,128]{1,0:T(8,128)S(1)}, f32[36,128]{1,0:T(8,128)S(1)}, u32[]{:S(2)}, u32[]{:S(2)}) collective-permute-start(f32[36,128]{1,0:T(8,128)S(1)} %constant_dynamic-slice_fusion.4), channel_id=1, source_target_pairs={{0,16},{4,20},{8,24},{12,28},{16,0},{20,4},{24,8},{28,12},{32,48},... | collective-permute-start | bytes 55304 | tf_op jit(solution)/shard_map/ppermute | solution.py:45
  134.9 4.1 %collective-permute-done.13 = f32[36,128]{1,0:T(8,128)S(1)} collective-permute-done((f32[36,128]{1,0:T(8,128)S(1)}, f32[36,128]{1,0:T(8,128)S(1)}, u32[]{:S(2)}, u32[]{:S(2)}) %collective-permute-start.13) | collective-permute-done | bytes 18464 | tf_op jit(solution)/shard_map/ppermute | solution.py:45
  139.0 2.0 collective-permute-start.14
  141.0 1.1 collective-permute-done.14
  142.1 2.7 %collective-permute-start.15 = (f32[9,128]{1,0:T(8,128)S(1)}, f32[9,128]{1,0:T(8,128)S(1)}, u32[]{:S(2)}, u32[]{:S(2)}) collective-permute-start(f32[9,128]{1,0:T(8,128)S(1)} %constant_dynamic-slice_fusion), channel_id=1, source_target_pairs={{0,2},{1,3},{2,0},{3,1},{4,6},{5,7},{6,4},{7,5},{8,10},{9,11},{10,... | collective-permute-start | bytes 13832 | tf_op jit(solution)/shard_map/ppermute | solution.py:45
  144.8 1.4 collective-permute-done.15
  146.2 2.7 %collective-permute-start.16 = (f32[9,128]{1,0:T(8,128)S(1)}, f32[9,128]{1,0:T(8,128)S(1)}, u32[]{:S(2)}, u32[]{:S(2)}) collective-permute-start(f32[9,128]{1,0:T(8,128)S(1)} %fusion.62), channel_id=1, source_target_pairs={{0,2},{1,3},{2,0},{3,1},{4,6},{5,7},{6,4},{7,5},{8,10},{9,11},{10,... | collective-permute-start | bytes 13832 | tf_op jit(solution)/shard_map/ppermute | solution.py:49
  148.9 1.4 collective-permute-done.16
  150.3 1.5 collective-permute-start.17
  151.8 1.4 collective-permute-done.17
  153.3 2.2 %collective-permute-start.18 = (f32[36,128]{1,0:T(8,128)S(1)}, f32[36,128]{1,0:T(8,128)S(1)}, u32[]{:S(2)}, u32[]{:S(2)}) collective-permute-start(f32[36,128]{1,0:T(8,128)S(1)} %pad_maximum_fusion.15), channel_id=1, source_target_pairs={{0,16},{4,20},{8,24},{12,28},{16,0},{20,4},{24,8},{28,12},{32,48},... | collective-permute-start | bytes 55304 | tf_op jit(solution)/shard_map/ppermute | solution.py:49
  155.5 4.4 %collective-permute-done.18 = f32[36,128]{1,0:T(8,128)S(1)} collective-permute-done((f32[36,128]{1,0:T(8,128)S(1)}, f32[36,128]{1,0:T(8,128)S(1)}, u32[]{:S(2)}, u32[]{:S(2)}) %collective-permute-start.18) | collective-permute-done | bytes 18464 | tf_op jit(solution)/shard_map/ppermute | solution.py:49
  159.9 2.4 %collective-permute-start.19 = (f32[72,128]{1,0:T(8,128)S(1)}, f32[72,128]{1,0:T(8,128)S(1)}, u32[]{:S(2)}, u32[]{:S(2)}) collective-permute-start(f32[72,128]{1,0:T(8,128)S(1)} %pad_maximum_fusion.14), channel_id=1, source_target_pairs={{0,8},{4,12},{8,0},{12,4},{16,24},{20,28},{24,16},{28,20},{32,40},... | collective-permute-start | bytes 110600 | tf_op jit(solution)/shard_map/ppermute | solution.py:49
  162.3 1.4 collective-permute-done.19
  163.8 1.2 collective-permute-start.20
  164.9 2.1 %collective-permute-done.20 = f32[144,128]{1,0:T(8,128)S(1)} collective-permute-done((f32[144,128]{1,0:T(8,128)S(1)}, f32[144,128]{1,0:T(8,128)S(1)}, u32[]{:S(2)}, u32[]{:S(2)}) %collective-permute-start.20) | collective-permute-done | bytes 73760 | tf_op jit(solution)/shard_map/ppermute | solution.py:49
  167.1 1.5 collective-permute-start.21
  168.6 4.1 %collective-permute-done.21 = f32[288,128]{1,0:T(8,128)S(1)} collective-permute-done((f32[288,128]{1,0:T(8,128)S(1)}, f32[288,128]{1,0:T(8,128)S(1)}, u32[]{:S(2)}, u32[]{:S(2)}) %collective-permute-start.21) | collective-permute-done | bytes 147488 | tf_op jit(solution)/shard_map/ppermute | solution.py:49
  172.8 1.1 collective-permute-start.22
  173.9 4.5 %collective-permute-done.22 = f32[576,128]{1,0:T(8,128)S(1)} collective-permute-done((f32[576,128]{1,0:T(8,128)S(1)}, f32[576,128]{1,0:T(8,128)S(1)}, u32[]{:S(2)}, u32[]{:S(2)}) %collective-permute-start.22) | collective-permute-done | bytes 294944 | tf_op jit(solution)/shard_map/ppermute | solution.py:49
  178.7 15.7 %collective-permute-start.23 = (f32[1152,128]{1,0:T(8,128)S(1)}, f32[1152,128]{1,0:T(8,128)S(1)}, u32[]{:S(2)}, u32[]{:S(2)}) collective-permute-start(f32[1152,128]{1,0:T(8,128)S(1)} %get-tuple-element.66), channel_id=1, source_target_pairs={{0,1},{1,0},{2,3},{3,2},{4,5},{5,4},{6,7},{7,6},{8,9},{9,8},{10,11... | collective-permute-start | bytes 1769480 | tf_op jit(solution)/shard_map/ppermute | solution.py:49
  194.4 4.5 %fusion.8 = bf16[2048,128]{1,0:T(8,128)(2,1)} fusion(bf16[2048,1152]{1,0:T(8,128)(2,1)} %bitcast.164, bf16[1152,128]{1,0:T(8,128)(2,1)S(1)} %bitcast.187, bf16[2048,128]{1,0:T(8,128)(2,1)S(1)} %bitcast.186), kind=kOutput, calls=%fused_computation.12 | convolution fusion | flops 604766208 | bytes 6062080 | tf_op jit(solution)/shard_map/dot_general | solution.py:134
  198.9 1.2 fusion.27
  (119 shorter events, 24.7 us)
Async XLA Ops:
  0.6 7.6 %copy-start = (bf16[1,640,512]{2,1,0:T(8,128)(2,1)S(1)}, bf16[1,640,512]{2,1,0:T(8,128)(2,1)}, u32[]{:S(2)}) copy-start(bf16[1,640,512]{2,1,0:T(8,128)(2,1)} %param.15) | copy-start | bytes 1966084
  8.2 17.3 %copy-start.1 = (bf16[1,32,64,128]{3,2,1,0:T(8,128)(2,1)S(1)}, bf16[1,32,64,128]{3,2,1,0:T(8,128)(2,1)}, u32[]{:S(2)}) copy-start(bf16[1,32,64,128]{3,2,1,0:T(8,128)(2,1)} %param.21) | copy-start | bytes 1572868
  8.2 21.6 %copy-start.5 = (bf16[3,3,128,128]{3,2,1,0:T(8,128)(2,1)S(1)}, bf16[3,3,128,128]{3,2,1,0:T(8,128)(2,1)}, u32[]{:S(2)}) copy-start(bf16[3,3,128,128]{3,2,1,0:T(8,128)(2,1)} %param.20) | copy-start | bytes 884740
  12.0 39.0 %all-to-all-start = ((f32[64,21,128]{2,1,0:T(8,128)}), f32[64,21,128]{2,1,0:T(8,128)S(1)}, u32[]{:S(2)}, u32[]{:S(2)}) async-start(f32[64,21,128]{2,1,0:T(8,128)} %select_maximum_fusion), calls=%async_computation | async-start | bytes 1572864 | tf_op jit(solution)/shard_map/all_to_all | solution.py:99
  25.5 5.3 %collective-permute-start.4 = (bf16[2,64,128]{2,1,0:T(8,128)(2,1)S(1)}, bf16[2,64,128]{2,1,0:T(8,128)(2,1)S(1)}, u32[]{:S(2)}, u32[]{:S(2)}) collective-permute-start(bf16[2,64,128]{2,1,0:T(8,128)(2,1)S(1)} %get-tuple-element.76), channel_id=1, source_target_pairs={{0,64},{64,128},{128,192},{1,65},{65,129},{129,193},{2,66},{66,130... | collective-permute-start | bytes 98312 | tf_op jit(solution)/shard_map/ppermute | solution.py:16
  28.4 5.4 %collective-permute-start.5 = (bf16[2,64,128]{2,1,0:T(8,128)(2,1)S(1)}, bf16[2,64,128]{2,1,0:T(8,128)(2,1)S(1)}, u32[]{:S(2)}, u32[]{:S(2)}) collective-permute-start(bf16[2,64,128]{2,1,0:T(8,128)(2,1)S(1)} %get-tuple-element.77), channel_id=1, source_target_pairs={{64,0},{128,64},{192,128},{65,1},{129,65},{193,129},{66,2},{130,66... | collective-permute-start | bytes 98312 | tf_op jit(solution)/shard_map/ppermute | solution.py:17
  33.9 5.3 %collective-permute-start.6 = (bf16[36,2,128]{2,1,0:T(2,128)(2,1)S(1)}, bf16[36,2,128]{2,1,0:T(2,128)(2,1)S(1)}, u32[]{:S(2)}, u32[]{:S(2)}) collective-permute-start(bf16[36,2,128]{2,1,0:T(2,128)(2,1)S(1)} %get-tuple-element.73), channel_id=1, source_target_pairs={{0,4},{4,8},{8,12},{12,16},{16,20},{20,24},{24,28},{28,32},{32,36}... | collective-permute-start | bytes 55304 | tf_op jit(solution)/shard_map/ppermute | solution.py:16
  36.5 6.5 %collective-permute-start.7 = (bf16[36,2,128]{2,1,0:T(2,128)(2,1)S(1)}, bf16[36,2,128]{2,1,0:T(2,128)(2,1)S(1)}, u32[]{:S(2)}, u32[]{:S(2)}) collective-permute-start(bf16[36,2,128]{2,1,0:T(2,128)(2,1)S(1)} %get-tuple-element.72), channel_id=1, source_target_pairs={{4,0},{8,4},{12,8},{16,12},{20,16},{24,20},{28,24},{32,28},{36,32}... | collective-permute-start | bytes 55304 | tf_op jit(solution)/shard_map/ppermute | solution.py:17
  52.2 4.1 %copy-start.4 = (bf16[1,32,64,128]{3,2,1,0:T(8,128)(2,1)S(1)}, bf16[1,32,64,128]{3,2,1,0:T(8,128)(2,1)}, u32[]{:S(2)}) copy-start(bf16[1,32,64,128]{3,2,1,0:T(8,128)(2,1)} %param.14) | copy-start | bytes 1572868
  56.6 5.3 %collective-permute-start = (bf16[3,64,128]{2,1,0:T(8,128)(2,1)S(1)}, bf16[3,64,128]{2,1,0:T(8,128)(2,1)S(1)}, u32[]{:S(2)}, u32[]{:S(2)}) collective-permute-start(bf16[3,64,128]{2,1,0:T(8,128)(2,1)S(1)} %bitcast.194), channel_id=1, source_target_pairs={{0,64},{64,128},{128,192},{1,65},{65,129},{129,193},{2,66},{66,130... | collective-permute-start | bytes 147464 | tf_op jit(solution)/shard_map/ppermute | solution.py:16
  59.8 4.8 %collective-permute-start.1 = (bf16[3,64,128]{2,1,0:T(8,128)(2,1)S(1)}, bf16[3,64,128]{2,1,0:T(8,128)(2,1)S(1)}, u32[]{:S(2)}, u32[]{:S(2)}) collective-permute-start(bf16[3,64,128]{2,1,0:T(8,128)(2,1)S(1)} %bitcast.193), channel_id=1, source_target_pairs={{64,0},{128,64},{192,128},{65,1},{129,65},{193,129},{66,2},{130,66... | collective-permute-start | bytes 147464 | tf_op jit(solution)/shard_map/ppermute | solution.py:17
  64.6 4.6 %collective-permute-start.2 = (bf16[38,3,128]{2,1,0:T(4,128)(2,1)S(1)}, bf16[38,3,128]{2,1,0:T(4,128)(2,1)S(1)}, u32[]{:S(2)}, u32[]{:S(2)}) collective-permute-start(bf16[38,3,128]{2,1,0:T(4,128)(2,1)S(1)} %get-tuple-element.64), channel_id=1, source_target_pairs={{0,4},{4,8},{8,12},{12,16},{16,20},{20,24},{24,28},{28,32},{32,36}... | collective-permute-start | bytes 87560 | tf_op jit(solution)/shard_map/ppermute | solution.py:16
  67.7 4.7 %collective-permute-start.3 = (bf16[38,3,128]{2,1,0:T(4,128)(2,1)S(1)}, bf16[38,3,128]{2,1,0:T(4,128)(2,1)S(1)}, u32[]{:S(2)}, u32[]{:S(2)}) collective-permute-start(bf16[38,3,128]{2,1,0:T(4,128)(2,1)S(1)} %get-tuple-element.65), channel_id=1, source_target_pairs={{4,0},{8,4},{12,8},{16,12},{20,16},{24,20},{28,24},{32,28},{36,32}... | collective-permute-start | bytes 87560 | tf_op jit(solution)/shard_map/ppermute | solution.py:17
  78.7 1.9 copy-start.7
  87.0 5.0 %copy-start.2 = (bf16[32,64,1152]{2,1,0:T(8,128)(2,1)}, bf16[32,64,1152]{2,1,0:T(8,128)(2,1)S(1)}, u32[]{:S(2)}) copy-start(bf16[32,64,1152]{2,1,0:T(8,128)(2,1)S(1)} %slice_dynamic-update-slice_fusion.9) | copy-start | bytes 14155780
  100.6 7.2 %collective-permute-start.8 = (f32[1152,128]{1,0:T(8,128)S(1)}, f32[1152,128]{1,0:T(8,128)}, u32[]{:S(2)}, u32[]{:S(2)}) collective-permute-start(f32[1152,128]{1,0:T(8,128)S(1)} %fusion.30), channel_id=1, source_target_pairs={{0,1},{1,0},{2,3},{3,2},{4,5},{5,4},{6,7},{7,6},{8,9},{9,8},{10,11... | collective-permute-start | bytes 1769480 | tf_op jit(solution)/shard_map/ppermute | solution.py:45
  109.1 85.2 %copy-start.3 = (bf16[32,64,128]{2,1,0:T(8,128)(2,1)S(1)}, bf16[32,64,128]{2,1,0:T(8,128)(2,1)}, u32[]{:S(2)}) copy-start(bf16[32,64,128]{2,1,0:T(8,128)(2,1)} %get-tuple-element.57) | copy-start | bytes 1572868
  109.1 85.2 %copy-start.6 = (bf16[3,3,128,128]{3,2,1,0:T(8,128)(2,1)S(1)}, bf16[3,3,128,128]{3,2,1,0:T(8,128)(2,1)}, u32[]{:S(2)}) copy-start(bf16[3,3,128,128]{3,2,1,0:T(8,128)(2,1)} %param.20) | copy-start | bytes 884740
  109.2 8.3 %collective-permute-start.9 = (f32[576,128]{1,0:T(8,128)S(1)}, f32[576,128]{1,0:T(8,128)S(1)}, u32[]{:S(2)}, u32[]{:S(2)}) collective-permute-start(f32[576,128]{1,0:T(8,128)S(1)} %constant_dynamic-slice_fusion.8), channel_id=1, source_target_pairs={{0,64},{64,0},{128,192},{192,128},{1,65},{65,1},{129,193},{193,129... | collective-permute-start | bytes 884744 | tf_op jit(solution)/shard_map/ppermute | solution.py:45
  117.5 5.6 %collective-permute-start.10 = (f32[288,128]{1,0:T(8,128)S(1)}, f32[288,128]{1,0:T(8,128)S(1)}, u32[]{:S(2)}, u32[]{:S(2)}) collective-permute-start(f32[288,128]{1,0:T(8,128)S(1)} %constant_dynamic-slice_fusion.7), channel_id=1, source_target_pairs={{0,128},{64,192},{128,0},{192,64},{1,129},{65,193},{129,1},{193,65... | collective-permute-start | bytes 442376 | tf_op jit(solution)/shard_map/ppermute | solution.py:45
  123.2 4.6 %collective-permute-start.11 = (f32[144,128]{1,0:T(8,128)S(1)}, f32[144,128]{1,0:T(8,128)S(1)}, u32[]{:S(2)}, u32[]{:S(2)}) collective-permute-start(f32[144,128]{1,0:T(8,128)S(1)} %constant_dynamic-slice_fusion.6), channel_id=1, source_target_pairs={{0,4},{4,0},{8,12},{12,8},{16,20},{20,16},{24,28},{28,24},{32,36},... | collective-permute-start | bytes 221192 | tf_op jit(solution)/shard_map/ppermute | solution.py:45
  127.8 4.4 %collective-permute-start.12 = (f32[72,128]{1,0:T(8,128)S(1)}, f32[72,128]{1,0:T(8,128)S(1)}, u32[]{:S(2)}, u32[]{:S(2)}) collective-permute-start(f32[72,128]{1,0:T(8,128)S(1)} %constant_dynamic-slice_fusion.5), channel_id=1, source_target_pairs={{0,8},{4,12},{8,0},{12,4},{16,24},{20,28},{24,16},{28,20},{32,40},... | collective-permute-start | bytes 110600 | tf_op jit(solution)/shard_map/ppermute | solution.py:45
  132.2 6.7 %collective-permute-start.13 = (f32[36,128]{1,0:T(8,128)S(1)}, f32[36,128]{1,0:T(8,128)S(1)}, u32[]{:S(2)}, u32[]{:S(2)}) collective-permute-start(f32[36,128]{1,0:T(8,128)S(1)} %constant_dynamic-slice_fusion.4), channel_id=1, source_target_pairs={{0,16},{4,20},{8,24},{12,28},{16,0},{20,4},{24,8},{28,12},{32,48},... | collective-permute-start | bytes 55304 | tf_op jit(solution)/shard_map/ppermute | solution.py:45
  139.0 3.1 %collective-permute-start.14 = (f32[18,128]{1,0:T(8,128)S(1)}, f32[18,128]{1,0:T(8,128)S(1)}, u32[]{:S(2)}, u32[]{:S(2)}) collective-permute-start(f32[18,128]{1,0:T(8,128)S(1)} %constant_dynamic-slice_fusion.2), channel_id=1, source_target_pairs={{0,32},{4,36},{8,40},{12,44},{16,48},{20,52},{24,56},{28,60},{32,0... | collective-permute-start | bytes 27656 | tf_op jit(solution)/shard_map/ppermute | solution.py:45
  142.1 4.1 %collective-permute-start.15 = (f32[9,128]{1,0:T(8,128)S(1)}, f32[9,128]{1,0:T(8,128)S(1)}, u32[]{:S(2)}, u32[]{:S(2)}) collective-permute-start(f32[9,128]{1,0:T(8,128)S(1)} %constant_dynamic-slice_fusion), channel_id=1, source_target_pairs={{0,2},{1,3},{2,0},{3,1},{4,6},{5,7},{6,4},{7,5},{8,10},{9,11},{10,... | collective-permute-start | bytes 13832 | tf_op jit(solution)/shard_map/ppermute | solution.py:45
  146.2 4.1 %collective-permute-start.16 = (f32[9,128]{1,0:T(8,128)S(1)}, f32[9,128]{1,0:T(8,128)S(1)}, u32[]{:S(2)}, u32[]{:S(2)}) collective-permute-start(f32[9,128]{1,0:T(8,128)S(1)} %fusion.62), channel_id=1, source_target_pairs={{0,2},{1,3},{2,0},{3,1},{4,6},{5,7},{6,4},{7,5},{8,10},{9,11},{10,... | collective-permute-start | bytes 13832 | tf_op jit(solution)/shard_map/ppermute | solution.py:49
  150.3 2.9 %collective-permute-start.17 = (f32[18,128]{1,0:T(8,128)S(1)}, f32[18,128]{1,0:T(8,128)S(1)}, u32[]{:S(2)}, u32[]{:S(2)}) collective-permute-start(f32[18,128]{1,0:T(8,128)S(1)} %pad_maximum_fusion.19), channel_id=1, source_target_pairs={{0,32},{4,36},{8,40},{12,44},{16,48},{20,52},{24,56},{28,60},{32,0... | collective-permute-start | bytes 27656 | tf_op jit(solution)/shard_map/ppermute | solution.py:49
  153.3 6.6 %collective-permute-start.18 = (f32[36,128]{1,0:T(8,128)S(1)}, f32[36,128]{1,0:T(8,128)S(1)}, u32[]{:S(2)}, u32[]{:S(2)}) collective-permute-start(f32[36,128]{1,0:T(8,128)S(1)} %pad_maximum_fusion.15), channel_id=1, source_target_pairs={{0,16},{4,20},{8,24},{12,28},{16,0},{20,4},{24,8},{28,12},{32,48},... | collective-permute-start | bytes 55304 | tf_op jit(solution)/shard_map/ppermute | solution.py:49
  159.9 3.8 %collective-permute-start.19 = (f32[72,128]{1,0:T(8,128)S(1)}, f32[72,128]{1,0:T(8,128)S(1)}, u32[]{:S(2)}, u32[]{:S(2)}) collective-permute-start(f32[72,128]{1,0:T(8,128)S(1)} %pad_maximum_fusion.14), channel_id=1, source_target_pairs={{0,8},{4,12},{8,0},{12,4},{16,24},{20,28},{24,16},{28,20},{32,40},... | collective-permute-start | bytes 110600 | tf_op jit(solution)/shard_map/ppermute | solution.py:49
  163.8 3.3 %collective-permute-start.20 = (f32[144,128]{1,0:T(8,128)S(1)}, f32[144,128]{1,0:T(8,128)S(1)}, u32[]{:S(2)}, u32[]{:S(2)}) collective-permute-start(f32[144,128]{1,0:T(8,128)S(1)} %get-tuple-element.90), channel_id=1, source_target_pairs={{0,4},{4,0},{8,12},{12,8},{16,20},{20,16},{24,28},{28,24},{32,36},... | collective-permute-start | bytes 221192 | tf_op jit(solution)/shard_map/ppermute | solution.py:49
  167.1 5.6 %collective-permute-start.21 = (f32[288,128]{1,0:T(8,128)S(1)}, f32[288,128]{1,0:T(8,128)S(1)}, u32[]{:S(2)}, u32[]{:S(2)}) collective-permute-start(f32[288,128]{1,0:T(8,128)S(1)} %get-tuple-element.86), channel_id=1, source_target_pairs={{0,128},{64,192},{128,0},{192,64},{1,129},{65,193},{129,1},{193,65... | collective-permute-start | bytes 442376 | tf_op jit(solution)/shard_map/ppermute | solution.py:49
  172.8 5.7 %collective-permute-start.22 = (f32[576,128]{1,0:T(8,128)S(1)}, f32[576,128]{1,0:T(8,128)S(1)}, u32[]{:S(2)}, u32[]{:S(2)}) collective-permute-start(f32[576,128]{1,0:T(8,128)S(1)} %get-tuple-element.82), channel_id=1, source_target_pairs={{0,64},{64,0},{128,192},{192,128},{1,65},{65,1},{129,193},{193,129... | collective-permute-start | bytes 884744 | tf_op jit(solution)/shard_map/ppermute | solution.py:49
  178.7 20.2 %collective-permute-start.23 = (f32[1152,128]{1,0:T(8,128)S(1)}, f32[1152,128]{1,0:T(8,128)S(1)}, u32[]{:S(2)}, u32[]{:S(2)}) collective-permute-start(f32[1152,128]{1,0:T(8,128)S(1)} %get-tuple-element.66), channel_id=1, source_target_pairs={{0,1},{1,0},{2,3},{3,2},{4,5},{5,4},{6,7},{7,6},{8,9},{9,8},{10,11... | collective-permute-start | bytes 1769480 | tf_op jit(solution)/shard_map/ppermute | solution.py:49

commit v3 on v2

--- a/solution.py
+++ b/solution.py
@@ -102,13 +102,12 @@
     spread = (
         arrived_ids[None, :] == jnp.arange(rows * cols, dtype=jnp.float32)[:, None]
     ).astype(jnp.bfloat16)
-    top = embedded.astype(jnp.bfloat16)
-    rest = embedded - top.astype(jnp.float32)
-    middle = rest.astype(jnp.bfloat16)
-    bottom = (rest - middle.astype(jnp.float32)).astype(jnp.bfloat16)
-    pieces = jnp.dot(
-        spread, jnp.concatenate([top, middle, bottom], axis=1), preferred_element_type=jnp.float32
-    )
+    top = lax.reduce_precision(embedded, exponent_bits=8, mantissa_bits=7)
+    rest = embedded - top
+    middle = lax.reduce_precision(rest, exponent_bits=8, mantissa_bits=7)
+    bottom = rest - middle
+    split = jnp.concatenate([top, middle, bottom], axis=1).astype(jnp.bfloat16)
+    pieces = jnp.dot(spread, split, preferred_element_type=jnp.float32)
     placed = pieces[:, :chans] + pieces[:, chans : 2 * chans] + pieces[:, 2 * chans :]
     first_in = (
         (cells.astype(jnp.float32).reshape(rows * cols, chans) + placed)

time: 201 us -> 201 us (level)
    another operation x6 -> x7, other arithmetic: 5.5 us -> 6.5 us
where the time goes in v3:
time: 201 us; the launch traced here: 200 us
  starting transfers between devices  80.8 us (40%)
  waiting for transfers between devices  55.3 us (28%)
  local copies, waits for them, and re-layouts  24.1 us (12%)
  matrix products  23.9 us (12%)
  other arithmetic  14.8 us (7%)
    ppermute x8, starting transfers between devices, tree_sum(): got = lax.ppermute(x, axis, pairs)  28.4 us
    ppermute x8, waiting for transfers between devices, tree_sum(): x = kept + lax.ppermute(sent, axis, pairs)  22.1 us
    ppermute x8, starting transfers between devices, tree_sum(): x = kept + lax.ppermute(sent, axis, pairs)  21.8 us
    ppermute x8, waiting for transfers between devices, tree_sum(): got = lax.ppermute(x, axis, pairs)  19.3 us
    unnamed x48, local copies, waits for them, and re-layouts  17.6 us
    all_to_all x1, starting transfers between devices, on_device(): lax.all_to_all(payload, ('row', 'col'), split_axis=0, concat_axis=0, tile...  13.5 us
    ppermute x4, waiting for transfers between devices, with_halo(): after = lax.ppermute(leading, axis, down)  12.7 us
    ppermute x4, starting transfers between devices, with_halo(): before = lax.ppermute(last, axis, up)  11.8 us
  transfers between devices with their start and end apart: 25, of which 20 were waited for; matrix products, arithmetic and copies ran while one was open for 7% of the time, Pallas kernels for 0%

profile of v3, /device:TPU:1, one launch (start us, length us, event | category | flops | bytes accessed | tf_op | source)
XLA Modules:
  0.0 200.1 jit_solution(2278743591582561256)
XLA Ops:
  2.6 1.5 reduce-window.6
  4.6 1.3 broadcast_select_fusion
  5.9 1.4 broadcast_select_fusion.1
  8.2 2.7 %fusion.11 = f32[1280,128]{1,0:T(8,128)S(1)} fusion(bf16[512,128]{1,0:T(8,128)(2,1)} %param.18, s32[640]{0:T(1024)S(1)} %add_add_fusion, bf16[1,640,512]{2,1,0:T(8,128)(2,1)S(1)} %copy-done), kind=kOutput, calls=%fused_computation.23 | convolution fusion | flops 1008107520 | bytes 1444352 | tf_op jit(solution)/shard_map/dot_general | solution.py:91
  11.0 1.0 select_maximum_fusion
  12.0 13.5 %all-to-all-start = ((f32[64,21,128]{2,1,0:T(8,128)}), f32[64,21,128]{2,1,0:T(8,128)S(1)}, u32[]{:S(2)}, u32[]{:S(2)}) async-start(f32[64,21,128]{2,1,0:T(8,128)} %select_maximum_fusion), calls=%async_computation | async-start | bytes 1572864 | tf_op jit(solution)/shard_map/all_to_all | solution.py:99
  25.5 2.9 %collective-permute-start.4 = (bf16[2,64,128]{2,1,0:T(8,128)(2,1)S(1)}, bf16[2,64,128]{2,1,0:T(8,128)(2,1)S(1)}, u32[]{:S(2)}, u32[]{:S(2)}) collective-permute-start(bf16[2,64,128]{2,1,0:T(8,128)(2,1)S(1)} %get-tuple-element.76), channel_id=1, source_target_pairs={{0,64},{64,128},{128,192},{1,65},{65,129},{129,193},{2,66},{66,130... | collective-permute-start | bytes 98312 | tf_op jit(solution)/shard_map/ppermute | solution.py:16
  28.4 1.3 collective-permute-start.5
  30.8 3.0 %collective-permute-done.5 = bf16[2,64,128]{2,1,0:T(8,128)(2,1)S(1)} collective-permute-done((bf16[2,64,128]{2,1,0:T(8,128)(2,1)S(1)}, bf16[2,64,128]{2,1,0:T(8,128)(2,1)S(1)}, u32[]{:S(2)}, u32[]{:S(2)}) %collective-permute-start.5) | collective-permute-done | bytes 32800 | tf_op jit(solution)/shard_map/ppermute | solution.py:17
  33.9 2.7 %collective-permute-start.6 = (bf16[36,2,128]{2,1,0:T(2,128)(2,1)S(1)}, bf16[36,2,128]{2,1,0:T(2,128)(2,1)S(1)}, u32[]{:S(2)}, u32[]{:S(2)}) collective-permute-start(bf16[36,2,128]{2,1,0:T(2,128)(2,1)S(1)} %get-tuple-element.73), channel_id=1, source_target_pairs={{0,4},{4,8},{8,12},{12,16},{16,20},{20,24},{24,28},{28,32},{32,36}... | collective-permute-start | bytes 55304 | tf_op jit(solution)/shard_map/ppermute | solution.py:16
  36.5 1.3 collective-permute-start.7
  37.9 1.3 collective-permute-done.6
  39.2 3.9 %collective-permute-done.7 = bf16[36,2,128]{2,1,0:T(2,128)(2,1)S(1)} collective-permute-done((bf16[36,2,128]{2,1,0:T(2,128)(2,1)S(1)}, bf16[36,2,128]{2,1,0:T(2,128)(2,1)S(1)}, u32[]{:S(2)}, u32[]{:S(2)}) %collective-permute-start.7) | collective-permute-done | bytes 18464 | tf_op jit(solution)/shard_map/ppermute | solution.py:17
  45.7 0.9 constant_dynamic-update-slice_fusion.16
  51.1 1.0 reduce-precision_convert_fusion.1
  52.3 4.0 %fusion = f32[2048,384]{1,0:T(8,128)S(1)} fusion(f32[1280]{0:T(1024)S(1)} %eq.112, bf16[1280,128]{1,0:T(8,128)(2,1)} %get-tuple-element.60, bf16[1280,128]{1,0:T(8,128)(2,1)} %get-tuple-element.61, bf16[1280,128]{1,0:T(8,128)(2,1)S(1)} %get-tuple-element.59), kind=kOutput, calls=%fused_computation.1 | convolution fusion | flops 2018836480 | bytes 4133888 | tf_op jit(solution)/shard_map/dot_general | solution.py:110
  56.6 3.2 %collective-permute-start = (bf16[3,64,128]{2,1,0:T(8,128)(2,1)S(1)}, bf16[3,64,128]{2,1,0:T(8,128)(2,1)S(1)}, u32[]{:S(2)}, u32[]{:S(2)}) collective-permute-start(bf16[3,64,128]{2,1,0:T(8,128)(2,1)S(1)} %bitcast.194), channel_id=1, source_target_pairs={{0,64},{64,128},{128,192},{1,65},{65,129},{129,193},{2,66},{66,130... | collective-permute-start | bytes 147464 | tf_op jit(solution)/shard_map/ppermute | solution.py:16
  59.8 1.3 collective-permute-start.1
  62.0 2.7 %collective-permute-done.1 = bf16[3,64,128]{2,1,0:T(8,128)(2,1)S(1)} collective-permute-done((bf16[3,64,128]{2,1,0:T(8,128)(2,1)S(1)}, bf16[3,64,128]{2,1,0:T(8,128)(2,1)S(1)}, u32[]{:S(2)}, u32[]{:S(2)}) %collective-permute-start.1) | collective-permute-done | bytes 49184 | tf_op jit(solution)/shard_map/ppermute | solution.py:17
  64.7 3.0 %collective-permute-start.2 = (bf16[38,3,128]{2,1,0:T(4,128)(2,1)S(1)}, bf16[38,3,128]{2,1,0:T(4,128)(2,1)S(1)}, u32[]{:S(2)}, u32[]{:S(2)}) collective-permute-start(bf16[38,3,128]{2,1,0:T(4,128)(2,1)S(1)} %get-tuple-element.64), channel_id=1, source_target_pairs={{0,4},{4,8},{8,12},{12,16},{16,20},{20,24},{24,28},{28,32},{32,36}... | collective-permute-start | bytes 87560 | tf_op jit(solution)/shard_map/ppermute | solution.py:16
  67.7 1.5 collective-permute-start.3
  69.3 3.2 %collective-permute-done.3 = bf16[38,3,128]{2,1,0:T(4,128)(2,1)S(1)} collective-permute-done((bf16[38,3,128]{2,1,0:T(4,128)(2,1)S(1)}, bf16[38,3,128]{2,1,0:T(4,128)(2,1)S(1)}, u32[]{:S(2)}, u32[]{:S(2)}) %collective-permute-start.3) | collective-permute-done | bytes 29216 | tf_op jit(solution)/shard_map/ppermute | solution.py:17
  73.6 0.9 constant_dynamic-update-slice_fusion.9
  75.3 0.9 constant_dynamic-update-slice_fusion.7
  80.6 2.2 %select_convert_fusion = (bf16[36,68,128]{2,1,0:T(8,128)(2,1)S(1)}, f32[36,68,128]{2,1,0:T(8,128)S(1)}) fusion(pred[36,68]{1,0:T(8,128)(4,1)S(1)} %broadcast_and_fusion, bf16[36,68,1152]{2,1,0:T(8,128)(2,1)S(1)} %slice_dynamic-update-slice_fusion, bf16[1152,128,1]{1,0,2:T(8,128)(2,1)S(1)} %bitcast.201), kind=kOutput, calls=%fused_computation.24 | convolution fusion | flops 723824640 | bytes 7817616 | tf_op jit(solution)/shard_map/dot_general | solution.py:120
  83.0 1.3 fusion.16
  85.0 1.1 fusion.78
  87.0 1.4 fusion.80
  89.3 0.9 constant_dynamic-update-slice_fusion.3
  92.0 8.3 %fusion.23 = f32[1152,128]{1,0:T(8,128)S(1)} fusion(bf16[2048,1152]{1,0:T(8,128)(2,1)} %constant_dynamic-update-slice_fusion.1, f32[2048,128]{1,0:T(8,128)} %get-tuple-element.44, f32[2048,128]{1,0:T(8,128)S(1)} %get-tuple-element.43, bf16[2048,1152]{1,0:T(8,128)(2,1)} %constant_dynamic-update-slice_fusion.10, bf16[1152,128]{1,0:T(8,128)(2,1)} %bitcast.182, ...), kind=kOutput, calls=%fused_computation.46 | convolution fusion | flops 1209270272 | bytes 12943360 | tf_op jit(solution)/shard_map/dot_general | solution.py:69
  100.6 5.4 %collective-permute-start.8 = (f32[1152,128]{1,0:T(8,128)S(1)}, f32[1152,128]{1,0:T(8,128)}, u32[]{:S(2)}, u32[]{:S(2)}) collective-permute-start(f32[1152,128]{1,0:T(8,128)S(1)} %fusion.31), channel_id=1, source_target_pairs={{0,1},{1,0},{2,3},{3,2},{4,5},{5,4},{6,7},{7,6},{8,9},{9,8},{10,11... | collective-permute-start | bytes 1769480 | tf_op jit(solution)/shard_map/ppermute | solution.py:45
  106.0 1.8 collective-permute-done.8
  107.7 1.4 fusion.33
  109.2 1.4 collective-permute-start.9
  110.6 6.9 %collective-permute-done.9 = f32[576,128]{1,0:T(8,128)S(1)} collective-permute-done((f32[576,128]{1,0:T(8,128)S(1)}, f32[576,128]{1,0:T(8,128)S(1)}, u32[]{:S(2)}, u32[]{:S(2)}) %collective-permute-start.9) | collective-permute-done | bytes 294944 | tf_op jit(solution)/shard_map/ppermute | solution.py:45
  117.6 1.7 collective-permute-start.10
  119.3 3.8 %collective-permute-done.10 = f32[288,128]{1,0:T(8,128)S(1)} collective-permute-done((f32[288,128]{1,0:T(8,128)S(1)}, f32[288,128]{1,0:T(8,128)S(1)}, u32[]{:S(2)}, u32[]{:S(2)}) %collective-permute-start.10) | collective-permute-done | bytes 147488 | tf_op jit(solution)/shard_map/ppermute | solution.py:45
  123.2 2.9 %collective-permute-start.11 = (f32[144,128]{1,0:T(8,128)S(1)}, f32[144,128]{1,0:T(8,128)S(1)}, u32[]{:S(2)}, u32[]{:S(2)}) collective-permute-start(f32[144,128]{1,0:T(8,128)S(1)} %constant_dynamic-slice_fusion.6), channel_id=1, source_target_pairs={{0,4},{4,0},{8,12},{12,8},{16,20},{20,16},{24,28},{28,24},{32,36},... | collective-permute-start | bytes 221192 | tf_op jit(solution)/shard_map/ppermute | solution.py:45
  126.1 1.7 collective-permute-done.11
  127.9 3.0 %collective-permute-start.12 = (f32[72,128]{1,0:T(8,128)S(1)}, f32[72,128]{1,0:T(8,128)S(1)}, u32[]{:S(2)}, u32[]{:S(2)}) collective-permute-start(f32[72,128]{1,0:T(8,128)S(1)} %constant_dynamic-slice_fusion.5), channel_id=1, source_target_pairs={{0,8},{4,12},{8,0},{12,4},{16,24},{20,28},{24,16},{28,20},{32,40},... | collective-permute-start | bytes 110600 | tf_op jit(solution)/shard_map/ppermute | solution.py:45
  130.9 1.3 collective-permute-done.12
  132.2 2.7 %collective-permute-start.13 = (f32[36,128]{1,0:T(8,128)S(1)}, f32[36,128]{1,0:T(8,128)S(1)}, u32[]{:S(2)}, u32[]{:S(2)}) collective-permute-start(f32[36,128]{1,0:T(8,128)S(1)} %constant_dynamic-slice_fusion.4), channel_id=1, source_target_pairs={{0,16},{4,20},{8,24},{12,28},{16,0},{20,4},{24,8},{28,12},{32,48},... | collective-permute-start | bytes 55304 | tf_op jit(solution)/shard_map/ppermute | solution.py:45
  134.9 4.0 %collective-permute-done.13 = f32[36,128]{1,0:T(8,128)S(1)} collective-permute-done((f32[36,128]{1,0:T(8,128)S(1)}, f32[36,128]{1,0:T(8,128)S(1)}, u32[]{:S(2)}, u32[]{:S(2)}) %collective-permute-start.13) | collective-permute-done | bytes 18464 | tf_op jit(solution)/shard_map/ppermute | solution.py:45
  138.9 2.1 %collective-permute-start.14 = (f32[18,128]{1,0:T(8,128)S(1)}, f32[18,128]{1,0:T(8,128)S(1)}, u32[]{:S(2)}, u32[]{:S(2)}) collective-permute-start(f32[18,128]{1,0:T(8,128)S(1)} %constant_dynamic-slice_fusion.2), channel_id=1, source_target_pairs={{0,32},{4,36},{8,40},{12,44},{16,48},{20,52},{24,56},{28,60},{32,0... | collective-permute-start | bytes 27656 | tf_op jit(solution)/shard_map/ppermute | solution.py:45
  141.0 1.1 collective-permute-done.14
  142.1 2.7 %collective-permute-start.15 = (f32[9,128]{1,0:T(8,128)S(1)}, f32[9,128]{1,0:T(8,128)S(1)}, u32[]{:S(2)}, u32[]{:S(2)}) collective-permute-start(f32[9,128]{1,0:T(8,128)S(1)} %constant_dynamic-slice_fusion), channel_id=1, source_target_pairs={{0,2},{1,3},{2,0},{3,1},{4,6},{5,7},{6,4},{7,5},{8,10},{9,11},{10,... | collective-permute-start | bytes 13832 | tf_op jit(solution)/shard_map/ppermute | solution.py:45
  144.8 1.4 collective-permute-done.15
  146.2 2.7 %collective-permute-start.16 = (f32[9,128]{1,0:T(8,128)S(1)}, f32[9,128]{1,0:T(8,128)S(1)}, u32[]{:S(2)}, u32[]{:S(2)}) collective-permute-start(f32[9,128]{1,0:T(8,128)S(1)} %fusion.62), channel_id=1, source_target_pairs={{0,2},{1,3},{2,0},{3,1},{4,6},{5,7},{6,4},{7,5},{8,10},{9,11},{10,... | collective-permute-start | bytes 13832 | tf_op jit(solution)/shard_map/ppermute | solution.py:49
  148.9 1.4 collective-permute-done.16
  150.3 1.5 collective-permute-start.17
  151.9 1.4 collective-permute-done.17
  153.3 2.2 %collective-permute-start.18 = (f32[36,128]{1,0:T(8,128)S(1)}, f32[36,128]{1,0:T(8,128)S(1)}, u32[]{:S(2)}, u32[]{:S(2)}) collective-permute-start(f32[36,128]{1,0:T(8,128)S(1)} %pad_maximum_fusion.15), channel_id=1, source_target_pairs={{0,16},{4,20},{8,24},{12,28},{16,0},{20,4},{24,8},{28,12},{32,48},... | collective-permute-start | bytes 55304 | tf_op jit(solution)/shard_map/ppermute | solution.py:49
  155.5 4.4 %collective-permute-done.18 = f32[36,128]{1,0:T(8,128)S(1)} collective-permute-done((f32[36,128]{1,0:T(8,128)S(1)}, f32[36,128]{1,0:T(8,128)S(1)}, u32[]{:S(2)}, u32[]{:S(2)}) %collective-permute-start.18) | collective-permute-done | bytes 18464 | tf_op jit(solution)/shard_map/ppermute | solution.py:49
  160.0 2.4 %collective-permute-start.19 = (f32[72,128]{1,0:T(8,128)S(1)}, f32[72,128]{1,0:T(8,128)S(1)}, u32[]{:S(2)}, u32[]{:S(2)}) collective-permute-start(f32[72,128]{1,0:T(8,128)S(1)} %pad_maximum_fusion.14), channel_id=1, source_target_pairs={{0,8},{4,12},{8,0},{12,4},{16,24},{20,28},{24,16},{28,20},{32,40},... | collective-permute-start | bytes 110600 | tf_op jit(solution)/shard_map/ppermute | solution.py:49
  162.3 1.4 collective-permute-done.19
  163.8 1.2 collective-permute-start.20
  165.0 2.1 %collective-permute-done.20 = f32[144,128]{1,0:T(8,128)S(1)} collective-permute-done((f32[144,128]{1,0:T(8,128)S(1)}, f32[144,128]{1,0:T(8,128)S(1)}, u32[]{:S(2)}, u32[]{:S(2)}) %collective-permute-start.20) | collective-permute-done | bytes 73760 | tf_op jit(solution)/shard_map/ppermute | solution.py:49
  167.2 1.5 collective-permute-start.21
  168.7 4.1 %collective-permute-done.21 = f32[288,128]{1,0:T(8,128)S(1)} collective-permute-done((f32[288,128]{1,0:T(8,128)S(1)}, f32[288,128]{1,0:T(8,128)S(1)}, u32[]{:S(2)}, u32[]{:S(2)}) %collective-permute-start.21) | collective-permute-done | bytes 147488 | tf_op jit(solution)/shard_map/ppermute | solution.py:49
  172.9 1.1 collective-permute-start.22
  174.0 4.5 %collective-permute-done.22 = f32[576,128]{1,0:T(8,128)S(1)} collective-permute-done((f32[576,128]{1,0:T(8,128)S(1)}, f32[576,128]{1,0:T(8,128)S(1)}, u32[]{:S(2)}, u32[]{:S(2)}) %collective-permute-start.22) | collective-permute-done | bytes 294944 | tf_op jit(solution)/shard_map/ppermute | solution.py:49
  178.7 15.7 %collective-permute-start.23 = (f32[1152,128]{1,0:T(8,128)S(1)}, f32[1152,128]{1,0:T(8,128)S(1)}, u32[]{:S(2)}, u32[]{:S(2)}) collective-permute-start(f32[1152,128]{1,0:T(8,128)S(1)} %get-tuple-element.66), channel_id=1, source_target_pairs={{0,1},{1,0},{2,3},{3,2},{4,5},{5,4},{6,7},{7,6},{8,9},{9,8},{10,11... | collective-permute-start | bytes 1769480 | tf_op jit(solution)/shard_map/ppermute | solution.py:49
  194.4 4.5 %fusion.8 = bf16[2048,128]{1,0:T(8,128)(2,1)} fusion(bf16[2048,1152]{1,0:T(8,128)(2,1)} %bitcast.164, bf16[1152,128]{1,0:T(8,128)(2,1)S(1)} %bitcast.187, bf16[2048,128]{1,0:T(8,128)(2,1)S(1)} %bitcast.186), kind=kOutput, calls=%fused_computation.12 | convolution fusion | flops 604766208 | bytes 6062080 | tf_op jit(solution)/shard_map/dot_general | solution.py:133
  198.9 1.2 fusion.28
  (119 shorter events, 24.7 us)
Async XLA Ops:
  0.6 7.6 %copy-start = (bf16[1,640,512]{2,1,0:T(8,128)(2,1)S(1)}, bf16[1,640,512]{2,1,0:T(8,128)(2,1)}, u32[]{:S(2)}) copy-start(bf16[1,640,512]{2,1,0:T(8,128)(2,1)} %param.15) | copy-start | bytes 1966084
  8.2 17.3 %copy-start.1 = (bf16[1,32,64,128]{3,2,1,0:T(8,128)(2,1)S(1)}, bf16[1,32,64,128]{3,2,1,0:T(8,128)(2,1)}, u32[]{:S(2)}) copy-start(bf16[1,32,64,128]{3,2,1,0:T(8,128)(2,1)} %param.21) | copy-start | bytes 1572868
  8.2 21.6 %copy-start.5 = (bf16[3,3,128,128]{3,2,1,0:T(8,128)(2,1)S(1)}, bf16[3,3,128,128]{3,2,1,0:T(8,128)(2,1)}, u32[]{:S(2)}) copy-start(bf16[3,3,128,128]{3,2,1,0:T(8,128)(2,1)} %param.20) | copy-start | bytes 884740
  12.0 39.0 %all-to-all-start = ((f32[64,21,128]{2,1,0:T(8,128)}), f32[64,21,128]{2,1,0:T(8,128)S(1)}, u32[]{:S(2)}, u32[]{:S(2)}) async-start(f32[64,21,128]{2,1,0:T(8,128)} %select_maximum_fusion), calls=%async_computation | async-start | bytes 1572864 | tf_op jit(solution)/shard_map/all_to_all | solution.py:99
  25.5 5.3 %collective-permute-start.4 = (bf16[2,64,128]{2,1,0:T(8,128)(2,1)S(1)}, bf16[2,64,128]{2,1,0:T(8,128)(2,1)S(1)}, u32[]{:S(2)}, u32[]{:S(2)}) collective-permute-start(bf16[2,64,128]{2,1,0:T(8,128)(2,1)S(1)} %get-tuple-element.76), channel_id=1, source_target_pairs={{0,64},{64,128},{128,192},{1,65},{65,129},{129,193},{2,66},{66,130... | collective-permute-start | bytes 98312 | tf_op jit(solution)/shard_map/ppermute | solution.py:16
  28.4 5.4 %collective-permute-start.5 = (bf16[2,64,128]{2,1,0:T(8,128)(2,1)S(1)}, bf16[2,64,128]{2,1,0:T(8,128)(2,1)S(1)}, u32[]{:S(2)}, u32[]{:S(2)}) collective-permute-start(bf16[2,64,128]{2,1,0:T(8,128)(2,1)S(1)} %get-tuple-element.77), channel_id=1, source_target_pairs={{64,0},{128,64},{192,128},{65,1},{129,65},{193,129},{66,2},{130,66... | collective-permute-start | bytes 98312 | tf_op jit(solution)/shard_map/ppermute | solution.py:17
  33.9 5.3 %collective-permute-start.6 = (bf16[36,2,128]{2,1,0:T(2,128)(2,1)S(1)}, bf16[36,2,128]{2,1,0:T(2,128)(2,1)S(1)}, u32[]{:S(2)}, u32[]{:S(2)}) collective-permute-start(bf16[36,2,128]{2,1,0:T(2,128)(2,1)S(1)} %get-tuple-element.73), channel_id=1, source_target_pairs={{0,4},{4,8},{8,12},{12,16},{16,20},{20,24},{24,28},{28,32},{32,36}... | collective-permute-start | bytes 55304 | tf_op jit(solution)/shard_map/ppermute | solution.py:16
  36.5 6.5 %collective-permute-start.7 = (bf16[36,2,128]{2,1,0:T(2,128)(2,1)S(1)}, bf16[36,2,128]{2,1,0:T(2,128)(2,1)S(1)}, u32[]{:S(2)}, u32[]{:S(2)}) collective-permute-start(bf16[36,2,128]{2,1,0:T(2,128)(2,1)S(1)} %get-tuple-element.72), channel_id=1, source_target_pairs={{4,0},{8,4},{12,8},{16,12},{20,16},{24,20},{28,24},{32,28},{36,32}... | collective-permute-start | bytes 55304 | tf_op jit(solution)/shard_map/ppermute | solution.py:17
  52.3 4.1 %copy-start.4 = (bf16[1,32,64,128]{3,2,1,0:T(8,128)(2,1)S(1)}, bf16[1,32,64,128]{3,2,1,0:T(8,128)(2,1)}, u32[]{:S(2)}) copy-start(bf16[1,32,64,128]{3,2,1,0:T(8,128)(2,1)} %param.14) | copy-start | bytes 1572868
  56.6 5.4 %collective-permute-start = (bf16[3,64,128]{2,1,0:T(8,128)(2,1)S(1)}, bf16[3,64,128]{2,1,0:T(8,128)(2,1)S(1)}, u32[]{:S(2)}, u32[]{:S(2)}) collective-permute-start(bf16[3,64,128]{2,1,0:T(8,128)(2,1)S(1)} %bitcast.194), channel_id=1, source_target_pairs={{0,64},{64,128},{128,192},{1,65},{65,129},{129,193},{2,66},{66,130... | collective-permute-start | bytes 147464 | tf_op jit(solution)/shard_map/ppermute | solution.py:16
  59.8 4.8 %collective-permute-start.1 = (bf16[3,64,128]{2,1,0:T(8,128)(2,1)S(1)}, bf16[3,64,128]{2,1,0:T(8,128)(2,1)S(1)}, u32[]{:S(2)}, u32[]{:S(2)}) collective-permute-start(bf16[3,64,128]{2,1,0:T(8,128)(2,1)S(1)} %bitcast.193), channel_id=1, source_target_pairs={{64,0},{128,64},{192,128},{65,1},{129,65},{193,129},{66,2},{130,66... | collective-permute-start | bytes 147464 | tf_op jit(solution)/shard_map/ppermute | solution.py:17
  64.7 4.6 %collective-permute-start.2 = (bf16[38,3,128]{2,1,0:T(4,128)(2,1)S(1)}, bf16[38,3,128]{2,1,0:T(4,128)(2,1)S(1)}, u32[]{:S(2)}, u32[]{:S(2)}) collective-permute-start(bf16[38,3,128]{2,1,0:T(4,128)(2,1)S(1)} %get-tuple-element.64), channel_id=1, source_target_pairs={{0,4},{4,8},{8,12},{12,16},{16,20},{20,24},{24,28},{28,32},{32,36}... | collective-permute-start | bytes 87560 | tf_op jit(solution)/shard_map/ppermute | solution.py:16
  67.7 4.7 %collective-permute-start.3 = (bf16[38,3,128]{2,1,0:T(4,128)(2,1)S(1)}, bf16[38,3,128]{2,1,0:T(4,128)(2,1)S(1)}, u32[]{:S(2)}, u32[]{:S(2)}) collective-permute-start(bf16[38,3,128]{2,1,0:T(4,128)(2,1)S(1)} %get-tuple-element.65), channel_id=1, source_target_pairs={{4,0},{8,4},{12,8},{16,12},{20,16},{24,20},{28,24},{32,28},{36,32}... | collective-permute-start | bytes 87560 | tf_op jit(solution)/shard_map/ppermute | solution.py:17
  78.7 1.9 copy-start.7
  87.0 5.0 %copy-start.2 = (bf16[32,64,1152]{2,1,0:T(8,128)(2,1)}, bf16[32,64,1152]{2,1,0:T(8,128)(2,1)S(1)}, u32[]{:S(2)}) copy-start(bf16[32,64,1152]{2,1,0:T(8,128)(2,1)S(1)} %slice_dynamic-update-slice_fusion.9) | copy-start | bytes 14155780
  100.6 7.1 %collective-permute-start.8 = (f32[1152,128]{1,0:T(8,128)S(1)}, f32[1152,128]{1,0:T(8,128)}, u32[]{:S(2)}, u32[]{:S(2)}) collective-permute-start(f32[1152,128]{1,0:T(8,128)S(1)} %fusion.31), channel_id=1, source_target_pairs={{0,1},{1,0},{2,3},{3,2},{4,5},{5,4},{6,7},{7,6},{8,9},{9,8},{10,11... | collective-permute-start | bytes 1769480 | tf_op jit(solution)/shard_map/ppermute | solution.py:45
  109.1 85.2 %copy-start.3 = (bf16[32,64,128]{2,1,0:T(8,128)(2,1)S(1)}, bf16[32,64,128]{2,1,0:T(8,128)(2,1)}, u32[]{:S(2)}) copy-start(bf16[32,64,128]{2,1,0:T(8,128)(2,1)} %get-tuple-element.57) | copy-start | bytes 1572868
  109.2 85.2 %copy-start.6 = (bf16[3,3,128,128]{3,2,1,0:T(8,128)(2,1)S(1)}, bf16[3,3,128,128]{3,2,1,0:T(8,128)(2,1)}, u32[]{:S(2)}) copy-start(bf16[3,3,128,128]{3,2,1,0:T(8,128)(2,1)} %param.20) | copy-start | bytes 884740
  109.2 8.3 %collective-permute-start.9 = (f32[576,128]{1,0:T(8,128)S(1)}, f32[576,128]{1,0:T(8,128)S(1)}, u32[]{:S(2)}, u32[]{:S(2)}) collective-permute-start(f32[576,128]{1,0:T(8,128)S(1)} %constant_dynamic-slice_fusion.8), channel_id=1, source_target_pairs={{0,64},{64,0},{128,192},{192,128},{1,65},{65,1},{129,193},{193,129... | collective-permute-start | bytes 884744 | tf_op jit(solution)/shard_map/ppermute | solution.py:45
  117.6 5.6 %collective-permute-start.10 = (f32[288,128]{1,0:T(8,128)S(1)}, f32[288,128]{1,0:T(8,128)S(1)}, u32[]{:S(2)}, u32[]{:S(2)}) collective-permute-start(f32[288,128]{1,0:T(8,128)S(1)} %constant_dynamic-slice_fusion.7), channel_id=1, source_target_pairs={{0,128},{64,192},{128,0},{192,64},{1,129},{65,193},{129,1},{193,65... | collective-permute-start | bytes 442376 | tf_op jit(solution)/shard_map/ppermute | solution.py:45
  123.2 4.7 %collective-permute-start.11 = (f32[144,128]{1,0:T(8,128)S(1)}, f32[144,128]{1,0:T(8,128)S(1)}, u32[]{:S(2)}, u32[]{:S(2)}) collective-permute-start(f32[144,128]{1,0:T(8,128)S(1)} %constant_dynamic-slice_fusion.6), channel_id=1, source_target_pairs={{0,4},{4,0},{8,12},{12,8},{16,20},{20,16},{24,28},{28,24},{32,36},... | collective-permute-start | bytes 221192 | tf_op jit(solution)/shard_map/ppermute | solution.py:45
  127.9 4.3 %collective-permute-start.12 = (f32[72,128]{1,0:T(8,128)S(1)}, f32[72,128]{1,0:T(8,128)S(1)}, u32[]{:S(2)}, u32[]{:S(2)}) collective-permute-start(f32[72,128]{1,0:T(8,128)S(1)} %constant_dynamic-slice_fusion.5), channel_id=1, source_target_pairs={{0,8},{4,12},{8,0},{12,4},{16,24},{20,28},{24,16},{28,20},{32,40},... | collective-permute-start | bytes 110600 | tf_op jit(solution)/shard_map/ppermute | solution.py:45
  132.2 6.7 %collective-permute-start.13 = (f32[36,128]{1,0:T(8,128)S(1)}, f32[36,128]{1,0:T(8,128)S(1)}, u32[]{:S(2)}, u32[]{:S(2)}) collective-permute-start(f32[36,128]{1,0:T(8,128)S(1)} %constant_dynamic-slice_fusion.4), channel_id=1, source_target_pairs={{0,16},{4,20},{8,24},{12,28},{16,0},{20,4},{24,8},{28,12},{32,48},... | collective-permute-start | bytes 55304 | tf_op jit(solution)/shard_map/ppermute | solution.py:45
  138.9 3.1 %collective-permute-start.14 = (f32[18,128]{1,0:T(8,128)S(1)}, f32[18,128]{1,0:T(8,128)S(1)}, u32[]{:S(2)}, u32[]{:S(2)}) collective-permute-start(f32[18,128]{1,0:T(8,128)S(1)} %constant_dynamic-slice_fusion.2), channel_id=1, source_target_pairs={{0,32},{4,36},{8,40},{12,44},{16,48},{20,52},{24,56},{28,60},{32,0... | collective-permute-start | bytes 27656 | tf_op jit(solution)/shard_map/ppermute | solution.py:45
  142.1 4.1 %collective-permute-start.15 = (f32[9,128]{1,0:T(8,128)S(1)}, f32[9,128]{1,0:T(8,128)S(1)}, u32[]{:S(2)}, u32[]{:S(2)}) collective-permute-start(f32[9,128]{1,0:T(8,128)S(1)} %constant_dynamic-slice_fusion), channel_id=1, source_target_pairs={{0,2},{1,3},{2,0},{3,1},{4,6},{5,7},{6,4},{7,5},{8,10},{9,11},{10,... | collective-permute-start | bytes 13832 | tf_op jit(solution)/shard_map/ppermute | solution.py:45
  146.2 4.1 %collective-permute-start.16 = (f32[9,128]{1,0:T(8,128)S(1)}, f32[9,128]{1,0:T(8,128)S(1)}, u32[]{:S(2)}, u32[]{:S(2)}) collective-permute-start(f32[9,128]{1,0:T(8,128)S(1)} %fusion.62), channel_id=1, source_target_pairs={{0,2},{1,3},{2,0},{3,1},{4,6},{5,7},{6,4},{7,5},{8,10},{9,11},{10,... | collective-permute-start | bytes 13832 | tf_op jit(solution)/shard_map/ppermute | solution.py:49
  150.3 2.9 %collective-permute-start.17 = (f32[18,128]{1,0:T(8,128)S(1)}, f32[18,128]{1,0:T(8,128)S(1)}, u32[]{:S(2)}, u32[]{:S(2)}) collective-permute-start(f32[18,128]{1,0:T(8,128)S(1)} %pad_maximum_fusion.19), channel_id=1, source_target_pairs={{0,32},{4,36},{8,40},{12,44},{16,48},{20,52},{24,56},{28,60},{32,0... | collective-permute-start | bytes 27656 | tf_op jit(solution)/shard_map/ppermute | solution.py:49
  153.3 6.6 %collective-permute-start.18 = (f32[36,128]{1,0:T(8,128)S(1)}, f32[36,128]{1,0:T(8,128)S(1)}, u32[]{:S(2)}, u32[]{:S(2)}) collective-permute-start(f32[36,128]{1,0:T(8,128)S(1)} %pad_maximum_fusion.15), channel_id=1, source_target_pairs={{0,16},{4,20},{8,24},{12,28},{16,0},{20,4},{24,8},{28,12},{32,48},... | collective-permute-start | bytes 55304 | tf_op jit(solution)/shard_map/ppermute | solution.py:49
  160.0 3.8 %collective-permute-start.19 = (f32[72,128]{1,0:T(8,128)S(1)}, f32[72,128]{1,0:T(8,128)S(1)}, u32[]{:S(2)}, u32[]{:S(2)}) collective-permute-start(f32[72,128]{1,0:T(8,128)S(1)} %pad_maximum_fusion.14), channel_id=1, source_target_pairs={{0,8},{4,12},{8,0},{12,4},{16,24},{20,28},{24,16},{28,20},{32,40},... | collective-permute-start | bytes 110600 | tf_op jit(solution)/shard_map/ppermute | solution.py:49
  163.8 3.3 %collective-permute-start.20 = (f32[144,128]{1,0:T(8,128)S(1)}, f32[144,128]{1,0:T(8,128)S(1)}, u32[]{:S(2)}, u32[]{:S(2)}) collective-permute-start(f32[144,128]{1,0:T(8,128)S(1)} %get-tuple-element.90), channel_id=1, source_target_pairs={{0,4},{4,0},{8,12},{12,8},{16,20},{20,16},{24,28},{28,24},{32,36},... | collective-permute-start | bytes 221192 | tf_op jit(solution)/shard_map/ppermute | solution.py:49
  167.2 5.6 %collective-permute-start.21 = (f32[288,128]{1,0:T(8,128)S(1)}, f32[288,128]{1,0:T(8,128)S(1)}, u32[]{:S(2)}, u32[]{:S(2)}) collective-permute-start(f32[288,128]{1,0:T(8,128)S(1)} %get-tuple-element.86), channel_id=1, source_target_pairs={{0,128},{64,192},{128,0},{192,64},{1,129},{65,193},{129,1},{193,65... | collective-permute-start | bytes 442376 | tf_op jit(solution)/shard_map/ppermute | solution.py:49
  172.9 5.7 %collective-permute-start.22 = (f32[576,128]{1,0:T(8,128)S(1)}, f32[576,128]{1,0:T(8,128)S(1)}, u32[]{:S(2)}, u32[]{:S(2)}) collective-permute-start(f32[576,128]{1,0:T(8,128)S(1)} %get-tuple-element.82), channel_id=1, source_target_pairs={{0,64},{64,0},{128,192},{192,128},{1,65},{65,1},{129,193},{193,129... | collective-permute-start | bytes 884744 | tf_op jit(solution)/shard_map/ppermute | solution.py:49
  178.7 20.2 %collective-permute-start.23 = (f32[1152,128]{1,0:T(8,128)S(1)}, f32[1152,128]{1,0:T(8,128)S(1)}, u32[]{:S(2)}, u32[]{:S(2)}) collective-permute-start(f32[1152,128]{1,0:T(8,128)S(1)} %get-tuple-element.66), channel_id=1, source_target_pairs={{0,1},{1,0},{2,3},{3,2},{4,5},{5,4},{6,7},{7,6},{8,9},{9,8},{10,11... | collective-permute-start | bytes 1769480 | tf_op jit(solution)/shard_map/ppermute | solution.py:49

commit v4 on v3

--- a/solution.py
+++ b/solution.py
@@ -145,6 +145,7 @@
     )
     sigmoid_pre = jax.nn.sigmoid(pre1)
     grad_pre1 = (grad_act1 * sigmoid_pre * (1.0 + pre1 * (1.0 - sigmoid_pre))).astype(jnp.bfloat16)
+    grad_pre1 = lax.optimization_barrier(grad_pre1)
     first_term = contract_rows(patches0, grad_pre1)
     second_term = contract_rows(patches1, back_flat)
     first_sum, second_sum = jnp.split(tree_sum(jnp.concatenate([first_term, second_term])), 2)

time: 201 us -> 189 us (0.940)
  local copies, waits for them, and re-layouts: 24.1 us -> 16.7 us
  matrix products: 23.9 us -> 20.9 us
    dot_general x2, matrix products: 9.68 us -> 2.86 us  [contract_rows(): lax.dot_general(left, right, (((0,), (0,)), ((), ())), preferred_element_...]
    unnamed x48, local copies, waits for them, and re-layouts: 17.6 us -> 11.9 us
    dot_general x0 -> x1, matrix products: none -> 3.8 us  [on_device(): jnp.dot(unfold(padded_back, 2, rows, cols), w_turned, preferred_element_t...]
where the time goes in v4:
time: 189 us
  starting transfers between devices  80.8 us (43%)
  waiting for transfers between devices  55.9 us (30%)
  matrix products  20.9 us (11%)
  local copies, waits for them, and re-layouts  16.7 us (9%)
  other arithmetic  12.8 us (7%)
    ppermute x8, starting transfers between devices, tree_sum(): got = lax.ppermute(x, axis, pairs)  28.3 us
    ppermute x8, waiting for transfers between devices, tree_sum(): x = kept + lax.ppermute(sent, axis, pairs)  22 us
    ppermute x8, starting transfers between devices, tree_sum(): x = kept + lax.ppermute(sent, axis, pairs)  21.8 us
    ppermute x8, waiting for transfers between devices, tree_sum(): got = lax.ppermute(x, axis, pairs)  19.3 us
    all_to_all x1, starting transfers between devices, on_device(): lax.all_to_all(payload, ('row', 'col'), split_axis=0, concat_axis=0, tile...  13.5 us
    ppermute x4, waiting for transfers between devices, with_halo(): after = lax.ppermute(leading, axis, down)  13.3 us
    unnamed x48, local copies, waits for them, and re-layouts  11.9 us
    ppermute x4, starting transfers between devices, with_halo(): before = lax.ppermute(last, axis, up)  11.8 us
  transfers between devices with their start and end apart: 25, of which 20 were waited for; matrix products, arithmetic and copies ran while one was open for 7% of the time, Pallas kernels for 0%

profile of v4, /device:TPU:1, one launch (start us, length us, event | category | flops | bytes accessed | tf_op | source)
XLA Modules:
  0.0 188.5 jit_solution(4634426476611673208)
XLA Ops:
  2.6 1.5 reduce-window.6
  4.6 1.3 broadcast_select_fusion
  5.9 1.4 broadcast_select_fusion.1
  8.2 2.7 %fusion.11 = f32[1280,128]{1,0:T(8,128)S(1)} fusion(bf16[512,128]{1,0:T(8,128)(2,1)} %param.18, s32[640]{0:T(1024)S(1)} %add_add_fusion, bf16[1,640,512]{2,1,0:T(8,128)(2,1)S(1)} %copy-done), kind=kOutput, calls=%fused_computation.23 | convolution fusion | flops 1008107520 | bytes 1444352 | tf_op jit(solution)/shard_map/dot_general | solution.py:91
  11.0 1.0 select_maximum_fusion
  12.0 13.5 %all-to-all-start = ((f32[64,21,128]{2,1,0:T(8,128)}), f32[64,21,128]{2,1,0:T(8,128)S(1)}, u32[]{:S(2)}, u32[]{:S(2)}) async-start(f32[64,21,128]{2,1,0:T(8,128)} %select_maximum_fusion), calls=%async_computation | async-start | bytes 1572864 | tf_op jit(solution)/shard_map/all_to_all | solution.py:99
  25.5 2.9 %collective-permute-start.4 = (bf16[2,64,128]{2,1,0:T(8,128)(2,1)S(1)}, bf16[2,64,128]{2,1,0:T(8,128)(2,1)S(1)}, u32[]{:S(2)}, u32[]{:S(2)}) collective-permute-start(bf16[2,64,128]{2,1,0:T(8,128)(2,1)S(1)} %get-tuple-element.76), channel_id=1, source_target_pairs={{0,64},{64,128},{128,192},{1,65},{65,129},{129,193},{2,66},{66,130... | collective-permute-start | bytes 98312 | tf_op jit(solution)/shard_map/ppermute | solution.py:16
  28.5 1.3 collective-permute-start.5
  30.2 3.7 %collective-permute-done.5 = bf16[2,64,128]{2,1,0:T(8,128)(2,1)S(1)} collective-permute-done((bf16[2,64,128]{2,1,0:T(8,128)(2,1)S(1)}, bf16[2,64,128]{2,1,0:T(8,128)(2,1)S(1)}, u32[]{:S(2)}, u32[]{:S(2)}) %collective-permute-start.5) | collective-permute-done | bytes 32800 | tf_op jit(solution)/shard_map/ppermute | solution.py:17
  33.9 2.7 %collective-permute-start.6 = (bf16[36,2,128]{2,1,0:T(2,128)(2,1)S(1)}, bf16[36,2,128]{2,1,0:T(2,128)(2,1)S(1)}, u32[]{:S(2)}, u32[]{:S(2)}) collective-permute-start(bf16[36,2,128]{2,1,0:T(2,128)(2,1)S(1)} %get-tuple-element.73), channel_id=1, source_target_pairs={{0,4},{4,8},{8,12},{12,16},{16,20},{20,24},{24,28},{28,32},{32,36}... | collective-permute-start | bytes 55304 | tf_op jit(solution)/shard_map/ppermute | solution.py:16
  36.5 1.3 collective-permute-start.7
  37.9 1.3 collective-permute-done.6
  39.2 3.9 %collective-permute-done.7 = bf16[36,2,128]{2,1,0:T(2,128)(2,1)S(1)} collective-permute-done((bf16[36,2,128]{2,1,0:T(2,128)(2,1)S(1)}, bf16[36,2,128]{2,1,0:T(2,128)(2,1)S(1)}, u32[]{:S(2)}, u32[]{:S(2)}) %collective-permute-start.7) | collective-permute-done | bytes 18464 | tf_op jit(solution)/shard_map/ppermute | solution.py:17
  46.6 0.9 constant_dynamic-update-slice_fusion.15
  47.6 0.9 constant_dynamic-update-slice_fusion.14
  48.5 0.9 constant_dynamic-update-slice_fusion.13
  49.4 0.9 constant_dynamic-update-slice_fusion.12
  50.3 0.9 constant_dynamic-update-slice_fusion.11
  51.2 1.1 reduce-precision_convert_fusion.1
  52.5 4.1 %fusion = f32[2048,384]{1,0:T(8,128)S(1)} fusion(f32[1280]{0:T(1024)S(1)} %eq.112, bf16[1280,128]{1,0:T(8,128)(2,1)} %get-tuple-element.60, bf16[1280,128]{1,0:T(8,128)(2,1)} %get-tuple-element.61, bf16[1280,128]{1,0:T(8,128)(2,1)} %get-tuple-element.59), kind=kOutput, calls=%fused_computation.1 | convolution fusion | flops 2018836480 | bytes 4133888 | tf_op jit(solution)/shard_map/dot_general | solution.py:110
  56.9 3.2 %collective-permute-start = (bf16[3,64,128]{2,1,0:T(8,128)(2,1)S(1)}, bf16[3,64,128]{2,1,0:T(8,128)(2,1)S(1)}, u32[]{:S(2)}, u32[]{:S(2)}) collective-permute-start(bf16[3,64,128]{2,1,0:T(8,128)(2,1)S(1)} %bitcast.195), channel_id=1, source_target_pairs={{0,64},{64,128},{128,192},{1,65},{65,129},{129,193},{2,66},{66,130... | collective-permute-start | bytes 147464 | tf_op jit(solution)/shard_map/ppermute | solution.py:16
  60.1 1.3 collective-permute-start.1
  62.3 2.7 %collective-permute-done.1 = bf16[3,64,128]{2,1,0:T(8,128)(2,1)S(1)} collective-permute-done((bf16[3,64,128]{2,1,0:T(8,128)(2,1)S(1)}, bf16[3,64,128]{2,1,0:T(8,128)(2,1)S(1)}, u32[]{:S(2)}, u32[]{:S(2)}) %collective-permute-start.1) | collective-permute-done | bytes 49184 | tf_op jit(solution)/shard_map/ppermute | solution.py:17
  65.0 3.0 %collective-permute-start.2 = (bf16[38,3,128]{2,1,0:T(4,128)(2,1)S(1)}, bf16[38,3,128]{2,1,0:T(4,128)(2,1)S(1)}, u32[]{:S(2)}, u32[]{:S(2)}) collective-permute-start(bf16[38,3,128]{2,1,0:T(4,128)(2,1)S(1)} %get-tuple-element.64), channel_id=1, source_target_pairs={{0,4},{4,8},{8,12},{12,16},{16,20},{20,24},{24,28},{28,32},{32,36}... | collective-permute-start | bytes 87560 | tf_op jit(solution)/shard_map/ppermute | solution.py:16
  68.0 1.5 collective-permute-start.3
  69.6 3.2 %collective-permute-done.3 = bf16[38,3,128]{2,1,0:T(4,128)(2,1)S(1)} collective-permute-done((bf16[38,3,128]{2,1,0:T(4,128)(2,1)S(1)}, bf16[38,3,128]{2,1,0:T(4,128)(2,1)S(1)}, u32[]{:S(2)}, u32[]{:S(2)}) %collective-permute-start.3) | collective-permute-done | bytes 29216 | tf_op jit(solution)/shard_map/ppermute | solution.py:17
  75.4 2.2 %select_convert_fusion = (bf16[36,68,128]{2,1,0:T(8,128)(2,1)S(1)}, f32[36,68,128]{2,1,0:T(8,128)S(1)}) fusion(pred[36,68]{1,0:T(8,128)(4,1)S(1)} %broadcast_and_fusion, bf16[36,68,1152]{2,1,0:T(8,128)(2,1)S(1)} %slice_dynamic-update-slice_fusion, bf16[1152,128,1]{1,0,2:T(8,128)(2,1)S(1)} %bitcast.202), kind=kOutput, calls=%fused_computation.24 | convolution fusion | flops 723824640 | bytes 7817616 | tf_op jit(solution)/shard_map/dot_general | solution.py:120
  78.0 3.8 %fusion.7 = bf16[2048,128]{1,0:T(8,128)(2,1)S(1)} fusion(f32[2048,128]{1,0:T(8,128)S(1)} %get-tuple-element.44, f32[2048,128]{1,0:T(8,128)S(1)} %get-tuple-element.43, bf16[2048,1152]{1,0:T(8,128)(2,1)} %constant_dynamic-update-slice_fusion.10, bf16[1152,128]{1,0:T(8,128)(2,1)S(1)} %bitcast.183, bf16[2048,128]{1,0:T(8,128)(2,1)S(1)} %bitcast.158), kind=kOutput, calls=%fused_computation.11 | convolution fusion | flops 605290496 | bytes 8159232 | tf_op jit(solution)/shard_map/dot_general | solution.py:143
  84.3 1.1 fusion.77
  86.2 1.4 fusion.80
  88.4 1.4 fusion.79
  90.2 5.2 %collective-permute-start.8 = (f32[1152,128]{1,0:T(8,128)S(1)}, f32[1152,128]{1,0:T(8,128)S(1)}, u32[]{:S(2)}, u32[]{:S(2)}) collective-permute-start(f32[1152,128]{1,0:T(8,128)S(1)} %fusion.30), channel_id=1, source_target_pairs={{0,1},{1,0},{2,3},{3,2},{4,5},{5,4},{6,7},{7,6},{8,9},{9,8},{10,11... | collective-permute-start | bytes 1769480 | tf_op jit(solution)/shard_map/ppermute | solution.py:45
  95.3 1.6 collective-permute-done.8
  97.4 1.4 collective-permute-start.9
  98.7 6.9 %collective-permute-done.9 = f32[576,128]{1,0:T(8,128)S(1)} collective-permute-done((f32[576,128]{1,0:T(8,128)S(1)}, f32[576,128]{1,0:T(8,128)S(1)}, u32[]{:S(2)}, u32[]{:S(2)}) %collective-permute-start.9) | collective-permute-done | bytes 294944 | tf_op jit(solution)/shard_map/ppermute | solution.py:45
  105.7 1.7 collective-permute-start.10
  107.5 3.9 %collective-permute-done.10 = f32[288,128]{1,0:T(8,128)S(1)} collective-permute-done((f32[288,128]{1,0:T(8,128)S(1)}, f32[288,128]{1,0:T(8,128)S(1)}, u32[]{:S(2)}, u32[]{:S(2)}) %collective-permute-start.10) | collective-permute-done | bytes 147488 | tf_op jit(solution)/shard_map/ppermute | solution.py:45
  111.4 3.1 %collective-permute-start.11 = (f32[144,128]{1,0:T(8,128)S(1)}, f32[144,128]{1,0:T(8,128)S(1)}, u32[]{:S(2)}, u32[]{:S(2)}) collective-permute-start(f32[144,128]{1,0:T(8,128)S(1)} %constant_dynamic-slice_fusion.6), channel_id=1, source_target_pairs={{0,4},{4,0},{8,12},{12,8},{16,20},{20,16},{24,28},{28,24},{32,36},... | collective-permute-start | bytes 221192 | tf_op jit(solution)/shard_map/ppermute | solution.py:45
  114.5 1.7 collective-permute-done.11
  116.3 3.0 %collective-permute-start.12 = (f32[72,128]{1,0:T(8,128)S(1)}, f32[72,128]{1,0:T(8,128)S(1)}, u32[]{:S(2)}, u32[]{:S(2)}) collective-permute-start(f32[72,128]{1,0:T(8,128)S(1)} %constant_dynamic-slice_fusion.5), channel_id=1, source_target_pairs={{0,8},{4,12},{8,0},{12,4},{16,24},{20,28},{24,16},{28,20},{32,40},... | collective-permute-start | bytes 110600 | tf_op jit(solution)/shard_map/ppermute | solution.py:45
  119.3 1.3 collective-permute-done.12
  120.6 2.7 %collective-permute-start.13 = (f32[36,128]{1,0:T(8,128)S(1)}, f32[36,128]{1,0:T(8,128)S(1)}, u32[]{:S(2)}, u32[]{:S(2)}) collective-permute-start(f32[36,128]{1,0:T(8,128)S(1)} %constant_dynamic-slice_fusion.4), channel_id=1, source_target_pairs={{0,16},{4,20},{8,24},{12,28},{16,0},{20,4},{24,8},{28,12},{32,48},... | collective-permute-start | bytes 55304 | tf_op jit(solution)/shard_map/ppermute | solution.py:45
  123.3 4.0 %collective-permute-done.13 = f32[36,128]{1,0:T(8,128)S(1)} collective-permute-done((f32[36,128]{1,0:T(8,128)S(1)}, f32[36,128]{1,0:T(8,128)S(1)}, u32[]{:S(2)}, u32[]{:S(2)}) %collective-permute-start.13) | collective-permute-done | bytes 18464 | tf_op jit(solution)/shard_map/ppermute | solution.py:45
  127.3 2.1 %collective-permute-start.14 = (f32[18,128]{1,0:T(8,128)S(1)}, f32[18,128]{1,0:T(8,128)S(1)}, u32[]{:S(2)}, u32[]{:S(2)}) collective-permute-start(f32[18,128]{1,0:T(8,128)S(1)} %constant_dynamic-slice_fusion.2), channel_id=1, source_target_pairs={{0,32},{4,36},{8,40},{12,44},{16,48},{20,52},{24,56},{28,60},{32,0... | collective-permute-start | bytes 27656 | tf_op jit(solution)/shard_map/ppermute | solution.py:45
  129.4 1.1 collective-permute-done.14
  130.5 2.7 %collective-permute-start.15 = (f32[9,128]{1,0:T(8,128)S(1)}, f32[9,128]{1,0:T(8,128)S(1)}, u32[]{:S(2)}, u32[]{:S(2)}) collective-permute-start(f32[9,128]{1,0:T(8,128)S(1)} %constant_dynamic-slice_fusion), channel_id=1, source_target_pairs={{0,2},{1,3},{2,0},{3,1},{4,6},{5,7},{6,4},{7,5},{8,10},{9,11},{10,... | collective-permute-start | bytes 13832 | tf_op jit(solution)/shard_map/ppermute | solution.py:45
  133.2 1.4 collective-permute-done.15
  134.6 2.7 %collective-permute-start.16 = (f32[9,128]{1,0:T(8,128)S(1)}, f32[9,128]{1,0:T(8,128)S(1)}, u32[]{:S(2)}, u32[]{:S(2)}) collective-permute-start(f32[9,128]{1,0:T(8,128)S(1)} %fusion.61), channel_id=1, source_target_pairs={{0,2},{1,3},{2,0},{3,1},{4,6},{5,7},{6,4},{7,5},{8,10},{9,11},{10,... | collective-permute-start | bytes 13832 | tf_op jit(solution)/shard_map/ppermute | solution.py:49
  137.3 1.4 collective-permute-done.16
  138.7 1.5 collective-permute-start.17
  140.3 1.4 collective-permute-done.17
  141.7 2.2 %collective-permute-start.18 = (f32[36,128]{1,0:T(8,128)S(1)}, f32[36,128]{1,0:T(8,128)S(1)}, u32[]{:S(2)}, u32[]{:S(2)}) collective-permute-start(f32[36,128]{1,0:T(8,128)S(1)} %pad_maximum_fusion.15), channel_id=1, source_target_pairs={{0,16},{4,20},{8,24},{12,28},{16,0},{20,4},{24,8},{28,12},{32,48},... | collective-permute-start | bytes 55304 | tf_op jit(solution)/shard_map/ppermute | solution.py:49
  143.9 4.4 %collective-permute-done.18 = f32[36,128]{1,0:T(8,128)S(1)} collective-permute-done((f32[36,128]{1,0:T(8,128)S(1)}, f32[36,128]{1,0:T(8,128)S(1)}, u32[]{:S(2)}, u32[]{:S(2)}) %collective-permute-start.18) | collective-permute-done | bytes 18464 | tf_op jit(solution)/shard_map/ppermute | solution.py:49
  148.3 2.4 %collective-permute-start.19 = (f32[72,128]{1,0:T(8,128)S(1)}, f32[72,128]{1,0:T(8,128)S(1)}, u32[]{:S(2)}, u32[]{:S(2)}) collective-permute-start(f32[72,128]{1,0:T(8,128)S(1)} %pad_maximum_fusion.14), channel_id=1, source_target_pairs={{0,8},{4,12},{8,0},{12,4},{16,24},{20,28},{24,16},{28,20},{32,40},... | collective-permute-start | bytes 110600 | tf_op jit(solution)/shard_map/ppermute | solution.py:49
  150.7 1.4 collective-permute-done.19
  152.2 1.2 collective-permute-start.20
  153.4 2.1 %collective-permute-done.20 = f32[144,128]{1,0:T(8,128)S(1)} collective-permute-done((f32[144,128]{1,0:T(8,128)S(1)}, f32[144,128]{1,0:T(8,128)S(1)}, u32[]{:S(2)}, u32[]{:S(2)}) %collective-permute-start.20) | collective-permute-done | bytes 73760 | tf_op jit(solution)/shard_map/ppermute | solution.py:49
  155.5 1.5 collective-permute-start.21
  157.0 4.1 %collective-permute-done.21 = f32[288,128]{1,0:T(8,128)S(1)} collective-permute-done((f32[288,128]{1,0:T(8,128)S(1)}, f32[288,128]{1,0:T(8,128)S(1)}, u32[]{:S(2)}, u32[]{:S(2)}) %collective-permute-start.21) | collective-permute-done | bytes 147488 | tf_op jit(solution)/shard_map/ppermute | solution.py:49
  161.2 1.1 collective-permute-start.22
  162.4 4.5 %collective-permute-done.22 = f32[576,128]{1,0:T(8,128)S(1)} collective-permute-done((f32[576,128]{1,0:T(8,128)S(1)}, f32[576,128]{1,0:T(8,128)S(1)}, u32[]{:S(2)}, u32[]{:S(2)}) %collective-permute-start.22) | collective-permute-done | bytes 294944 | tf_op jit(solution)/shard_map/ppermute | solution.py:49
  167.1 15.7 %collective-permute-start.23 = (f32[1152,128]{1,0:T(8,128)S(1)}, f32[1152,128]{1,0:T(8,128)S(1)}, u32[]{:S(2)}, u32[]{:S(2)}) collective-permute-start(f32[1152,128]{1,0:T(8,128)S(1)} %get-tuple-element.66), channel_id=1, source_target_pairs={{0,1},{1,0},{2,3},{3,2},{4,5},{5,4},{6,7},{7,6},{8,9},{9,8},{10,11... | collective-permute-start | bytes 1769480 | tf_op jit(solution)/shard_map/ppermute | solution.py:49
  182.8 4.5 %fusion.8 = bf16[2048,128]{1,0:T(8,128)(2,1)} fusion(bf16[2048,1152]{1,0:T(8,128)(2,1)} %bitcast.165, bf16[1152,128]{1,0:T(8,128)(2,1)S(1)} %bitcast.188, bf16[2048,128]{1,0:T(8,128)(2,1)S(1)} %bitcast.187), kind=kOutput, calls=%fused_computation.12 | convolution fusion | flops 604766208 | bytes 6062080 | tf_op jit(solution)/shard_map/dot_general | solution.py:133
  187.3 1.2 fusion.27
  (120 shorter events, 17.1 us)
Async XLA Ops:
  0.6 7.6 %copy-start = (bf16[1,640,512]{2,1,0:T(8,128)(2,1)S(1)}, bf16[1,640,512]{2,1,0:T(8,128)(2,1)}, u32[]{:S(2)}) copy-start(bf16[1,640,512]{2,1,0:T(8,128)(2,1)} %param.15) | copy-start | bytes 1966084
  8.2 17.3 %copy-start.1 = (bf16[1,32,64,128]{3,2,1,0:T(8,128)(2,1)S(1)}, bf16[1,32,64,128]{3,2,1,0:T(8,128)(2,1)}, u32[]{:S(2)}) copy-start(bf16[1,32,64,128]{3,2,1,0:T(8,128)(2,1)} %param.21) | copy-start | bytes 1572868
  8.2 21.6 %copy-start.5 = (bf16[3,3,128,128]{3,2,1,0:T(8,128)(2,1)S(1)}, bf16[3,3,128,128]{3,2,1,0:T(8,128)(2,1)}, u32[]{:S(2)}) copy-start(bf16[3,3,128,128]{3,2,1,0:T(8,128)(2,1)} %param.20) | copy-start | bytes 884740
  12.0 39.2 %all-to-all-start = ((f32[64,21,128]{2,1,0:T(8,128)}), f32[64,21,128]{2,1,0:T(8,128)S(1)}, u32[]{:S(2)}, u32[]{:S(2)}) async-start(f32[64,21,128]{2,1,0:T(8,128)} %select_maximum_fusion), calls=%async_computation | async-start | bytes 1572864 | tf_op jit(solution)/shard_map/all_to_all | solution.py:99
  25.5 4.6 %collective-permute-start.4 = (bf16[2,64,128]{2,1,0:T(8,128)(2,1)S(1)}, bf16[2,64,128]{2,1,0:T(8,128)(2,1)S(1)}, u32[]{:S(2)}, u32[]{:S(2)}) collective-permute-start(bf16[2,64,128]{2,1,0:T(8,128)(2,1)S(1)} %get-tuple-element.76), channel_id=1, source_target_pairs={{0,64},{64,128},{128,192},{1,65},{65,129},{129,193},{2,66},{66,130... | collective-permute-start | bytes 98312 | tf_op jit(solution)/shard_map/ppermute | solution.py:16
  28.5 5.4 %collective-permute-start.5 = (bf16[2,64,128]{2,1,0:T(8,128)(2,1)S(1)}, bf16[2,64,128]{2,1,0:T(8,128)(2,1)S(1)}, u32[]{:S(2)}, u32[]{:S(2)}) collective-permute-start(bf16[2,64,128]{2,1,0:T(8,128)(2,1)S(1)} %get-tuple-element.77), channel_id=1, source_target_pairs={{64,0},{128,64},{192,128},{65,1},{129,65},{193,129},{66,2},{130,66... | collective-permute-start | bytes 98312 | tf_op jit(solution)/shard_map/ppermute | solution.py:17
  33.9 5.3 %collective-permute-start.6 = (bf16[36,2,128]{2,1,0:T(2,128)(2,1)S(1)}, bf16[36,2,128]{2,1,0:T(2,128)(2,1)S(1)}, u32[]{:S(2)}, u32[]{:S(2)}) collective-permute-start(bf16[36,2,128]{2,1,0:T(2,128)(2,1)S(1)} %get-tuple-element.73), channel_id=1, source_target_pairs={{0,4},{4,8},{8,12},{12,16},{16,20},{20,24},{24,28},{28,32},{32,36}... | collective-permute-start | bytes 55304 | tf_op jit(solution)/shard_map/ppermute | solution.py:16
  36.5 6.5 %collective-permute-start.7 = (bf16[36,2,128]{2,1,0:T(2,128)(2,1)S(1)}, bf16[36,2,128]{2,1,0:T(2,128)(2,1)S(1)}, u32[]{:S(2)}, u32[]{:S(2)}) collective-permute-start(bf16[36,2,128]{2,1,0:T(2,128)(2,1)S(1)} %get-tuple-element.72), channel_id=1, source_target_pairs={{4,0},{8,4},{12,8},{16,12},{20,16},{24,20},{28,24},{32,28},{36,32}... | collective-permute-start | bytes 55304 | tf_op jit(solution)/shard_map/ppermute | solution.py:17
  52.5 4.1 %copy-start.4 = (bf16[1,32,64,128]{3,2,1,0:T(8,128)(2,1)S(1)}, bf16[1,32,64,128]{3,2,1,0:T(8,128)(2,1)}, u32[]{:S(2)}) copy-start(bf16[1,32,64,128]{3,2,1,0:T(8,128)(2,1)} %param.14) | copy-start | bytes 1572868
  56.9 5.4 %collective-permute-start = (bf16[3,64,128]{2,1,0:T(8,128)(2,1)S(1)}, bf16[3,64,128]{2,1,0:T(8,128)(2,1)S(1)}, u32[]{:S(2)}, u32[]{:S(2)}) collective-permute-start(bf16[3,64,128]{2,1,0:T(8,128)(2,1)S(1)} %bitcast.195), channel_id=1, source_target_pairs={{0,64},{64,128},{128,192},{1,65},{65,129},{129,193},{2,66},{66,130... | collective-permute-start | bytes 147464 | tf_op jit(solution)/shard_map/ppermute | solution.py:16
  60.1 4.8 %collective-permute-start.1 = (bf16[3,64,128]{2,1,0:T(8,128)(2,1)S(1)}, bf16[3,64,128]{2,1,0:T(8,128)(2,1)S(1)}, u32[]{:S(2)}, u32[]{:S(2)}) collective-permute-start(bf16[3,64,128]{2,1,0:T(8,128)(2,1)S(1)} %bitcast.194), channel_id=1, source_target_pairs={{64,0},{128,64},{192,128},{65,1},{129,65},{193,129},{66,2},{130,66... | collective-permute-start | bytes 147464 | tf_op jit(solution)/shard_map/ppermute | solution.py:17
  65.0 4.6 %collective-permute-start.2 = (bf16[38,3,128]{2,1,0:T(4,128)(2,1)S(1)}, bf16[38,3,128]{2,1,0:T(4,128)(2,1)S(1)}, u32[]{:S(2)}, u32[]{:S(2)}) collective-permute-start(bf16[38,3,128]{2,1,0:T(4,128)(2,1)S(1)} %get-tuple-element.64), channel_id=1, source_target_pairs={{0,4},{4,8},{8,12},{12,16},{16,20},{20,24},{24,28},{28,32},{32,36}... | collective-permute-start | bytes 87560 | tf_op jit(solution)/shard_map/ppermute | solution.py:16
  68.0 4.7 %collective-permute-start.3 = (bf16[38,3,128]{2,1,0:T(4,128)(2,1)S(1)}, bf16[38,3,128]{2,1,0:T(4,128)(2,1)S(1)}, u32[]{:S(2)}, u32[]{:S(2)}) collective-permute-start(bf16[38,3,128]{2,1,0:T(4,128)(2,1)S(1)} %get-tuple-element.65), channel_id=1, source_target_pairs={{4,0},{8,4},{12,8},{16,12},{20,16},{24,20},{28,24},{32,28},{36,32}... | collective-permute-start | bytes 87560 | tf_op jit(solution)/shard_map/ppermute | solution.py:17
  73.5 1.9 %copy-start.7 = (bf16[3,3,128,128]{3,2,1,0:T(8,128)(2,1)S(1)}, bf16[3,3,128,128]{3,2,1,0:T(8,128)(2,1)}, u32[]{:S(2)}) copy-start(bf16[3,3,128,128]{3,2,1,0:T(8,128)(2,1)} %param.19) | copy-start | bytes 884740
  86.2 2.1 %copy-start.2 = (bf16[32,64,1152]{2,1,0:T(8,128)(2,1)}, bf16[32,64,1152]{2,1,0:T(8,128)(2,1)S(1)}, u32[]{:S(2)}) copy-start(bf16[32,64,1152]{2,1,0:T(8,128)(2,1)S(1)} %slice_dynamic-update-slice_fusion.9) | copy-start | bytes 14155780
  90.2 6.8 %collective-permute-start.8 = (f32[1152,128]{1,0:T(8,128)S(1)}, f32[1152,128]{1,0:T(8,128)S(1)}, u32[]{:S(2)}, u32[]{:S(2)}) collective-permute-start(f32[1152,128]{1,0:T(8,128)S(1)} %fusion.30), channel_id=1, source_target_pairs={{0,1},{1,0},{2,3},{3,2},{4,5},{5,4},{6,7},{7,6},{8,9},{9,8},{10,11... | collective-permute-start | bytes 1769480 | tf_op jit(solution)/shard_map/ppermute | solution.py:45
  97.3 85.5 %copy-start.3 = (bf16[32,64,128]{2,1,0:T(8,128)(2,1)S(1)}, bf16[32,64,128]{2,1,0:T(8,128)(2,1)}, u32[]{:S(2)}) copy-start(bf16[32,64,128]{2,1,0:T(8,128)(2,1)} %get-tuple-element.57) | copy-start | bytes 1572868
  97.3 85.4 %copy-start.6 = (bf16[3,3,128,128]{3,2,1,0:T(8,128)(2,1)S(1)}, bf16[3,3,128,128]{3,2,1,0:T(8,128)(2,1)}, u32[]{:S(2)}) copy-start(bf16[3,3,128,128]{3,2,1,0:T(8,128)(2,1)} %param.20) | copy-start | bytes 884740
  97.4 8.3 %collective-permute-start.9 = (f32[576,128]{1,0:T(8,128)S(1)}, f32[576,128]{1,0:T(8,128)S(1)}, u32[]{:S(2)}, u32[]{:S(2)}) collective-permute-start(f32[576,128]{1,0:T(8,128)S(1)} %constant_dynamic-slice_fusion.8), channel_id=1, source_target_pairs={{0,64},{64,0},{128,192},{192,128},{1,65},{65,1},{129,193},{193,129... | collective-permute-start | bytes 884744 | tf_op jit(solution)/shard_map/ppermute | solution.py:45
  105.7 5.6 %collective-permute-start.10 = (f32[288,128]{1,0:T(8,128)S(1)}, f32[288,128]{1,0:T(8,128)S(1)}, u32[]{:S(2)}, u32[]{:S(2)}) collective-permute-start(f32[288,128]{1,0:T(8,128)S(1)} %constant_dynamic-slice_fusion.7), channel_id=1, source_target_pairs={{0,128},{64,192},{128,0},{192,64},{1,129},{65,193},{129,1},{193,65... | collective-permute-start | bytes 442376 | tf_op jit(solution)/shard_map/ppermute | solution.py:45
  111.4 4.9 %collective-permute-start.11 = (f32[144,128]{1,0:T(8,128)S(1)}, f32[144,128]{1,0:T(8,128)S(1)}, u32[]{:S(2)}, u32[]{:S(2)}) collective-permute-start(f32[144,128]{1,0:T(8,128)S(1)} %constant_dynamic-slice_fusion.6), channel_id=1, source_target_pairs={{0,4},{4,0},{8,12},{12,8},{16,20},{20,16},{24,28},{28,24},{32,36},... | collective-permute-start | bytes 221192 | tf_op jit(solution)/shard_map/ppermute | solution.py:45
  116.3 4.3 %collective-permute-start.12 = (f32[72,128]{1,0:T(8,128)S(1)}, f32[72,128]{1,0:T(8,128)S(1)}, u32[]{:S(2)}, u32[]{:S(2)}) collective-permute-start(f32[72,128]{1,0:T(8,128)S(1)} %constant_dynamic-slice_fusion.5), channel_id=1, source_target_pairs={{0,8},{4,12},{8,0},{12,4},{16,24},{20,28},{24,16},{28,20},{32,40},... | collective-permute-start | bytes 110600 | tf_op jit(solution)/shard_map/ppermute | solution.py:45
  120.6 6.7 %collective-permute-start.13 = (f32[36,128]{1,0:T(8,128)S(1)}, f32[36,128]{1,0:T(8,128)S(1)}, u32[]{:S(2)}, u32[]{:S(2)}) collective-permute-start(f32[36,128]{1,0:T(8,128)S(1)} %constant_dynamic-slice_fusion.4), channel_id=1, source_target_pairs={{0,16},{4,20},{8,24},{12,28},{16,0},{20,4},{24,8},{28,12},{32,48},... | collective-permute-start | bytes 55304 | tf_op jit(solution)/shard_map/ppermute | solution.py:45
  127.3 3.1 %collective-permute-start.14 = (f32[18,128]{1,0:T(8,128)S(1)}, f32[18,128]{1,0:T(8,128)S(1)}, u32[]{:S(2)}, u32[]{:S(2)}) collective-permute-start(f32[18,128]{1,0:T(8,128)S(1)} %constant_dynamic-slice_fusion.2), channel_id=1, source_target_pairs={{0,32},{4,36},{8,40},{12,44},{16,48},{20,52},{24,56},{28,60},{32,0... | collective-permute-start | bytes 27656 | tf_op jit(solution)/shard_map/ppermute | solution.py:45
  130.5 4.1 %collective-permute-start.15 = (f32[9,128]{1,0:T(8,128)S(1)}, f32[9,128]{1,0:T(8,128)S(1)}, u32[]{:S(2)}, u32[]{:S(2)}) collective-permute-start(f32[9,128]{1,0:T(8,128)S(1)} %constant_dynamic-slice_fusion), channel_id=1, source_target_pairs={{0,2},{1,3},{2,0},{3,1},{4,6},{5,7},{6,4},{7,5},{8,10},{9,11},{10,... | collective-permute-start | bytes 13832 | tf_op jit(solution)/shard_map/ppermute | solution.py:45
  134.6 4.1 %collective-permute-start.16 = (f32[9,128]{1,0:T(8,128)S(1)}, f32[9,128]{1,0:T(8,128)S(1)}, u32[]{:S(2)}, u32[]{:S(2)}) collective-permute-start(f32[9,128]{1,0:T(8,128)S(1)} %fusion.61), channel_id=1, source_target_pairs={{0,2},{1,3},{2,0},{3,1},{4,6},{5,7},{6,4},{7,5},{8,10},{9,11},{10,... | collective-permute-start | bytes 13832 | tf_op jit(solution)/shard_map/ppermute | solution.py:49
  138.7 2.9 %collective-permute-start.17 = (f32[18,128]{1,0:T(8,128)S(1)}, f32[18,128]{1,0:T(8,128)S(1)}, u32[]{:S(2)}, u32[]{:S(2)}) collective-permute-start(f32[18,128]{1,0:T(8,128)S(1)} %pad_maximum_fusion.19), channel_id=1, source_target_pairs={{0,32},{4,36},{8,40},{12,44},{16,48},{20,52},{24,56},{28,60},{32,0... | collective-permute-start | bytes 27656 | tf_op jit(solution)/shard_map/ppermute | solution.py:49
  141.7 6.6 %collective-permute-start.18 = (f32[36,128]{1,0:T(8,128)S(1)}, f32[36,128]{1,0:T(8,128)S(1)}, u32[]{:S(2)}, u32[]{:S(2)}) collective-permute-start(f32[36,128]{1,0:T(8,128)S(1)} %pad_maximum_fusion.15), channel_id=1, source_target_pairs={{0,16},{4,20},{8,24},{12,28},{16,0},{20,4},{24,8},{28,12},{32,48},... | collective-permute-start | bytes 55304 | tf_op jit(solution)/shard_map/ppermute | solution.py:49
  148.3 3.8 %collective-permute-start.19 = (f32[72,128]{1,0:T(8,128)S(1)}, f32[72,128]{1,0:T(8,128)S(1)}, u32[]{:S(2)}, u32[]{:S(2)}) collective-permute-start(f32[72,128]{1,0:T(8,128)S(1)} %pad_maximum_fusion.14), channel_id=1, source_target_pairs={{0,8},{4,12},{8,0},{12,4},{16,24},{20,28},{24,16},{28,20},{32,40},... | collective-permute-start | bytes 110600 | tf_op jit(solution)/shard_map/ppermute | solution.py:49
  152.2 3.3 %collective-permute-start.20 = (f32[144,128]{1,0:T(8,128)S(1)}, f32[144,128]{1,0:T(8,128)S(1)}, u32[]{:S(2)}, u32[]{:S(2)}) collective-permute-start(f32[144,128]{1,0:T(8,128)S(1)} %get-tuple-element.90), channel_id=1, source_target_pairs={{0,4},{4,0},{8,12},{12,8},{16,20},{20,16},{24,28},{28,24},{32,36},... | collective-permute-start | bytes 221192 | tf_op jit(solution)/shard_map/ppermute | solution.py:49
  155.5 5.6 %collective-permute-start.21 = (f32[288,128]{1,0:T(8,128)S(1)}, f32[288,128]{1,0:T(8,128)S(1)}, u32[]{:S(2)}, u32[]{:S(2)}) collective-permute-start(f32[288,128]{1,0:T(8,128)S(1)} %get-tuple-element.86), channel_id=1, source_target_pairs={{0,128},{64,192},{128,0},{192,64},{1,129},{65,193},{129,1},{193,65... | collective-permute-start | bytes 442376 | tf_op jit(solution)/shard_map/ppermute | solution.py:49
  161.2 5.7 %collective-permute-start.22 = (f32[576,128]{1,0:T(8,128)S(1)}, f32[576,128]{1,0:T(8,128)S(1)}, u32[]{:S(2)}, u32[]{:S(2)}) collective-permute-start(f32[576,128]{1,0:T(8,128)S(1)} %get-tuple-element.82), channel_id=1, source_target_pairs={{0,64},{64,0},{128,192},{192,128},{1,65},{65,1},{129,193},{193,129... | collective-permute-start | bytes 884744 | tf_op jit(solution)/shard_map/ppermute | solution.py:49
  167.1 20.2 %collective-permute-start.23 = (f32[1152,128]{1,0:T(8,128)S(1)}, f32[1152,128]{1,0:T(8,128)S(1)}, u32[]{:S(2)}, u32[]{:S(2)}) collective-permute-start(f32[1152,128]{1,0:T(8,128)S(1)} %get-tuple-element.66), channel_id=1, source_target_pairs={{0,1},{1,0},{2,3},{3,2},{4,5},{5,4},{6,7},{7,6},{8,9},{9,8},{10,11... | collective-permute-start | bytes 1769480 | tf_op jit(solution)/shard_map/ppermute | solution.py:49

commit v5 on v4

--- a/solution.py
+++ b/solution.py
@@ -6,17 +6,39 @@
 from jax.sharding import PartitionSpec as P
 
 
-def with_halo(array, sides, width):
-    for axis, dim in sides:
-        count, length = (lax.axis_size(axis), array.shape[dim])
-        up = [(i, (i + 1) % count) for i in range(count - 1)]
-        down = [(j, i) for i, j in up]
-        last = lax.slice_in_dim(array, length - width, length, axis=dim)
-        leading = lax.slice_in_dim(array, 0, width, axis=dim)
-        before = lax.ppermute(last, axis, up)
-        after = lax.ppermute(leading, axis, down)
-        array = jnp.concatenate([before, array, after], axis=dim)
-    return array
+def with_halo(array, width):
+    n_row, n_col = lax.axis_size("row"), lax.axis_size("col")
+
+    def moved(block, d_row, d_col):
+        if d_col == 0:
+            count = n_row
+            pairs = [(i, i + d_row) for i in range(count) if 0 <= i + d_row < count]
+            return lax.ppermute(block, "row", pairs)
+        if d_row == 0:
+            count = n_col
+            pairs = [(i, i + d_col) for i in range(count) if 0 <= i + d_col < count]
+            return lax.ppermute(block, "col", pairs)
+        pairs = [
+            (r * n_col + c, (r + d_row) * n_col + c + d_col)
+            for r in range(n_row)
+            for c in range(n_col)
+            if 0 <= r + d_row < n_row and 0 <= c + d_col < n_col
+        ]
+        return lax.ppermute(block, ("row", "col"), pairs)
+
+    w = width
+    north = moved(array[-w:, :], 1, 0)
+    south = moved(array[:w, :], -1, 0)
+    west = moved(array[:, -w:], 0, 1)
+    east = moved(array[:, :w], 0, -1)
+    north_west = moved(array[-w:, -w:], 1, 1)
+    north_east = moved(array[-w:, :w], 1, -1)
+    south_west = moved(array[:w, -w:], -1, 1)
+    south_east = moved(array[:w, :w], -1, -1)
+    top = jnp.concatenate([north_west, north, north_east], axis=1)
+    middle = jnp.concatenate([west, array, east], axis=1)
+    bottom = jnp.concatenate([south_west, south, south_east], axis=1)
+    return jnp.concatenate([top, middle, bottom], axis=0)
 
 
 def halving_steps():
@@ -116,7 +138,7 @@
     )
     w_one = w_first.reshape(9 * chans, chans)
     w_two = w_second.reshape(9 * chans, chans)
-    deep = with_halo(first_in, (("row", 0), ("col", 1)), 3)
+    deep = with_halo(first_in, 3)
     pre_wide = jnp.dot(
         unfold(deep, 1, rows + 4, cols + 4), w_one, preferred_element_type=jnp.float32
     ).reshape(rows + 4, cols + 4, chans)
@@ -137,7 +159,7 @@
         .reshape(1, rows, cols, chans)
     )
     back = cotangent[0]
-    padded_back = with_halo(back, (("row", 0), ("col", 1)), 2)
+    padded_back = with_halo(back, 2)
     w_turned = jnp.transpose(w_second[::-1, ::-1], (0, 1, 3, 2)).reshape(9 * chans, chans)
     back_flat = back.reshape(rows * cols, chans)
     grad_act1 = back_flat.astype(jnp.float32) + jnp.dot(

time: 189 us -> 217 us (1.15)
  starting transfers between devices: 80.8 us -> 115 us
  waiting for transfers between devices: 55.9 us -> 47.7 us
    ppermute x8 -> x16, starting transfers between devices: 17.1 us -> 48.5 us  [the longest x8 18 us: moved(): return lax.ppermute(block, ('row', 'col'), pairs)]
    ppermute x8 -> x16, waiting for transfers between devices: 14.6 us -> 3.55 us  [the longest x4 3.52 us: moved(): return lax.ppermute(block, 'row', pairs)]
    ppermute x8, starting transfers between devices: 21.8 us -> 30.6 us  [tree_sum(): x = kept + lax.ppermute(sent, axis, pairs)]
    ppermute x8, starting transfers between devices: 28.3 us -> 22.6 us  [tree_sum(): got = lax.ppermute(x, axis, pairs)]
    ppermute x8, waiting for transfers between devices: 19.3 us -> 24.5 us  [tree_sum(): got = lax.ppermute(x, axis, pairs)]
    ppermute x8, waiting for transfers between devices: 22 us -> 19.6 us  [tree_sum(): x = kept + lax.ppermute(sent, axis, pairs)]
  transfers between devices with their start and end apart: 25 -> 33, of which waited for: 20 -> 17; matrix products, arithmetic and copies ran while one was open for 7% -> 7% of each run, Pallas kernels for 0% -> 0%
where the time goes in v5:
time: 217 us; the launch traced here: 216 us
  starting transfers between devices  115 us (53%)
  waiting for transfers between devices  47.7 us (22%)
  matrix products  20.8 us (10%)
  local copies, waits for them, and re-layouts  17.3 us (8%)
  other arithmetic  13.2 us (6%)
    ppermute x8, starting transfers between devices, tree_sum(): x = kept + lax.ppermute(sent, axis, pairs)  30.6 us
    ppermute x8, waiting for transfers between devices, tree_sum(): got = lax.ppermute(x, axis, pairs)  24.5 us
    ppermute x8, starting transfers between devices, tree_sum(): got = lax.ppermute(x, axis, pairs)  22.6 us
    ppermute x8, waiting for transfers between devices, tree_sum(): x = kept + lax.ppermute(sent, axis, pairs)  19.6 us
    ppermute x8, starting transfers between devices, moved(): return lax.ppermute(block, ('row', 'col'), pairs)  18 us
    ppermute x4, starting transfers between devices, moved(): return lax.ppermute(block, 'col', pairs)  15.7 us
    ppermute x4, starting transfers between devices, moved(): return lax.ppermute(block, 'row', pairs)  14.7 us
    all_to_all x1, starting transfers between devices, on_device(): lax.all_to_all(payload, ('row', 'col'), split_axis=0, concat_axis=0, tile...  13.5 us
  transfers between devices with their start and end apart: 33, of which 17 were waited for; matrix products, arithmetic and copies ran while one was open for 7% of the time, Pallas kernels for 0%

profile of v5, /device:TPU:1, one launch (start us, length us, event | category | flops | bytes accessed | tf_op | source)
XLA Modules:
  0.0 215.7 jit_solution(16566056781915797352)
XLA Ops:
  2.6 1.5 reduce-window.6
  4.6 1.3 broadcast_select_fusion
  5.9 1.4 broadcast_select_fusion.1
  8.2 2.7 %fusion.11 = f32[1280,128]{1,0:T(8,128)S(1)} fusion(bf16[512,128]{1,0:T(8,128)(2,1)} %param.18, s32[640]{0:T(1024)S(1)} %add_add_fusion, bf16[1,640,512]{2,1,0:T(8,128)(2,1)S(1)} %copy-done), kind=kOutput, calls=%fused_computation.23 | convolution fusion | flops 1008107520 | bytes 1444352 | tf_op jit(solution)/shard_map/dot_general | solution.py:113
  11.0 1.0 select_maximum_fusion
  12.0 13.5 %all-to-all-start = ((f32[64,21,128]{2,1,0:T(8,128)}), f32[64,21,128]{2,1,0:T(8,128)S(1)}, u32[]{:S(2)}, u32[]{:S(2)}) async-start(f32[64,21,128]{2,1,0:T(8,128)} %select_maximum_fusion), calls=%async_computation | async-start | bytes 1572864 | tf_op jit(solution)/shard_map/all_to_all | solution.py:121
  26.9 1.3 collective-permute-start.15
  28.2 6.0 %collective-permute-start.11 = (bf16[32,2,128]{2,1,0:T(2,128)(2,1)S(1)}, bf16[32,2,128]{2,1,0:T(2,128)(2,1)S(1)}, u32[]{:S(2)}, u32[]{:S(2)}) collective-permute-start(bf16[32,2,128]{2,1,0:T(2,128)(2,1)S(1)} %get-tuple-element.78), channel_id=1, source_target_pairs={{0,4},{4,8},{8,12},{12,16},{16,20},{20,24},{24,28},{28,32},{32,36}... | collective-permute-start | bytes 49160 | tf_op jit(solution)/shard_map/ppermute | solution.py:20
  34.2 1.3 collective-permute-start.12
  35.9 8.4 %collective-permute-start.8 = (bf16[2,2,128]{2,1,0:T(2,128)(2,1)S(1)}, bf16[2,2,128]{2,1,0:T(2,128)(2,1)S(1)}, u32[]{:S(2)}, u32[]{:S(2)}) collective-permute-start(bf16[2,2,128]{2,1,0:T(2,128)(2,1)S(1)} %get-tuple-element.73), channel_id=1, source_target_pairs={{0,68},{4,72},{8,76},{12,80},{16,84},{20,88},{24,92},{28,96},{32,1... | collective-permute-start | bytes 3080 | tf_op jit(solution)/shard_map/ppermute | solution.py:27
  44.4 1.3 collective-permute-start.14
  45.7 4.0 %collective-permute-start.9 = (bf16[2,64,128]{2,1,0:T(8,128)(2,1)S(1)}, bf16[2,64,128]{2,1,0:T(8,128)(2,1)S(1)}, u32[]{:S(2)}, u32[]{:S(2)}) collective-permute-start(bf16[2,64,128]{2,1,0:T(8,128)(2,1)S(1)} %get-tuple-element.75), channel_id=1, source_target_pairs={{0,64},{64,128},{128,192},{1,65},{65,129},{129,193},{2,66},{66,130... | collective-permute-start | bytes 98312 | tf_op jit(solution)/shard_map/ppermute | solution.py:16
  51.7 0.9 constant_dynamic-update-slice_fusion.18
  52.6 0.9 constant_dynamic-update-slice_fusion.17
  54.4 0.9 constant_dynamic-update-slice_fusion.15
  55.3 0.9 constant_dynamic-update-slice_fusion.14
  56.2 0.9 constant_dynamic-update-slice_fusion.13
  57.1 0.9 constant_dynamic-update-slice_fusion.12
  58.0 0.9 constant_dynamic-update-slice_fusion.11
  58.9 0.9 constant_dynamic-update-slice_fusion.10
  59.9 1.0 reduce-precision_convert_fusion.1
  61.1 4.0 %fusion = f32[2048,384]{1,0:T(8,128)S(1)} fusion(f32[1280]{0:T(1024)S(1)} %eq.112, bf16[1280,128]{1,0:T(8,128)(2,1)} %get-tuple-element.48, bf16[1280,128]{1,0:T(8,128)(2,1)} %get-tuple-element.49, bf16[1280,128]{1,0:T(8,128)(2,1)S(1)} %get-tuple-element.47), kind=kOutput, calls=%fused_computation.1 | convolution fusion | flops 2018836480 | bytes 4133888 | tf_op jit(solution)/shard_map/dot_general | solution.py:132
  65.4 4.4 %collective-permute-start = (bf16[3,3,128]{2,1,0:T(4,128)(2,1)S(1)}, bf16[3,3,128]{2,1,0:T(4,128)(2,1)S(1)}, u32[]{:S(2)}, u32[]{:S(2)}) collective-permute-start(bf16[3,3,128]{2,1,0:T(4,128)(2,1)S(1)} %get-tuple-element.82), channel_id=1, source_target_pairs={{0,68},{4,72},{8,76},{12,80},{16,84},{20,88},{24,92},{28,96},{32,1... | collective-permute-start | bytes 6920 | tf_op jit(solution)/shard_map/ppermute | solution.py:27
  69.8 7.2 %collective-permute-start.3 = (bf16[32,3,128]{2,1,0:T(4,128)(2,1)S(1)}, bf16[32,3,128]{2,1,0:T(4,128)(2,1)S(1)}, u32[]{:S(2)}, u32[]{:S(2)}) collective-permute-start(bf16[32,3,128]{2,1,0:T(4,128)(2,1)S(1)} %get-tuple-element.88), channel_id=1, source_target_pairs={{0,4},{4,8},{8,12},{12,16},{16,20},{20,24},{24,28},{28,32},{32,36}... | collective-permute-start | bytes 73736 | tf_op jit(solution)/shard_map/ppermute | solution.py:20
  77.0 1.3 collective-permute-start.4
  79.7 1.3 collective-permute-start.7
  81.0 8.0 %collective-permute-start.1 = (bf16[3,64,128]{2,1,0:T(8,128)(2,1)S(1)}, bf16[3,64,128]{2,1,0:T(8,128)(2,1)S(1)}, u32[]{:S(2)}, u32[]{:S(2)}) collective-permute-start(bf16[3,64,128]{2,1,0:T(8,128)(2,1)S(1)} %bitcast.197), channel_id=1, source_target_pairs={{0,64},{64,128},{128,192},{1,65},{65,129},{129,193},{2,66},{66,130... | collective-permute-start | bytes 147464 | tf_op jit(solution)/shard_map/ppermute | solution.py:16
  89.0 1.5 collective-permute-start.6
  90.9 2.9 %collective-permute-done.6 = bf16[3,64,128]{2,1,0:T(8,128)(2,1)S(1)} collective-permute-done((bf16[3,64,128]{2,1,0:T(8,128)(2,1)S(1)}, bf16[3,64,128]{2,1,0:T(8,128)(2,1)S(1)}, u32[]{:S(2)}, u32[]{:S(2)}) %collective-permute-start.6) | collective-permute-done | bytes 49184 | tf_op jit(solution)/shard_map/ppermute | solution.py:16
  96.4 2.2 %select_convert_fusion = (bf16[36,68,128]{2,1,0:T(8,128)(2,1)S(1)}, f32[36,68,128]{2,1,0:T(8,128)S(1)}) fusion(pred[36,68]{1,0:T(8,128)(4,1)S(1)} %broadcast_and_fusion, bf16[36,68,1152]{2,1,0:T(8,128)(2,1)S(1)} %slice_dynamic-update-slice_fusion, bf16[1152,128,1]{1,0,2:T(8,128)(2,1)S(1)} %bitcast.204), kind=kOutput, calls=%fused_computation.24 | convolution fusion | flops 723824640 | bytes 7817616 | tf_op jit(solution)/shard_map/dot_general | solution.py:142
  99.1 3.8 %fusion.7 = bf16[2048,128]{1,0:T(8,128)(2,1)S(1)} fusion(f32[2048,128]{1,0:T(8,128)S(1)} %get-tuple-element.44, f32[2048,128]{1,0:T(8,128)S(1)} %get-tuple-element.43, bf16[2048,1152]{1,0:T(8,128)(2,1)} %constant_dynamic-update-slice_fusion.10, bf16[1152,128]{1,0:T(8,128)(2,1)S(1)} %bitcast.185, bf16[2048,128]{1,0:T(8,128)(2,1)S(1)} %bitcast.159), kind=kOutput, calls=%fused_computation.11 | convolution fusion | flops 605290496 | bytes 8159232 | tf_op jit(solution)/shard_map/dot_general | solution.py:165
  103.2 0.9 fusion.74
  105.5 1.1 fusion.73
  107.5 1.4 fusion.84
  109.6 1.4 fusion.83
  111.4 6.2 %collective-permute-start.16 = (f32[1152,128]{1,0:T(8,128)S(1)}, f32[1152,128]{1,0:T(8,128)S(1)}, u32[]{:S(2)}, u32[]{:S(2)}) collective-permute-start(f32[1152,128]{1,0:T(8,128)S(1)} %fusion.30), channel_id=1, source_target_pairs={{0,1},{1,0},{2,3},{3,2},{4,5},{5,4},{6,7},{7,6},{8,9},{9,8},{10,11... | collective-permute-start | bytes 1769480 | tf_op jit(solution)/shard_map/ppermute | solution.py:67
  117.7 1.6 collective-permute-done.16
  119.7 1.3 collective-permute-start.17
  121.0 7.0 %collective-permute-done.17 = f32[576,128]{1,0:T(8,128)S(1)} collective-permute-done((f32[576,128]{1,0:T(8,128)S(1)}, f32[576,128]{1,0:T(8,128)S(1)}, u32[]{:S(2)}, u32[]{:S(2)}) %collective-permute-start.17) | collective-permute-done | bytes 294944 | tf_op jit(solution)/shard_map/ppermute | solution.py:67
  128.1 1.9 collective-permute-start.18
  130.0 3.7 %collective-permute-done.18 = f32[288,128]{1,0:T(8,128)S(1)} collective-permute-done((f32[288,128]{1,0:T(8,128)S(1)}, f32[288,128]{1,0:T(8,128)S(1)}, u32[]{:S(2)}, u32[]{:S(2)}) %collective-permute-start.18) | collective-permute-done | bytes 147488 | tf_op jit(solution)/shard_map/ppermute | solution.py:67
  133.7 3.3 %collective-permute-start.19 = (f32[144,128]{1,0:T(8,128)S(1)}, f32[144,128]{1,0:T(8,128)S(1)}, u32[]{:S(2)}, u32[]{:S(2)}) collective-permute-start(f32[144,128]{1,0:T(8,128)S(1)} %constant_dynamic-slice_fusion.6), channel_id=1, source_target_pairs={{0,4},{4,0},{8,12},{12,8},{16,20},{20,16},{24,28},{28,24},{32,36},... | collective-permute-start | bytes 221192 | tf_op jit(solution)/shard_map/ppermute | solution.py:67
  137.0 1.7 collective-permute-done.19
  138.8 3.4 %collective-permute-start.20 = (f32[72,128]{1,0:T(8,128)S(1)}, f32[72,128]{1,0:T(8,128)S(1)}, u32[]{:S(2)}, u32[]{:S(2)}) collective-permute-start(f32[72,128]{1,0:T(8,128)S(1)} %constant_dynamic-slice_fusion.5), channel_id=1, source_target_pairs={{0,8},{4,12},{8,0},{12,4},{16,24},{20,28},{24,16},{28,20},{32,40},... | collective-permute-start | bytes 110600 | tf_op jit(solution)/shard_map/ppermute | solution.py:67
  142.2 1.3 collective-permute-done.20
  143.6 4.9 %collective-permute-start.21 = (f32[36,128]{1,0:T(8,128)S(1)}, f32[36,128]{1,0:T(8,128)S(1)}, u32[]{:S(2)}, u32[]{:S(2)}) collective-permute-start(f32[36,128]{1,0:T(8,128)S(1)} %constant_dynamic-slice_fusion.4), channel_id=1, source_target_pairs={{0,16},{4,20},{8,24},{12,28},{16,0},{20,4},{24,8},{28,12},{32,48},... | collective-permute-start | bytes 55304 | tf_op jit(solution)/shard_map/ppermute | solution.py:67
  148.5 1.7 collective-permute-done.21
  150.2 6.8 %collective-permute-start.22 = (f32[18,128]{1,0:T(8,128)S(1)}, f32[18,128]{1,0:T(8,128)S(1)}, u32[]{:S(2)}, u32[]{:S(2)}) collective-permute-start(f32[18,128]{1,0:T(8,128)S(1)} %constant_dynamic-slice_fusion.2), channel_id=1, source_target_pairs={{0,32},{4,36},{8,40},{12,44},{16,48},{20,52},{24,56},{28,60},{32,0... | collective-permute-start | bytes 27656 | tf_op jit(solution)/shard_map/ppermute | solution.py:67
  157.1 1.1 collective-permute-done.22
  158.2 2.7 %collective-permute-start.23 = (f32[9,128]{1,0:T(8,128)S(1)}, f32[9,128]{1,0:T(8,128)S(1)}, u32[]{:S(2)}, u32[]{:S(2)}) collective-permute-start(f32[9,128]{1,0:T(8,128)S(1)} %constant_dynamic-slice_fusion), channel_id=1, source_target_pairs={{0,2},{1,3},{2,0},{3,1},{4,6},{5,7},{6,4},{7,5},{8,10},{9,11},{10,... | collective-permute-start | bytes 13832 | tf_op jit(solution)/shard_map/ppermute | solution.py:67
  160.9 1.4 collective-permute-done.23
  162.3 2.7 %collective-permute-start.24 = (f32[9,128]{1,0:T(8,128)S(1)}, f32[9,128]{1,0:T(8,128)S(1)}, u32[]{:S(2)}, u32[]{:S(2)}) collective-permute-start(f32[9,128]{1,0:T(8,128)S(1)} %fusion.61), channel_id=1, source_target_pairs={{0,2},{1,3},{2,0},{3,1},{4,6},{5,7},{6,4},{7,5},{8,10},{9,11},{10,... | collective-permute-start | bytes 13832 | tf_op jit(solution)/shard_map/ppermute | solution.py:71
  165.0 1.5 collective-permute-done.24
  166.5 1.8 collective-permute-start.25
  168.2 1.1 collective-permute-done.25
  169.5 6.5 %collective-permute-done.26 = f32[36,128]{1,0:T(8,128)S(1)} collective-permute-done((f32[36,128]{1,0:T(8,128)S(1)}, f32[36,128]{1,0:T(8,128)S(1)}, u32[]{:S(2)}, u32[]{:S(2)}) %collective-permute-start.26) | collective-permute-done | bytes 18464 | tf_op jit(solution)/shard_map/ppermute | solution.py:71
  176.1 3.9 %collective-permute-done.27 = f32[72,128]{1,0:T(8,128)S(1)} collective-permute-done((f32[72,128]{1,0:T(8,128)S(1)}, f32[72,128]{1,0:T(8,128)S(1)}, u32[]{:S(2)}, u32[]{:S(2)}) %collective-permute-start.27) | collective-permute-done | bytes 36896 | tf_op jit(solution)/shard_map/ppermute | solution.py:71
  180.2 3.2 %collective-permute-done.28 = f32[144,128]{1,0:T(8,128)S(1)} collective-permute-done((f32[144,128]{1,0:T(8,128)S(1)}, f32[144,128]{1,0:T(8,128)S(1)}, u32[]{:S(2)}, u32[]{:S(2)}) %collective-permute-start.28) | collective-permute-done | bytes 73760 | tf_op jit(solution)/shard_map/ppermute | solution.py:71
  183.5 2.4 %collective-permute-start.29 = (f32[288,128]{1,0:T(8,128)S(1)}, f32[288,128]{1,0:T(8,128)S(1)}, u32[]{:S(2)}, u32[]{:S(2)}) collective-permute-start(f32[288,128]{1,0:T(8,128)S(1)} %get-tuple-element.94), channel_id=1, source_target_pairs={{0,128},{64,192},{128,0},{192,64},{1,129},{65,193},{129,1},{193,65... | collective-permute-start | bytes 442376 | tf_op jit(solution)/shard_map/ppermute | solution.py:71
  185.9 3.2 %collective-permute-done.29 = f32[288,128]{1,0:T(8,128)S(1)} collective-permute-done((f32[288,128]{1,0:T(8,128)S(1)}, f32[288,128]{1,0:T(8,128)S(1)}, u32[]{:S(2)}, u32[]{:S(2)}) %collective-permute-start.29) | collective-permute-done | bytes 147488 | tf_op jit(solution)/shard_map/ppermute | solution.py:71
  190.0 5.2 %collective-permute-done.30 = f32[576,128]{1,0:T(8,128)S(1)} collective-permute-done((f32[576,128]{1,0:T(8,128)S(1)}, f32[576,128]{1,0:T(8,128)S(1)}, u32[]{:S(2)}, u32[]{:S(2)}) %collective-permute-start.30) | collective-permute-done | bytes 294944 | tf_op jit(solution)/shard_map/ppermute | solution.py:71
  195.3 14.6 %collective-permute-start.31 = (f32[1152,128]{1,0:T(8,128)S(1)}, f32[1152,128]{1,0:T(8,128)S(1)}, u32[]{:S(2)}, u32[]{:S(2)}) collective-permute-start(f32[1152,128]{1,0:T(8,128)S(1)} %get-tuple-element.62), channel_id=1, source_target_pairs={{0,1},{1,0},{2,3},{3,2},{4,5},{5,4},{6,7},{7,6},{8,9},{9,8},{10,11... | collective-permute-start | bytes 1769480 | tf_op jit(solution)/shard_map/ppermute | solution.py:71
  210.0 4.5 %fusion.8 = bf16[2048,128]{1,0:T(8,128)(2,1)} fusion(bf16[2048,1152]{1,0:T(8,128)(2,1)} %bitcast.167, bf16[1152,128]{1,0:T(8,128)(2,1)S(1)} %bitcast.190, bf16[2048,128]{1,0:T(8,128)(2,1)S(1)} %bitcast.189), kind=kOutput, calls=%fused_computation.12 | convolution fusion | flops 604766208 | bytes 6062080 | tf_op jit(solution)/shard_map/dot_general | solution.py:155
  214.5 1.2 fusion.27
  (138 shorter events, 18.9 us)
Async XLA Ops:
  0.6 7.6 %copy-start = (bf16[1,640,512]{2,1,0:T(8,128)(2,1)S(1)}, bf16[1,640,512]{2,1,0:T(8,128)(2,1)}, u32[]{:S(2)}) copy-start(bf16[1,640,512]{2,1,0:T(8,128)(2,1)} %param.15) | copy-start | bytes 1966084
  8.2 17.3 %copy-start.1 = (bf16[1,32,64,128]{3,2,1,0:T(8,128)(2,1)S(1)}, bf16[1,32,64,128]{3,2,1,0:T(8,128)(2,1)}, u32[]{:S(2)}) copy-start(bf16[1,32,64,128]{3,2,1,0:T(8,128)(2,1)} %param.21) | copy-start | bytes 1572868
  8.2 27.4 %copy-start.5 = (bf16[3,3,128,128]{3,2,1,0:T(8,128)(2,1)S(1)}, bf16[3,3,128,128]{3,2,1,0:T(8,128)(2,1)}, u32[]{:S(2)}) copy-start(bf16[3,3,128,128]{3,2,1,0:T(8,128)(2,1)} %param.20) | copy-start | bytes 884740
  12.0 47.8 %all-to-all-start = ((f32[64,21,128]{2,1,0:T(8,128)}), f32[64,21,128]{2,1,0:T(8,128)S(1)}, u32[]{:S(2)}, u32[]{:S(2)}) async-start(f32[64,21,128]{2,1,0:T(8,128)} %select_maximum_fusion), calls=%async_computation | async-start | bytes 1572864 | tf_op jit(solution)/shard_map/all_to_all | solution.py:121
  25.5 10.4 %collective-permute-start.10 = (bf16[2,2,128]{2,1,0:T(2,128)(2,1)S(1)}, bf16[2,2,128]{2,1,0:T(2,128)(2,1)S(1)}, u32[]{:S(2)}, u32[]{:S(2)}) collective-permute-start(bf16[2,2,128]{2,1,0:T(2,128)(2,1)S(1)} %get-tuple-element.72), channel_id=1, source_target_pairs={{4,64},{8,68},{12,72},{16,76},{20,80},{24,84},{28,88},{32,92},{36,... | collective-permute-start | bytes 3080 | tf_op jit(solution)/shard_map/ppermute | solution.py:27
  26.2 23.8 %collective-permute-start.13 = (bf16[2,2,128]{2,1,0:T(2,128)(2,1)S(1)}, bf16[2,2,128]{2,1,0:T(2,128)(2,1)S(1)}, u32[]{:S(2)}, u32[]{:S(2)}) collective-permute-start(bf16[2,2,128]{2,1,0:T(2,128)(2,1)S(1)} %get-tuple-element.70), channel_id=1, source_target_pairs={{64,4},{68,8},{72,12},{76,16},{80,20},{84,24},{88,28},{92,32},{96,... | collective-permute-start | bytes 3080 | tf_op jit(solution)/shard_map/ppermute | solution.py:27
  26.9 23.2 %collective-permute-start.15 = (bf16[2,2,128]{2,1,0:T(2,128)(2,1)S(1)}, bf16[2,2,128]{2,1,0:T(2,128)(2,1)S(1)}, u32[]{:S(2)}, u32[]{:S(2)}) collective-permute-start(bf16[2,2,128]{2,1,0:T(2,128)(2,1)S(1)} %get-tuple-element.71), channel_id=1, source_target_pairs={{68,0},{72,4},{76,8},{80,12},{84,16},{88,20},{92,24},{96,28},{100,... | collective-permute-start | bytes 3080 | tf_op jit(solution)/shard_map/ppermute | solution.py:27
  28.2 16.1 %collective-permute-start.11 = (bf16[32,2,128]{2,1,0:T(2,128)(2,1)S(1)}, bf16[32,2,128]{2,1,0:T(2,128)(2,1)S(1)}, u32[]{:S(2)}, u32[]{:S(2)}) collective-permute-start(bf16[32,2,128]{2,1,0:T(2,128)(2,1)S(1)} %get-tuple-element.78), channel_id=1, source_target_pairs={{0,4},{4,8},{8,12},{12,16},{16,20},{20,24},{24,28},{28,32},{32,36}... | collective-permute-start | bytes 49160 | tf_op jit(solution)/shard_map/ppermute | solution.py:20
  34.2 11.5 %collective-permute-start.12 = (bf16[32,2,128]{2,1,0:T(2,128)(2,1)S(1)}, bf16[32,2,128]{2,1,0:T(2,128)(2,1)S(1)}, u32[]{:S(2)}, u32[]{:S(2)}) collective-permute-start(bf16[32,2,128]{2,1,0:T(2,128)(2,1)S(1)} %get-tuple-element.79), channel_id=1, source_target_pairs={{4,0},{8,4},{12,8},{16,12},{20,16},{24,20},{28,24},{32,28},{36,32}... | collective-permute-start | bytes 49160 | tf_op jit(solution)/shard_map/ppermute | solution.py:20
  35.9 14.1 %collective-permute-start.8 = (bf16[2,2,128]{2,1,0:T(2,128)(2,1)S(1)}, bf16[2,2,128]{2,1,0:T(2,128)(2,1)S(1)}, u32[]{:S(2)}, u32[]{:S(2)}) collective-permute-start(bf16[2,2,128]{2,1,0:T(2,128)(2,1)S(1)} %get-tuple-element.73), channel_id=1, source_target_pairs={{0,68},{4,72},{8,76},{12,80},{16,84},{20,88},{24,92},{28,96},{32,1... | collective-permute-start | bytes 3080 | tf_op jit(solution)/shard_map/ppermute | solution.py:27
  44.4 5.7 %collective-permute-start.14 = (bf16[2,64,128]{2,1,0:T(8,128)(2,1)S(1)}, bf16[2,64,128]{2,1,0:T(8,128)(2,1)S(1)}, u32[]{:S(2)}, u32[]{:S(2)}) collective-permute-start(bf16[2,64,128]{2,1,0:T(8,128)(2,1)S(1)} %get-tuple-element.74), channel_id=1, source_target_pairs={{64,0},{128,64},{192,128},{65,1},{129,65},{193,129},{66,2},{130,66... | collective-permute-start | bytes 98312 | tf_op jit(solution)/shard_map/ppermute | solution.py:16
  45.7 5.0 %collective-permute-start.9 = (bf16[2,64,128]{2,1,0:T(8,128)(2,1)S(1)}, bf16[2,64,128]{2,1,0:T(8,128)(2,1)S(1)}, u32[]{:S(2)}, u32[]{:S(2)}) collective-permute-start(bf16[2,64,128]{2,1,0:T(8,128)(2,1)S(1)} %get-tuple-element.75), channel_id=1, source_target_pairs={{0,64},{64,128},{128,192},{1,65},{65,129},{129,193},{2,66},{66,130... | collective-permute-start | bytes 98312 | tf_op jit(solution)/shard_map/ppermute | solution.py:16
  61.1 4.1 %copy-start.4 = (bf16[1,32,64,128]{3,2,1,0:T(8,128)(2,1)S(1)}, bf16[1,32,64,128]{3,2,1,0:T(8,128)(2,1)}, u32[]{:S(2)}) copy-start(bf16[1,32,64,128]{3,2,1,0:T(8,128)(2,1)} %param.14) | copy-start | bytes 1572868
  65.4 14.2 %collective-permute-start = (bf16[3,3,128]{2,1,0:T(4,128)(2,1)S(1)}, bf16[3,3,128]{2,1,0:T(4,128)(2,1)S(1)}, u32[]{:S(2)}, u32[]{:S(2)}) collective-permute-start(bf16[3,3,128]{2,1,0:T(4,128)(2,1)S(1)} %get-tuple-element.82), channel_id=1, source_target_pairs={{0,68},{4,72},{8,76},{12,80},{16,84},{20,88},{24,92},{28,96},{32,1... | collective-permute-start | bytes 6920 | tf_op jit(solution)/shard_map/ppermute | solution.py:27
  69.8 11.2 %collective-permute-start.3 = (bf16[32,3,128]{2,1,0:T(4,128)(2,1)S(1)}, bf16[32,3,128]{2,1,0:T(4,128)(2,1)S(1)}, u32[]{:S(2)}, u32[]{:S(2)}) collective-permute-start(bf16[32,3,128]{2,1,0:T(4,128)(2,1)S(1)} %get-tuple-element.88), channel_id=1, source_target_pairs={{0,4},{4,8},{8,12},{12,16},{16,20},{20,24},{24,28},{28,32},{32,36}... | collective-permute-start | bytes 73736 | tf_op jit(solution)/shard_map/ppermute | solution.py:20
  77.0 11.9 %collective-permute-start.4 = (bf16[32,3,128]{2,1,0:T(4,128)(2,1)S(1)}, bf16[32,3,128]{2,1,0:T(4,128)(2,1)S(1)}, u32[]{:S(2)}, u32[]{:S(2)}) collective-permute-start(bf16[32,3,128]{2,1,0:T(4,128)(2,1)S(1)} %get-tuple-element.89), channel_id=1, source_target_pairs={{4,0},{8,4},{12,8},{16,12},{20,16},{24,20},{28,24},{32,28},{36,32}... | collective-permute-start | bytes 73736 | tf_op jit(solution)/shard_map/ppermute | solution.py:20
  78.3 12.5 %collective-permute-start.2 = (bf16[3,3,128]{2,1,0:T(4,128)(2,1)S(1)}, bf16[3,3,128]{2,1,0:T(4,128)(2,1)S(1)}, u32[]{:S(2)}, u32[]{:S(2)}) collective-permute-start(bf16[3,3,128]{2,1,0:T(4,128)(2,1)S(1)} %get-tuple-element.85), channel_id=1, source_target_pairs={{4,64},{8,68},{12,72},{16,76},{20,80},{24,84},{28,88},{32,92},{36,... | collective-permute-start | bytes 6920 | tf_op jit(solution)/shard_map/ppermute | solution.py:27
  79.0 11.8 %collective-permute-start.5 = (bf16[3,3,128]{2,1,0:T(4,128)(2,1)S(1)}, bf16[3,3,128]{2,1,0:T(4,128)(2,1)S(1)}, u32[]{:S(2)}, u32[]{:S(2)}) collective-permute-start(bf16[3,3,128]{2,1,0:T(4,128)(2,1)S(1)} %get-tuple-element.84), channel_id=1, source_target_pairs={{64,4},{68,8},{72,12},{76,16},{80,20},{84,24},{88,28},{92,32},{96,... | collective-permute-start | bytes 6920 | tf_op jit(solution)/shard_map/ppermute | solution.py:27
  79.7 11.2 %collective-permute-start.7 = (bf16[3,3,128]{2,1,0:T(4,128)(2,1)S(1)}, bf16[3,3,128]{2,1,0:T(4,128)(2,1)S(1)}, u32[]{:S(2)}, u32[]{:S(2)}) collective-permute-start(bf16[3,3,128]{2,1,0:T(4,128)(2,1)S(1)} %get-tuple-element.83), channel_id=1, source_target_pairs={{68,0},{72,4},{76,8},{80,12},{84,16},{88,20},{92,24},{96,28},{100,... | collective-permute-start | bytes 6920 | tf_op jit(solution)/shard_map/ppermute | solution.py:27
  81.0 9.9 %collective-permute-start.1 = (bf16[3,64,128]{2,1,0:T(8,128)(2,1)S(1)}, bf16[3,64,128]{2,1,0:T(8,128)(2,1)S(1)}, u32[]{:S(2)}, u32[]{:S(2)}) collective-permute-start(bf16[3,64,128]{2,1,0:T(8,128)(2,1)S(1)} %bitcast.197), channel_id=1, source_target_pairs={{0,64},{64,128},{128,192},{1,65},{65,129},{129,193},{2,66},{66,130... | collective-permute-start | bytes 147464 | tf_op jit(solution)/shard_map/ppermute | solution.py:16
  89.0 4.8 %collective-permute-start.6 = (bf16[3,64,128]{2,1,0:T(8,128)(2,1)S(1)}, bf16[3,64,128]{2,1,0:T(8,128)(2,1)S(1)}, u32[]{:S(2)}, u32[]{:S(2)}) collective-permute-start(bf16[3,64,128]{2,1,0:T(8,128)(2,1)S(1)} %bitcast.196), channel_id=1, source_target_pairs={{64,0},{128,64},{192,128},{65,1},{129,65},{193,129},{66,2},{130,66... | collective-permute-start | bytes 147464 | tf_op jit(solution)/shard_map/ppermute | solution.py:16
  94.5 1.9 copy-start.7
  107.5 2.1 copy-start.2
  111.4 7.9 %collective-permute-start.16 = (f32[1152,128]{1,0:T(8,128)S(1)}, f32[1152,128]{1,0:T(8,128)S(1)}, u32[]{:S(2)}, u32[]{:S(2)}) collective-permute-start(f32[1152,128]{1,0:T(8,128)S(1)} %fusion.30), channel_id=1, source_target_pairs={{0,1},{1,0},{2,3},{3,2},{4,5},{5,4},{6,7},{7,6},{8,9},{9,8},{10,11... | collective-permute-start | bytes 1769480 | tf_op jit(solution)/shard_map/ppermute | solution.py:67
  119.7 90.3 %copy-start.3 = (bf16[32,64,128]{2,1,0:T(8,128)(2,1)S(1)}, bf16[32,64,128]{2,1,0:T(8,128)(2,1)}, u32[]{:S(2)}) copy-start(bf16[32,64,128]{2,1,0:T(8,128)(2,1)} %get-tuple-element.45) | copy-start | bytes 1572868
  119.7 90.3 %copy-start.6 = (bf16[3,3,128,128]{3,2,1,0:T(8,128)(2,1)S(1)}, bf16[3,3,128,128]{3,2,1,0:T(8,128)(2,1)}, u32[]{:S(2)}) copy-start(bf16[3,3,128,128]{3,2,1,0:T(8,128)(2,1)} %param.20) | copy-start | bytes 884740
  119.7 8.3 %collective-permute-start.17 = (f32[576,128]{1,0:T(8,128)S(1)}, f32[576,128]{1,0:T(8,128)S(1)}, u32[]{:S(2)}, u32[]{:S(2)}) collective-permute-start(f32[576,128]{1,0:T(8,128)S(1)} %constant_dynamic-slice_fusion.8), channel_id=1, source_target_pairs={{0,64},{64,0},{128,192},{192,128},{1,65},{65,1},{129,193},{193,129... | collective-permute-start | bytes 884744 | tf_op jit(solution)/shard_map/ppermute | solution.py:67
  128.1 5.6 %collective-permute-start.18 = (f32[288,128]{1,0:T(8,128)S(1)}, f32[288,128]{1,0:T(8,128)S(1)}, u32[]{:S(2)}, u32[]{:S(2)}) collective-permute-start(f32[288,128]{1,0:T(8,128)S(1)} %constant_dynamic-slice_fusion.7), channel_id=1, source_target_pairs={{0,128},{64,192},{128,0},{192,64},{1,129},{65,193},{129,1},{193,65... | collective-permute-start | bytes 442376 | tf_op jit(solution)/shard_map/ppermute | solution.py:67
  133.7 5.0 %collective-permute-start.19 = (f32[144,128]{1,0:T(8,128)S(1)}, f32[144,128]{1,0:T(8,128)S(1)}, u32[]{:S(2)}, u32[]{:S(2)}) collective-permute-start(f32[144,128]{1,0:T(8,128)S(1)} %constant_dynamic-slice_fusion.6), channel_id=1, source_target_pairs={{0,4},{4,0},{8,12},{12,8},{16,20},{20,16},{24,28},{28,24},{32,36},... | collective-permute-start | bytes 221192 | tf_op jit(solution)/shard_map/ppermute | solution.py:67
  138.8 4.8 %collective-permute-start.20 = (f32[72,128]{1,0:T(8,128)S(1)}, f32[72,128]{1,0:T(8,128)S(1)}, u32[]{:S(2)}, u32[]{:S(2)}) collective-permute-start(f32[72,128]{1,0:T(8,128)S(1)} %constant_dynamic-slice_fusion.5), channel_id=1, source_target_pairs={{0,8},{4,12},{8,0},{12,4},{16,24},{20,28},{24,16},{28,20},{32,40},... | collective-permute-start | bytes 110600 | tf_op jit(solution)/shard_map/ppermute | solution.py:67
  143.6 6.6 %collective-permute-start.21 = (f32[36,128]{1,0:T(8,128)S(1)}, f32[36,128]{1,0:T(8,128)S(1)}, u32[]{:S(2)}, u32[]{:S(2)}) collective-permute-start(f32[36,128]{1,0:T(8,128)S(1)} %constant_dynamic-slice_fusion.4), channel_id=1, source_target_pairs={{0,16},{4,20},{8,24},{12,28},{16,0},{20,4},{24,8},{28,12},{32,48},... | collective-permute-start | bytes 55304 | tf_op jit(solution)/shard_map/ppermute | solution.py:67
  150.2 7.9 %collective-permute-start.22 = (f32[18,128]{1,0:T(8,128)S(1)}, f32[18,128]{1,0:T(8,128)S(1)}, u32[]{:S(2)}, u32[]{:S(2)}) collective-permute-start(f32[18,128]{1,0:T(8,128)S(1)} %constant_dynamic-slice_fusion.2), channel_id=1, source_target_pairs={{0,32},{4,36},{8,40},{12,44},{16,48},{20,52},{24,56},{28,60},{32,0... | collective-permute-start | bytes 27656 | tf_op jit(solution)/shard_map/ppermute | solution.py:67
  158.2 4.1 %collective-permute-start.23 = (f32[9,128]{1,0:T(8,128)S(1)}, f32[9,128]{1,0:T(8,128)S(1)}, u32[]{:S(2)}, u32[]{:S(2)}) collective-permute-start(f32[9,128]{1,0:T(8,128)S(1)} %constant_dynamic-slice_fusion), channel_id=1, source_target_pairs={{0,2},{1,3},{2,0},{3,1},{4,6},{5,7},{6,4},{7,5},{8,10},{9,11},{10,... | collective-permute-start | bytes 13832 | tf_op jit(solution)/shard_map/ppermute | solution.py:67
  162.3 4.2 %collective-permute-start.24 = (f32[9,128]{1,0:T(8,128)S(1)}, f32[9,128]{1,0:T(8,128)S(1)}, u32[]{:S(2)}, u32[]{:S(2)}) collective-permute-start(f32[9,128]{1,0:T(8,128)S(1)} %fusion.61), channel_id=1, source_target_pairs={{0,2},{1,3},{2,0},{3,1},{4,6},{5,7},{6,4},{7,5},{8,10},{9,11},{10,... | collective-permute-start | bytes 13832 | tf_op jit(solution)/shard_map/ppermute | solution.py:71
  166.5 2.8 %collective-permute-start.25 = (f32[18,128]{1,0:T(8,128)S(1)}, f32[18,128]{1,0:T(8,128)S(1)}, u32[]{:S(2)}, u32[]{:S(2)}) collective-permute-start(f32[18,128]{1,0:T(8,128)S(1)} %pad_maximum_fusion.10), channel_id=1, source_target_pairs={{0,32},{4,36},{8,40},{12,44},{16,48},{20,52},{24,56},{28,60},{32,0... | collective-permute-start | bytes 27656 | tf_op jit(solution)/shard_map/ppermute | solution.py:71
  169.3 6.6 %collective-permute-start.26 = (f32[36,128]{1,0:T(8,128)S(1)}, f32[36,128]{1,0:T(8,128)S(1)}, u32[]{:S(2)}, u32[]{:S(2)}) collective-permute-start(f32[36,128]{1,0:T(8,128)S(1)} %pad_maximum_fusion.9), channel_id=1, source_target_pairs={{0,16},{4,20},{8,24},{12,28},{16,0},{20,4},{24,8},{28,12},{32,48},... | collective-permute-start | bytes 55304 | tf_op jit(solution)/shard_map/ppermute | solution.py:71
  176.0 4.1 %collective-permute-start.27 = (f32[72,128]{1,0:T(8,128)S(1)}, f32[72,128]{1,0:T(8,128)S(1)}, u32[]{:S(2)}, u32[]{:S(2)}) collective-permute-start(f32[72,128]{1,0:T(8,128)S(1)} %pad_maximum_fusion.8), channel_id=1, source_target_pairs={{0,8},{4,12},{8,0},{12,4},{16,24},{20,28},{24,16},{28,20},{32,40},... | collective-permute-start | bytes 110600 | tf_op jit(solution)/shard_map/ppermute | solution.py:71
  180.1 3.3 %collective-permute-start.28 = (f32[144,128]{1,0:T(8,128)S(1)}, f32[144,128]{1,0:T(8,128)S(1)}, u32[]{:S(2)}, u32[]{:S(2)}) collective-permute-start(f32[144,128]{1,0:T(8,128)S(1)} %get-tuple-element.98), channel_id=1, source_target_pairs={{0,4},{4,0},{8,12},{12,8},{16,20},{20,16},{24,28},{28,24},{32,36},... | collective-permute-start | bytes 221192 | tf_op jit(solution)/shard_map/ppermute | solution.py:71
  183.5 5.6 %collective-permute-start.29 = (f32[288,128]{1,0:T(8,128)S(1)}, f32[288,128]{1,0:T(8,128)S(1)}, u32[]{:S(2)}, u32[]{:S(2)}) collective-permute-start(f32[288,128]{1,0:T(8,128)S(1)} %get-tuple-element.94), channel_id=1, source_target_pairs={{0,128},{64,192},{128,0},{192,64},{1,129},{65,193},{129,1},{193,65... | collective-permute-start | bytes 442376 | tf_op jit(solution)/shard_map/ppermute | solution.py:71
  189.2 6.0 %collective-permute-start.30 = (f32[576,128]{1,0:T(8,128)S(1)}, f32[576,128]{1,0:T(8,128)S(1)}, u32[]{:S(2)}, u32[]{:S(2)}) collective-permute-start(f32[576,128]{1,0:T(8,128)S(1)} %get-tuple-element.90), channel_id=1, source_target_pairs={{0,64},{64,0},{128,192},{192,128},{1,65},{65,1},{129,193},{193,129... | collective-permute-start | bytes 884744 | tf_op jit(solution)/shard_map/ppermute | solution.py:71
  195.3 19.2 %collective-permute-start.31 = (f32[1152,128]{1,0:T(8,128)S(1)}, f32[1152,128]{1,0:T(8,128)S(1)}, u32[]{:S(2)}, u32[]{:S(2)}) collective-permute-start(f32[1152,128]{1,0:T(8,128)S(1)} %get-tuple-element.62), channel_id=1, source_target_pairs={{0,1},{1,0},{2,3},{3,2},{4,5},{5,4},{6,7},{7,6},{8,9},{9,8},{10,11... | collective-permute-start | bytes 1769480 | tf_op jit(solution)/shard_map/ppermute | solution.py:71

commit v6 on v4

--- a/solution.py
+++ b/solution.py
@@ -33,9 +33,11 @@
     return steps
 
 
-def tree_sum(x):
+def tree_sum(x, rider):
     steps = halving_steps()
-    for axis, d in steps:
+    for step, (axis, d) in enumerate(steps):
+        if step == 2:
+            x, rider = lax.optimization_barrier((x, rider))
         pairs = [(i, i ^ d) for i in range(lax.axis_size(axis))]
         upper = (lax.axis_index(axis) // d) % 2 == 1
         half = x.shape[0] // 2
@@ -53,7 +55,7 @@
             [lax.dynamic_index_in_dim(both, side, keepdims=False),
              lax.dynamic_index_in_dim(both, 1 - side, keepdims=False)]
         )
-    return x
+    return x, rider
 
 
 def unfold(padded, step, rows, cols):
@@ -130,12 +132,6 @@
     act1 = padded1[2:-2, 2:-2]
     patches0 = unfold(deep[2:-2, 2:-2], 1, rows, cols)
     patches1 = unfold(padded1, 2, rows, cols)
-    pre2 = jnp.dot(patches1, w_two, preferred_element_type=jnp.float32)
-    output = (
-        (act1.astype(jnp.float32).reshape(rows * cols, chans) + pre2)
-        .astype(jnp.bfloat16)
-        .reshape(1, rows, cols, chans)
-    )
     back = cotangent[0]
     padded_back = with_halo(back, (("row", 0), ("col", 1)), 2)
     w_turned = jnp.transpose(w_second[::-1, ::-1], (0, 1, 3, 2)).reshape(9 * chans, chans)
@@ -148,7 +144,6 @@
     grad_pre1 = lax.optimization_barrier(grad_pre1)
     first_term = contract_rows(patches0, grad_pre1)
     second_term = contract_rows(patches1, back_flat)
-    first_sum, second_sum = jnp.split(tree_sum(jnp.concatenate([first_term, second_term])), 2)
     total_cells = (
         rows
         * lax.axis_size("row")
@@ -158,8 +153,17 @@
         * cells_per_sample_factor(grid_feats)
     )
     scale = 1.0 / math.sqrt(total_cells)
-    grad_first = (first_sum * scale).reshape(3, 3, chans, chans)
-    grad_second = (second_sum * scale).reshape(3, 3, chans, chans)
+    terms = jnp.concatenate([first_term, second_term]) * scale
+    pre2 = jnp.dot(patches1, w_two, preferred_element_type=jnp.float32)
+    output = (
+        (act1.astype(jnp.float32).reshape(rows * cols, chans) + pre2)
+        .astype(jnp.bfloat16)
+        .reshape(1, rows, cols, chans)
+    )
+    summed, output = tree_sum(terms, output)
+    first_sum, second_sum = jnp.split(summed, 2)
+    grad_first = first_sum.reshape(3, 3, chans, chans)
+    grad_second = second_sum.reshape(3, 3, chans, chans)
     return (output, grad_first, grad_second)
 
 

time: 189 us -> 185 us (0.979)
  waiting for transfers between devices: 55.9 us -> 53 us
    ppermute x8, waiting for transfers between devices: 22 us -> 17.5 us  [tree_sum(): x = kept + lax.ppermute(sent, axis, pairs)]
    unnamed x48 -> x44, local copies, waits for them, and re-layouts: 11.9 us -> 11.9 us
  transfers between devices with their start and end apart: 25 -> 25, of which waited for: 20 -> 21; matrix products, arithmetic and copies ran while one was open for 7% -> 8% of each run, Pallas kernels for 0% -> 0%
where the time goes in v6:
time: 185 us; the launch traced here: 184 us
  starting transfers between devices  80.7 us (44%)
  waiting for transfers between devices  53 us (29%)
  matrix products  21 us (11%)
  local copies, waits for them, and re-layouts  15.9 us (9%)
  other arithmetic  12.2 us (7%)
    ppermute x8, starting transfers between devices, tree_sum(): got = lax.ppermute(x, axis, pairs)  28.3 us
    ppermute x8, starting transfers between devices, tree_sum(): x = kept + lax.ppermute(sent, axis, pairs)  21.7 us
    ppermute x8, waiting for transfers between devices, tree_sum(): got = lax.ppermute(x, axis, pairs)  20.9 us
    ppermute x8, waiting for transfers between devices, tree_sum(): x = kept + lax.ppermute(sent, axis, pairs)  17.5 us
    all_to_all x1, starting transfers between devices, on_device(): lax.all_to_all(payload, ('row', 'col'), split_axis=0, concat_axis=0, tile...  13.5 us
    ppermute x4, waiting for transfers between devices, with_halo(): after = lax.ppermute(leading, axis, down)  13.3 us
    unnamed x44, local copies, waits for them, and re-layouts  11.9 us
    ppermute x4, starting transfers between devices, with_halo(): before = lax.ppermute(last, axis, up)  11.8 us
  transfers between devices with their start and end apart: 25, of which 21 were waited for; matrix products, arithmetic and copies ran while one was open for 8% of the time, Pallas kernels for 0%

profile of v6, /device:TPU:1, one launch (start us, length us, event | category | flops | bytes accessed | tf_op | source)
XLA Modules:
  0.0 184.2 jit_solution(4535455284066866000)
XLA Ops:
  2.6 1.5 reduce-window.6
  4.6 1.3 broadcast_select_fusion
  5.9 1.4 broadcast_select_fusion.1
  8.2 2.7 %fusion.11 = f32[1280,128]{1,0:T(8,128)S(1)} fusion(bf16[512,128]{1,0:T(8,128)(2,1)} %param.18, s32[640]{0:T(1024)S(1)} %add_add_fusion, bf16[1,640,512]{2,1,0:T(8,128)(2,1)S(1)} %copy-done), kind=kOutput, calls=%fused_computation.19 | convolution fusion | flops 1008107520 | bytes 1444352 | tf_op jit(solution)/shard_map/dot_general | solution.py:93
  11.0 1.0 select_maximum_fusion
  12.0 13.5 %all-to-all-start = ((f32[64,21,128]{2,1,0:T(8,128)}), f32[64,21,128]{2,1,0:T(8,128)S(1)}, u32[]{:S(2)}, u32[]{:S(2)}) async-start(f32[64,21,128]{2,1,0:T(8,128)} %select_maximum_fusion), calls=%async_computation | async-start | bytes 1572864 | tf_op jit(solution)/shard_map/all_to_all | solution.py:101
  25.5 2.9 %collective-permute-start.4 = (bf16[2,64,128]{2,1,0:T(8,128)(2,1)S(1)}, bf16[2,64,128]{2,1,0:T(8,128)(2,1)S(1)}, u32[]{:S(2)}, u32[]{:S(2)}) collective-permute-start(bf16[2,64,128]{2,1,0:T(8,128)(2,1)S(1)} %get-tuple-element.80), channel_id=1, source_target_pairs={{0,64},{64,128},{128,192},{1,65},{65,129},{129,193},{2,66},{66,130... | collective-permute-start | bytes 98312 | tf_op jit(solution)/shard_map/ppermute | solution.py:16
  28.4 1.3 collective-permute-start.5
  30.1 3.7 %collective-permute-done.5 = bf16[2,64,128]{2,1,0:T(8,128)(2,1)S(1)} collective-permute-done((bf16[2,64,128]{2,1,0:T(8,128)(2,1)S(1)}, bf16[2,64,128]{2,1,0:T(8,128)(2,1)S(1)}, u32[]{:S(2)}, u32[]{:S(2)}) %collective-permute-start.5) | collective-permute-done | bytes 32800 | tf_op jit(solution)/shard_map/ppermute | solution.py:17
  33.9 2.7 %collective-permute-start.6 = (bf16[36,2,128]{2,1,0:T(2,128)(2,1)S(1)}, bf16[36,2,128]{2,1,0:T(2,128)(2,1)S(1)}, u32[]{:S(2)}, u32[]{:S(2)}) collective-permute-start(bf16[36,2,128]{2,1,0:T(2,128)(2,1)S(1)} %get-tuple-element.77), channel_id=1, source_target_pairs={{0,4},{4,8},{8,12},{12,16},{16,20},{20,24},{24,28},{28,32},{32,36}... | collective-permute-start | bytes 55304 | tf_op jit(solution)/shard_map/ppermute | solution.py:16
  36.5 1.3 collective-permute-start.7
  37.9 1.3 collective-permute-done.6
  39.2 3.9 %collective-permute-done.7 = bf16[36,2,128]{2,1,0:T(2,128)(2,1)S(1)} collective-permute-done((bf16[36,2,128]{2,1,0:T(2,128)(2,1)S(1)}, bf16[36,2,128]{2,1,0:T(2,128)(2,1)S(1)}, u32[]{:S(2)}, u32[]{:S(2)}) %collective-permute-start.7) | collective-permute-done | bytes 18464 | tf_op jit(solution)/shard_map/ppermute | solution.py:17
  44.0 0.9 constant_dynamic-update-slice_fusion.17
  44.9 0.9 constant_dynamic-update-slice_fusion.16
  45.8 0.9 constant_dynamic-update-slice_fusion.15
  46.7 0.9 constant_dynamic-update-slice_fusion.14
  48.5 0.9 constant_dynamic-update-slice_fusion.12
  51.2 1.1 reduce-precision_convert_fusion.1
  52.5 4.1 %fusion = f32[2048,384]{1,0:T(8,128)S(1)} fusion(f32[1280]{0:T(1024)S(1)} %eq.112, bf16[1280,128]{1,0:T(8,128)(2,1)} %get-tuple-element.64, bf16[1280,128]{1,0:T(8,128)(2,1)} %get-tuple-element.65, bf16[1280,128]{1,0:T(8,128)(2,1)} %get-tuple-element.63), kind=kOutput, calls=%fused_computation.1 | convolution fusion | flops 2018836480 | bytes 4133888 | tf_op jit(solution)/shard_map/dot_general | solution.py:112
  56.9 3.2 %collective-permute-start = (bf16[3,64,128]{2,1,0:T(8,128)(2,1)S(1)}, bf16[3,64,128]{2,1,0:T(8,128)(2,1)S(1)}, u32[]{:S(2)}, u32[]{:S(2)}) collective-permute-start(bf16[3,64,128]{2,1,0:T(8,128)(2,1)S(1)} %bitcast.195), channel_id=1, source_target_pairs={{0,64},{64,128},{128,192},{1,65},{65,129},{129,193},{2,66},{66,130... | collective-permute-start | bytes 147464 | tf_op jit(solution)/shard_map/ppermute | solution.py:16
  60.1 1.3 collective-permute-start.1
  62.3 2.7 %collective-permute-done.1 = bf16[3,64,128]{2,1,0:T(8,128)(2,1)S(1)} collective-permute-done((bf16[3,64,128]{2,1,0:T(8,128)(2,1)S(1)}, bf16[3,64,128]{2,1,0:T(8,128)(2,1)S(1)}, u32[]{:S(2)}, u32[]{:S(2)}) %collective-permute-start.1) | collective-permute-done | bytes 49184 | tf_op jit(solution)/shard_map/ppermute | solution.py:17
  65.0 3.0 %collective-permute-start.2 = (bf16[38,3,128]{2,1,0:T(4,128)(2,1)S(1)}, bf16[38,3,128]{2,1,0:T(4,128)(2,1)S(1)}, u32[]{:S(2)}, u32[]{:S(2)}) collective-permute-start(bf16[38,3,128]{2,1,0:T(4,128)(2,1)S(1)} %get-tuple-element.68), channel_id=1, source_target_pairs={{0,4},{4,8},{8,12},{12,16},{16,20},{20,24},{24,28},{28,32},{32,36}... | collective-permute-start | bytes 87560 | tf_op jit(solution)/shard_map/ppermute | solution.py:16
  68.0 1.5 collective-permute-start.3
  69.6 3.2 %collective-permute-done.3 = bf16[38,3,128]{2,1,0:T(4,128)(2,1)S(1)} collective-permute-done((bf16[38,3,128]{2,1,0:T(4,128)(2,1)S(1)}, bf16[38,3,128]{2,1,0:T(4,128)(2,1)S(1)}, u32[]{:S(2)}, u32[]{:S(2)}) %collective-permute-start.3) | collective-permute-done | bytes 29216 | tf_op jit(solution)/shard_map/ppermute | solution.py:17
  75.4 2.2 %select_convert_fusion = (bf16[36,68,128]{2,1,0:T(8,128)(2,1)S(1)}, f32[36,68,128]{2,1,0:T(8,128)S(1)}) fusion(pred[36,68]{1,0:T(8,128)(4,1)S(1)} %broadcast_and_fusion, bf16[36,68,1152]{2,1,0:T(8,128)(2,1)S(1)} %slice_dynamic-update-slice_fusion, bf16[1152,128,1]{1,0,2:T(8,128)(2,1)S(1)} %bitcast.202), kind=kOutput, calls=%fused_computation.20 | convolution fusion | flops 723824640 | bytes 7817616 | tf_op jit(solution)/shard_map/dot_general | solution.py:122
  78.0 3.8 %fusion.7 = bf16[2048,128]{1,0:T(8,128)(2,1)S(1)} fusion(f32[2048,128]{1,0:T(8,128)S(1)} %get-tuple-element.48, f32[2048,128]{1,0:T(8,128)S(1)} %get-tuple-element.47, bf16[2048,1152]{1,0:T(8,128)(2,1)} %constant_dynamic-update-slice_fusion.9, bf16[1152,128]{1,0:T(8,128)(2,1)S(1)} %bitcast.183, bf16[2048,128]{1,0:T(8,128)(2,1)S(1)} %bitcast.158), kind=kOutput, calls=%fused_computation.11 | convolution fusion | flops 605290496 | bytes 8159232 | tf_op jit(solution)/shard_map/dot_general | solution.py:139
  85.3 1.4 fusion.74
  87.5 1.4 fusion.73
  89.1 5.2 %collective-permute-start.8 = (f32[1152,128]{1,0:T(8,128)S(1)}, f32[1152,128]{1,0:T(8,128)S(1)}, u32[]{:S(2)}, u32[]{:S(2)}) collective-permute-start(f32[1152,128]{1,0:T(8,128)S(1)} %constant_dynamic-slice_fusion.8), channel_id=1, source_target_pairs={{0,1},{1,0},{2,3},{3,2},{4,5},{5,4},{6,7},{7,6},{8,9},{9,8},{10,11... | collective-permute-start | bytes 1769480 | tf_op jit(solution)/shard_map/ppermute | solution.py:47
  94.2 1.6 collective-permute-done.8
  96.0 1.4 collective-permute-start.9
  97.3 4.6 %fusion.8 = bf16[2048,128]{1,0:T(8,128)(2,1)} fusion(bf16[2048,1152]{1,0:T(8,128)(2,1)} %bitcast.165, bf16[1152,128]{1,0:T(8,128)(2,1)} %bitcast.188, bf16[2048,128]{1,0:T(8,128)(2,1)S(1)} %bitcast.187), kind=kOutput, calls=%fused_computation.12 | convolution fusion | flops 604766208 | bytes 6062080 | tf_op jit(solution)/shard_map/dot_general | solution.py:157
  101.9 2.4 %collective-permute-done.9 = f32[576,128]{1,0:T(8,128)S(1)} collective-permute-done((f32[576,128]{1,0:T(8,128)S(1)}, f32[576,128]{1,0:T(8,128)S(1)}, u32[]{:S(2)}, u32[]{:S(2)}) %collective-permute-start.9) | collective-permute-done | bytes 294944 | tf_op jit(solution)/shard_map/ppermute | solution.py:47
  104.3 2.0 %collective-permute-start.10 = (f32[288,128]{1,0:T(8,128)S(1)}, f32[288,128]{1,0:T(8,128)S(1)}, u32[]{:S(2)}, u32[]{:S(2)}) collective-permute-start(f32[288,128]{1,0:T(8,128)S(1)} %constant_dynamic-slice_fusion.6), channel_id=1, source_target_pairs={{0,128},{64,192},{128,0},{192,64},{1,129},{65,193},{129,1},{193,65... | collective-permute-start | bytes 442376 | tf_op jit(solution)/shard_map/ppermute | solution.py:47
  106.3 3.8 %collective-permute-done.10 = f32[288,128]{1,0:T(8,128)S(1)} collective-permute-done((f32[288,128]{1,0:T(8,128)S(1)}, f32[288,128]{1,0:T(8,128)S(1)}, u32[]{:S(2)}, u32[]{:S(2)}) %collective-permute-start.10) | collective-permute-done | bytes 147488 | tf_op jit(solution)/shard_map/ppermute | solution.py:47
  110.2 2.9 %collective-permute-start.11 = (f32[144,128]{1,0:T(8,128)S(1)}, f32[144,128]{1,0:T(8,128)S(1)}, u32[]{:S(2)}, u32[]{:S(2)}) collective-permute-start(f32[144,128]{1,0:T(8,128)S(1)} %constant_dynamic-slice_fusion.5), channel_id=1, source_target_pairs={{0,4},{4,0},{8,12},{12,8},{16,20},{20,16},{24,28},{28,24},{32,36},... | collective-permute-start | bytes 221192 | tf_op jit(solution)/shard_map/ppermute | solution.py:47
  113.1 1.7 collective-permute-done.11
  114.9 3.0 %collective-permute-start.12 = (f32[72,128]{1,0:T(8,128)S(1)}, f32[72,128]{1,0:T(8,128)S(1)}, u32[]{:S(2)}, u32[]{:S(2)}) collective-permute-start(f32[72,128]{1,0:T(8,128)S(1)} %constant_dynamic-slice_fusion.4), channel_id=1, source_target_pairs={{0,8},{4,12},{8,0},{12,4},{16,24},{20,28},{24,16},{28,20},{32,40},... | collective-permute-start | bytes 110600 | tf_op jit(solution)/shard_map/ppermute | solution.py:47
  117.9 1.3 collective-permute-done.12
  119.2 2.6 %collective-permute-start.13 = (f32[36,128]{1,0:T(8,128)S(1)}, f32[36,128]{1,0:T(8,128)S(1)}, u32[]{:S(2)}, u32[]{:S(2)}) collective-permute-start(f32[36,128]{1,0:T(8,128)S(1)} %constant_dynamic-slice_fusion.3), channel_id=1, source_target_pairs={{0,16},{4,20},{8,24},{12,28},{16,0},{20,4},{24,8},{28,12},{32,48},... | collective-permute-start | bytes 55304 | tf_op jit(solution)/shard_map/ppermute | solution.py:47
  121.9 4.1 %collective-permute-done.13 = f32[36,128]{1,0:T(8,128)S(1)} collective-permute-done((f32[36,128]{1,0:T(8,128)S(1)}, f32[36,128]{1,0:T(8,128)S(1)}, u32[]{:S(2)}, u32[]{:S(2)}) %collective-permute-start.13) | collective-permute-done | bytes 18464 | tf_op jit(solution)/shard_map/ppermute | solution.py:47
  126.0 2.0 %collective-permute-start.14 = (f32[18,128]{1,0:T(8,128)S(1)}, f32[18,128]{1,0:T(8,128)S(1)}, u32[]{:S(2)}, u32[]{:S(2)}) collective-permute-start(f32[18,128]{1,0:T(8,128)S(1)} %constant_dynamic-slice_fusion.2), channel_id=1, source_target_pairs={{0,32},{4,36},{8,40},{12,44},{16,48},{20,52},{24,56},{28,60},{32,0... | collective-permute-start | bytes 27656 | tf_op jit(solution)/shard_map/ppermute | solution.py:47
  128.0 1.1 collective-permute-done.14
  129.1 2.7 %collective-permute-start.15 = (f32[9,128]{1,0:T(8,128)S(1)}, f32[9,128]{1,0:T(8,128)S(1)}, u32[]{:S(2)}, u32[]{:S(2)}) collective-permute-start(f32[9,128]{1,0:T(8,128)S(1)} %constant_dynamic-slice_fusion), channel_id=1, source_target_pairs={{0,2},{1,3},{2,0},{3,1},{4,6},{5,7},{6,4},{7,5},{8,10},{9,11},{10,... | collective-permute-start | bytes 13832 | tf_op jit(solution)/shard_map/ppermute | solution.py:47
  131.8 1.4 collective-permute-done.15
  133.2 2.7 %collective-permute-start.16 = (f32[9,128]{1,0:T(8,128)S(1)}, f32[9,128]{1,0:T(8,128)S(1)}, u32[]{:S(2)}, u32[]{:S(2)}) collective-permute-start(f32[9,128]{1,0:T(8,128)S(1)} %fusion.55), channel_id=1, source_target_pairs={{0,2},{1,3},{2,0},{3,1},{4,6},{5,7},{6,4},{7,5},{8,10},{9,11},{10,... | collective-permute-start | bytes 13832 | tf_op jit(solution)/shard_map/ppermute | solution.py:51
  135.9 1.4 collective-permute-done.16
  137.3 1.5 collective-permute-start.17
  138.9 1.4 collective-permute-done.17
  140.3 2.2 %collective-permute-start.18 = (f32[36,128]{1,0:T(8,128)S(1)}, f32[36,128]{1,0:T(8,128)S(1)}, u32[]{:S(2)}, u32[]{:S(2)}) collective-permute-start(f32[36,128]{1,0:T(8,128)S(1)} %pad_maximum_fusion.15), channel_id=1, source_target_pairs={{0,16},{4,20},{8,24},{12,28},{16,0},{20,4},{24,8},{28,12},{32,48},... | collective-permute-start | bytes 55304 | tf_op jit(solution)/shard_map/ppermute | solution.py:51
  142.5 4.4 %collective-permute-done.18 = f32[36,128]{1,0:T(8,128)S(1)} collective-permute-done((f32[36,128]{1,0:T(8,128)S(1)}, f32[36,128]{1,0:T(8,128)S(1)}, u32[]{:S(2)}, u32[]{:S(2)}) %collective-permute-start.18) | collective-permute-done | bytes 18464 | tf_op jit(solution)/shard_map/ppermute | solution.py:51
  147.0 2.4 %collective-permute-start.19 = (f32[72,128]{1,0:T(8,128)S(1)}, f32[72,128]{1,0:T(8,128)S(1)}, u32[]{:S(2)}, u32[]{:S(2)}) collective-permute-start(f32[72,128]{1,0:T(8,128)S(1)} %pad_maximum_fusion.14), channel_id=1, source_target_pairs={{0,8},{4,12},{8,0},{12,4},{16,24},{20,28},{24,16},{28,20},{32,40},... | collective-permute-start | bytes 110600 | tf_op jit(solution)/shard_map/ppermute | solution.py:51
  149.3 1.4 collective-permute-done.19
  150.8 1.2 collective-permute-start.20
  152.0 2.1 %collective-permute-done.20 = f32[144,128]{1,0:T(8,128)S(1)} collective-permute-done((f32[144,128]{1,0:T(8,128)S(1)}, f32[144,128]{1,0:T(8,128)S(1)}, u32[]{:S(2)}, u32[]{:S(2)}) %collective-permute-start.20) | collective-permute-done | bytes 73760 | tf_op jit(solution)/shard_map/ppermute | solution.py:51
  154.1 1.5 collective-permute-start.21
  155.7 4.1 %collective-permute-done.21 = f32[288,128]{1,0:T(8,128)S(1)} collective-permute-done((f32[288,128]{1,0:T(8,128)S(1)}, f32[288,128]{1,0:T(8,128)S(1)}, u32[]{:S(2)}, u32[]{:S(2)}) %collective-permute-start.21) | collective-permute-done | bytes 147488 | tf_op jit(solution)/shard_map/ppermute | solution.py:51
  159.8 1.1 collective-permute-start.22
  161.0 4.5 %collective-permute-done.22 = f32[576,128]{1,0:T(8,128)S(1)} collective-permute-done((f32[576,128]{1,0:T(8,128)S(1)}, f32[576,128]{1,0:T(8,128)S(1)}, u32[]{:S(2)}, u32[]{:S(2)}) %collective-permute-start.22) | collective-permute-done | bytes 294944 | tf_op jit(solution)/shard_map/ppermute | solution.py:51
  165.7 15.7 %collective-permute-start.23 = (f32[1152,128]{1,0:T(8,128)S(1)}, f32[1152,128]{1,0:T(8,128)S(1)}, u32[]{:S(2)}, u32[]{:S(2)}) collective-permute-start(f32[1152,128]{1,0:T(8,128)S(1)} %get-tuple-element.70), channel_id=1, source_target_pairs={{0,1},{1,0},{2,3},{3,2},{4,5},{5,4},{6,7},{7,6},{8,9},{9,8},{10,11... | collective-permute-start | bytes 1769480 | tf_op jit(solution)/shard_map/ppermute | solution.py:51
  181.4 1.6 collective-permute-done.23
  183.0 1.2 fusion.26
  (117 shorter events, 16.8 us)
Async XLA Ops:
  0.6 7.6 %copy-start = (bf16[1,640,512]{2,1,0:T(8,128)(2,1)S(1)}, bf16[1,640,512]{2,1,0:T(8,128)(2,1)}, u32[]{:S(2)}) copy-start(bf16[1,640,512]{2,1,0:T(8,128)(2,1)} %param.15) | copy-start | bytes 1966084
  8.2 17.3 %copy-start.1 = (bf16[1,32,64,128]{3,2,1,0:T(8,128)(2,1)S(1)}, bf16[1,32,64,128]{3,2,1,0:T(8,128)(2,1)}, u32[]{:S(2)}) copy-start(bf16[1,32,64,128]{3,2,1,0:T(8,128)(2,1)} %param.21) | copy-start | bytes 1572868
  8.2 21.6 %copy-start.4 = (bf16[3,3,128,128]{3,2,1,0:T(8,128)(2,1)S(1)}, bf16[3,3,128,128]{3,2,1,0:T(8,128)(2,1)}, u32[]{:S(2)}) copy-start(bf16[3,3,128,128]{3,2,1,0:T(8,128)(2,1)} %param.20) | copy-start | bytes 884740
  12.0 39.2 %all-to-all-start = ((f32[64,21,128]{2,1,0:T(8,128)}), f32[64,21,128]{2,1,0:T(8,128)S(1)}, u32[]{:S(2)}, u32[]{:S(2)}) async-start(f32[64,21,128]{2,1,0:T(8,128)} %select_maximum_fusion), calls=%async_computation | async-start | bytes 1572864 | tf_op jit(solution)/shard_map/all_to_all | solution.py:101
  25.5 4.6 %collective-permute-start.4 = (bf16[2,64,128]{2,1,0:T(8,128)(2,1)S(1)}, bf16[2,64,128]{2,1,0:T(8,128)(2,1)S(1)}, u32[]{:S(2)}, u32[]{:S(2)}) collective-permute-start(bf16[2,64,128]{2,1,0:T(8,128)(2,1)S(1)} %get-tuple-element.80), channel_id=1, source_target_pairs={{0,64},{64,128},{128,192},{1,65},{65,129},{129,193},{2,66},{66,130... | collective-permute-start | bytes 98312 | tf_op jit(solution)/shard_map/ppermute | solution.py:16
  28.4 5.4 %collective-permute-start.5 = (bf16[2,64,128]{2,1,0:T(8,128)(2,1)S(1)}, bf16[2,64,128]{2,1,0:T(8,128)(2,1)S(1)}, u32[]{:S(2)}, u32[]{:S(2)}) collective-permute-start(bf16[2,64,128]{2,1,0:T(8,128)(2,1)S(1)} %get-tuple-element.81), channel_id=1, source_target_pairs={{64,0},{128,64},{192,128},{65,1},{129,65},{193,129},{66,2},{130,66... | collective-permute-start | bytes 98312 | tf_op jit(solution)/shard_map/ppermute | solution.py:17
  33.9 5.3 %collective-permute-start.6 = (bf16[36,2,128]{2,1,0:T(2,128)(2,1)S(1)}, bf16[36,2,128]{2,1,0:T(2,128)(2,1)S(1)}, u32[]{:S(2)}, u32[]{:S(2)}) collective-permute-start(bf16[36,2,128]{2,1,0:T(2,128)(2,1)S(1)} %get-tuple-element.77), channel_id=1, source_target_pairs={{0,4},{4,8},{8,12},{12,16},{16,20},{20,24},{24,28},{28,32},{32,36}... | collective-permute-start | bytes 55304 | tf_op jit(solution)/shard_map/ppermute | solution.py:16
  36.5 6.5 %collective-permute-start.7 = (bf16[36,2,128]{2,1,0:T(2,128)(2,1)S(1)}, bf16[36,2,128]{2,1,0:T(2,128)(2,1)S(1)}, u32[]{:S(2)}, u32[]{:S(2)}) collective-permute-start(bf16[36,2,128]{2,1,0:T(2,128)(2,1)S(1)} %get-tuple-element.76), channel_id=1, source_target_pairs={{4,0},{8,4},{12,8},{16,12},{20,16},{24,20},{28,24},{32,28},{36,32}... | collective-permute-start | bytes 55304 | tf_op jit(solution)/shard_map/ppermute | solution.py:17
  52.5 4.2 %copy-start.3 = (bf16[1,32,64,128]{3,2,1,0:T(8,128)(2,1)S(1)}, bf16[1,32,64,128]{3,2,1,0:T(8,128)(2,1)}, u32[]{:S(2)}) copy-start(bf16[1,32,64,128]{3,2,1,0:T(8,128)(2,1)} %param.14) | copy-start | bytes 1572868
  56.9 5.4 %collective-permute-start = (bf16[3,64,128]{2,1,0:T(8,128)(2,1)S(1)}, bf16[3,64,128]{2,1,0:T(8,128)(2,1)S(1)}, u32[]{:S(2)}, u32[]{:S(2)}) collective-permute-start(bf16[3,64,128]{2,1,0:T(8,128)(2,1)S(1)} %bitcast.195), channel_id=1, source_target_pairs={{0,64},{64,128},{128,192},{1,65},{65,129},{129,193},{2,66},{66,130... | collective-permute-start | bytes 147464 | tf_op jit(solution)/shard_map/ppermute | solution.py:16
  60.1 4.8 %collective-permute-start.1 = (bf16[3,64,128]{2,1,0:T(8,128)(2,1)S(1)}, bf16[3,64,128]{2,1,0:T(8,128)(2,1)S(1)}, u32[]{:S(2)}, u32[]{:S(2)}) collective-permute-start(bf16[3,64,128]{2,1,0:T(8,128)(2,1)S(1)} %bitcast.194), channel_id=1, source_target_pairs={{64,0},{128,64},{192,128},{65,1},{129,65},{193,129},{66,2},{130,66... | collective-permute-start | bytes 147464 | tf_op jit(solution)/shard_map/ppermute | solution.py:17
  65.0 4.6 %collective-permute-start.2 = (bf16[38,3,128]{2,1,0:T(4,128)(2,1)S(1)}, bf16[38,3,128]{2,1,0:T(4,128)(2,1)S(1)}, u32[]{:S(2)}, u32[]{:S(2)}) collective-permute-start(bf16[38,3,128]{2,1,0:T(4,128)(2,1)S(1)} %get-tuple-element.68), channel_id=1, source_target_pairs={{0,4},{4,8},{8,12},{12,16},{16,20},{20,24},{24,28},{28,32},{32,36}... | collective-permute-start | bytes 87560 | tf_op jit(solution)/shard_map/ppermute | solution.py:16
  68.0 4.7 %collective-permute-start.3 = (bf16[38,3,128]{2,1,0:T(4,128)(2,1)S(1)}, bf16[38,3,128]{2,1,0:T(4,128)(2,1)S(1)}, u32[]{:S(2)}, u32[]{:S(2)}) collective-permute-start(bf16[38,3,128]{2,1,0:T(4,128)(2,1)S(1)} %get-tuple-element.69), channel_id=1, source_target_pairs={{4,0},{8,4},{12,8},{16,12},{20,16},{24,20},{28,24},{32,28},{36,32}... | collective-permute-start | bytes 87560 | tf_op jit(solution)/shard_map/ppermute | solution.py:17
  73.5 1.9 %copy-start.5 = (bf16[3,3,128,128]{3,2,1,0:T(8,128)(2,1)S(1)}, bf16[3,3,128,128]{3,2,1,0:T(8,128)(2,1)}, u32[]{:S(2)}) copy-start(bf16[3,3,128,128]{3,2,1,0:T(8,128)(2,1)} %param.19) | copy-start | bytes 884740
  85.3 2.2 %copy-start.2 = (bf16[32,64,1152]{2,1,0:T(8,128)(2,1)}, bf16[32,64,1152]{2,1,0:T(8,128)(2,1)S(1)}, u32[]{:S(2)}) copy-start(bf16[32,64,1152]{2,1,0:T(8,128)(2,1)S(1)} %slice_dynamic-update-slice_fusion.9) | copy-start | bytes 14155780
  89.1 6.8 %collective-permute-start.8 = (f32[1152,128]{1,0:T(8,128)S(1)}, f32[1152,128]{1,0:T(8,128)S(1)}, u32[]{:S(2)}, u32[]{:S(2)}) collective-permute-start(f32[1152,128]{1,0:T(8,128)S(1)} %constant_dynamic-slice_fusion.8), channel_id=1, source_target_pairs={{0,1},{1,0},{2,3},{3,2},{4,5},{5,4},{6,7},{7,6},{8,9},{9,8},{10,11... | collective-permute-start | bytes 1769480 | tf_op jit(solution)/shard_map/ppermute | solution.py:47
  96.0 8.3 %collective-permute-start.9 = (f32[576,128]{1,0:T(8,128)S(1)}, f32[576,128]{1,0:T(8,128)S(1)}, u32[]{:S(2)}, u32[]{:S(2)}) collective-permute-start(f32[576,128]{1,0:T(8,128)S(1)} %constant_dynamic-slice_fusion.7), channel_id=1, source_target_pairs={{0,64},{64,0},{128,192},{192,128},{1,65},{65,1},{129,193},{193,129... | collective-permute-start | bytes 884744 | tf_op jit(solution)/shard_map/ppermute | solution.py:47
  104.3 5.8 %collective-permute-start.10 = (f32[288,128]{1,0:T(8,128)S(1)}, f32[288,128]{1,0:T(8,128)S(1)}, u32[]{:S(2)}, u32[]{:S(2)}) collective-permute-start(f32[288,128]{1,0:T(8,128)S(1)} %constant_dynamic-slice_fusion.6), channel_id=1, source_target_pairs={{0,128},{64,192},{128,0},{192,64},{1,129},{65,193},{129,1},{193,65... | collective-permute-start | bytes 442376 | tf_op jit(solution)/shard_map/ppermute | solution.py:47
  110.2 4.7 %collective-permute-start.11 = (f32[144,128]{1,0:T(8,128)S(1)}, f32[144,128]{1,0:T(8,128)S(1)}, u32[]{:S(2)}, u32[]{:S(2)}) collective-permute-start(f32[144,128]{1,0:T(8,128)S(1)} %constant_dynamic-slice_fusion.5), channel_id=1, source_target_pairs={{0,4},{4,0},{8,12},{12,8},{16,20},{20,16},{24,28},{28,24},{32,36},... | collective-permute-start | bytes 221192 | tf_op jit(solution)/shard_map/ppermute | solution.py:47
  114.9 4.3 %collective-permute-start.12 = (f32[72,128]{1,0:T(8,128)S(1)}, f32[72,128]{1,0:T(8,128)S(1)}, u32[]{:S(2)}, u32[]{:S(2)}) collective-permute-start(f32[72,128]{1,0:T(8,128)S(1)} %constant_dynamic-slice_fusion.4), channel_id=1, source_target_pairs={{0,8},{4,12},{8,0},{12,4},{16,24},{20,28},{24,16},{28,20},{32,40},... | collective-permute-start | bytes 110600 | tf_op jit(solution)/shard_map/ppermute | solution.py:47
  119.2 6.7 %collective-permute-start.13 = (f32[36,128]{1,0:T(8,128)S(1)}, f32[36,128]{1,0:T(8,128)S(1)}, u32[]{:S(2)}, u32[]{:S(2)}) collective-permute-start(f32[36,128]{1,0:T(8,128)S(1)} %constant_dynamic-slice_fusion.3), channel_id=1, source_target_pairs={{0,16},{4,20},{8,24},{12,28},{16,0},{20,4},{24,8},{28,12},{32,48},... | collective-permute-start | bytes 55304 | tf_op jit(solution)/shard_map/ppermute | solution.py:47
  126.0 3.1 %collective-permute-start.14 = (f32[18,128]{1,0:T(8,128)S(1)}, f32[18,128]{1,0:T(8,128)S(1)}, u32[]{:S(2)}, u32[]{:S(2)}) collective-permute-start(f32[18,128]{1,0:T(8,128)S(1)} %constant_dynamic-slice_fusion.2), channel_id=1, source_target_pairs={{0,32},{4,36},{8,40},{12,44},{16,48},{20,52},{24,56},{28,60},{32,0... | collective-permute-start | bytes 27656 | tf_op jit(solution)/shard_map/ppermute | solution.py:47
  129.1 4.1 %collective-permute-start.15 = (f32[9,128]{1,0:T(8,128)S(1)}, f32[9,128]{1,0:T(8,128)S(1)}, u32[]{:S(2)}, u32[]{:S(2)}) collective-permute-start(f32[9,128]{1,0:T(8,128)S(1)} %constant_dynamic-slice_fusion), channel_id=1, source_target_pairs={{0,2},{1,3},{2,0},{3,1},{4,6},{5,7},{6,4},{7,5},{8,10},{9,11},{10,... | collective-permute-start | bytes 13832 | tf_op jit(solution)/shard_map/ppermute | solution.py:47
  133.2 4.1 %collective-permute-start.16 = (f32[9,128]{1,0:T(8,128)S(1)}, f32[9,128]{1,0:T(8,128)S(1)}, u32[]{:S(2)}, u32[]{:S(2)}) collective-permute-start(f32[9,128]{1,0:T(8,128)S(1)} %fusion.55), channel_id=1, source_target_pairs={{0,2},{1,3},{2,0},{3,1},{4,6},{5,7},{6,4},{7,5},{8,10},{9,11},{10,... | collective-permute-start | bytes 13832 | tf_op jit(solution)/shard_map/ppermute | solution.py:51
  137.3 2.9 %collective-permute-start.17 = (f32[18,128]{1,0:T(8,128)S(1)}, f32[18,128]{1,0:T(8,128)S(1)}, u32[]{:S(2)}, u32[]{:S(2)}) collective-permute-start(f32[18,128]{1,0:T(8,128)S(1)} %pad_maximum_fusion.19), channel_id=1, source_target_pairs={{0,32},{4,36},{8,40},{12,44},{16,48},{20,52},{24,56},{28,60},{32,0... | collective-permute-start | bytes 27656 | tf_op jit(solution)/shard_map/ppermute | solution.py:51
  140.3 6.6 %collective-permute-start.18 = (f32[36,128]{1,0:T(8,128)S(1)}, f32[36,128]{1,0:T(8,128)S(1)}, u32[]{:S(2)}, u32[]{:S(2)}) collective-permute-start(f32[36,128]{1,0:T(8,128)S(1)} %pad_maximum_fusion.15), channel_id=1, source_target_pairs={{0,16},{4,20},{8,24},{12,28},{16,0},{20,4},{24,8},{28,12},{32,48},... | collective-permute-start | bytes 55304 | tf_op jit(solution)/shard_map/ppermute | solution.py:51
  147.0 3.8 %collective-permute-start.19 = (f32[72,128]{1,0:T(8,128)S(1)}, f32[72,128]{1,0:T(8,128)S(1)}, u32[]{:S(2)}, u32[]{:S(2)}) collective-permute-start(f32[72,128]{1,0:T(8,128)S(1)} %pad_maximum_fusion.14), channel_id=1, source_target_pairs={{0,8},{4,12},{8,0},{12,4},{16,24},{20,28},{24,16},{28,20},{32,40},... | collective-permute-start | bytes 110600 | tf_op jit(solution)/shard_map/ppermute | solution.py:51
  150.8 3.3 %collective-permute-start.20 = (f32[144,128]{1,0:T(8,128)S(1)}, f32[144,128]{1,0:T(8,128)S(1)}, u32[]{:S(2)}, u32[]{:S(2)}) collective-permute-start(f32[144,128]{1,0:T(8,128)S(1)} %get-tuple-element.94), channel_id=1, source_target_pairs={{0,4},{4,0},{8,12},{12,8},{16,20},{20,16},{24,28},{28,24},{32,36},... | collective-permute-start | bytes 221192 | tf_op jit(solution)/shard_map/ppermute | solution.py:51
  154.1 5.6 %collective-permute-start.21 = (f32[288,128]{1,0:T(8,128)S(1)}, f32[288,128]{1,0:T(8,128)S(1)}, u32[]{:S(2)}, u32[]{:S(2)}) collective-permute-start(f32[288,128]{1,0:T(8,128)S(1)} %get-tuple-element.90), channel_id=1, source_target_pairs={{0,128},{64,192},{128,0},{192,64},{1,129},{65,193},{129,1},{193,65... | collective-permute-start | bytes 442376 | tf_op jit(solution)/shard_map/ppermute | solution.py:51
  159.8 5.7 %collective-permute-start.22 = (f32[576,128]{1,0:T(8,128)S(1)}, f32[576,128]{1,0:T(8,128)S(1)}, u32[]{:S(2)}, u32[]{:S(2)}) collective-permute-start(f32[576,128]{1,0:T(8,128)S(1)} %get-tuple-element.86), channel_id=1, source_target_pairs={{0,64},{64,0},{128,192},{192,128},{1,65},{65,1},{129,193},{193,129... | collective-permute-start | bytes 884744 | tf_op jit(solution)/shard_map/ppermute | solution.py:51
  165.7 17.3 %collective-permute-start.23 = (f32[1152,128]{1,0:T(8,128)S(1)}, f32[1152,128]{1,0:T(8,128)S(1)}, u32[]{:S(2)}, u32[]{:S(2)}) collective-permute-start(f32[1152,128]{1,0:T(8,128)S(1)} %get-tuple-element.70), channel_id=1, source_target_pairs={{0,1},{1,0},{2,3},{3,2},{4,5},{5,4},{6,7},{7,6},{8,9},{9,8},{10,11... | collective-permute-start | bytes 1769480 | tf_op jit(solution)/shard_map/ppermute | solution.py:51

commit v7 on v6

--- a/solution.py
+++ b/solution.py
@@ -118,7 +118,15 @@
     )
     w_one = w_first.reshape(9 * chans, chans)
     w_two = w_second.reshape(9 * chans, chans)
+    back = cotangent[0]
+    padded_back = with_halo(back, (("row", 0), ("col", 1)), 2)
+    w_turned = jnp.transpose(w_second[::-1, ::-1], (0, 1, 3, 2)).reshape(9 * chans, chans)
+    back_flat = back.reshape(rows * cols, chans)
+    grad_act1 = back_flat.astype(jnp.float32) + jnp.dot(
+        unfold(padded_back, 2, rows, cols), w_turned, preferred_element_type=jnp.float32
+    )
     deep = with_halo(first_in, (("row", 0), ("col", 1)), 3)
+    deep, grad_act1 = lax.optimization_barrier((deep, grad_act1))
     pre_wide = jnp.dot(
         unfold(deep, 1, rows + 4, cols + 4), w_one, preferred_element_type=jnp.float32
     ).reshape(rows + 4, cols + 4, chans)
@@ -132,13 +140,6 @@
     act1 = padded1[2:-2, 2:-2]
     patches0 = unfold(deep[2:-2, 2:-2], 1, rows, cols)
     patches1 = unfold(padded1, 2, rows, cols)
-    back = cotangent[0]
-    padded_back = with_halo(back, (("row", 0), ("col", 1)), 2)
-    w_turned = jnp.transpose(w_second[::-1, ::-1], (0, 1, 3, 2)).reshape(9 * chans, chans)
-    back_flat = back.reshape(rows * cols, chans)
-    grad_act1 = back_flat.astype(jnp.float32) + jnp.dot(
-        unfold(padded_back, 2, rows, cols), w_turned, preferred_element_type=jnp.float32
-    )
     sigmoid_pre = jax.nn.sigmoid(pre1)
     grad_pre1 = (grad_act1 * sigmoid_pre * (1.0 + pre1 * (1.0 - sigmoid_pre))).astype(jnp.bfloat16)
     grad_pre1 = lax.optimization_barrier(grad_pre1)

time: 185 us -> 182 us (0.984)
  waiting for transfers between devices: 53 us -> 47 us
  starting transfers between devices: 80.7 us -> 84 us
    ppermute x4, waiting for transfers between devices: 13.3 us -> 10.1 us  [with_halo(): after = lax.ppermute(leading, axis, down)]
  transfers between devices with their start and end apart: 25 -> 25, of which waited for: 21 -> 20; matrix products, arithmetic and copies ran while one was open for 8% -> 10% of each run, Pallas kernels for 0% -> 0%
where the time goes in v7:
time: 182 us; the launch traced here: 181 us
  starting transfers between devices  84 us (46%)
  waiting for transfers between devices  47 us (26%)
  matrix products  20.9 us (11%)
  local copies, waits for them, and re-layouts  16.1 us (9%)
  other arithmetic  11.9 us (7%)
    ppermute x8, starting transfers between devices, tree_sum(): got = lax.ppermute(x, axis, pairs)  30 us
    ppermute x8, starting transfers between devices, tree_sum(): x = kept + lax.ppermute(sent, axis, pairs)  23.4 us
    ppermute x8, waiting for transfers between devices, tree_sum(): got = lax.ppermute(x, axis, pairs)  19.5 us
    ppermute x8, waiting for transfers between devices, tree_sum(): x = kept + lax.ppermute(sent, axis, pairs)  16 us
    all_to_all x1, starting transfers between devices, on_device(): lax.all_to_all(payload, ('row', 'col'), split_axis=0, concat_axis=0, tile...  13.5 us
    unnamed x44, local copies, waits for them, and re-layouts  12.4 us
    ppermute x4, starting transfers between devices, with_halo(): before = lax.ppermute(last, axis, up)  11.8 us
    ppermute x4, waiting for transfers between devices, with_halo(): after = lax.ppermute(leading, axis, down)  10.1 us
  transfers between devices with their start and end apart: 25, of which 20 were waited for; matrix products, arithmetic and copies ran while one was open for 10% of the time, Pallas kernels for 0%

profile of v7, /device:TPU:1, one launch (start us, length us, event | category | flops | bytes accessed | tf_op | source)
XLA Modules:
  0.0 181.3 jit_solution(14780336114282309013)
XLA Ops:
  2.6 1.5 reduce-window.6
  4.6 1.3 broadcast_select_fusion
  5.9 1.4 broadcast_select_fusion.1
  8.2 2.7 %fusion.8 = f32[1280,128]{1,0:T(8,128)S(1)} fusion(bf16[512,128]{1,0:T(8,128)(2,1)} %param.18, s32[640]{0:T(1024)S(1)} %add_add_fusion, bf16[1,640,512]{2,1,0:T(8,128)(2,1)S(1)} %copy-done), kind=kOutput, calls=%fused_computation.16 | convolution fusion | flops 1008107520 | bytes 1444352 | tf_op jit(solution)/shard_map/dot_general | solution.py:93
  11.0 1.0 select_maximum_fusion
  12.0 13.5 %all-to-all-start = ((f32[64,21,128]{2,1,0:T(8,128)}), f32[64,21,128]{2,1,0:T(8,128)S(1)}, u32[]{:S(2)}, u32[]{:S(2)}) async-start(f32[64,21,128]{2,1,0:T(8,128)} %select_maximum_fusion), calls=%async_computation | async-start | bytes 1572864 | tf_op jit(solution)/shard_map/all_to_all | solution.py:101
  25.5 2.9 %collective-permute-start.4 = (bf16[2,64,128]{2,1,0:T(8,128)(2,1)S(1)}, bf16[2,64,128]{2,1,0:T(8,128)(2,1)S(1)}, u32[]{:S(2)}, u32[]{:S(2)}) collective-permute-start(bf16[2,64,128]{2,1,0:T(8,128)(2,1)S(1)} %get-tuple-element.74), channel_id=1, source_target_pairs={{0,64},{64,128},{128,192},{1,65},{65,129},{129,193},{2,66},{66,130... | collective-permute-start | bytes 98312 | tf_op jit(solution)/shard_map/ppermute | solution.py:16
  28.5 1.3 collective-permute-start.5
  30.2 3.7 %collective-permute-done.5 = bf16[2,64,128]{2,1,0:T(8,128)(2,1)S(1)} collective-permute-done((bf16[2,64,128]{2,1,0:T(8,128)(2,1)S(1)}, bf16[2,64,128]{2,1,0:T(8,128)(2,1)S(1)}, u32[]{:S(2)}, u32[]{:S(2)}) %collective-permute-start.5) | collective-permute-done | bytes 32800 | tf_op jit(solution)/shard_map/ppermute | solution.py:17
  33.9 2.7 %collective-permute-start.6 = (bf16[36,2,128]{2,1,0:T(2,128)(2,1)S(1)}, bf16[36,2,128]{2,1,0:T(2,128)(2,1)S(1)}, u32[]{:S(2)}, u32[]{:S(2)}) collective-permute-start(bf16[36,2,128]{2,1,0:T(2,128)(2,1)S(1)} %get-tuple-element.71), channel_id=1, source_target_pairs={{0,4},{4,8},{8,12},{12,16},{16,20},{20,24},{24,28},{28,32},{32,36}... | collective-permute-start | bytes 55304 | tf_op jit(solution)/shard_map/ppermute | solution.py:16
  36.6 1.3 collective-permute-start.7
  37.9 1.3 collective-permute-done.6
  39.2 3.9 %collective-permute-done.7 = bf16[36,2,128]{2,1,0:T(2,128)(2,1)S(1)} collective-permute-done((bf16[36,2,128]{2,1,0:T(2,128)(2,1)S(1)}, bf16[36,2,128]{2,1,0:T(2,128)(2,1)S(1)}, u32[]{:S(2)}, u32[]{:S(2)}) %collective-permute-start.7) | collective-permute-done | bytes 18464 | tf_op jit(solution)/shard_map/ppermute | solution.py:17
  44.0 0.9 constant_dynamic-update-slice_fusion.8
  44.9 0.9 constant_dynamic-update-slice_fusion.7
  48.4 0.9 constant_dynamic-update-slice_fusion.3
  49.3 0.9 constant_dynamic-update-slice_fusion.2
  50.2 0.9 constant_dynamic-update-slice_fusion.1
  51.2 1.1 reduce-precision_convert_fusion.1
  52.5 4.1 %fusion = f32[2048,384]{1,0:T(8,128)S(1)} fusion(f32[1280]{0:T(1024)S(1)} %eq.112, bf16[1280,128]{1,0:T(8,128)(2,1)} %get-tuple-element.60, bf16[1280,128]{1,0:T(8,128)(2,1)} %get-tuple-element.61, bf16[1280,128]{1,0:T(8,128)(2,1)} %get-tuple-element.59), kind=kOutput, calls=%fused_computation.1 | convolution fusion | flops 2018836480 | bytes 4133888 | tf_op jit(solution)/shard_map/dot_general | solution.py:112
  56.9 3.2 %collective-permute-start = (bf16[3,64,128]{2,1,0:T(8,128)(2,1)S(1)}, bf16[3,64,128]{2,1,0:T(8,128)(2,1)S(1)}, u32[]{:S(2)}, u32[]{:S(2)}) collective-permute-start(bf16[3,64,128]{2,1,0:T(8,128)(2,1)S(1)} %bitcast.183), channel_id=1, source_target_pairs={{0,64},{64,128},{128,192},{1,65},{65,129},{129,193},{2,66},{66,130... | collective-permute-start | bytes 147464 | tf_op jit(solution)/shard_map/ppermute | solution.py:16
  60.1 1.3 collective-permute-start.1
  61.4 0.9 constant_dynamic-update-slice_fusion
  62.3 2.6 %collective-permute-done.1 = bf16[3,64,128]{2,1,0:T(8,128)(2,1)S(1)} collective-permute-done((bf16[3,64,128]{2,1,0:T(8,128)(2,1)S(1)}, bf16[3,64,128]{2,1,0:T(8,128)(2,1)S(1)}, u32[]{:S(2)}, u32[]{:S(2)}) %collective-permute-start.1) | collective-permute-done | bytes 49184 | tf_op jit(solution)/shard_map/ppermute | solution.py:17
  64.9 3.0 %collective-permute-start.2 = (bf16[38,3,128]{2,1,0:T(4,128)(2,1)S(1)}, bf16[38,3,128]{2,1,0:T(4,128)(2,1)S(1)}, u32[]{:S(2)}, u32[]{:S(2)}) collective-permute-start(bf16[38,3,128]{2,1,0:T(4,128)(2,1)S(1)} %get-tuple-element.62), channel_id=1, source_target_pairs={{0,4},{4,8},{8,12},{12,16},{16,20},{20,24},{24,28},{28,32},{32,36}... | collective-permute-start | bytes 87560 | tf_op jit(solution)/shard_map/ppermute | solution.py:16
  68.0 1.5 collective-permute-start.3
  69.4 3.8 %convolution_add_fusion.1 = f32[2048,128]{1,0:T(8,128)S(1)} fusion(bf16[2048,1152]{1,0:T(8,128)(2,1)} %constant_dynamic-update-slice_fusion, bf16[1152,128]{1,0:T(8,128)(2,1)S(1)} %bitcast.171, bf16[2048,128]{1,0:T(8,128)(2,1)S(1)} %bitcast.155), kind=kOutput, calls=%fused_computation.8 | convolution fusion | flops 604504064 | bytes 6586368 | tf_op jit(solution)/shard_map/dot_general | solution.py:125
  76.0 2.2 %select_convert_fusion = (bf16[36,68,128]{2,1,0:T(8,128)(2,1)S(1)}, f32[36,68,128]{2,1,0:T(8,128)S(1)}) fusion(pred[36,68]{1,0:T(8,128)(4,1)S(1)} %broadcast_and_fusion, bf16[36,68,1152]{2,1,0:T(8,128)(2,1)S(1)} %slice_dynamic-update-slice_fusion, bf16[1152,128,1]{1,0,2:T(8,128)(2,1)S(1)} %bitcast.190), kind=kOutput, calls=%fused_computation.17 | convolution fusion | flops 723824640 | bytes 7817616 | tf_op jit(solution)/shard_map/dot_general | solution.py:130
  82.7 1.4 fusion.71
  84.1 1.4 fusion.70
  85.7 4.6 %collective-permute-start.8 = (f32[1152,128]{1,0:T(8,128)S(1)}, f32[1152,128]{1,0:T(8,128)S(1)}, u32[]{:S(2)}, u32[]{:S(2)}) collective-permute-start(f32[1152,128]{1,0:T(8,128)S(1)} %constant_dynamic-slice_fusion.8), channel_id=1, source_target_pairs={{0,1},{1,0},{2,3},{3,2},{4,5},{5,4},{6,7},{7,6},{8,9},{9,8},{10,11... | collective-permute-start | bytes 1769480 | tf_op jit(solution)/shard_map/ppermute | solution.py:47
  90.3 1.6 collective-permute-done.8
  92.1 1.4 collective-permute-start.9
  93.5 4.6 %fusion.5 = bf16[2048,128]{1,0:T(8,128)(2,1)} fusion(bf16[2048,1152]{1,0:T(8,128)(2,1)} %bitcast.159, bf16[1152,128]{1,0:T(8,128)(2,1)} %bitcast.176, bf16[2048,128]{1,0:T(8,128)(2,1)S(1)} %bitcast.175), kind=kOutput, calls=%fused_computation.9 | convolution fusion | flops 604766208 | bytes 6062080 | tf_op jit(solution)/shard_map/dot_general | solution.py:158
  98.0 2.3 %collective-permute-done.9 = f32[576,128]{1,0:T(8,128)S(1)} collective-permute-done((f32[576,128]{1,0:T(8,128)S(1)}, f32[576,128]{1,0:T(8,128)S(1)}, u32[]{:S(2)}, u32[]{:S(2)}) %collective-permute-start.9) | collective-permute-done | bytes 294944 | tf_op jit(solution)/shard_map/ppermute | solution.py:47
  100.4 1.7 collective-permute-start.10
  102.2 3.9 %collective-permute-done.10 = f32[288,128]{1,0:T(8,128)S(1)} collective-permute-done((f32[288,128]{1,0:T(8,128)S(1)}, f32[288,128]{1,0:T(8,128)S(1)}, u32[]{:S(2)}, u32[]{:S(2)}) %collective-permute-start.10) | collective-permute-done | bytes 147488 | tf_op jit(solution)/shard_map/ppermute | solution.py:47
  106.1 2.9 %collective-permute-start.11 = (f32[144,128]{1,0:T(8,128)S(1)}, f32[144,128]{1,0:T(8,128)S(1)}, u32[]{:S(2)}, u32[]{:S(2)}) collective-permute-start(f32[144,128]{1,0:T(8,128)S(1)} %constant_dynamic-slice_fusion.5), channel_id=1, source_target_pairs={{0,4},{4,0},{8,12},{12,8},{16,20},{20,16},{24,28},{28,24},{32,36},... | collective-permute-start | bytes 221192 | tf_op jit(solution)/shard_map/ppermute | solution.py:47
  109.0 1.7 collective-permute-done.11
  110.8 3.5 %collective-permute-start.12 = (f32[72,128]{1,0:T(8,128)S(1)}, f32[72,128]{1,0:T(8,128)S(1)}, u32[]{:S(2)}, u32[]{:S(2)}) collective-permute-start(f32[72,128]{1,0:T(8,128)S(1)} %constant_dynamic-slice_fusion.4), channel_id=1, source_target_pairs={{0,8},{4,12},{8,0},{12,4},{16,24},{20,28},{24,16},{28,20},{32,40},... | collective-permute-start | bytes 110600 | tf_op jit(solution)/shard_map/ppermute | solution.py:47
  114.3 1.3 collective-permute-done.12
  115.6 4.4 %collective-permute-start.13 = (f32[36,128]{1,0:T(8,128)S(1)}, f32[36,128]{1,0:T(8,128)S(1)}, u32[]{:S(2)}, u32[]{:S(2)}) collective-permute-start(f32[36,128]{1,0:T(8,128)S(1)} %constant_dynamic-slice_fusion.3), channel_id=1, source_target_pairs={{0,16},{4,20},{8,24},{12,28},{16,0},{20,4},{24,8},{28,12},{32,48},... | collective-permute-start | bytes 55304 | tf_op jit(solution)/shard_map/ppermute | solution.py:47
  120.0 2.3 %collective-permute-done.13 = f32[36,128]{1,0:T(8,128)S(1)} collective-permute-done((f32[36,128]{1,0:T(8,128)S(1)}, f32[36,128]{1,0:T(8,128)S(1)}, u32[]{:S(2)}, u32[]{:S(2)}) %collective-permute-start.13) | collective-permute-done | bytes 18464 | tf_op jit(solution)/shard_map/ppermute | solution.py:47
  122.4 2.2 %collective-permute-start.14 = (f32[18,128]{1,0:T(8,128)S(1)}, f32[18,128]{1,0:T(8,128)S(1)}, u32[]{:S(2)}, u32[]{:S(2)}) collective-permute-start(f32[18,128]{1,0:T(8,128)S(1)} %constant_dynamic-slice_fusion.2), channel_id=1, source_target_pairs={{0,32},{4,36},{8,40},{12,44},{16,48},{20,52},{24,56},{28,60},{32,0... | collective-permute-start | bytes 27656 | tf_op jit(solution)/shard_map/ppermute | solution.py:47
  124.6 1.4 collective-permute-done.14
  126.0 2.7 %collective-permute-start.15 = (f32[9,128]{1,0:T(8,128)S(1)}, f32[9,128]{1,0:T(8,128)S(1)}, u32[]{:S(2)}, u32[]{:S(2)}) collective-permute-start(f32[9,128]{1,0:T(8,128)S(1)} %constant_dynamic-slice_fusion), channel_id=1, source_target_pairs={{0,2},{1,3},{2,0},{3,1},{4,6},{5,7},{6,4},{7,5},{8,10},{9,11},{10,... | collective-permute-start | bytes 13832 | tf_op jit(solution)/shard_map/ppermute | solution.py:47
  128.7 1.4 collective-permute-done.15
  130.1 2.7 %collective-permute-start.16 = (f32[9,128]{1,0:T(8,128)S(1)}, f32[9,128]{1,0:T(8,128)S(1)}, u32[]{:S(2)}, u32[]{:S(2)}) collective-permute-start(f32[9,128]{1,0:T(8,128)S(1)} %fusion.54), channel_id=1, source_target_pairs={{0,2},{1,3},{2,0},{3,1},{4,6},{5,7},{6,4},{7,5},{8,10},{9,11},{10,... | collective-permute-start | bytes 13832 | tf_op jit(solution)/shard_map/ppermute | solution.py:51
  132.8 1.4 collective-permute-done.16
  134.2 1.3 collective-permute-start.17
  135.5 1.7 collective-permute-done.17
  137.2 3.6 %collective-permute-start.18 = (f32[36,128]{1,0:T(8,128)S(1)}, f32[36,128]{1,0:T(8,128)S(1)}, u32[]{:S(2)}, u32[]{:S(2)}) collective-permute-start(f32[36,128]{1,0:T(8,128)S(1)} %pad_maximum_fusion.12), channel_id=1, source_target_pairs={{0,16},{4,20},{8,24},{12,28},{16,0},{20,4},{24,8},{28,12},{32,48},... | collective-permute-start | bytes 55304 | tf_op jit(solution)/shard_map/ppermute | solution.py:51
  140.8 3.0 %collective-permute-done.18 = f32[36,128]{1,0:T(8,128)S(1)} collective-permute-done((f32[36,128]{1,0:T(8,128)S(1)}, f32[36,128]{1,0:T(8,128)S(1)}, u32[]{:S(2)}, u32[]{:S(2)}) %collective-permute-start.18) | collective-permute-done | bytes 18464 | tf_op jit(solution)/shard_map/ppermute | solution.py:51
  143.8 1.6 collective-permute-start.19
  145.5 2.1 %collective-permute-done.19 = f32[72,128]{1,0:T(8,128)S(1)} collective-permute-done((f32[72,128]{1,0:T(8,128)S(1)}, f32[72,128]{1,0:T(8,128)S(1)}, u32[]{:S(2)}, u32[]{:S(2)}) %collective-permute-start.19) | collective-permute-done | bytes 36896 | tf_op jit(solution)/shard_map/ppermute | solution.py:51
  147.7 1.0 collective-permute-start.20
  148.7 2.3 %collective-permute-done.20 = f32[144,128]{1,0:T(8,128)S(1)} collective-permute-done((f32[144,128]{1,0:T(8,128)S(1)}, f32[144,128]{1,0:T(8,128)S(1)}, u32[]{:S(2)}, u32[]{:S(2)}) %collective-permute-start.20) | collective-permute-done | bytes 73760 | tf_op jit(solution)/shard_map/ppermute | solution.py:51
  151.0 2.5 %collective-permute-start.21 = (f32[288,128]{1,0:T(8,128)S(1)}, f32[288,128]{1,0:T(8,128)S(1)}, u32[]{:S(2)}, u32[]{:S(2)}) collective-permute-start(f32[288,128]{1,0:T(8,128)S(1)} %get-tuple-element.82), channel_id=1, source_target_pairs={{0,128},{64,192},{128,0},{192,64},{1,129},{65,193},{129,1},{193,65... | collective-permute-start | bytes 442376 | tf_op jit(solution)/shard_map/ppermute | solution.py:51
  153.5 3.1 %collective-permute-done.21 = f32[288,128]{1,0:T(8,128)S(1)} collective-permute-done((f32[288,128]{1,0:T(8,128)S(1)}, f32[288,128]{1,0:T(8,128)S(1)}, u32[]{:S(2)}, u32[]{:S(2)}) %collective-permute-start.21) | collective-permute-done | bytes 147488 | tf_op jit(solution)/shard_map/ppermute | solution.py:51
  156.7 1.3 collective-permute-start.22
  158.1 4.3 %collective-permute-done.22 = f32[576,128]{1,0:T(8,128)S(1)} collective-permute-done((f32[576,128]{1,0:T(8,128)S(1)}, f32[576,128]{1,0:T(8,128)S(1)}, u32[]{:S(2)}, u32[]{:S(2)}) %collective-permute-start.22) | collective-permute-done | bytes 294944 | tf_op jit(solution)/shard_map/ppermute | solution.py:51
  162.6 15.9 %collective-permute-start.23 = (f32[1152,128]{1,0:T(8,128)S(1)}, f32[1152,128]{1,0:T(8,128)S(1)}, u32[]{:S(2)}, u32[]{:S(2)}) collective-permute-start(f32[1152,128]{1,0:T(8,128)S(1)} %get-tuple-element.64), channel_id=1, source_target_pairs={{0,1},{1,0},{2,3},{3,2},{4,5},{5,4},{6,7},{7,6},{8,9},{9,8},{10,11... | collective-permute-start | bytes 1769480 | tf_op jit(solution)/shard_map/ppermute | solution.py:51
  178.5 1.6 collective-permute-done.23
  180.1 1.2 fusion.25
  (114 shorter events, 15.8 us)
Async XLA Ops:
  0.6 7.6 %copy-start = (bf16[1,640,512]{2,1,0:T(8,128)(2,1)S(1)}, bf16[1,640,512]{2,1,0:T(8,128)(2,1)}, u32[]{:S(2)}) copy-start(bf16[1,640,512]{2,1,0:T(8,128)(2,1)} %param.15) | copy-start | bytes 1966084
  8.2 17.3 %copy-start.1 = (bf16[1,32,64,128]{3,2,1,0:T(8,128)(2,1)S(1)}, bf16[1,32,64,128]{3,2,1,0:T(8,128)(2,1)}, u32[]{:S(2)}) copy-start(bf16[1,32,64,128]{3,2,1,0:T(8,128)(2,1)} %param.21) | copy-start | bytes 1572868
  8.2 21.6 %copy-start.4 = (bf16[3,3,128,128]{3,2,1,0:T(8,128)(2,1)S(1)}, bf16[3,3,128,128]{3,2,1,0:T(8,128)(2,1)}, u32[]{:S(2)}) copy-start(bf16[3,3,128,128]{3,2,1,0:T(8,128)(2,1)} %param.20) | copy-start | bytes 884740
  12.0 39.1 %all-to-all-start = ((f32[64,21,128]{2,1,0:T(8,128)}), f32[64,21,128]{2,1,0:T(8,128)S(1)}, u32[]{:S(2)}, u32[]{:S(2)}) async-start(f32[64,21,128]{2,1,0:T(8,128)} %select_maximum_fusion), calls=%async_computation | async-start | bytes 1572864 | tf_op jit(solution)/shard_map/all_to_all | solution.py:101
  25.5 4.6 %collective-permute-start.4 = (bf16[2,64,128]{2,1,0:T(8,128)(2,1)S(1)}, bf16[2,64,128]{2,1,0:T(8,128)(2,1)S(1)}, u32[]{:S(2)}, u32[]{:S(2)}) collective-permute-start(bf16[2,64,128]{2,1,0:T(8,128)(2,1)S(1)} %get-tuple-element.74), channel_id=1, source_target_pairs={{0,64},{64,128},{128,192},{1,65},{65,129},{129,193},{2,66},{66,130... | collective-permute-start | bytes 98312 | tf_op jit(solution)/shard_map/ppermute | solution.py:16
  28.5 5.4 %collective-permute-start.5 = (bf16[2,64,128]{2,1,0:T(8,128)(2,1)S(1)}, bf16[2,64,128]{2,1,0:T(8,128)(2,1)S(1)}, u32[]{:S(2)}, u32[]{:S(2)}) collective-permute-start(bf16[2,64,128]{2,1,0:T(8,128)(2,1)S(1)} %get-tuple-element.75), channel_id=1, source_target_pairs={{64,0},{128,64},{192,128},{65,1},{129,65},{193,129},{66,2},{130,66... | collective-permute-start | bytes 98312 | tf_op jit(solution)/shard_map/ppermute | solution.py:17
  33.9 5.3 %collective-permute-start.6 = (bf16[36,2,128]{2,1,0:T(2,128)(2,1)S(1)}, bf16[36,2,128]{2,1,0:T(2,128)(2,1)S(1)}, u32[]{:S(2)}, u32[]{:S(2)}) collective-permute-start(bf16[36,2,128]{2,1,0:T(2,128)(2,1)S(1)} %get-tuple-element.71), channel_id=1, source_target_pairs={{0,4},{4,8},{8,12},{12,16},{16,20},{20,24},{24,28},{28,32},{32,36}... | collective-permute-start | bytes 55304 | tf_op jit(solution)/shard_map/ppermute | solution.py:16
  36.6 6.5 %collective-permute-start.7 = (bf16[36,2,128]{2,1,0:T(2,128)(2,1)S(1)}, bf16[36,2,128]{2,1,0:T(2,128)(2,1)S(1)}, u32[]{:S(2)}, u32[]{:S(2)}) collective-permute-start(bf16[36,2,128]{2,1,0:T(2,128)(2,1)S(1)} %get-tuple-element.70), channel_id=1, source_target_pairs={{4,0},{8,4},{12,8},{16,12},{20,16},{24,20},{28,24},{32,28},{36,32}... | collective-permute-start | bytes 55304 | tf_op jit(solution)/shard_map/ppermute | solution.py:17
  52.5 4.2 %copy-start.3 = (bf16[1,32,64,128]{3,2,1,0:T(8,128)(2,1)S(1)}, bf16[1,32,64,128]{3,2,1,0:T(8,128)(2,1)}, u32[]{:S(2)}) copy-start(bf16[1,32,64,128]{3,2,1,0:T(8,128)(2,1)} %param.14) | copy-start | bytes 1572868
  56.9 5.4 %collective-permute-start = (bf16[3,64,128]{2,1,0:T(8,128)(2,1)S(1)}, bf16[3,64,128]{2,1,0:T(8,128)(2,1)S(1)}, u32[]{:S(2)}, u32[]{:S(2)}) collective-permute-start(bf16[3,64,128]{2,1,0:T(8,128)(2,1)S(1)} %bitcast.183), channel_id=1, source_target_pairs={{0,64},{64,128},{128,192},{1,65},{65,129},{129,193},{2,66},{66,130... | collective-permute-start | bytes 147464 | tf_op jit(solution)/shard_map/ppermute | solution.py:16
  60.1 4.8 %collective-permute-start.1 = (bf16[3,64,128]{2,1,0:T(8,128)(2,1)S(1)}, bf16[3,64,128]{2,1,0:T(8,128)(2,1)S(1)}, u32[]{:S(2)}, u32[]{:S(2)}) collective-permute-start(bf16[3,64,128]{2,1,0:T(8,128)(2,1)S(1)} %bitcast.182), channel_id=1, source_target_pairs={{64,0},{128,64},{192,128},{65,1},{129,65},{193,129},{66,2},{130,66... | collective-permute-start | bytes 147464 | tf_op jit(solution)/shard_map/ppermute | solution.py:17
  64.9 8.3 %collective-permute-start.2 = (bf16[38,3,128]{2,1,0:T(4,128)(2,1)S(1)}, bf16[38,3,128]{2,1,0:T(4,128)(2,1)S(1)}, u32[]{:S(2)}, u32[]{:S(2)}) collective-permute-start(bf16[38,3,128]{2,1,0:T(4,128)(2,1)S(1)} %get-tuple-element.62), channel_id=1, source_target_pairs={{0,4},{4,8},{8,12},{12,16},{16,20},{20,24},{24,28},{28,32},{32,36}... | collective-permute-start | bytes 87560 | tf_op jit(solution)/shard_map/ppermute | solution.py:16
  68.0 5.3 %collective-permute-start.3 = (bf16[38,3,128]{2,1,0:T(4,128)(2,1)S(1)}, bf16[38,3,128]{2,1,0:T(4,128)(2,1)S(1)}, u32[]{:S(2)}, u32[]{:S(2)}) collective-permute-start(bf16[38,3,128]{2,1,0:T(4,128)(2,1)S(1)} %get-tuple-element.63), channel_id=1, source_target_pairs={{4,0},{8,4},{12,8},{16,12},{20,16},{24,20},{28,24},{32,28},{36,32}... | collective-permute-start | bytes 87560 | tf_op jit(solution)/shard_map/ppermute | solution.py:17
  74.2 1.9 %copy-start.5 = (bf16[3,3,128,128]{3,2,1,0:T(8,128)(2,1)S(1)}, bf16[3,3,128,128]{3,2,1,0:T(8,128)(2,1)}, u32[]{:S(2)}) copy-start(bf16[3,3,128,128]{3,2,1,0:T(8,128)(2,1)} %param.19) | copy-start | bytes 884740
  80.2 2.4 %copy-start.2 = (bf16[32,64,1152]{2,1,0:T(8,128)(2,1)}, bf16[32,64,1152]{2,1,0:T(8,128)(2,1)S(1)}, u32[]{:S(2)}) copy-start(bf16[32,64,1152]{2,1,0:T(8,128)(2,1)S(1)} %slice_dynamic-update-slice_fusion.9) | copy-start | bytes 14155780
  85.7 6.2 %collective-permute-start.8 = (f32[1152,128]{1,0:T(8,128)S(1)}, f32[1152,128]{1,0:T(8,128)S(1)}, u32[]{:S(2)}, u32[]{:S(2)}) collective-permute-start(f32[1152,128]{1,0:T(8,128)S(1)} %constant_dynamic-slice_fusion.8), channel_id=1, source_target_pairs={{0,1},{1,0},{2,3},{3,2},{4,5},{5,4},{6,7},{7,6},{8,9},{9,8},{10,11... | collective-permute-start | bytes 1769480 | tf_op jit(solution)/shard_map/ppermute | solution.py:47
  92.1 8.3 %collective-permute-start.9 = (f32[576,128]{1,0:T(8,128)S(1)}, f32[576,128]{1,0:T(8,128)S(1)}, u32[]{:S(2)}, u32[]{:S(2)}) collective-permute-start(f32[576,128]{1,0:T(8,128)S(1)} %constant_dynamic-slice_fusion.7), channel_id=1, source_target_pairs={{0,64},{64,0},{128,192},{192,128},{1,65},{65,1},{129,193},{193,129... | collective-permute-start | bytes 884744 | tf_op jit(solution)/shard_map/ppermute | solution.py:47
  100.4 5.6 %collective-permute-start.10 = (f32[288,128]{1,0:T(8,128)S(1)}, f32[288,128]{1,0:T(8,128)S(1)}, u32[]{:S(2)}, u32[]{:S(2)}) collective-permute-start(f32[288,128]{1,0:T(8,128)S(1)} %constant_dynamic-slice_fusion.6), channel_id=1, source_target_pairs={{0,128},{64,192},{128,0},{192,64},{1,129},{65,193},{129,1},{193,65... | collective-permute-start | bytes 442376 | tf_op jit(solution)/shard_map/ppermute | solution.py:47
  106.1 4.7 %collective-permute-start.11 = (f32[144,128]{1,0:T(8,128)S(1)}, f32[144,128]{1,0:T(8,128)S(1)}, u32[]{:S(2)}, u32[]{:S(2)}) collective-permute-start(f32[144,128]{1,0:T(8,128)S(1)} %constant_dynamic-slice_fusion.5), channel_id=1, source_target_pairs={{0,4},{4,0},{8,12},{12,8},{16,20},{20,16},{24,28},{28,24},{32,36},... | collective-permute-start | bytes 221192 | tf_op jit(solution)/shard_map/ppermute | solution.py:47
  110.8 4.9 %collective-permute-start.12 = (f32[72,128]{1,0:T(8,128)S(1)}, f32[72,128]{1,0:T(8,128)S(1)}, u32[]{:S(2)}, u32[]{:S(2)}) collective-permute-start(f32[72,128]{1,0:T(8,128)S(1)} %constant_dynamic-slice_fusion.4), channel_id=1, source_target_pairs={{0,8},{4,12},{8,0},{12,4},{16,24},{20,28},{24,16},{28,20},{32,40},... | collective-permute-start | bytes 110600 | tf_op jit(solution)/shard_map/ppermute | solution.py:47
  115.6 6.7 %collective-permute-start.13 = (f32[36,128]{1,0:T(8,128)S(1)}, f32[36,128]{1,0:T(8,128)S(1)}, u32[]{:S(2)}, u32[]{:S(2)}) collective-permute-start(f32[36,128]{1,0:T(8,128)S(1)} %constant_dynamic-slice_fusion.3), channel_id=1, source_target_pairs={{0,16},{4,20},{8,24},{12,28},{16,0},{20,4},{24,8},{28,12},{32,48},... | collective-permute-start | bytes 55304 | tf_op jit(solution)/shard_map/ppermute | solution.py:47
  122.4 3.6 %collective-permute-start.14 = (f32[18,128]{1,0:T(8,128)S(1)}, f32[18,128]{1,0:T(8,128)S(1)}, u32[]{:S(2)}, u32[]{:S(2)}) collective-permute-start(f32[18,128]{1,0:T(8,128)S(1)} %constant_dynamic-slice_fusion.2), channel_id=1, source_target_pairs={{0,32},{4,36},{8,40},{12,44},{16,48},{20,52},{24,56},{28,60},{32,0... | collective-permute-start | bytes 27656 | tf_op jit(solution)/shard_map/ppermute | solution.py:47
  126.0 4.1 %collective-permute-start.15 = (f32[9,128]{1,0:T(8,128)S(1)}, f32[9,128]{1,0:T(8,128)S(1)}, u32[]{:S(2)}, u32[]{:S(2)}) collective-permute-start(f32[9,128]{1,0:T(8,128)S(1)} %constant_dynamic-slice_fusion), channel_id=1, source_target_pairs={{0,2},{1,3},{2,0},{3,1},{4,6},{5,7},{6,4},{7,5},{8,10},{9,11},{10,... | collective-permute-start | bytes 13832 | tf_op jit(solution)/shard_map/ppermute | solution.py:47
  130.1 4.1 %collective-permute-start.16 = (f32[9,128]{1,0:T(8,128)S(1)}, f32[9,128]{1,0:T(8,128)S(1)}, u32[]{:S(2)}, u32[]{:S(2)}) collective-permute-start(f32[9,128]{1,0:T(8,128)S(1)} %fusion.54), channel_id=1, source_target_pairs={{0,2},{1,3},{2,0},{3,1},{4,6},{5,7},{6,4},{7,5},{8,10},{9,11},{10,... | collective-permute-start | bytes 13832 | tf_op jit(solution)/shard_map/ppermute | solution.py:51
  134.2 2.9 %collective-permute-start.17 = (f32[18,128]{1,0:T(8,128)S(1)}, f32[18,128]{1,0:T(8,128)S(1)}, u32[]{:S(2)}, u32[]{:S(2)}) collective-permute-start(f32[18,128]{1,0:T(8,128)S(1)} %pad_maximum_fusion.16), channel_id=1, source_target_pairs={{0,32},{4,36},{8,40},{12,44},{16,48},{20,52},{24,56},{28,60},{32,0... | collective-permute-start | bytes 27656 | tf_op jit(solution)/shard_map/ppermute | solution.py:51
  137.2 6.6 %collective-permute-start.18 = (f32[36,128]{1,0:T(8,128)S(1)}, f32[36,128]{1,0:T(8,128)S(1)}, u32[]{:S(2)}, u32[]{:S(2)}) collective-permute-start(f32[36,128]{1,0:T(8,128)S(1)} %pad_maximum_fusion.12), channel_id=1, source_target_pairs={{0,16},{4,20},{8,24},{12,28},{16,0},{20,4},{24,8},{28,12},{32,48},... | collective-permute-start | bytes 55304 | tf_op jit(solution)/shard_map/ppermute | solution.py:51
  143.8 3.8 %collective-permute-start.19 = (f32[72,128]{1,0:T(8,128)S(1)}, f32[72,128]{1,0:T(8,128)S(1)}, u32[]{:S(2)}, u32[]{:S(2)}) collective-permute-start(f32[72,128]{1,0:T(8,128)S(1)} %pad_maximum_fusion.11), channel_id=1, source_target_pairs={{0,8},{4,12},{8,0},{12,4},{16,24},{20,28},{24,16},{28,20},{32,40},... | collective-permute-start | bytes 110600 | tf_op jit(solution)/shard_map/ppermute | solution.py:51
  147.7 3.3 %collective-permute-start.20 = (f32[144,128]{1,0:T(8,128)S(1)}, f32[144,128]{1,0:T(8,128)S(1)}, u32[]{:S(2)}, u32[]{:S(2)}) collective-permute-start(f32[144,128]{1,0:T(8,128)S(1)} %get-tuple-element.86), channel_id=1, source_target_pairs={{0,4},{4,0},{8,12},{12,8},{16,20},{20,16},{24,28},{28,24},{32,36},... | collective-permute-start | bytes 221192 | tf_op jit(solution)/shard_map/ppermute | solution.py:51
  151.0 5.6 %collective-permute-start.21 = (f32[288,128]{1,0:T(8,128)S(1)}, f32[288,128]{1,0:T(8,128)S(1)}, u32[]{:S(2)}, u32[]{:S(2)}) collective-permute-start(f32[288,128]{1,0:T(8,128)S(1)} %get-tuple-element.82), channel_id=1, source_target_pairs={{0,128},{64,192},{128,0},{192,64},{1,129},{65,193},{129,1},{193,65... | collective-permute-start | bytes 442376 | tf_op jit(solution)/shard_map/ppermute | solution.py:51
  156.7 5.7 %collective-permute-start.22 = (f32[576,128]{1,0:T(8,128)S(1)}, f32[576,128]{1,0:T(8,128)S(1)}, u32[]{:S(2)}, u32[]{:S(2)}) collective-permute-start(f32[576,128]{1,0:T(8,128)S(1)} %get-tuple-element.78), channel_id=1, source_target_pairs={{0,64},{64,0},{128,192},{192,128},{1,65},{65,1},{129,193},{193,129... | collective-permute-start | bytes 884744 | tf_op jit(solution)/shard_map/ppermute | solution.py:51
  162.6 17.6 %collective-permute-start.23 = (f32[1152,128]{1,0:T(8,128)S(1)}, f32[1152,128]{1,0:T(8,128)S(1)}, u32[]{:S(2)}, u32[]{:S(2)}) collective-permute-start(f32[1152,128]{1,0:T(8,128)S(1)} %get-tuple-element.64), channel_id=1, source_target_pairs={{0,1},{1,0},{2,3},{3,2},{4,5},{5,4},{6,7},{7,6},{8,9},{9,8},{10,11... | collective-permute-start | bytes 1769480 | tf_op jit(solution)/shard_map/ppermute | solution.py:51

commit v8 on v7

--- a/solution.py
+++ b/solution.py
@@ -21,11 +21,10 @@
 
 def halving_steps():
     steps = [("batch", 1)]
-    for axis in ("row", "col"):
-        d = 1
-        while d < lax.axis_size(axis):
-            steps.append((axis, d))
-            d *= 2
+    d = 1
+    while d < lax.axis_size("row"):
+        steps.append(("row", d))
+        d *= 2
     d = 2
     while d < lax.axis_size("batch"):
         steps.append(("batch", d))
@@ -45,6 +44,11 @@
         kept = lax.dynamic_slice_in_dim(x, side * half, half)
         sent = lax.dynamic_slice_in_dim(x, (1 - side) * half, half)
         x = kept + lax.ppermute(sent, axis, pairs)
+    spread_over = lax.axis_size("col")
+    parts = x.reshape(spread_over, x.shape[0] // spread_over, x.shape[1])
+    x = lax.all_to_all(parts, "col", 0, 0, tiled=True).sum(0)
+    copies = jnp.broadcast_to(x[None], (spread_over,) + x.shape)
+    x = lax.all_to_all(copies, "col", 0, 0, tiled=True).reshape(-1, x.shape[1])
     for axis, d in steps[::-1]:
         pairs = [(i, i ^ d) for i in range(lax.axis_size(axis))]
         upper = (lax.axis_index(axis) // d) % 2 == 1

time: 182 us -> 168 us (0.923)
  starting transfers between devices: 84 us -> 55.1 us
  blocking collectives: 0 us -> 26.9 us
  waiting for transfers between devices: 47 us -> 35.9 us
    all_to_all x0 -> x2, blocking collectives: none -> 26.9 us  [the longest x1 16.4 us: tree_sum(): x = lax.all_to_all(parts, 'col', 0, 0, tiled=True).sum(0)]
    ppermute x8 -> x4, starting transfers between devices: 30 us -> 14 us  [tree_sum(): got = lax.ppermute(x, axis, pairs)]
    ppermute x8 -> x4, starting transfers between devices: 23.4 us -> 10.4 us  [tree_sum(): x = kept + lax.ppermute(sent, axis, pairs)]
    ppermute x8 -> x4, waiting for transfers between devices: 16 us -> 9.91 us  [tree_sum(): x = kept + lax.ppermute(sent, axis, pairs)]
    ppermute x8 -> x4, waiting for transfers between devices: 19.5 us -> 14.6 us  [tree_sum(): got = lax.ppermute(x, axis, pairs)]
  transfers between devices with their start and end apart: 25 -> 17, of which waited for: 20 -> 12; matrix products, arithmetic and copies ran while one was open for 10% -> 10% of each run, Pallas kernels for 0% -> 0%
where the time goes in v8:
time: 168 us
  starting transfers between devices  55.1 us (33%)
  waiting for transfers between devices  35.9 us (21%)
  blocking collectives  26.9 us (16%)
  matrix products  20.9 us (12%)
  local copies, waits for them, and re-layouts  15.9 us (9%)
  other arithmetic  11.8 us (7%)
    all_to_all x1, blocking collectives, tree_sum(): x = lax.all_to_all(parts, 'col', 0, 0, tiled=True).sum(0)  16.4 us
    ppermute x4, waiting for transfers between devices, tree_sum(): got = lax.ppermute(x, axis, pairs)  14.6 us
    ppermute x4, starting transfers between devices, tree_sum(): got = lax.ppermute(x, axis, pairs)  14 us
    all_to_all x1, starting transfers between devices, on_device(): lax.all_to_all(payload, ('row', 'col'), split_axis=0, concat_axis=0, tile...  13.5 us
    unnamed x44, local copies, waits for them, and re-layouts  12.4 us
    ppermute x4, starting transfers between devices, with_halo(): before = lax.ppermute(last, axis, up)  11.8 us
    all_to_all x1, blocking collectives, tree_sum(): x = lax.all_to_all(copies, 'col', 0, 0, tiled=True).reshape(-1, x.shape[1])  10.5 us
    ppermute x4, starting transfers between devices, tree_sum(): x = kept + lax.ppermute(sent, axis, pairs)  10.4 us
  transfers between devices with their start and end apart: 17, of which 12 were waited for; matrix products, arithmetic and copies ran while one was open for 10% of the time, Pallas kernels for 0%

profile of v8, /device:TPU:1, one launch (start us, length us, event | category | flops | bytes accessed | tf_op | source)
XLA Modules:
  0.0 167.9 jit_solution(5170517368218954736)
XLA Ops:
  0.6 0.6 compare_reduce_fusion
  1.3 0.6 compare_reduce_fusion.1
  1.9 0.7 reduce.16
  2.6 1.5 reduce-window.6
  4.6 1.3 broadcast_select_fusion
  5.9 1.4 broadcast_select_fusion.1
  7.4 0.7 fusion.2
  8.2 2.7 %fusion.8 = f32[1280,128]{1,0:T(8,128)S(1)} fusion(bf16[512,128]{1,0:T(8,128)(2,1)} %param.18, s32[640]{0:T(1024)S(1)} %add_add_fusion, bf16[1,640,512]{2,1,0:T(8,128)(2,1)S(1)} %copy-done), kind=kOutput, calls=%fused_computation.16 | convolution fusion | flops 1008107520 | bytes 1444352 | tf_op jit(solution)/shard_map/dot_general | solution.py:97
  11.0 1.0 select_maximum_fusion
  12.0 13.5 %all-to-all-start = ((f32[64,21,128]{2,1,0:T(8,128)}), f32[64,21,128]{2,1,0:T(8,128)S(1)}, u32[]{:S(2)}, u32[]{:S(2)}) async-start(f32[64,21,128]{2,1,0:T(8,128)} %select_maximum_fusion), calls=%async_computation | async-start | bytes 1572864 | tf_op jit(solution)/shard_map/all_to_all | solution.py:105
  25.5 2.9 %collective-permute-start.4 = (bf16[2,64,128]{2,1,0:T(8,128)(2,1)S(1)}, bf16[2,64,128]{2,1,0:T(8,128)(2,1)S(1)}, u32[]{:S(2)}, u32[]{:S(2)}) collective-permute-start(bf16[2,64,128]{2,1,0:T(8,128)(2,1)S(1)} %get-tuple-element.74), channel_id=1, source_target_pairs={{0,64},{64,128},{128,192},{1,65},{65,129},{129,193},{2,66},{66,130... | collective-permute-start | bytes 98312 | tf_op jit(solution)/shard_map/ppermute | solution.py:16
  28.5 1.3 collective-permute-start.5
  30.2 3.7 %collective-permute-done.5 = bf16[2,64,128]{2,1,0:T(8,128)(2,1)S(1)} collective-permute-done((bf16[2,64,128]{2,1,0:T(8,128)(2,1)S(1)}, bf16[2,64,128]{2,1,0:T(8,128)(2,1)S(1)}, u32[]{:S(2)}, u32[]{:S(2)}) %collective-permute-start.5) | collective-permute-done | bytes 32800 | tf_op jit(solution)/shard_map/ppermute | solution.py:17
  33.9 2.7 %collective-permute-start.6 = (bf16[36,2,128]{2,1,0:T(2,128)(2,1)S(1)}, bf16[36,2,128]{2,1,0:T(2,128)(2,1)S(1)}, u32[]{:S(2)}, u32[]{:S(2)}) collective-permute-start(bf16[36,2,128]{2,1,0:T(2,128)(2,1)S(1)} %get-tuple-element.71), channel_id=1, source_target_pairs={{0,4},{4,8},{8,12},{12,16},{16,20},{20,24},{24,28},{28,32},{32,36}... | collective-permute-start | bytes 55304 | tf_op jit(solution)/shard_map/ppermute | solution.py:16
  36.6 1.3 collective-permute-start.7
  37.9 1.3 collective-permute-done.6
  39.2 3.9 %collective-permute-done.7 = bf16[36,2,128]{2,1,0:T(2,128)(2,1)S(1)} collective-permute-done((bf16[36,2,128]{2,1,0:T(2,128)(2,1)S(1)}, bf16[36,2,128]{2,1,0:T(2,128)(2,1)S(1)}, u32[]{:S(2)}, u32[]{:S(2)}) %collective-permute-start.7) | collective-permute-done | bytes 18464 | tf_op jit(solution)/shard_map/ppermute | solution.py:17
  43.1 0.4 pad_maximum_fusion.1
  43.4 0.6 fusion.49
  44.0 0.9 constant_dynamic-update-slice_fusion.8
  44.9 0.9 constant_dynamic-update-slice_fusion.7
  45.8 0.9 constant_dynamic-update-slice_fusion.6
  46.7 0.9 constant_dynamic-update-slice_fusion.5
  47.5 0.9 constant_dynamic-update-slice_fusion.4
  48.4 0.9 constant_dynamic-update-slice_fusion.3
  49.3 0.9 constant_dynamic-update-slice_fusion.2
  50.1 0.9 constant_dynamic-update-slice_fusion.1
  51.1 1.1 reduce-precision_convert_fusion.1
  52.4 4.1 %fusion = f32[2048,384]{1,0:T(8,128)S(1)} fusion(f32[1280]{0:T(1024)S(1)} %eq.88, bf16[1280,128]{1,0:T(8,128)(2,1)} %get-tuple-element.60, bf16[1280,128]{1,0:T(8,128)(2,1)} %get-tuple-element.61, bf16[1280,128]{1,0:T(8,128)(2,1)} %get-tuple-element.59), kind=kOutput, calls=%fused_computation.1 | convolution fusion | flops 2018836480 | bytes 4133888 | tf_op jit(solution)/shard_map/dot_general | solution.py:116
  56.8 3.2 %collective-permute-start = (bf16[3,64,128]{2,1,0:T(8,128)(2,1)S(1)}, bf16[3,64,128]{2,1,0:T(8,128)(2,1)S(1)}, u32[]{:S(2)}, u32[]{:S(2)}) collective-permute-start(bf16[3,64,128]{2,1,0:T(8,128)(2,1)S(1)} %bitcast.154), channel_id=1, source_target_pairs={{0,64},{64,128},{128,192},{1,65},{65,129},{129,193},{2,66},{66,130... | collective-permute-start | bytes 147464 | tf_op jit(solution)/shard_map/ppermute | solution.py:16
  60.0 1.3 collective-permute-start.1
  61.3 0.9 constant_dynamic-update-slice_fusion
  62.2 2.6 %collective-permute-done.1 = bf16[3,64,128]{2,1,0:T(8,128)(2,1)S(1)} collective-permute-done((bf16[3,64,128]{2,1,0:T(8,128)(2,1)S(1)}, bf16[3,64,128]{2,1,0:T(8,128)(2,1)S(1)}, u32[]{:S(2)}, u32[]{:S(2)}) %collective-permute-start.1) | collective-permute-done | bytes 49184 | tf_op jit(solution)/shard_map/ppermute | solution.py:17
  64.8 3.0 %collective-permute-start.2 = (bf16[38,3,128]{2,1,0:T(4,128)(2,1)S(1)}, bf16[38,3,128]{2,1,0:T(4,128)(2,1)S(1)}, u32[]{:S(2)}, u32[]{:S(2)}) collective-permute-start(bf16[38,3,128]{2,1,0:T(4,128)(2,1)S(1)} %get-tuple-element.62), channel_id=1, source_target_pairs={{0,4},{4,8},{8,12},{12,16},{16,20},{20,24},{24,28},{28,32},{32,36}... | collective-permute-start | bytes 87560 | tf_op jit(solution)/shard_map/ppermute | solution.py:16
  67.9 1.5 collective-permute-start.3
  69.4 3.8 %convolution_add_fusion.1 = f32[2048,128]{1,0:T(8,128)S(1)} fusion(bf16[2048,1152]{1,0:T(8,128)(2,1)} %constant_dynamic-update-slice_fusion, bf16[1152,128]{1,0:T(8,128)(2,1)S(1)} %bitcast.142, bf16[2048,128]{1,0:T(8,128)(2,1)S(1)} %bitcast.126), kind=kOutput, calls=%fused_computation.8 | convolution fusion | flops 604504064 | bytes 6586368 | tf_op jit(solution)/shard_map/dot_general | solution.py:129
  73.1 0.3 pad_maximum_fusion
  73.8 0.3 slice_dynamic-update-slice_fusion.7
  74.1 0.3 slice_dynamic-update-slice_fusion.6
  76.0 2.2 %select_convert_fusion = (bf16[36,68,128]{2,1,0:T(8,128)(2,1)S(1)}, f32[36,68,128]{2,1,0:T(8,128)S(1)}) fusion(pred[36,68]{1,0:T(8,128)(4,1)S(1)} %broadcast_and_fusion, bf16[36,68,1152]{2,1,0:T(8,128)(2,1)S(1)} %slice_dynamic-update-slice_fusion, bf16[1152,128,1]{1,0,2:T(8,128)(2,1)S(1)} %bitcast.156), kind=kOutput, calls=%fused_computation.17 | convolution fusion | flops 723824640 | bytes 7817616 | tf_op jit(solution)/shard_map/dot_general | solution.py:134
  78.9 0.3 fusion.48
  82.2 0.4 fusion.16
  82.6 1.4 fusion.53
  84.0 1.4 fusion.52
  85.6 4.6 %collective-permute-start.8 = (f32[1152,128]{1,0:T(8,128)S(1)}, f32[1152,128]{1,0:T(8,128)S(1)}, u32[]{:S(2)}, u32[]{:S(2)}) collective-permute-start(f32[1152,128]{1,0:T(8,128)S(1)} %constant_dynamic-slice_fusion.3), channel_id=1, source_target_pairs={{0,1},{1,0},{2,3},{3,2},{4,5},{5,4},{6,7},{7,6},{8,9},{9,8},{10,11... | collective-permute-start | bytes 1769480 | tf_op jit(solution)/shard_map/ppermute | solution.py:46
  90.3 1.6 collective-permute-done.8
  92.0 1.4 collective-permute-start.9
  93.4 4.6 %fusion.5 = bf16[2048,128]{1,0:T(8,128)(2,1)} fusion(bf16[2048,1152]{1,0:T(8,128)(2,1)} %bitcast.130, bf16[1152,128]{1,0:T(8,128)(2,1)} %bitcast.147, bf16[2048,128]{1,0:T(8,128)(2,1)S(1)} %bitcast.146), kind=kOutput, calls=%fused_computation.9 | convolution fusion | flops 604766208 | bytes 6062080 | tf_op jit(solution)/shard_map/dot_general | solution.py:162
  97.9 2.3 %collective-permute-done.9 = f32[576,128]{1,0:T(8,128)S(1)} collective-permute-done((f32[576,128]{1,0:T(8,128)S(1)}, f32[576,128]{1,0:T(8,128)S(1)}, u32[]{:S(2)}, u32[]{:S(2)}) %collective-permute-start.9) | collective-permute-done | bytes 294944 | tf_op jit(solution)/shard_map/ppermute | solution.py:46
  100.3 1.7 %collective-permute-start.10 = (f32[288,128]{1,0:T(8,128)S(1)}, f32[288,128]{1,0:T(8,128)S(1)}, u32[]{:S(2)}, u32[]{:S(2)}) collective-permute-start(f32[288,128]{1,0:T(8,128)S(1)} %constant_dynamic-slice_fusion.1), channel_id=1, source_target_pairs={{0,128},{64,192},{128,0},{192,64},{1,129},{65,193},{129,1},{193,65... | collective-permute-start | bytes 442376 | tf_op jit(solution)/shard_map/ppermute | solution.py:46
  102.1 3.8 %collective-permute-done.10 = f32[288,128]{1,0:T(8,128)S(1)} collective-permute-done((f32[288,128]{1,0:T(8,128)S(1)}, f32[288,128]{1,0:T(8,128)S(1)}, u32[]{:S(2)}, u32[]{:S(2)}) %collective-permute-start.10) | collective-permute-done | bytes 147488 | tf_op jit(solution)/shard_map/ppermute | solution.py:46
  106.0 2.7 %collective-permute-start.11 = (f32[144,128]{1,0:T(8,128)S(1)}, f32[144,128]{1,0:T(8,128)S(1)}, u32[]{:S(2)}, u32[]{:S(2)}) collective-permute-start(f32[144,128]{1,0:T(8,128)S(1)} %constant_dynamic-slice_fusion), channel_id=1, source_target_pairs={{0,2},{1,3},{2,0},{3,1},{4,6},{5,7},{6,4},{7,5},{8,10},{9,11},{10,... | collective-permute-start | bytes 221192 | tf_op jit(solution)/shard_map/ppermute | solution.py:46
  108.7 2.1 %collective-permute-done.11 = f32[144,128]{1,0:T(8,128)S(1)} collective-permute-done((f32[144,128]{1,0:T(8,128)S(1)}, f32[144,128]{1,0:T(8,128)S(1)}, u32[]{:S(2)}, u32[]{:S(2)}) %collective-permute-start.11) | collective-permute-done | bytes 73760 | tf_op jit(solution)/shard_map/ppermute | solution.py:46
  110.8 16.4 %all_to_all.15 = f32[16,9,128]{2,1,0:T(8,128)S(1)} all-to-all(f32[16,9,128]{2,1,0:T(8,128)S(1)} %reshape.337), channel_id=1, replica_groups=mesh['row'=4,'col'=16,'batch'=4] {'col'}, dimensions={0} | all-to-all | bytes 147456 | tf_op jit(solution)/shard_map/all_to_all | solution.py:49
  127.2 10.5 %all_to_all.16 = f32[16,9,128]{2,1,0:T(8,128)S(1)} all-to-all(f32[16,9,128]{2,1,0:T(8,128)S(1)} %broadcast_in_dim.12), channel_id=1, replica_groups=mesh['row'=4,'col'=16,'batch'=4] {'col'}, dimensions={0} | all-to-all | bytes 147456 | tf_op jit(solution)/shard_map/all_to_all | solution.py:51
  137.7 2.7 %collective-permute-start.12 = (f32[144,128]{1,0:T(8,128)S(1)}, f32[144,128]{1,0:T(8,128)S(1)}, u32[]{:S(2)}, u32[]{:S(2)}) collective-permute-start(f32[144,128]{1,0:T(8,128)S(1)} %reshape.338), channel_id=1, source_target_pairs={{0,2},{1,3},{2,0},{3,1},{4,6},{5,7},{6,4},{7,5},{8,10},{9,11},{10,... | collective-permute-start | bytes 221192 | tf_op jit(solution)/shard_map/ppermute | solution.py:55
  140.5 2.4 %collective-permute-done.12 = f32[144,128]{1,0:T(8,128)S(1)} collective-permute-done((f32[144,128]{1,0:T(8,128)S(1)}, f32[144,128]{1,0:T(8,128)S(1)}, u32[]{:S(2)}, u32[]{:S(2)}) %collective-permute-start.12) | collective-permute-done | bytes 73760 | tf_op jit(solution)/shard_map/ppermute | solution.py:55
  143.0 1.8 %collective-permute-start.13 = (f32[288,128]{1,0:T(8,128)S(1)}, f32[288,128]{1,0:T(8,128)S(1)}, u32[]{:S(2)}, u32[]{:S(2)}) collective-permute-start(f32[288,128]{1,0:T(8,128)S(1)} %get-tuple-element.82), channel_id=1, source_target_pairs={{0,128},{64,192},{128,0},{192,64},{1,129},{65,193},{129,1},{193,65... | collective-permute-start | bytes 442376 | tf_op jit(solution)/shard_map/ppermute | solution.py:55
  144.8 4.1 %collective-permute-done.13 = f32[288,128]{1,0:T(8,128)S(1)} collective-permute-done((f32[288,128]{1,0:T(8,128)S(1)}, f32[288,128]{1,0:T(8,128)S(1)}, u32[]{:S(2)}, u32[]{:S(2)}) %collective-permute-start.13) | collective-permute-done | bytes 147488 | tf_op jit(solution)/shard_map/ppermute | solution.py:55
  149.0 1.1 collective-permute-start.14
  150.1 6.4 %collective-permute-done.14 = f32[576,128]{1,0:T(8,128)S(1)} collective-permute-done((f32[576,128]{1,0:T(8,128)S(1)}, f32[576,128]{1,0:T(8,128)S(1)}, u32[]{:S(2)}, u32[]{:S(2)}) %collective-permute-start.14) | collective-permute-done | bytes 294944 | tf_op jit(solution)/shard_map/ppermute | solution.py:55
  156.7 8.4 %collective-permute-start.15 = (f32[1152,128]{1,0:T(8,128)S(1)}, f32[1152,128]{1,0:T(8,128)S(1)}, u32[]{:S(2)}, u32[]{:S(2)}) collective-permute-start(f32[1152,128]{1,0:T(8,128)S(1)} %get-tuple-element.64), channel_id=1, source_target_pairs={{0,1},{1,0},{2,3},{3,2},{4,5},{5,4},{6,7},{7,6},{8,9},{9,8},{10,11... | collective-permute-start | bytes 1769480 | tf_op jit(solution)/shard_map/ppermute | solution.py:55
  165.1 1.6 collective-permute-done.15
  166.7 1.2 fusion.25
  (86 shorter events, 7.8 us)
Async XLA Ops:
  0.6 7.6 %copy-start = (bf16[1,640,512]{2,1,0:T(8,128)(2,1)S(1)}, bf16[1,640,512]{2,1,0:T(8,128)(2,1)}, u32[]{:S(2)}) copy-start(bf16[1,640,512]{2,1,0:T(8,128)(2,1)} %param.15) | copy-start | bytes 1966084
  8.2 17.3 %copy-start.1 = (bf16[1,32,64,128]{3,2,1,0:T(8,128)(2,1)S(1)}, bf16[1,32,64,128]{3,2,1,0:T(8,128)(2,1)}, u32[]{:S(2)}) copy-start(bf16[1,32,64,128]{3,2,1,0:T(8,128)(2,1)} %param.21) | copy-start | bytes 1572868
  8.2 21.6 %copy-start.4 = (bf16[3,3,128,128]{3,2,1,0:T(8,128)(2,1)S(1)}, bf16[3,3,128,128]{3,2,1,0:T(8,128)(2,1)}, u32[]{:S(2)}) copy-start(bf16[3,3,128,128]{3,2,1,0:T(8,128)(2,1)} %param.20) | copy-start | bytes 884740
  12.0 39.0 %all-to-all-start = ((f32[64,21,128]{2,1,0:T(8,128)}), f32[64,21,128]{2,1,0:T(8,128)S(1)}, u32[]{:S(2)}, u32[]{:S(2)}) async-start(f32[64,21,128]{2,1,0:T(8,128)} %select_maximum_fusion), calls=%async_computation | async-start | bytes 1572864 | tf_op jit(solution)/shard_map/all_to_all | solution.py:105
  25.5 4.6 %collective-permute-start.4 = (bf16[2,64,128]{2,1,0:T(8,128)(2,1)S(1)}, bf16[2,64,128]{2,1,0:T(8,128)(2,1)S(1)}, u32[]{:S(2)}, u32[]{:S(2)}) collective-permute-start(bf16[2,64,128]{2,1,0:T(8,128)(2,1)S(1)} %get-tuple-element.74), channel_id=1, source_target_pairs={{0,64},{64,128},{128,192},{1,65},{65,129},{129,193},{2,66},{66,130... | collective-permute-start | bytes 98312 | tf_op jit(solution)/shard_map/ppermute | solution.py:16
  28.5 5.4 %collective-permute-start.5 = (bf16[2,64,128]{2,1,0:T(8,128)(2,1)S(1)}, bf16[2,64,128]{2,1,0:T(8,128)(2,1)S(1)}, u32[]{:S(2)}, u32[]{:S(2)}) collective-permute-start(bf16[2,64,128]{2,1,0:T(8,128)(2,1)S(1)} %get-tuple-element.75), channel_id=1, source_target_pairs={{64,0},{128,64},{192,128},{65,1},{129,65},{193,129},{66,2},{130,66... | collective-permute-start | bytes 98312 | tf_op jit(solution)/shard_map/ppermute | solution.py:17
  33.9 5.3 %collective-permute-start.6 = (bf16[36,2,128]{2,1,0:T(2,128)(2,1)S(1)}, bf16[36,2,128]{2,1,0:T(2,128)(2,1)S(1)}, u32[]{:S(2)}, u32[]{:S(2)}) collective-permute-start(bf16[36,2,128]{2,1,0:T(2,128)(2,1)S(1)} %get-tuple-element.71), channel_id=1, source_target_pairs={{0,4},{4,8},{8,12},{12,16},{16,20},{20,24},{24,28},{28,32},{32,36}... | collective-permute-start | bytes 55304 | tf_op jit(solution)/shard_map/ppermute | solution.py:16
  36.6 6.5 %collective-permute-start.7 = (bf16[36,2,128]{2,1,0:T(2,128)(2,1)S(1)}, bf16[36,2,128]{2,1,0:T(2,128)(2,1)S(1)}, u32[]{:S(2)}, u32[]{:S(2)}) collective-permute-start(bf16[36,2,128]{2,1,0:T(2,128)(2,1)S(1)} %get-tuple-element.70), channel_id=1, source_target_pairs={{4,0},{8,4},{12,8},{16,12},{20,16},{24,20},{28,24},{32,28},{36,32}... | collective-permute-start | bytes 55304 | tf_op jit(solution)/shard_map/ppermute | solution.py:17
  52.4 4.1 %copy-start.3 = (bf16[1,32,64,128]{3,2,1,0:T(8,128)(2,1)S(1)}, bf16[1,32,64,128]{3,2,1,0:T(8,128)(2,1)}, u32[]{:S(2)}) copy-start(bf16[1,32,64,128]{3,2,1,0:T(8,128)(2,1)} %param.14) | copy-start | bytes 1572868
  56.8 5.4 %collective-permute-start = (bf16[3,64,128]{2,1,0:T(8,128)(2,1)S(1)}, bf16[3,64,128]{2,1,0:T(8,128)(2,1)S(1)}, u32[]{:S(2)}, u32[]{:S(2)}) collective-permute-start(bf16[3,64,128]{2,1,0:T(8,128)(2,1)S(1)} %bitcast.154), channel_id=1, source_target_pairs={{0,64},{64,128},{128,192},{1,65},{65,129},{129,193},{2,66},{66,130... | collective-permute-start | bytes 147464 | tf_op jit(solution)/shard_map/ppermute | solution.py:16
  60.0 4.8 %collective-permute-start.1 = (bf16[3,64,128]{2,1,0:T(8,128)(2,1)S(1)}, bf16[3,64,128]{2,1,0:T(8,128)(2,1)S(1)}, u32[]{:S(2)}, u32[]{:S(2)}) collective-permute-start(bf16[3,64,128]{2,1,0:T(8,128)(2,1)S(1)} %bitcast.153), channel_id=1, source_target_pairs={{64,0},{128,64},{192,128},{65,1},{129,65},{193,129},{66,2},{130,66... | collective-permute-start | bytes 147464 | tf_op jit(solution)/shard_map/ppermute | solution.py:17
  64.8 8.3 %collective-permute-start.2 = (bf16[38,3,128]{2,1,0:T(4,128)(2,1)S(1)}, bf16[38,3,128]{2,1,0:T(4,128)(2,1)S(1)}, u32[]{:S(2)}, u32[]{:S(2)}) collective-permute-start(bf16[38,3,128]{2,1,0:T(4,128)(2,1)S(1)} %get-tuple-element.62), channel_id=1, source_target_pairs={{0,4},{4,8},{8,12},{12,16},{16,20},{20,24},{24,28},{28,32},{32,36}... | collective-permute-start | bytes 87560 | tf_op jit(solution)/shard_map/ppermute | solution.py:16
  67.9 5.3 %collective-permute-start.3 = (bf16[38,3,128]{2,1,0:T(4,128)(2,1)S(1)}, bf16[38,3,128]{2,1,0:T(4,128)(2,1)S(1)}, u32[]{:S(2)}, u32[]{:S(2)}) collective-permute-start(bf16[38,3,128]{2,1,0:T(4,128)(2,1)S(1)} %get-tuple-element.63), channel_id=1, source_target_pairs={{4,0},{8,4},{12,8},{16,12},{20,16},{24,20},{28,24},{32,28},{36,32}... | collective-permute-start | bytes 87560 | tf_op jit(solution)/shard_map/ppermute | solution.py:17
  74.1 1.9 %copy-start.5 = (bf16[3,3,128,128]{3,2,1,0:T(8,128)(2,1)S(1)}, bf16[3,3,128,128]{3,2,1,0:T(8,128)(2,1)}, u32[]{:S(2)}) copy-start(bf16[3,3,128,128]{3,2,1,0:T(8,128)(2,1)} %param.19) | copy-start | bytes 884740
  80.1 2.4 %copy-start.2 = (bf16[32,64,1152]{2,1,0:T(8,128)(2,1)}, bf16[32,64,1152]{2,1,0:T(8,128)(2,1)S(1)}, u32[]{:S(2)}) copy-start(bf16[32,64,1152]{2,1,0:T(8,128)(2,1)S(1)} %slice_dynamic-update-slice_fusion.9) | copy-start | bytes 14155780
  85.6 6.2 %collective-permute-start.8 = (f32[1152,128]{1,0:T(8,128)S(1)}, f32[1152,128]{1,0:T(8,128)S(1)}, u32[]{:S(2)}, u32[]{:S(2)}) collective-permute-start(f32[1152,128]{1,0:T(8,128)S(1)} %constant_dynamic-slice_fusion.3), channel_id=1, source_target_pairs={{0,1},{1,0},{2,3},{3,2},{4,5},{5,4},{6,7},{7,6},{8,9},{9,8},{10,11... | collective-permute-start | bytes 1769480 | tf_op jit(solution)/shard_map/ppermute | solution.py:46
  92.0 8.3 %collective-permute-start.9 = (f32[576,128]{1,0:T(8,128)S(1)}, f32[576,128]{1,0:T(8,128)S(1)}, u32[]{:S(2)}, u32[]{:S(2)}) collective-permute-start(f32[576,128]{1,0:T(8,128)S(1)} %constant_dynamic-slice_fusion.2), channel_id=1, source_target_pairs={{0,64},{64,0},{128,192},{192,128},{1,65},{65,1},{129,193},{193,129... | collective-permute-start | bytes 884744 | tf_op jit(solution)/shard_map/ppermute | solution.py:46
  100.3 5.6 %collective-permute-start.10 = (f32[288,128]{1,0:T(8,128)S(1)}, f32[288,128]{1,0:T(8,128)S(1)}, u32[]{:S(2)}, u32[]{:S(2)}) collective-permute-start(f32[288,128]{1,0:T(8,128)S(1)} %constant_dynamic-slice_fusion.1), channel_id=1, source_target_pairs={{0,128},{64,192},{128,0},{192,64},{1,129},{65,193},{129,1},{193,65... | collective-permute-start | bytes 442376 | tf_op jit(solution)/shard_map/ppermute | solution.py:46
  106.0 4.8 %collective-permute-start.11 = (f32[144,128]{1,0:T(8,128)S(1)}, f32[144,128]{1,0:T(8,128)S(1)}, u32[]{:S(2)}, u32[]{:S(2)}) collective-permute-start(f32[144,128]{1,0:T(8,128)S(1)} %constant_dynamic-slice_fusion), channel_id=1, source_target_pairs={{0,2},{1,3},{2,0},{3,1},{4,6},{5,7},{6,4},{7,5},{8,10},{9,11},{10,... | collective-permute-start | bytes 221192 | tf_op jit(solution)/shard_map/ppermute | solution.py:46
  137.7 5.2 %collective-permute-start.12 = (f32[144,128]{1,0:T(8,128)S(1)}, f32[144,128]{1,0:T(8,128)S(1)}, u32[]{:S(2)}, u32[]{:S(2)}) collective-permute-start(f32[144,128]{1,0:T(8,128)S(1)} %reshape.338), channel_id=1, source_target_pairs={{0,2},{1,3},{2,0},{3,1},{4,6},{5,7},{6,4},{7,5},{8,10},{9,11},{10,... | collective-permute-start | bytes 221192 | tf_op jit(solution)/shard_map/ppermute | solution.py:55
  143.0 5.9 %collective-permute-start.13 = (f32[288,128]{1,0:T(8,128)S(1)}, f32[288,128]{1,0:T(8,128)S(1)}, u32[]{:S(2)}, u32[]{:S(2)}) collective-permute-start(f32[288,128]{1,0:T(8,128)S(1)} %get-tuple-element.82), channel_id=1, source_target_pairs={{0,128},{64,192},{128,0},{192,64},{1,129},{65,193},{129,1},{193,65... | collective-permute-start | bytes 442376 | tf_op jit(solution)/shard_map/ppermute | solution.py:55
  149.0 7.5 %collective-permute-start.14 = (f32[576,128]{1,0:T(8,128)S(1)}, f32[576,128]{1,0:T(8,128)S(1)}, u32[]{:S(2)}, u32[]{:S(2)}) collective-permute-start(f32[576,128]{1,0:T(8,128)S(1)} %get-tuple-element.78), channel_id=1, source_target_pairs={{0,64},{64,0},{128,192},{192,128},{1,65},{65,1},{129,193},{193,129... | collective-permute-start | bytes 884744 | tf_op jit(solution)/shard_map/ppermute | solution.py:55
  156.7 10.0 %collective-permute-start.15 = (f32[1152,128]{1,0:T(8,128)S(1)}, f32[1152,128]{1,0:T(8,128)S(1)}, u32[]{:S(2)}, u32[]{:S(2)}) collective-permute-start(f32[1152,128]{1,0:T(8,128)S(1)} %get-tuple-element.64), channel_id=1, source_target_pairs={{0,1},{1,0},{2,3},{3,2},{4,5},{5,4},{6,7},{7,6},{8,9},{9,8},{10,11... | collective-permute-start | bytes 1769480 | tf_op jit(solution)/shard_map/ppermute | solution.py:55

commit v9 on v7

--- a/solution.py
+++ b/solution.py
@@ -19,25 +19,25 @@
     return array
 
 
-def halving_steps():
-    steps = [("batch", 1)]
-    for axis in ("row", "col"):
-        d = 1
-        while d < lax.axis_size(axis):
-            steps.append((axis, d))
-            d *= 2
+def halving_stages():
+    stages = [("batch", 1), ("row", 0)]
     d = 2
     while d < lax.axis_size("batch"):
-        steps.append(("batch", d))
+        stages.append(("batch", d))
         d *= 2
-    return steps
+    return stages + [("col", 0)]
 
 
 def tree_sum(x, rider):
-    steps = halving_steps()
-    for step, (axis, d) in enumerate(steps):
-        if step == 2:
+    stages = halving_stages()
+    for stage, (axis, d) in enumerate(stages):
+        if stage == 2:
             x, rider = lax.optimization_barrier((x, rider))
+        if d == 0:
+            n = lax.axis_size(axis)
+            parts = x.reshape(n, x.shape[0] // n, x.shape[1])
+            x = lax.all_to_all(parts, axis, 0, 0, tiled=True).sum(0)
+            continue
         pairs = [(i, i ^ d) for i in range(lax.axis_size(axis))]
         upper = (lax.axis_index(axis) // d) % 2 == 1
         half = x.shape[0] // 2
@@ -45,7 +45,12 @@
         kept = lax.dynamic_slice_in_dim(x, side * half, half)
         sent = lax.dynamic_slice_in_dim(x, (1 - side) * half, half)
         x = kept + lax.ppermute(sent, axis, pairs)
-    for axis, d in steps[::-1]:
+    for axis, d in stages[::-1]:
+        if d == 0:
+            n = lax.axis_size(axis)
+            copies = jnp.broadcast_to(x[None], (n,) + x.shape)
+            x = lax.all_to_all(copies, axis, 0, 0, tiled=True).reshape(-1, x.shape[1])
+            continue
         pairs = [(i, i ^ d) for i in range(lax.axis_size(axis))]
         upper = (lax.axis_index(axis) // d) % 2 == 1
         got = lax.ppermute(x, axis, pairs)

time: 182 us -> 169 us (0.929)
  blocking collectives: 0 us -> 36.6 us
  starting transfers between devices: 84 us -> 52.4 us
  waiting for transfers between devices: 47 us -> 28 us
    all_to_all x0 -> x3, blocking collectives: none -> 36.6 us  [the longest x2 20.2 us: tree_sum(): x = lax.all_to_all(copies, axis, 0, 0, tiled=True).reshape(-1, x.shape[1])]
    ppermute x8 -> x2, starting transfers between devices: 30 us -> 10.1 us  [tree_sum(): got = lax.ppermute(x, axis, pairs)]
    ppermute x8 -> x2, starting transfers between devices: 23.4 us -> 7.46 us  [tree_sum(): x = kept + lax.ppermute(sent, axis, pairs)]
    ppermute x8 -> x2, waiting for transfers between devices: 19.5 us -> 3.89 us  [tree_sum(): got = lax.ppermute(x, axis, pairs)]
    ppermute x8 -> x2, waiting for transfers between devices: 16 us -> 3.73 us  [tree_sum(): x = kept + lax.ppermute(sent, axis, pairs)]
    ppermute x4, waiting for transfers between devices: 1.29 us -> 7.77 us  [with_halo(): before = lax.ppermute(last, axis, up)]
    all_to_all x0 -> x1, waiting for transfers between devices: none -> 5.05 us  [tree_sum(): x = lax.all_to_all(parts, axis, 0, 0, tiled=True).sum(0)]
    all_to_all x0 -> x1, starting transfers between devices: none -> 3.89 us  [tree_sum(): x = lax.all_to_all(parts, axis, 0, 0, tiled=True).sum(0)]
  transfers between devices with their start and end apart: 25 -> 14, of which waited for: 20 -> 9; matrix products, arithmetic and copies ran while one was open for 10% -> 17% of each run, Pallas kernels for 0% -> 0%
where the time goes in v9:
time: 169 us; the launch traced here: 168 us
  starting transfers between devices  52.4 us (31%)
  blocking collectives  36.6 us (22%)
  waiting for transfers between devices  28 us (17%)
  matrix products  20.9 us (12%)
  local copies, waits for them, and re-layouts  16.7 us (10%)
  other arithmetic  12.2 us (7%)
    all_to_all x2, blocking collectives, tree_sum(): x = lax.all_to_all(copies, axis, 0, 0, tiled=True).reshape(-1, x.shape[1])  20.2 us
    all_to_all x1, blocking collectives, tree_sum(): x = lax.all_to_all(parts, axis, 0, 0, tiled=True).sum(0)  16.5 us
    all_to_all x1, starting transfers between devices, on_device(): lax.all_to_all(payload, ('row', 'col'), split_axis=0, concat_axis=0, tile...  13.5 us
    unnamed x44, local copies, waits for them, and re-layouts  12.3 us
    ppermute x4, starting transfers between devices, with_halo(): before = lax.ppermute(last, axis, up)  12.1 us
    ppermute x2, starting transfers between devices, tree_sum(): got = lax.ppermute(x, axis, pairs)  10.1 us
    ppermute x4, waiting for transfers between devices, with_halo(): before = lax.ppermute(last, axis, up)  7.77 us
    ppermute x4, waiting for transfers between devices, with_halo(): after = lax.ppermute(leading, axis, down)  7.57 us
  transfers between devices with their start and end apart: 14, of which 9 were waited for; matrix products, arithmetic and copies ran while one was open for 17% of the time, Pallas kernels for 0%

profile of v9, /device:TPU:1, one launch (start us, length us, event | category | flops | bytes accessed | tf_op | source)
XLA Modules:
  0.0 168.3 jit_solution(14591755791064553235)
XLA Ops:
  0.6 0.8 slice_bitcast_fusion.1
  1.5 3.9 %collective-permute-start.4 = (bf16[2,64,128]{2,1,0:T(8,128)(2,1)S(1)}, bf16[2,64,128]{2,1,0:T(8,128)(2,1)S(1)}, u32[]{:S(2)}, u32[]{:S(2)}) collective-permute-start(bf16[2,64,128]{2,1,0:T(8,128)(2,1)S(1)} %get-tuple-element.70), channel_id=1, source_target_pairs={{0,64},{64,128},{128,192},{1,65},{65,129},{129,193},{2,66},{66,130... | collective-permute-start | bytes 98312 | tf_op jit(solution)/shard_map/ppermute | solution.py:16
  5.4 1.3 collective-permute-start.5
  6.7 0.6 compare_reduce_fusion
  7.4 0.6 compare_reduce_fusion.1
  8.0 0.7 reduce.16
  8.7 1.5 reduce-window.6
  10.7 1.3 broadcast_select_fusion
  12.0 1.4 broadcast_select_fusion.1
  13.4 0.7 fusion.2
  14.3 2.7 %fusion.8 = f32[1280,128]{1,0:T(8,128)S(1)} fusion(bf16[512,128]{1,0:T(8,128)(2,1)} %param.18, s32[640]{0:T(1024)S(1)} %add_add_fusion, bf16[1,640,512]{2,1,0:T(8,128)(2,1)S(1)} %copy-done), kind=kOutput, calls=%fused_computation.16 | convolution fusion | flops 1008107520 | bytes 1444352 | tf_op jit(solution)/shard_map/dot_general | solution.py:98
  17.1 1.0 select_maximum_fusion
  18.1 13.5 %all-to-all-start = ((f32[64,21,128]{2,1,0:T(8,128)}), f32[64,21,128]{2,1,0:T(8,128)S(1)}, u32[]{:S(2)}, u32[]{:S(2)}) async-start(f32[64,21,128]{2,1,0:T(8,128)} %select_maximum_fusion), calls=%async_computation | async-start | bytes 1572864 | tf_op jit(solution)/shard_map/all_to_all | solution.py:106
  32.1 2.9 %collective-permute-start.6 = (bf16[36,2,128]{2,1,0:T(2,128)(2,1)S(1)}, bf16[36,2,128]{2,1,0:T(2,128)(2,1)S(1)}, u32[]{:S(2)}, u32[]{:S(2)}) collective-permute-start(bf16[36,2,128]{2,1,0:T(2,128)(2,1)S(1)} %get-tuple-element.67), channel_id=1, source_target_pairs={{0,4},{4,8},{8,12},{12,16},{16,20},{20,24},{24,28},{28,32},{32,36}... | collective-permute-start | bytes 55304 | tf_op jit(solution)/shard_map/ppermute | solution.py:16
  35.0 1.3 collective-permute-start.7
  36.4 7.8 %collective-permute-done.6 = bf16[36,2,128]{2,1,0:T(2,128)(2,1)S(1)} collective-permute-done((bf16[36,2,128]{2,1,0:T(2,128)(2,1)S(1)}, bf16[36,2,128]{2,1,0:T(2,128)(2,1)S(1)}, u32[]{:S(2)}, u32[]{:S(2)}) %collective-permute-start.6) | collective-permute-done | bytes 18464 | tf_op jit(solution)/shard_map/ppermute | solution.py:16
  44.1 4.5 %collective-permute-done.7 = bf16[36,2,128]{2,1,0:T(2,128)(2,1)S(1)} collective-permute-done((bf16[36,2,128]{2,1,0:T(2,128)(2,1)S(1)}, bf16[36,2,128]{2,1,0:T(2,128)(2,1)S(1)}, u32[]{:S(2)}, u32[]{:S(2)}) %collective-permute-start.7) | collective-permute-done | bytes 18464 | tf_op jit(solution)/shard_map/ppermute | solution.py:17
  48.6 0.4 pad_maximum_fusion.1
  49.0 0.6 fusion.38
  49.5 0.9 constant_dynamic-update-slice_fusion.8
  50.4 0.9 constant_dynamic-update-slice_fusion.7
  51.3 0.9 constant_dynamic-update-slice_fusion.6
  52.2 0.9 constant_dynamic-update-slice_fusion.5
  53.0 0.9 constant_dynamic-update-slice_fusion.4
  53.9 0.9 constant_dynamic-update-slice_fusion.3
  54.8 0.9 constant_dynamic-update-slice_fusion.2
  55.7 0.9 constant_dynamic-update-slice_fusion.1
  56.6 1.1 reduce-precision_convert_fusion.1
  57.9 4.1 %fusion = f32[2048,384]{1,0:T(8,128)S(1)} fusion(f32[1280]{0:T(1024)S(1)} %eq.76, bf16[1280,128]{1,0:T(8,128)(2,1)} %get-tuple-element.60, bf16[1280,128]{1,0:T(8,128)(2,1)} %get-tuple-element.61, bf16[1280,128]{1,0:T(8,128)(2,1)} %get-tuple-element.59), kind=kOutput, calls=%fused_computation.1 | convolution fusion | flops 2018836480 | bytes 4133888 | tf_op jit(solution)/shard_map/dot_general | solution.py:117
  62.3 3.2 %collective-permute-start = (bf16[3,64,128]{2,1,0:T(8,128)(2,1)S(1)}, bf16[3,64,128]{2,1,0:T(8,128)(2,1)S(1)}, u32[]{:S(2)}, u32[]{:S(2)}) collective-permute-start(bf16[3,64,128]{2,1,0:T(8,128)(2,1)S(1)} %bitcast.141), channel_id=1, source_target_pairs={{0,64},{64,128},{128,192},{1,65},{65,129},{129,193},{2,66},{66,130... | collective-permute-start | bytes 147464 | tf_op jit(solution)/shard_map/ppermute | solution.py:16
  65.5 1.3 collective-permute-start.1
  66.8 0.9 constant_dynamic-update-slice_fusion
  67.7 2.6 %collective-permute-done.1 = bf16[3,64,128]{2,1,0:T(8,128)(2,1)S(1)} collective-permute-done((bf16[3,64,128]{2,1,0:T(8,128)(2,1)S(1)}, bf16[3,64,128]{2,1,0:T(8,128)(2,1)S(1)}, u32[]{:S(2)}, u32[]{:S(2)}) %collective-permute-start.1) | collective-permute-done | bytes 49184 | tf_op jit(solution)/shard_map/ppermute | solution.py:17
  70.3 2.1 %collective-permute-start.2 = (bf16[38,3,128]{2,1,0:T(4,128)(2,1)S(1)}, bf16[38,3,128]{2,1,0:T(4,128)(2,1)S(1)}, u32[]{:S(2)}, u32[]{:S(2)}) collective-permute-start(bf16[38,3,128]{2,1,0:T(4,128)(2,1)S(1)} %get-tuple-element.62), channel_id=1, source_target_pairs={{0,4},{4,8},{8,12},{12,16},{16,20},{20,24},{24,28},{28,32},{32,36}... | collective-permute-start | bytes 87560 | tf_op jit(solution)/shard_map/ppermute | solution.py:16
  72.4 1.5 collective-permute-start.3
  73.9 3.8 %convolution_add_fusion.1 = f32[2048,128]{1,0:T(8,128)S(1)} fusion(bf16[2048,1152]{1,0:T(8,128)(2,1)} %constant_dynamic-update-slice_fusion, bf16[1152,128]{1,0:T(8,128)(2,1)S(1)} %bitcast.131, bf16[2048,128]{1,0:T(8,128)(2,1)S(1)} %bitcast.113), kind=kOutput, calls=%fused_computation.8 | convolution fusion | flops 604504064 | bytes 6586368 | tf_op jit(solution)/shard_map/dot_general | solution.py:130
  77.6 0.5 collective-permute-done.3
  78.1 0.3 pad_maximum_fusion
  78.7 0.3 slice_dynamic-update-slice_fusion.7
  79.0 0.3 slice_dynamic-update-slice_fusion.6
  79.5 0.3 slice_dynamic-update-slice_fusion.4
  79.8 0.3 slice_dynamic-update-slice_fusion.3
  80.3 0.3 slice_dynamic-update-slice_fusion.1
  80.9 2.2 %select_convert_fusion = (bf16[36,68,128]{2,1,0:T(8,128)(2,1)S(1)}, f32[36,68,128]{2,1,0:T(8,128)S(1)}) fusion(pred[36,68]{1,0:T(8,128)(4,1)S(1)} %broadcast_and_fusion, bf16[36,68,1152]{2,1,0:T(8,128)(2,1)S(1)} %slice_dynamic-update-slice_fusion, bf16[1152,128,1]{1,0,2:T(8,128)(2,1)S(1)} %bitcast.143), kind=kOutput, calls=%fused_computation.17 | convolution fusion | flops 723824640 | bytes 7817616 | tf_op jit(solution)/shard_map/dot_general | solution.py:135
  83.9 0.3 fusion.37
  87.1 0.4 fusion.16
  87.6 1.4 fusion.42
  89.0 1.4 fusion.41
  90.6 4.8 %collective-permute-start.8 = (f32[1152,128]{1,0:T(8,128)S(1)}, f32[1152,128]{1,0:T(8,128)S(1)}, u32[]{:S(2)}, u32[]{:S(2)}) collective-permute-start(f32[1152,128]{1,0:T(8,128)S(1)} %constant_dynamic-slice_fusion.1), channel_id=1, source_target_pairs={{0,1},{1,0},{2,3},{3,2},{4,5},{5,4},{6,7},{7,6},{8,9},{9,8},{10,11... | collective-permute-start | bytes 1769480 | tf_op jit(solution)/shard_map/ppermute | solution.py:47
  95.4 1.6 collective-permute-done.8
  97.0 0.9 dynamic-slice_add_fusion
  97.9 3.9 %all-to-all-start.1 = ((f32[4,288,128]{2,1,0:T(8,128)}), f32[4,288,128]{2,1,0:T(8,128)S(1)}, u32[]{:S(2)}, u32[]{:S(2)}) async-start(f32[4,288,128]{2,1,0:T(8,128)} %bitcast.27), calls=%async_computation.1 | async-start | bytes 1179648 | tf_op jit(solution)/shard_map/all_to_all | solution.py:39
  101.8 4.6 %fusion.5 = bf16[2048,128]{1,0:T(8,128)(2,1)} fusion(bf16[2048,1152]{1,0:T(8,128)(2,1)} %bitcast.117, bf16[1152,128]{1,0:T(8,128)(2,1)} %bitcast.136, bf16[2048,128]{1,0:T(8,128)(2,1)S(1)} %bitcast.135), kind=kOutput, calls=%fused_computation.9 | convolution fusion | flops 604766208 | bytes 6062080 | tf_op jit(solution)/shard_map/dot_general | solution.py:163
  106.3 5.0 %all-to-all-done.1 = f32[4,288,128]{2,1,0:T(8,128)S(1)} async-done(((f32[4,288,128]{2,1,0:T(8,128)}), f32[4,288,128]{2,1,0:T(8,128)S(1)}, u32[]{:S(2)}, u32[]{:S(2)}) %all-to-all-start.1) | async-done | bytes 589856 | tf_op jit(solution)/shard_map/all_to_all | solution.py:39
  111.5 2.7 %collective-permute-start.9 = (f32[144,128]{1,0:T(8,128)S(1)}, f32[144,128]{1,0:T(8,128)S(1)}, u32[]{:S(2)}, u32[]{:S(2)}) collective-permute-start(f32[144,128]{1,0:T(8,128)S(1)} %constant_dynamic-slice_fusion), channel_id=1, source_target_pairs={{0,2},{1,3},{2,0},{3,1},{4,6},{5,7},{6,4},{7,5},{8,10},{9,11},{10,... | collective-permute-start | bytes 221192 | tf_op jit(solution)/shard_map/ppermute | solution.py:47
  114.1 2.1 %collective-permute-done.9 = f32[144,128]{1,0:T(8,128)S(1)} collective-permute-done((f32[144,128]{1,0:T(8,128)S(1)}, f32[144,128]{1,0:T(8,128)S(1)}, u32[]{:S(2)}, u32[]{:S(2)}) %collective-permute-start.9) | collective-permute-done | bytes 73760 | tf_op jit(solution)/shard_map/ppermute | solution.py:47
  116.3 16.5 %all_to_all.25 = f32[16,9,128]{2,1,0:T(8,128)S(1)} all-to-all(f32[16,9,128]{2,1,0:T(8,128)S(1)} %reshape.345), channel_id=1, replica_groups=mesh['row'=4,'col'=16,'batch'=4] {'col'}, dimensions={0} | all-to-all | bytes 147456 | tf_op jit(solution)/shard_map/all_to_all | solution.py:39
  132.8 10.5 %all_to_all.26 = f32[16,9,128]{2,1,0:T(8,128)S(1)} all-to-all(f32[16,9,128]{2,1,0:T(8,128)S(1)} %broadcast_in_dim.18), channel_id=1, replica_groups=mesh['row'=4,'col'=16,'batch'=4] {'col'}, dimensions={0} | all-to-all | bytes 147456 | tf_op jit(solution)/shard_map/all_to_all | solution.py:52
  143.3 2.7 %collective-permute-start.10 = (f32[144,128]{1,0:T(8,128)S(1)}, f32[144,128]{1,0:T(8,128)S(1)}, u32[]{:S(2)}, u32[]{:S(2)}) collective-permute-start(f32[144,128]{1,0:T(8,128)S(1)} %reshape.346), channel_id=1, source_target_pairs={{0,2},{1,3},{2,0},{3,1},{4,6},{5,7},{6,4},{7,5},{8,10},{9,11},{10,... | collective-permute-start | bytes 221192 | tf_op jit(solution)/shard_map/ppermute | solution.py:56
  146.0 2.3 %collective-permute-done.10 = f32[144,128]{1,0:T(8,128)S(1)} collective-permute-done((f32[144,128]{1,0:T(8,128)S(1)}, f32[144,128]{1,0:T(8,128)S(1)}, u32[]{:S(2)}, u32[]{:S(2)}) %collective-permute-start.10) | collective-permute-done | bytes 73760 | tf_op jit(solution)/shard_map/ppermute | solution.py:56
  148.4 9.7 %all_to_all.27 = f32[4,288,128]{2,1,0:T(8,128)S(1)} all-to-all(f32[4,288,128]{2,1,0:T(8,128)S(1)} %broadcast_in_dim.19), channel_id=1, replica_groups=mesh['row'=4,'col'=16,'batch'=4] {'row'}, dimensions={0} | all-to-all | bytes 1179648 | tf_op jit(solution)/shard_map/all_to_all | solution.py:52
  158.0 7.4 %collective-permute-start.11 = (f32[1152,128]{1,0:T(8,128)S(1)}, f32[1152,128]{1,0:T(8,128)S(1)}, u32[]{:S(2)}, u32[]{:S(2)}) collective-permute-start(f32[1152,128]{1,0:T(8,128)S(1)} %bitcast.121), channel_id=1, source_target_pairs={{0,1},{1,0},{2,3},{3,2},{4,5},{5,4},{6,7},{7,6},{8,9},{9,8},{10,11... | collective-permute-start | bytes 1769480 | tf_op jit(solution)/shard_map/ppermute | solution.py:56
  165.5 1.6 collective-permute-done.11
  167.1 1.2 fusion.25
  (75 shorter events, 6.5 us)
Async XLA Ops:
  0.6 13.7 %copy-start = (bf16[1,640,512]{2,1,0:T(8,128)(2,1)S(1)}, bf16[1,640,512]{2,1,0:T(8,128)(2,1)}, u32[]{:S(2)}) copy-start(bf16[1,640,512]{2,1,0:T(8,128)(2,1)} %param.15) | copy-start | bytes 1966084
  1.5 30.5 %collective-permute-start.4 = (bf16[2,64,128]{2,1,0:T(8,128)(2,1)S(1)}, bf16[2,64,128]{2,1,0:T(8,128)(2,1)S(1)}, u32[]{:S(2)}, u32[]{:S(2)}) collective-permute-start(bf16[2,64,128]{2,1,0:T(8,128)(2,1)S(1)} %get-tuple-element.70), channel_id=1, source_target_pairs={{0,64},{64,128},{128,192},{1,65},{65,129},{129,193},{2,66},{66,130... | collective-permute-start | bytes 98312 | tf_op jit(solution)/shard_map/ppermute | solution.py:16
  5.4 26.6 %collective-permute-start.5 = (bf16[2,64,128]{2,1,0:T(8,128)(2,1)S(1)}, bf16[2,64,128]{2,1,0:T(8,128)(2,1)S(1)}, u32[]{:S(2)}, u32[]{:S(2)}) collective-permute-start(bf16[2,64,128]{2,1,0:T(8,128)(2,1)S(1)} %get-tuple-element.71), channel_id=1, source_target_pairs={{64,0},{128,64},{192,128},{65,1},{129,65},{193,129},{66,2},{130,66... | collective-permute-start | bytes 98312 | tf_op jit(solution)/shard_map/ppermute | solution.py:17
  14.3 17.4 %copy-start.4 = (bf16[3,3,128,128]{3,2,1,0:T(8,128)(2,1)S(1)}, bf16[3,3,128,128]{3,2,1,0:T(8,128)(2,1)}, u32[]{:S(2)}) copy-start(bf16[3,3,128,128]{3,2,1,0:T(8,128)(2,1)} %param.20) | copy-start | bytes 884740
  14.3 17.7 %copy-start.1 = (bf16[1,32,64,128]{3,2,1,0:T(8,128)(2,1)S(1)}, bf16[1,32,64,128]{3,2,1,0:T(8,128)(2,1)}, u32[]{:S(2)}) copy-start(bf16[1,32,64,128]{3,2,1,0:T(8,128)(2,1)} %param.21) | copy-start | bytes 1572868
  18.1 38.5 %all-to-all-start = ((f32[64,21,128]{2,1,0:T(8,128)}), f32[64,21,128]{2,1,0:T(8,128)S(1)}, u32[]{:S(2)}, u32[]{:S(2)}) async-start(f32[64,21,128]{2,1,0:T(8,128)} %select_maximum_fusion), calls=%async_computation | async-start | bytes 1572864 | tf_op jit(solution)/shard_map/all_to_all | solution.py:106
  32.1 12.1 %collective-permute-start.6 = (bf16[36,2,128]{2,1,0:T(2,128)(2,1)S(1)}, bf16[36,2,128]{2,1,0:T(2,128)(2,1)S(1)}, u32[]{:S(2)}, u32[]{:S(2)}) collective-permute-start(bf16[36,2,128]{2,1,0:T(2,128)(2,1)S(1)} %get-tuple-element.67), channel_id=1, source_target_pairs={{0,4},{4,8},{8,12},{12,16},{16,20},{20,24},{24,28},{28,32},{32,36}... | collective-permute-start | bytes 55304 | tf_op jit(solution)/shard_map/ppermute | solution.py:16
  35.0 13.6 %collective-permute-start.7 = (bf16[36,2,128]{2,1,0:T(2,128)(2,1)S(1)}, bf16[36,2,128]{2,1,0:T(2,128)(2,1)S(1)}, u32[]{:S(2)}, u32[]{:S(2)}) collective-permute-start(bf16[36,2,128]{2,1,0:T(2,128)(2,1)S(1)} %get-tuple-element.66), channel_id=1, source_target_pairs={{4,0},{8,4},{12,8},{16,12},{20,16},{24,20},{28,24},{32,28},{36,32}... | collective-permute-start | bytes 55304 | tf_op jit(solution)/shard_map/ppermute | solution.py:17
  57.9 4.1 %copy-start.3 = (bf16[1,32,64,128]{3,2,1,0:T(8,128)(2,1)S(1)}, bf16[1,32,64,128]{3,2,1,0:T(8,128)(2,1)}, u32[]{:S(2)}) copy-start(bf16[1,32,64,128]{3,2,1,0:T(8,128)(2,1)} %param.14) | copy-start | bytes 1572868
  62.3 5.4 %collective-permute-start = (bf16[3,64,128]{2,1,0:T(8,128)(2,1)S(1)}, bf16[3,64,128]{2,1,0:T(8,128)(2,1)S(1)}, u32[]{:S(2)}, u32[]{:S(2)}) collective-permute-start(bf16[3,64,128]{2,1,0:T(8,128)(2,1)S(1)} %bitcast.141), channel_id=1, source_target_pairs={{0,64},{64,128},{128,192},{1,65},{65,129},{129,193},{2,66},{66,130... | collective-permute-start | bytes 147464 | tf_op jit(solution)/shard_map/ppermute | solution.py:16
  65.5 4.8 %collective-permute-start.1 = (bf16[3,64,128]{2,1,0:T(8,128)(2,1)S(1)}, bf16[3,64,128]{2,1,0:T(8,128)(2,1)S(1)}, u32[]{:S(2)}, u32[]{:S(2)}) collective-permute-start(bf16[3,64,128]{2,1,0:T(8,128)(2,1)S(1)} %bitcast.140), channel_id=1, source_target_pairs={{64,0},{128,64},{192,128},{65,1},{129,65},{193,129},{66,2},{130,66... | collective-permute-start | bytes 147464 | tf_op jit(solution)/shard_map/ppermute | solution.py:17
  70.3 7.3 %collective-permute-start.2 = (bf16[38,3,128]{2,1,0:T(4,128)(2,1)S(1)}, bf16[38,3,128]{2,1,0:T(4,128)(2,1)S(1)}, u32[]{:S(2)}, u32[]{:S(2)}) collective-permute-start(bf16[38,3,128]{2,1,0:T(4,128)(2,1)S(1)} %get-tuple-element.62), channel_id=1, source_target_pairs={{0,4},{4,8},{8,12},{12,16},{16,20},{20,24},{24,28},{28,32},{32,36}... | collective-permute-start | bytes 87560 | tf_op jit(solution)/shard_map/ppermute | solution.py:16
  72.4 5.7 %collective-permute-start.3 = (bf16[38,3,128]{2,1,0:T(4,128)(2,1)S(1)}, bf16[38,3,128]{2,1,0:T(4,128)(2,1)S(1)}, u32[]{:S(2)}, u32[]{:S(2)}) collective-permute-start(bf16[38,3,128]{2,1,0:T(4,128)(2,1)S(1)} %get-tuple-element.63), channel_id=1, source_target_pairs={{4,0},{8,4},{12,8},{16,12},{20,16},{24,20},{28,24},{32,28},{36,32}... | collective-permute-start | bytes 87560 | tf_op jit(solution)/shard_map/ppermute | solution.py:17
  79.0 1.9 %copy-start.5 = (bf16[3,3,128,128]{3,2,1,0:T(8,128)(2,1)S(1)}, bf16[3,3,128,128]{3,2,1,0:T(8,128)(2,1)}, u32[]{:S(2)}) copy-start(bf16[3,3,128,128]{3,2,1,0:T(8,128)(2,1)} %param.19) | copy-start | bytes 884740
  85.1 2.4 %copy-start.2 = (bf16[32,64,1152]{2,1,0:T(8,128)(2,1)}, bf16[32,64,1152]{2,1,0:T(8,128)(2,1)S(1)}, u32[]{:S(2)}) copy-start(bf16[32,64,1152]{2,1,0:T(8,128)(2,1)S(1)} %slice_dynamic-update-slice_fusion.9) | copy-start | bytes 14155780
  90.6 6.4 %collective-permute-start.8 = (f32[1152,128]{1,0:T(8,128)S(1)}, f32[1152,128]{1,0:T(8,128)S(1)}, u32[]{:S(2)}, u32[]{:S(2)}) collective-permute-start(f32[1152,128]{1,0:T(8,128)S(1)} %constant_dynamic-slice_fusion.1), channel_id=1, source_target_pairs={{0,1},{1,0},{2,3},{3,2},{4,5},{5,4},{6,7},{7,6},{8,9},{9,8},{10,11... | collective-permute-start | bytes 1769480 | tf_op jit(solution)/shard_map/ppermute | solution.py:47
  97.9 13.5 %all-to-all-start.1 = ((f32[4,288,128]{2,1,0:T(8,128)}), f32[4,288,128]{2,1,0:T(8,128)S(1)}, u32[]{:S(2)}, u32[]{:S(2)}) async-start(f32[4,288,128]{2,1,0:T(8,128)} %bitcast.27), calls=%async_computation.1 | async-start | bytes 1179648 | tf_op jit(solution)/shard_map/all_to_all | solution.py:39
  111.5 4.8 %collective-permute-start.9 = (f32[144,128]{1,0:T(8,128)S(1)}, f32[144,128]{1,0:T(8,128)S(1)}, u32[]{:S(2)}, u32[]{:S(2)}) collective-permute-start(f32[144,128]{1,0:T(8,128)S(1)} %constant_dynamic-slice_fusion), channel_id=1, source_target_pairs={{0,2},{1,3},{2,0},{3,1},{4,6},{5,7},{6,4},{7,5},{8,10},{9,11},{10,... | collective-permute-start | bytes 221192 | tf_op jit(solution)/shard_map/ppermute | solution.py:47
  143.3 5.0 %collective-permute-start.10 = (f32[144,128]{1,0:T(8,128)S(1)}, f32[144,128]{1,0:T(8,128)S(1)}, u32[]{:S(2)}, u32[]{:S(2)}) collective-permute-start(f32[144,128]{1,0:T(8,128)S(1)} %reshape.346), channel_id=1, source_target_pairs={{0,2},{1,3},{2,0},{3,1},{4,6},{5,7},{6,4},{7,5},{8,10},{9,11},{10,... | collective-permute-start | bytes 221192 | tf_op jit(solution)/shard_map/ppermute | solution.py:56
  158.0 9.1 %collective-permute-start.11 = (f32[1152,128]{1,0:T(8,128)S(1)}, f32[1152,128]{1,0:T(8,128)S(1)}, u32[]{:S(2)}, u32[]{:S(2)}) collective-permute-start(f32[1152,128]{1,0:T(8,128)S(1)} %bitcast.121), channel_id=1, source_target_pairs={{0,1},{1,0},{2,3},{3,2},{4,5},{5,4},{6,7},{7,6},{8,9},{9,8},{10,11... | collective-permute-start | bytes 1769480 | tf_op jit(solution)/shard_map/ppermute | solution.py:56

commit v10 on v7

--- a/solution.py
+++ b/solution.py
@@ -20,16 +20,12 @@
 
 
 def halving_steps():
-    steps = [("batch", 1)]
-    for axis in ("row", "col"):
+    steps = []
+    for axis in ("batch", "row"):
         d = 1
         while d < lax.axis_size(axis):
             steps.append((axis, d))
             d *= 2
-    d = 2
-    while d < lax.axis_size("batch"):
-        steps.append(("batch", d))
-        d *= 2
     return steps
 
 
@@ -45,6 +41,11 @@
         kept = lax.dynamic_slice_in_dim(x, side * half, half)
         sent = lax.dynamic_slice_in_dim(x, (1 - side) * half, half)
         x = kept + lax.ppermute(sent, axis, pairs)
+    spread_over = lax.axis_size("col")
+    parts = x.reshape(spread_over, x.shape[0] // spread_over, x.shape[1])
+    x = lax.all_to_all(parts, "col", 0, 0, tiled=True).sum(0)
+    copies = jnp.broadcast_to(x[None], (spread_over,) + x.shape)
+    x = lax.all_to_all(copies, "col", 0, 0, tiled=True).reshape(-1, x.shape[1])
     for axis, d in steps[::-1]:
         pairs = [(i, i ^ d) for i in range(lax.axis_size(axis))]
         upper = (lax.axis_index(axis) // d) % 2 == 1

time: 182 us -> 167 us (0.918)
  starting transfers between devices: 84 us -> 55.4 us
  blocking collectives: 0 us -> 27.1 us
  waiting for transfers between devices: 47 us -> 34.3 us
    all_to_all x0 -> x2, blocking collectives: none -> 27.1 us  [the longest x1 16.4 us: tree_sum(): x = lax.all_to_all(parts, 'col', 0, 0, tiled=True).sum(0)]
    ppermute x8 -> x4, starting transfers between devices: 30 us -> 14.4 us  [tree_sum(): got = lax.ppermute(x, axis, pairs)]
    ppermute x8 -> x4, starting transfers between devices: 23.4 us -> 10.4 us  [tree_sum(): x = kept + lax.ppermute(sent, axis, pairs)]
    ppermute x8 -> x4, waiting for transfers between devices: 19.5 us -> 12.9 us  [tree_sum(): got = lax.ppermute(x, axis, pairs)]
    ppermute x8 -> x4, waiting for transfers between devices: 16 us -> 9.91 us  [tree_sum(): x = kept + lax.ppermute(sent, axis, pairs)]
  transfers between devices with their start and end apart: 25 -> 17, of which waited for: 20 -> 12; matrix products, arithmetic and copies ran while one was open for 10% -> 11% of each run, Pallas kernels for 0% -> 0%
where the time goes in v10:
time: 167 us
  starting transfers between devices  55.4 us (33%)
  waiting for transfers between devices  34.3 us (21%)
  blocking collectives  27.1 us (16%)
  matrix products  20.9 us (13%)
  local copies, waits for them, and re-layouts  15.9 us (10%)
  other arithmetic  11.8 us (7%)
    all_to_all x1, blocking collectives, tree_sum(): x = lax.all_to_all(parts, 'col', 0, 0, tiled=True).sum(0)  16.4 us
    ppermute x4, starting transfers between devices, tree_sum(): got = lax.ppermute(x, axis, pairs)  14.4 us
    all_to_all x1, starting transfers between devices, on_device(): lax.all_to_all(payload, ('row', 'col'), split_axis=0, concat_axis=0, tile...  13.5 us
    ppermute x4, waiting for transfers between devices, tree_sum(): got = lax.ppermute(x, axis, pairs)  12.9 us
    unnamed x44, local copies, waits for them, and re-layouts  12.4 us
    ppermute x4, starting transfers between devices, with_halo(): before = lax.ppermute(last, axis, up)  11.8 us
    all_to_all x1, blocking collectives, tree_sum(): x = lax.all_to_all(copies, 'col', 0, 0, tiled=True).reshape(-1, x.shape[1])  10.7 us
    ppermute x4, starting transfers between devices, tree_sum(): x = kept + lax.ppermute(sent, axis, pairs)  10.4 us
  transfers between devices with their start and end apart: 17, of which 12 were waited for; matrix products, arithmetic and copies ran while one was open for 11% of the time, Pallas kernels for 0%

profile of v10, /device:TPU:1, one launch (start us, length us, event | category | flops | bytes accessed | tf_op | source)
XLA Modules:
  0.0 166.8 jit_solution(15263850796635466742)
XLA Ops:
  0.6 0.6 compare_reduce_fusion
  1.3 0.6 compare_reduce_fusion.1
  1.9 0.7 reduce.16
  2.6 1.5 reduce-window.6
  4.6 1.3 broadcast_select_fusion
  5.9 1.4 broadcast_select_fusion.1
  7.4 0.7 fusion.2
  8.2 2.7 %fusion.8 = f32[1280,128]{1,0:T(8,128)S(1)} fusion(bf16[512,128]{1,0:T(8,128)(2,1)} %param.18, s32[640]{0:T(1024)S(1)} %add_add_fusion, bf16[1,640,512]{2,1,0:T(8,128)(2,1)S(1)} %copy-done), kind=kOutput, calls=%fused_computation.16 | convolution fusion | flops 1008107520 | bytes 1444352 | tf_op jit(solution)/shard_map/dot_general | solution.py:94
  11.0 1.0 select_maximum_fusion
  12.0 13.5 %all-to-all-start = ((f32[64,21,128]{2,1,0:T(8,128)}), f32[64,21,128]{2,1,0:T(8,128)S(1)}, u32[]{:S(2)}, u32[]{:S(2)}) async-start(f32[64,21,128]{2,1,0:T(8,128)} %select_maximum_fusion), calls=%async_computation | async-start | bytes 1572864 | tf_op jit(solution)/shard_map/all_to_all | solution.py:102
  25.5 2.9 %collective-permute-start.4 = (bf16[2,64,128]{2,1,0:T(8,128)(2,1)S(1)}, bf16[2,64,128]{2,1,0:T(8,128)(2,1)S(1)}, u32[]{:S(2)}, u32[]{:S(2)}) collective-permute-start(bf16[2,64,128]{2,1,0:T(8,128)(2,1)S(1)} %get-tuple-element.74), channel_id=1, source_target_pairs={{0,64},{64,128},{128,192},{1,65},{65,129},{129,193},{2,66},{66,130... | collective-permute-start | bytes 98312 | tf_op jit(solution)/shard_map/ppermute | solution.py:16
  28.5 1.3 collective-permute-start.5
  30.2 3.7 %collective-permute-done.5 = bf16[2,64,128]{2,1,0:T(8,128)(2,1)S(1)} collective-permute-done((bf16[2,64,128]{2,1,0:T(8,128)(2,1)S(1)}, bf16[2,64,128]{2,1,0:T(8,128)(2,1)S(1)}, u32[]{:S(2)}, u32[]{:S(2)}) %collective-permute-start.5) | collective-permute-done | bytes 32800 | tf_op jit(solution)/shard_map/ppermute | solution.py:17
  33.9 2.7 %collective-permute-start.6 = (bf16[36,2,128]{2,1,0:T(2,128)(2,1)S(1)}, bf16[36,2,128]{2,1,0:T(2,128)(2,1)S(1)}, u32[]{:S(2)}, u32[]{:S(2)}) collective-permute-start(bf16[36,2,128]{2,1,0:T(2,128)(2,1)S(1)} %get-tuple-element.71), channel_id=1, source_target_pairs={{0,4},{4,8},{8,12},{12,16},{16,20},{20,24},{24,28},{28,32},{32,36}... | collective-permute-start | bytes 55304 | tf_op jit(solution)/shard_map/ppermute | solution.py:16
  36.6 1.3 collective-permute-start.7
  37.9 1.3 collective-permute-done.6
  39.2 3.9 %collective-permute-done.7 = bf16[36,2,128]{2,1,0:T(2,128)(2,1)S(1)} collective-permute-done((bf16[36,2,128]{2,1,0:T(2,128)(2,1)S(1)}, bf16[36,2,128]{2,1,0:T(2,128)(2,1)S(1)}, u32[]{:S(2)}, u32[]{:S(2)}) %collective-permute-start.7) | collective-permute-done | bytes 18464 | tf_op jit(solution)/shard_map/ppermute | solution.py:17
  43.1 0.4 pad_maximum_fusion.1
  43.4 0.6 fusion.49
  44.0 0.9 constant_dynamic-update-slice_fusion.8
  44.9 0.9 constant_dynamic-update-slice_fusion.7
  45.8 0.9 constant_dynamic-update-slice_fusion.6
  46.7 0.9 constant_dynamic-update-slice_fusion.5
  47.5 0.9 constant_dynamic-update-slice_fusion.4
  48.4 0.9 constant_dynamic-update-slice_fusion.3
  49.3 0.9 constant_dynamic-update-slice_fusion.2
  50.1 0.9 constant_dynamic-update-slice_fusion.1
  51.1 1.1 reduce-precision_convert_fusion.1
  52.4 4.1 %fusion = f32[2048,384]{1,0:T(8,128)S(1)} fusion(f32[1280]{0:T(1024)S(1)} %eq.88, bf16[1280,128]{1,0:T(8,128)(2,1)} %get-tuple-element.60, bf16[1280,128]{1,0:T(8,128)(2,1)} %get-tuple-element.61, bf16[1280,128]{1,0:T(8,128)(2,1)} %get-tuple-element.59), kind=kOutput, calls=%fused_computation.1 | convolution fusion | flops 2018836480 | bytes 4133888 | tf_op jit(solution)/shard_map/dot_general | solution.py:113
  56.8 3.2 %collective-permute-start = (bf16[3,64,128]{2,1,0:T(8,128)(2,1)S(1)}, bf16[3,64,128]{2,1,0:T(8,128)(2,1)S(1)}, u32[]{:S(2)}, u32[]{:S(2)}) collective-permute-start(bf16[3,64,128]{2,1,0:T(8,128)(2,1)S(1)} %bitcast.154), channel_id=1, source_target_pairs={{0,64},{64,128},{128,192},{1,65},{65,129},{129,193},{2,66},{66,130... | collective-permute-start | bytes 147464 | tf_op jit(solution)/shard_map/ppermute | solution.py:16
  60.0 1.3 collective-permute-start.1
  61.3 0.9 constant_dynamic-update-slice_fusion
  62.2 2.6 %collective-permute-done.1 = bf16[3,64,128]{2,1,0:T(8,128)(2,1)S(1)} collective-permute-done((bf16[3,64,128]{2,1,0:T(8,128)(2,1)S(1)}, bf16[3,64,128]{2,1,0:T(8,128)(2,1)S(1)}, u32[]{:S(2)}, u32[]{:S(2)}) %collective-permute-start.1) | collective-permute-done | bytes 49184 | tf_op jit(solution)/shard_map/ppermute | solution.py:17
  64.8 3.0 %collective-permute-start.2 = (bf16[38,3,128]{2,1,0:T(4,128)(2,1)S(1)}, bf16[38,3,128]{2,1,0:T(4,128)(2,1)S(1)}, u32[]{:S(2)}, u32[]{:S(2)}) collective-permute-start(bf16[38,3,128]{2,1,0:T(4,128)(2,1)S(1)} %get-tuple-element.62), channel_id=1, source_target_pairs={{0,4},{4,8},{8,12},{12,16},{16,20},{20,24},{24,28},{28,32},{32,36}... | collective-permute-start | bytes 87560 | tf_op jit(solution)/shard_map/ppermute | solution.py:16
  67.9 1.5 collective-permute-start.3
  69.4 3.8 %convolution_add_fusion.1 = f32[2048,128]{1,0:T(8,128)S(1)} fusion(bf16[2048,1152]{1,0:T(8,128)(2,1)} %constant_dynamic-update-slice_fusion, bf16[1152,128]{1,0:T(8,128)(2,1)S(1)} %bitcast.142, bf16[2048,128]{1,0:T(8,128)(2,1)S(1)} %bitcast.126), kind=kOutput, calls=%fused_computation.8 | convolution fusion | flops 604504064 | bytes 6586368 | tf_op jit(solution)/shard_map/dot_general | solution.py:126
  73.1 0.3 pad_maximum_fusion
  73.8 0.3 slice_dynamic-update-slice_fusion.7
  74.1 0.3 slice_dynamic-update-slice_fusion.6
  76.0 2.2 %select_convert_fusion = (bf16[36,68,128]{2,1,0:T(8,128)(2,1)S(1)}, f32[36,68,128]{2,1,0:T(8,128)S(1)}) fusion(pred[36,68]{1,0:T(8,128)(4,1)S(1)} %broadcast_and_fusion, bf16[36,68,1152]{2,1,0:T(8,128)(2,1)S(1)} %slice_dynamic-update-slice_fusion, bf16[1152,128,1]{1,0,2:T(8,128)(2,1)S(1)} %bitcast.156), kind=kOutput, calls=%fused_computation.17 | convolution fusion | flops 723824640 | bytes 7817616 | tf_op jit(solution)/shard_map/dot_general | solution.py:131
  78.9 0.3 fusion.48
  82.2 0.4 fusion.16
  82.6 1.4 fusion.53
  84.0 1.4 fusion.52
  85.6 4.6 %collective-permute-start.8 = (f32[1152,128]{1,0:T(8,128)S(1)}, f32[1152,128]{1,0:T(8,128)S(1)}, u32[]{:S(2)}, u32[]{:S(2)}) collective-permute-start(f32[1152,128]{1,0:T(8,128)S(1)} %constant_dynamic-slice_fusion.3), channel_id=1, source_target_pairs={{0,1},{1,0},{2,3},{3,2},{4,5},{5,4},{6,7},{7,6},{8,9},{9,8},{10,11... | collective-permute-start | bytes 1769480 | tf_op jit(solution)/shard_map/ppermute | solution.py:43
  90.3 1.6 collective-permute-done.8
  92.0 2.7 %collective-permute-start.9 = (f32[576,128]{1,0:T(8,128)S(1)}, f32[576,128]{1,0:T(8,128)S(1)}, u32[]{:S(2)}, u32[]{:S(2)}) collective-permute-start(f32[576,128]{1,0:T(8,128)S(1)} %constant_dynamic-slice_fusion.2), channel_id=1, source_target_pairs={{0,2},{1,3},{2,0},{3,1},{4,6},{5,7},{6,4},{7,5},{8,10},{9,11},{10,... | collective-permute-start | bytes 884744 | tf_op jit(solution)/shard_map/ppermute | solution.py:43
  94.7 4.6 %fusion.5 = bf16[2048,128]{1,0:T(8,128)(2,1)} fusion(bf16[2048,1152]{1,0:T(8,128)(2,1)} %bitcast.130, bf16[1152,128]{1,0:T(8,128)(2,1)} %bitcast.147, bf16[2048,128]{1,0:T(8,128)(2,1)S(1)} %bitcast.146), kind=kOutput, calls=%fused_computation.9 | convolution fusion | flops 604766208 | bytes 6062080 | tf_op jit(solution)/shard_map/dot_general | solution.py:159
  99.3 2.5 %collective-permute-done.9 = f32[576,128]{1,0:T(8,128)S(1)} collective-permute-done((f32[576,128]{1,0:T(8,128)S(1)}, f32[576,128]{1,0:T(8,128)S(1)}, u32[]{:S(2)}, u32[]{:S(2)}) %collective-permute-start.9) | collective-permute-done | bytes 294944 | tf_op jit(solution)/shard_map/ppermute | solution.py:43
  101.8 1.4 collective-permute-start.10
  103.2 2.7 %collective-permute-done.10 = f32[288,128]{1,0:T(8,128)S(1)} collective-permute-done((f32[288,128]{1,0:T(8,128)S(1)}, f32[288,128]{1,0:T(8,128)S(1)}, u32[]{:S(2)}, u32[]{:S(2)}) %collective-permute-start.10) | collective-permute-done | bytes 147488 | tf_op jit(solution)/shard_map/ppermute | solution.py:43
  106.0 1.7 %collective-permute-start.11 = (f32[144,128]{1,0:T(8,128)S(1)}, f32[144,128]{1,0:T(8,128)S(1)}, u32[]{:S(2)}, u32[]{:S(2)}) collective-permute-start(f32[144,128]{1,0:T(8,128)S(1)} %constant_dynamic-slice_fusion), channel_id=1, source_target_pairs={{0,128},{64,192},{128,0},{192,64},{1,129},{65,193},{129,1},{193,65... | collective-permute-start | bytes 221192 | tf_op jit(solution)/shard_map/ppermute | solution.py:43
  107.7 3.1 %collective-permute-done.11 = f32[144,128]{1,0:T(8,128)S(1)} collective-permute-done((f32[144,128]{1,0:T(8,128)S(1)}, f32[144,128]{1,0:T(8,128)S(1)}, u32[]{:S(2)}, u32[]{:S(2)}) %collective-permute-start.11) | collective-permute-done | bytes 73760 | tf_op jit(solution)/shard_map/ppermute | solution.py:43
  110.8 16.4 %all_to_all.15 = f32[16,9,128]{2,1,0:T(8,128)S(1)} all-to-all(f32[16,9,128]{2,1,0:T(8,128)S(1)} %reshape.337), channel_id=1, replica_groups=mesh['row'=4,'col'=16,'batch'=4] {'col'}, dimensions={0} | all-to-all | bytes 147456 | tf_op jit(solution)/shard_map/all_to_all | solution.py:46
  127.2 10.7 %all_to_all.16 = f32[16,9,128]{2,1,0:T(8,128)S(1)} all-to-all(f32[16,9,128]{2,1,0:T(8,128)S(1)} %broadcast_in_dim.12), channel_id=1, replica_groups=mesh['row'=4,'col'=16,'batch'=4] {'col'}, dimensions={0} | all-to-all | bytes 147456 | tf_op jit(solution)/shard_map/all_to_all | solution.py:48
  138.0 1.8 %collective-permute-start.12 = (f32[144,128]{1,0:T(8,128)S(1)}, f32[144,128]{1,0:T(8,128)S(1)}, u32[]{:S(2)}, u32[]{:S(2)}) collective-permute-start(f32[144,128]{1,0:T(8,128)S(1)} %reshape.338), channel_id=1, source_target_pairs={{0,128},{64,192},{128,0},{192,64},{1,129},{65,193},{129,1},{193,65... | collective-permute-start | bytes 221192 | tf_op jit(solution)/shard_map/ppermute | solution.py:52
  139.8 3.3 %collective-permute-done.12 = f32[144,128]{1,0:T(8,128)S(1)} collective-permute-done((f32[144,128]{1,0:T(8,128)S(1)}, f32[144,128]{1,0:T(8,128)S(1)}, u32[]{:S(2)}, u32[]{:S(2)}) %collective-permute-start.12) | collective-permute-done | bytes 73760 | tf_op jit(solution)/shard_map/ppermute | solution.py:52
  143.1 1.1 collective-permute-start.13
  144.2 3.6 %collective-permute-done.13 = f32[288,128]{1,0:T(8,128)S(1)} collective-permute-done((f32[288,128]{1,0:T(8,128)S(1)}, f32[288,128]{1,0:T(8,128)S(1)}, u32[]{:S(2)}, u32[]{:S(2)}) %collective-permute-start.13) | collective-permute-done | bytes 147488 | tf_op jit(solution)/shard_map/ppermute | solution.py:52
  147.9 2.7 %collective-permute-start.14 = (f32[576,128]{1,0:T(8,128)S(1)}, f32[576,128]{1,0:T(8,128)S(1)}, u32[]{:S(2)}, u32[]{:S(2)}) collective-permute-start(f32[576,128]{1,0:T(8,128)S(1)} %get-tuple-element.78), channel_id=1, source_target_pairs={{0,2},{1,3},{2,0},{3,1},{4,6},{5,7},{6,4},{7,5},{8,10},{9,11},{10,... | collective-permute-start | bytes 884744 | tf_op jit(solution)/shard_map/ppermute | solution.py:52
  150.7 4.4 %collective-permute-done.14 = f32[576,128]{1,0:T(8,128)S(1)} collective-permute-done((f32[576,128]{1,0:T(8,128)S(1)}, f32[576,128]{1,0:T(8,128)S(1)}, u32[]{:S(2)}, u32[]{:S(2)}) %collective-permute-start.14) | collective-permute-done | bytes 294944 | tf_op jit(solution)/shard_map/ppermute | solution.py:52
  155.3 8.7 %collective-permute-start.15 = (f32[1152,128]{1,0:T(8,128)S(1)}, f32[1152,128]{1,0:T(8,128)S(1)}, u32[]{:S(2)}, u32[]{:S(2)}) collective-permute-start(f32[1152,128]{1,0:T(8,128)S(1)} %get-tuple-element.64), channel_id=1, source_target_pairs={{0,1},{1,0},{2,3},{3,2},{4,5},{5,4},{6,7},{7,6},{8,9},{9,8},{10,11... | collective-permute-start | bytes 1769480 | tf_op jit(solution)/shard_map/ppermute | solution.py:52
  164.0 1.6 collective-permute-done.15
  165.7 1.2 fusion.25
  (86 shorter events, 7.8 us)
Async XLA Ops:
  0.6 7.6 %copy-start = (bf16[1,640,512]{2,1,0:T(8,128)(2,1)S(1)}, bf16[1,640,512]{2,1,0:T(8,128)(2,1)}, u32[]{:S(2)}) copy-start(bf16[1,640,512]{2,1,0:T(8,128)(2,1)} %param.15) | copy-start | bytes 1966084
  8.2 17.3 %copy-start.1 = (bf16[1,32,64,128]{3,2,1,0:T(8,128)(2,1)S(1)}, bf16[1,32,64,128]{3,2,1,0:T(8,128)(2,1)}, u32[]{:S(2)}) copy-start(bf16[1,32,64,128]{3,2,1,0:T(8,128)(2,1)} %param.21) | copy-start | bytes 1572868
  8.2 21.6 %copy-start.4 = (bf16[3,3,128,128]{3,2,1,0:T(8,128)(2,1)S(1)}, bf16[3,3,128,128]{3,2,1,0:T(8,128)(2,1)}, u32[]{:S(2)}) copy-start(bf16[3,3,128,128]{3,2,1,0:T(8,128)(2,1)} %param.20) | copy-start | bytes 884740
  12.0 39.0 %all-to-all-start = ((f32[64,21,128]{2,1,0:T(8,128)}), f32[64,21,128]{2,1,0:T(8,128)S(1)}, u32[]{:S(2)}, u32[]{:S(2)}) async-start(f32[64,21,128]{2,1,0:T(8,128)} %select_maximum_fusion), calls=%async_computation | async-start | bytes 1572864 | tf_op jit(solution)/shard_map/all_to_all | solution.py:102
  25.5 4.6 %collective-permute-start.4 = (bf16[2,64,128]{2,1,0:T(8,128)(2,1)S(1)}, bf16[2,64,128]{2,1,0:T(8,128)(2,1)S(1)}, u32[]{:S(2)}, u32[]{:S(2)}) collective-permute-start(bf16[2,64,128]{2,1,0:T(8,128)(2,1)S(1)} %get-tuple-element.74), channel_id=1, source_target_pairs={{0,64},{64,128},{128,192},{1,65},{65,129},{129,193},{2,66},{66,130... | collective-permute-start | bytes 98312 | tf_op jit(solution)/shard_map/ppermute | solution.py:16
  28.5 5.4 %collective-permute-start.5 = (bf16[2,64,128]{2,1,0:T(8,128)(2,1)S(1)}, bf16[2,64,128]{2,1,0:T(8,128)(2,1)S(1)}, u32[]{:S(2)}, u32[]{:S(2)}) collective-permute-start(bf16[2,64,128]{2,1,0:T(8,128)(2,1)S(1)} %get-tuple-element.75), channel_id=1, source_target_pairs={{64,0},{128,64},{192,128},{65,1},{129,65},{193,129},{66,2},{130,66... | collective-permute-start | bytes 98312 | tf_op jit(solution)/shard_map/ppermute | solution.py:17
  33.9 5.3 %collective-permute-start.6 = (bf16[36,2,128]{2,1,0:T(2,128)(2,1)S(1)}, bf16[36,2,128]{2,1,0:T(2,128)(2,1)S(1)}, u32[]{:S(2)}, u32[]{:S(2)}) collective-permute-start(bf16[36,2,128]{2,1,0:T(2,128)(2,1)S(1)} %get-tuple-element.71), channel_id=1, source_target_pairs={{0,4},{4,8},{8,12},{12,16},{16,20},{20,24},{24,28},{28,32},{32,36}... | collective-permute-start | bytes 55304 | tf_op jit(solution)/shard_map/ppermute | solution.py:16
  36.6 6.5 %collective-permute-start.7 = (bf16[36,2,128]{2,1,0:T(2,128)(2,1)S(1)}, bf16[36,2,128]{2,1,0:T(2,128)(2,1)S(1)}, u32[]{:S(2)}, u32[]{:S(2)}) collective-permute-start(bf16[36,2,128]{2,1,0:T(2,128)(2,1)S(1)} %get-tuple-element.70), channel_id=1, source_target_pairs={{4,0},{8,4},{12,8},{16,12},{20,16},{24,20},{28,24},{32,28},{36,32}... | collective-permute-start | bytes 55304 | tf_op jit(solution)/shard_map/ppermute | solution.py:17
  52.4 4.1 %copy-start.3 = (bf16[1,32,64,128]{3,2,1,0:T(8,128)(2,1)S(1)}, bf16[1,32,64,128]{3,2,1,0:T(8,128)(2,1)}, u32[]{:S(2)}) copy-start(bf16[1,32,64,128]{3,2,1,0:T(8,128)(2,1)} %param.14) | copy-start | bytes 1572868
  56.8 5.4 %collective-permute-start = (bf16[3,64,128]{2,1,0:T(8,128)(2,1)S(1)}, bf16[3,64,128]{2,1,0:T(8,128)(2,1)S(1)}, u32[]{:S(2)}, u32[]{:S(2)}) collective-permute-start(bf16[3,64,128]{2,1,0:T(8,128)(2,1)S(1)} %bitcast.154), channel_id=1, source_target_pairs={{0,64},{64,128},{128,192},{1,65},{65,129},{129,193},{2,66},{66,130... | collective-permute-start | bytes 147464 | tf_op jit(solution)/shard_map/ppermute | solution.py:16
  60.0 4.8 %collective-permute-start.1 = (bf16[3,64,128]{2,1,0:T(8,128)(2,1)S(1)}, bf16[3,64,128]{2,1,0:T(8,128)(2,1)S(1)}, u32[]{:S(2)}, u32[]{:S(2)}) collective-permute-start(bf16[3,64,128]{2,1,0:T(8,128)(2,1)S(1)} %bitcast.153), channel_id=1, source_target_pairs={{64,0},{128,64},{192,128},{65,1},{129,65},{193,129},{66,2},{130,66... | collective-permute-start | bytes 147464 | tf_op jit(solution)/shard_map/ppermute | solution.py:17
  64.8 8.3 %collective-permute-start.2 = (bf16[38,3,128]{2,1,0:T(4,128)(2,1)S(1)}, bf16[38,3,128]{2,1,0:T(4,128)(2,1)S(1)}, u32[]{:S(2)}, u32[]{:S(2)}) collective-permute-start(bf16[38,3,128]{2,1,0:T(4,128)(2,1)S(1)} %get-tuple-element.62), channel_id=1, source_target_pairs={{0,4},{4,8},{8,12},{12,16},{16,20},{20,24},{24,28},{28,32},{32,36}... | collective-permute-start | bytes 87560 | tf_op jit(solution)/shard_map/ppermute | solution.py:16
  67.9 5.3 %collective-permute-start.3 = (bf16[38,3,128]{2,1,0:T(4,128)(2,1)S(1)}, bf16[38,3,128]{2,1,0:T(4,128)(2,1)S(1)}, u32[]{:S(2)}, u32[]{:S(2)}) collective-permute-start(bf16[38,3,128]{2,1,0:T(4,128)(2,1)S(1)} %get-tuple-element.63), channel_id=1, source_target_pairs={{4,0},{8,4},{12,8},{16,12},{20,16},{24,20},{28,24},{32,28},{36,32}... | collective-permute-start | bytes 87560 | tf_op jit(solution)/shard_map/ppermute | solution.py:17
  74.1 1.9 %copy-start.5 = (bf16[3,3,128,128]{3,2,1,0:T(8,128)(2,1)S(1)}, bf16[3,3,128,128]{3,2,1,0:T(8,128)(2,1)}, u32[]{:S(2)}) copy-start(bf16[3,3,128,128]{3,2,1,0:T(8,128)(2,1)} %param.19) | copy-start | bytes 884740
  80.1 2.4 %copy-start.2 = (bf16[32,64,1152]{2,1,0:T(8,128)(2,1)}, bf16[32,64,1152]{2,1,0:T(8,128)(2,1)S(1)}, u32[]{:S(2)}) copy-start(bf16[32,64,1152]{2,1,0:T(8,128)(2,1)S(1)} %slice_dynamic-update-slice_fusion.9) | copy-start | bytes 14155780
  85.6 6.2 %collective-permute-start.8 = (f32[1152,128]{1,0:T(8,128)S(1)}, f32[1152,128]{1,0:T(8,128)S(1)}, u32[]{:S(2)}, u32[]{:S(2)}) collective-permute-start(f32[1152,128]{1,0:T(8,128)S(1)} %constant_dynamic-slice_fusion.3), channel_id=1, source_target_pairs={{0,1},{1,0},{2,3},{3,2},{4,5},{5,4},{6,7},{7,6},{8,9},{9,8},{10,11... | collective-permute-start | bytes 1769480 | tf_op jit(solution)/shard_map/ppermute | solution.py:43
  92.0 9.8 %collective-permute-start.9 = (f32[576,128]{1,0:T(8,128)S(1)}, f32[576,128]{1,0:T(8,128)S(1)}, u32[]{:S(2)}, u32[]{:S(2)}) collective-permute-start(f32[576,128]{1,0:T(8,128)S(1)} %constant_dynamic-slice_fusion.2), channel_id=1, source_target_pairs={{0,2},{1,3},{2,0},{3,1},{4,6},{5,7},{6,4},{7,5},{8,10},{9,11},{10,... | collective-permute-start | bytes 884744 | tf_op jit(solution)/shard_map/ppermute | solution.py:43
  101.8 4.1 %collective-permute-start.10 = (f32[288,128]{1,0:T(8,128)S(1)}, f32[288,128]{1,0:T(8,128)S(1)}, u32[]{:S(2)}, u32[]{:S(2)}) collective-permute-start(f32[288,128]{1,0:T(8,128)S(1)} %constant_dynamic-slice_fusion.1), channel_id=1, source_target_pairs={{0,64},{64,0},{128,192},{192,128},{1,65},{65,1},{129,193},{193,129... | collective-permute-start | bytes 442376 | tf_op jit(solution)/shard_map/ppermute | solution.py:43
  106.0 4.8 %collective-permute-start.11 = (f32[144,128]{1,0:T(8,128)S(1)}, f32[144,128]{1,0:T(8,128)S(1)}, u32[]{:S(2)}, u32[]{:S(2)}) collective-permute-start(f32[144,128]{1,0:T(8,128)S(1)} %constant_dynamic-slice_fusion), channel_id=1, source_target_pairs={{0,128},{64,192},{128,0},{192,64},{1,129},{65,193},{129,1},{193,65... | collective-permute-start | bytes 221192 | tf_op jit(solution)/shard_map/ppermute | solution.py:43
  138.0 5.1 %collective-permute-start.12 = (f32[144,128]{1,0:T(8,128)S(1)}, f32[144,128]{1,0:T(8,128)S(1)}, u32[]{:S(2)}, u32[]{:S(2)}) collective-permute-start(f32[144,128]{1,0:T(8,128)S(1)} %reshape.338), channel_id=1, source_target_pairs={{0,128},{64,192},{128,0},{192,64},{1,129},{65,193},{129,1},{193,65... | collective-permute-start | bytes 221192 | tf_op jit(solution)/shard_map/ppermute | solution.py:52
  143.1 4.7 %collective-permute-start.13 = (f32[288,128]{1,0:T(8,128)S(1)}, f32[288,128]{1,0:T(8,128)S(1)}, u32[]{:S(2)}, u32[]{:S(2)}) collective-permute-start(f32[288,128]{1,0:T(8,128)S(1)} %get-tuple-element.82), channel_id=1, source_target_pairs={{0,64},{64,0},{128,192},{192,128},{1,65},{65,1},{129,193},{193,129... | collective-permute-start | bytes 442376 | tf_op jit(solution)/shard_map/ppermute | solution.py:52
  147.9 7.2 %collective-permute-start.14 = (f32[576,128]{1,0:T(8,128)S(1)}, f32[576,128]{1,0:T(8,128)S(1)}, u32[]{:S(2)}, u32[]{:S(2)}) collective-permute-start(f32[576,128]{1,0:T(8,128)S(1)} %get-tuple-element.78), channel_id=1, source_target_pairs={{0,2},{1,3},{2,0},{3,1},{4,6},{5,7},{6,4},{7,5},{8,10},{9,11},{10,... | collective-permute-start | bytes 884744 | tf_op jit(solution)/shard_map/ppermute | solution.py:52
  155.3 10.3 %collective-permute-start.15 = (f32[1152,128]{1,0:T(8,128)S(1)}, f32[1152,128]{1,0:T(8,128)S(1)}, u32[]{:S(2)}, u32[]{:S(2)}) collective-permute-start(f32[1152,128]{1,0:T(8,128)S(1)} %get-tuple-element.64), channel_id=1, source_target_pairs={{0,1},{1,0},{2,3},{3,2},{4,5},{5,4},{6,7},{7,6},{8,9},{9,8},{10,11... | collective-permute-start | bytes 1769480 | tf_op jit(solution)/shard_map/ppermute | solution.py:52
